TPU v7x, 32 devices: a whole 2x2x4 slice. The times are simulated.
32 devices in a mesh: dp: 8 (over z, core), tensor: 4 (over y, x).
Axes of the slice: x: 2, y: 2, z: 4, core: 2. Of those that a mesh axis runs over, the one named last changes fastest.
Arguments:
- context: bfloat16 [2048, 3072], P('dp', 'tensor'), may hold values from -6 to 6
- residual_in: bfloat16 [2048, 3072], P('dp', 'tensor'), may hold values from -6 to 6
- out_proj: bfloat16 [3072, 3072], P('tensor'), may hold values from -0.15625 to 0.15625
- members: int32 [2048, 1], P('dp'), may hold values from 0 to 7; in each aligned block of 256 rows (0 to 255, 256 to 511, ...) at most 40 rows name the same one
- host_group: int32 [8], replicated, may hold values from 0 to 7, each once
- member_proj: bfloat16 [8, 3072, 3072], P('dp', None, 'tensor'), may hold values from -0.15625 to 0.15625
- member_head: float32 [8, 3072], P('dp', 'tensor'), may hold values from -6 to 6
Outputs:
- generated: bfloat16 [2048, 3072], P('dp', 'tensor')
- input_grad: bfloat16 [2048, 3072], P('dp', 'tensor')
Inputs may be any that keep to these rules, and one draw needn't show every extreme that they name: `members`: within the rows of one dp group (256 rows), no member index is named by more than 40 rows, and in every draw some index is named by exactly 40 rows of some group. `host_group`: each member is hosted by a different dp group.
All inputs are finite; a program needn't handle non-finite values.
Results may differ from a plain program's by a relative error of at most 0.02.
Values may be sent and summed in bfloat16 or wider, within the bound.
No kernel may reach another device: no remote copies, remote signals or barrier semaphores. Data moves between devices by JAX's collectives and lax.ppermute only.
A program may use at most 64 MiB of HBM per device.

v0:
```python
from functools import partial

import jax
import jax.numpy as jnp
from jax import lax
from jax.sharding import PartitionSpec as P


def slope_times(values, weights):
    _, back_fn = jax.vjp(partial(jax.nn.gelu, approximate=True), values)
    return back_fn(weights)[0]


def shards(context, residual_in, out_proj, members, host_group, member_proj, member_head):
    tok_rows = context.shape[0]
    group_count = lax.axis_size("dp")
    capacity = max(2, (5 * tok_rows + 4 * group_count - 1) // (4 * group_count))
    slot_count = group_count * capacity
    projection = member_proj[0]
    summed = lax.psum_scatter(
        lax.dot_general(
            out_proj, context, (((0,), (1,)), ((), ())), preferred_element_type=jnp.float32
        ).astype(jnp.bfloat16),
        "tensor",
        scatter_dimension=0,
        tiled=True,
    ).astype(jnp.float32)
    fresh_cols = (summed + residual_in.astype(jnp.float32).T).astype(jnp.bfloat16)
    generated = fresh_cols.T
    group_ids = lax.iota(jnp.int32, group_count)
    member_ids = members[:, 0]
    destination = jnp.sum(
        jnp.where(member_ids[:, None] == group_ids[None, :], host_group[None, :], 0), axis=1
    )
    dest_hot = (destination[:, None] == group_ids[None, :]).astype(jnp.int32)
    earlier = jnp.cumsum(dest_hot, axis=0) - dest_hot
    rank_in = jnp.sum(earlier * dest_hot, axis=1)
    slot_of = destination * capacity + rank_in
    placing = (slot_of[:, None] == lax.iota(jnp.int32, slot_count)[None, :]).astype(jnp.bfloat16)
    whole = lax.all_gather(generated, "tensor", axis=1, tiled=True)
    outgoing = lax.dot_general(
        placing, whole, (((0,), (0,)), ((), ())), preferred_element_type=jnp.float32
    ).astype(jnp.bfloat16)
    arrived = lax.all_to_all(outgoing, "dp", split_axis=0, concat_axis=0, tiled=True)
    pre_act = jnp.dot(arrived, projection, preferred_element_type=jnp.float32)
    head_row = jnp.broadcast_to(member_head[0][None, :], pre_act.shape)
    pre_grad = (-slope_times(pre_act, head_row)).astype(jnp.bfloat16)
    critic_grad = lax.psum_scatter(
        lax.dot_general(
            projection, pre_grad, (((1,), (1,)), ((), ())), preferred_element_type=jnp.float32
        ).astype(jnp.bfloat16),
        "tensor",
        scatter_dimension=0,
        tiled=True,
    )
    returned = lax.all_to_all(critic_grad, "dp", split_axis=1, concat_axis=1, tiled=True)
    input_grad = lax.dot_general(
        placing, returned, (((1,), (1,)), ((), ())), preferred_element_type=jnp.float32
    ).astype(jnp.bfloat16)
    return (generated, input_grad)


def solution(mesh):
    in_specs = (
        P("dp", "tensor"),
        P("dp", "tensor"),
        P("tensor", None),
        P("dp", None),
        P(),
        P("dp", None, "tensor"),
        P("dp", "tensor"),
    )
    out_specs = (P("dp", "tensor"), P("dp", "tensor"))
    return jax.shard_map(shards, mesh=mesh, in_specs=in_specs, out_specs=out_specs, check_vma=False)
```

profile of v0, /device:TPU:0, one launch (start us, length us, event | category | flops | bytes accessed | tf_op | source)
XLA Modules:
  0.0 203.9 jit_solution(10909714536548452579)
XLA Ops:
  7.2 0.0 reduce-scatter.3.cloned.1.call-start
  7.2 0.9 copy-done
  8.2 4.9 %convolution_convert_fusion.1 = bf16[3072,256]{1,0:T(8,128)(2,1)} fusion(bf16[768,3072]{1,0:T(8,128)(2,1)} %param.9, bf16[256,768]{1,0:T(8,128)(2,1)S(1)} %copy-done), kind=kOutput, calls=%fused_computation.6 | convolution fusion | flops 1208745984 | bytes 6684672 | tf_op jit(solution)/shard_map/dot_general | solution.py:21
  13.1 0.0 reduce-scatter.3.cloned.1.call-update
  13.1 0.0 all-gather.2.cloned.1.call-start
  13.2 0.2 copy.11
  13.4 33.6 %reduce-scatter.3.cloned.1.call-done = bf16[768,256]{1,0:T(8,128)(2,1)} async-done(((bf16[3072,256]{1,0:T(8,128)(2,1)}), bf16[768,256]{1,0:T(8,128)(2,1)}) %reduce-scatter.3.cloned.1.call-update) | async-done | bytes 393232 | tf_op jit(solution)/shard_map/reduce_scatter | solution.py:20
  47.0 1.8 fusion.31
  48.8 0.0 all-gather.2.cloned.1.call-update
  48.8 0.1 select_reduce_fusion
  48.9 0.6 reduce-window.6
  49.5 0.2 slice_reduce_fusion
  49.8 0.1 fusion.37
  49.9 30.5 %all-gather.2.cloned.1.call-done = bf16[256,3072]{0,1:T(8,128)(2,1)} async-done(((bf16[256,768]{0,1:T(8,128)(2,1)}), bf16[256,3072]{0,1:T(8,128)(2,1)}) %all-gather.2.cloned.1.call-update) | async-done | bytes 1572880 | tf_op jit(solution)/shard_map/all_gather | solution.py:40
  80.4 3.7 %convolution_convert_fusion = bf16[320,3072]{1,0:T(8,128)(2,1)} fusion(bf16[256,3072]{0,1:T(8,128)(2,1)} %all-gather.2.cloned.1.call-done, s32[256]{0:T(256)S(1)} %multiply_add_fusion), kind=kOutput, calls=%fused_computation.5 | convolution fusion | flops 504463360 | bytes 3539968 | tf_op jit(solution)/shard_map/dot_general | solution.py:41
  84.1 4.7 %all-to-all-start = ((bf16[8,40,3072]{2,1,0:T(8,128)(2,1)}), bf16[8,40,3072]{2,1,0:T(8,128)(2,1)S(1)}, u32[]{:S(2)}, u32[]{:S(2)}) async-start(bf16[8,40,3072]{2,1,0:T(8,128)(2,1)} %bitcast.6), calls=%async_computation.1 | async-start | bytes 3932160 | tf_op jit(solution)/shard_map/all_to_all | solution.py:44
  88.8 0.0 reduce-scatter.5.cloned.1.call-start
  88.9 46.2 %all-to-all-done = bf16[8,40,3072]{2,1,0:T(8,128)(2,1)S(1)} async-done(((bf16[8,40,3072]{2,1,0:T(8,128)(2,1)}), bf16[8,40,3072]{2,1,0:T(8,128)(2,1)S(1)}, u32[]{:S(2)}, u32[]{:S(2)}) %all-to-all-start) | async-done | bytes 1966112 | tf_op jit(solution)/shard_map/all_to_all | solution.py:44
  135.1 9.6 %fusion.7 = bf16[3072,320]{0,1:T(8,128)(2,1)} fusion(bf16[1,3072,768]{2,1,0:T(8,128)(2,1)} %param.12, bf16[320,3072]{1,0:T(8,128)(2,1)S(1)} %bitcast.42, f32[768]{0:T(1024)S(1)} %reduce.1, f32[768]{0:T(1024)S(1)} %broadcast_multiply_fusion), kind=kOutput, calls=%fused_computation.7 | convolution fusion | flops 3025797120 | bytes 8656896 | tf_op jit(solution)/shard_map/dot_general | solution.py:49
  144.7 32.2 %reduce-scatter.5.cloned.1.call-done = bf16[768,320]{0,1:T(8,128)(2,1)} async-done(((bf16[3072,320]{0,1:T(8,128)(2,1)}), bf16[768,320]{0,1:T(8,128)(2,1)}) %reduce-scatter.5.cloned.1.call-update) | async-done | bytes 491536 | tf_op jit(solution)/shard_map/reduce_scatter | solution.py:48
  176.9 4.6 %all-to-all-start.1 = ((bf16[768,8,40]{0,2,1:T(8,128)(2,1)}), bf16[768,8,40]{0,2,1:T(8,128)(2,1)S(1)}, u32[]{:S(2)}, u32[]{:S(2)}) async-start(bf16[768,8,40]{0,2,1:T(8,128)(2,1)} %bitcast.44), calls=%async_computation.3 | async-start | bytes 983040 | tf_op jit(solution)/shard_map/all_to_all | solution.py:56
  181.5 0.9 copy.12
  182.5 13.7 %all-to-all-done.1 = bf16[768,8,40]{0,2,1:T(8,128)(2,1)S(1)} async-done(((bf16[768,8,40]{0,2,1:T(8,128)(2,1)}), bf16[768,8,40]{0,2,1:T(8,128)(2,1)S(1)}, u32[]{:S(2)}, u32[]{:S(2)}) %all-to-all-start.1) | async-done | bytes 491552 | tf_op jit(solution)/shard_map/all_to_all | solution.py:56
  196.2 1.2 convolution_convert_fusion.2
  (18 shorter events, 0.1 us)
Async XLA Ops:
  7.2 1.0 copy-start
  7.2 6.0 %copy-start.2 = (bf16[256,768]{1,0:T(8,128)(2,1)S(1)}, bf16[256,768]{1,0:T(8,128)(2,1)}, u32[]{:S(2)}) copy-start(bf16[256,768]{1,0:T(8,128)(2,1)} %param.8) | copy-start | bytes 1179652
  7.2 39.8 %reduce-scatter.3.cloned.1.call-start = ((), (), s32[]{:S(2)}) async-start(), calls=%async_computation.4 | async-start | bytes 1966080 | tf_op jit(solution)/shard_map/reduce_scatter | solution.py:20
  13.1 35.7 %copy-start.4 = (s32[256,1]{0,1:T(1,128)S(1)}, s32[256,1]{0,1:T(1,128)}, u32[]{:S(2)}) copy-start(s32[256,1]{0,1:T(1,128)} %param.10) | copy-start | bytes 3076
  13.1 35.7 %copy-start.5 = (s32[8]{0:T(128)S(1)}, s32[8]{0:T(128)}, u32[]{:S(2)}) copy-start(s32[8]{0:T(128)} %param.11) | copy-start | bytes 100
  13.1 67.2 %all-gather.2.cloned.1.call-start = ((), (), s32[]{:S(2)}) async-start(), calls=%async_computation.5 | async-start | bytes 1966080 | tf_op jit(solution)/shard_map/all_gather | solution.py:40
  84.1 4.8 %copy-start.3 = (f32[1,768]{1,0:T(1,128)S(1)}, f32[1,768]{1,0:T(1,128)}, u32[]{:S(2)}) copy-start(f32[1,768]{1,0:T(1,128)} %param.13) | copy-start | bytes 9220
  84.1 51.0 %all-to-all-start = ((bf16[8,40,3072]{2,1,0:T(8,128)(2,1)}), bf16[8,40,3072]{2,1,0:T(8,128)(2,1)S(1)}, u32[]{:S(2)}, u32[]{:S(2)}) async-start(bf16[8,40,3072]{2,1,0:T(8,128)(2,1)} %bitcast.6), calls=%async_computation.1 | async-start | bytes 3932160 | tf_op jit(solution)/shard_map/all_to_all | solution.py:44
  88.8 88.1 %reduce-scatter.5.cloned.1.call-start = ((), (), s32[]{:S(2)}) async-start(), calls=%async_computation.6 | async-start | bytes 2457600 | tf_op jit(solution)/shard_map/reduce_scatter | solution.py:48
  144.7 36.8 %copy-start.1 = (bf16[256,768]{0,1:T(8,128)(2,1)S(1)}, bf16[256,768]{0,1:T(8,128)(2,1)}, u32[]{:S(2)}) copy-start(bf16[256,768]{0,1:T(8,128)(2,1)} %fusion.31) | copy-start | bytes 1179652
  176.9 19.3 %all-to-all-start.1 = ((bf16[768,8,40]{0,2,1:T(8,128)(2,1)}), bf16[768,8,40]{0,2,1:T(8,128)(2,1)S(1)}, u32[]{:S(2)}, u32[]{:S(2)}) async-start(bf16[768,8,40]{0,2,1:T(8,128)(2,1)} %bitcast.44), calls=%async_computation.3 | async-start | bytes 983040 | tf_op jit(solution)/shard_map/all_to_all | solution.py:56
Sparse Core Ops, SparseCore 0:
  13.3 33.6 reduce-scatter.2
  49.4 30.9 all-gather.1
  144.9 32.0 reduce-scatter.4
where the time goes:
time: 204 us
  waiting for transfers between devices  156 us (76%)
  matrix products  19.5 us (10%)
  between operations  13.8 us (7%)
  starting transfers between devices  9.47 us (5%)
  other arithmetic  2.67 us (1%)
  local copies, waits for them, and re-layouts  2.26 us (1%)
    all_to_all x1, waiting for transfers between devices, shards(): lax.all_to_all(outgoing, 'dp', split_axis=0, concat_axis=0, tiled=True)  46.2 us
    reduce_scatter x1, waiting for transfers between devices, shards(): lax.psum_scatter(lax.dot_general(out_proj, context, (((0,), (1,)), ((), (...  33.6 us
    reduce_scatter x1, waiting for transfers between devices, shards(): lax.psum_scatter(lax.dot_general(projection, pre_grad, (((1,), (1,)), (()...  32.2 us
    all_gather x1, waiting for transfers between devices, shards(): whole = lax.all_gather(generated, 'tensor', axis=1, tiled=True)  30.5 us
    all_to_all x1, waiting for transfers between devices, shards(): lax.all_to_all(critic_grad, 'dp', split_axis=1, concat_axis=1, tiled=True)  13.7 us
    dot_general x1, matrix products, shards(): lax.dot_general(projection, pre_grad, (((1,), (1,)), ((), ())), preferred...  9.62 us
    dot_general x1, matrix products, shards(): lax.dot_general(out_proj, context, (((0,), (1,)), ((), ())), preferred_el...  4.95 us
    all_to_all x1, starting transfers between devices, shards(): lax.all_to_all(outgoing, 'dp', split_axis=0, concat_axis=0, tiled=True)  4.74 us
  transfers between devices with their start and end apart: 5, of which 5 were waited for; matrix products, arithmetic and copies ran while one was open for 1% of the time, Pallas kernels for 0%

commit v1 on v0

v1 whole, which is shorter than its diff:
```python
from functools import partial

import jax
import jax.numpy as jnp
from jax import lax
from jax.sharding import PartitionSpec as P


def slope_times(values, weights):
    _, back_fn = jax.vjp(partial(jax.nn.gelu, approximate=True), values)
    return back_fn(weights)[0]


def is_pow2(n):
    return n & (n - 1) == 0


def partner_of(me, s, n):
    return me ^ s if is_pow2(n) else (me + s) % n


def pairs_for(s, n):
    if is_pow2(n):
        return [(i, i ^ s) for i in range(n)]
    return [(i, (i + s) % n) for i in range(n)]


def sources_for(s, n):
    if is_pow2(n):
        return lambda me: me ^ s
    return lambda me: (me - s) % n


def reduce_blocks(blocks, axis):
    n = blocks.shape[0]
    me = lax.axis_index(axis)
    total = lax.dynamic_index_in_dim(blocks, me, 0, keepdims=False).astype(jnp.float32)
    for s in range(1, n):
        chunk = lax.dynamic_index_in_dim(blocks, partner_of(me, s, n), 0, keepdims=False)
        total = total + lax.ppermute(chunk, axis, pairs_for(s, n)).astype(jnp.float32)
    return total


def gather_blocks(x, axis):
    n = lax.axis_size(axis)
    me = lax.axis_index(axis)
    got = [x] + [lax.ppermute(x, axis, pairs_for(s, n)) for s in range(1, n)]
    stacked = jnp.stack(got)
    if is_pow2(n):
        order = lax.iota(jnp.int32, n) ^ me
    else:
        order = (me - lax.iota(jnp.int32, n)) % n
    return jnp.take(stacked, order, axis=0)


def swap_blocks(blocks, axis):
    n = blocks.shape[0]
    if n > 16:
        return lax.all_to_all(blocks, axis, 0, 0, tiled=True)
    me = lax.axis_index(axis)
    got = [lax.dynamic_index_in_dim(blocks, me, 0, keepdims=False)]
    for s in range(1, n):
        chunk = lax.dynamic_index_in_dim(blocks, partner_of(me, s, n), 0, keepdims=False)
        got.append(lax.ppermute(chunk, axis, pairs_for(s, n)))
    stacked = jnp.stack(got)
    if is_pow2(n):
        order = lax.iota(jnp.int32, n) ^ me
    else:
        order = (me - lax.iota(jnp.int32, n)) % n
    return jnp.take(stacked, order, axis=0)


def shards(context, residual_in, out_proj, members, host_group, member_proj, member_head):
    tok_rows, width = context.shape
    group_count = lax.axis_size("dp")
    tensor_count = lax.axis_size("tensor")
    capacity = max(2, (5 * tok_rows + 4 * group_count - 1) // (4 * group_count))
    slot_count = group_count * capacity
    projection = member_proj[0]

    head_blocks = jnp.einsum(
        "rc,ckd->krd",
        context,
        out_proj.reshape(width, tensor_count, width),
        preferred_element_type=jnp.float32,
    ).astype(jnp.bfloat16)
    summed = reduce_blocks(head_blocks, "tensor")
    generated = (summed + residual_in.astype(jnp.float32)).astype(jnp.bfloat16)

    group_ids = lax.iota(jnp.int32, group_count)
    member_ids = members[:, 0]
    destination = jnp.sum(
        jnp.where(member_ids[:, None] == group_ids[None, :], host_group[None, :], 0), axis=1
    )
    dest_hot = (destination[:, None] == group_ids[None, :]).astype(jnp.int32)
    earlier = jnp.cumsum(dest_hot, axis=0) - dest_hot
    rank_in = jnp.sum(earlier * dest_hot, axis=1)
    slot_of = destination * capacity + rank_in
    placing = (slot_of[:, None] == lax.iota(jnp.int32, slot_count)[None, :]).astype(jnp.bfloat16)

    outgoing = lax.dot_general(
        placing, generated, (((0,), (0,)), ((), ())), preferred_element_type=jnp.float32
    ).astype(jnp.bfloat16)
    arrived = swap_blocks(outgoing.reshape(group_count, capacity, width), "dp")
    arrived = arrived.reshape(slot_count, width)
    gathered = gather_blocks(arrived, "tensor")
    pre_act = jnp.einsum(
        "ksd,kdo->so",
        gathered,
        projection.reshape(tensor_count, width, width),
        preferred_element_type=jnp.float32,
    )
    head_row = jnp.broadcast_to(member_head[0][None, :], pre_act.shape)
    pre_grad = (-slope_times(pre_act, head_row)).astype(jnp.bfloat16)
    back_blocks = jnp.einsum(
        "so,kdo->ksd",
        pre_grad,
        projection.reshape(tensor_count, width, width),
        preferred_element_type=jnp.float32,
    ).astype(jnp.bfloat16)
    critic_grad = reduce_blocks(back_blocks, "tensor").astype(jnp.bfloat16)
    returned = swap_blocks(critic_grad.reshape(group_count, capacity, width), "dp")
    returned = returned.reshape(slot_count, width)
    input_grad = jnp.dot(placing, returned, preferred_element_type=jnp.float32).astype(jnp.bfloat16)
    return (generated, input_grad)


def solution(mesh):
    in_specs = (
        P("dp", "tensor"),
        P("dp", "tensor"),
        P("tensor", None),
        P("dp", None),
        P(),
        P("dp", None, "tensor"),
        P("dp", "tensor"),
    )
    out_specs = (P("dp", "tensor"), P("dp", "tensor"))
    return jax.shard_map(shards, mesh=mesh, in_specs=in_specs, out_specs=out_specs, check_vma=False)
```

time: 204 us -> 133 us (0.65)
  waiting for transfers between devices: 156 us -> 65.4 us
  starting transfers between devices: 9.47 us -> 29.4 us
  local copies, waits for them, and re-layouts: 2.26 us -> 16 us
  between operations: 13.8 us -> 0.97 us
  matrix products: 19.5 us -> 14.3 us
  other arithmetic: 2.67 us -> 5.98 us
    reduce_scatter x2 -> x0, waiting for transfers between devices: 65.8 us -> none  [the longest x1 33.6 us: shards(): lax.psum_scatter(lax.dot_general(out_proj, context, (((0,), (1,)), ((), (...]
    ppermute x0 -> x23, waiting for transfers between devices: none -> 65.4 us  [the longest x6 31.5 us: reduce_blocks(): lax.ppermute(chunk, axis, pairs_for(s, n)).astype(jnp.float32)]
    all_to_all x2 -> x0, waiting for transfers between devices: 59.9 us -> none  [the longest x1 46.2 us: shards(): lax.all_to_all(outgoing, 'dp', split_axis=0, concat_axis=0, tiled=True)]
    all_gather x1 -> x0, waiting for transfers between devices: 30.5 us -> none  [shards(): whole = lax.all_gather(generated, 'tensor', axis=1, tiled=True)]
    ppermute x0 -> x23, starting transfers between devices: none -> 29.4 us  [the longest x14 17.9 us: swap_blocks(): got.append(lax.ppermute(chunk, axis, pairs_for(s, n)))]
    all_to_all x2 -> x0, starting transfers between devices: 9.35 us -> none  [the longest x1 4.74 us: shards(): lax.all_to_all(outgoing, 'dp', split_axis=0, concat_axis=0, tiled=True)]
    reshape x0 -> x1, local copies, waits for them, and re-layouts: none -> 6.69 us  [shards(): out_proj.reshape(width, tensor_count, width)]
    dot_general x4, matrix products: 19.5 us -> 14.3 us  [the longest x1 8.91 us: shards(): jnp.einsum('so,kdo->ksd', pre_grad, projection.reshape(tensor_count, widt...]
  transfers between devices with their start and end apart: 5 -> 23, of which waited for: 5 -> 9; matrix products, arithmetic and copies ran while one was open for 1% -> 5% of each run, Pallas kernels for 0% -> 0%
where the time goes in v1:
time: 133 us; the launch traced here: 132 us
  waiting for transfers between devices  65.4 us (49%)
  starting transfers between devices  29.4 us (22%)
  local copies, waits for them, and re-layouts  16 us (12%)
  matrix products  14.3 us (11%)
  other arithmetic  5.98 us (4%)
    ppermute x6, waiting for transfers between devices, reduce_blocks(): lax.ppermute(chunk, axis, pairs_for(s, n)).astype(jnp.float32)  31.5 us
    ppermute x3, waiting for transfers between devices, gather_blocks(): got = [x] + [lax.ppermute(x, axis, pairs_for(s, n)) for s in range(1, n)]  21.3 us
    ppermute x14, starting transfers between devices, swap_blocks(): got.append(lax.ppermute(chunk, axis, pairs_for(s, n)))  17.9 us
    ppermute x14, waiting for transfers between devices, swap_blocks(): got.append(lax.ppermute(chunk, axis, pairs_for(s, n)))  12.6 us
    dot_general x1, matrix products, shards(): jnp.einsum('so,kdo->ksd', pre_grad, projection.reshape(tensor_count, widt...  8.91 us
    ppermute x6, starting transfers between devices, reduce_blocks(): lax.ppermute(chunk, axis, pairs_for(s, n)).astype(jnp.float32)  8.02 us
    reshape x1, local copies, waits for them, and re-layouts, shards(): out_proj.reshape(width, tensor_count, width)  6.69 us
    dot_general x1, matrix products, shards(): jnp.einsum('rc,ckd->krd', context, out_proj.reshape(width, tensor_count,...  3.76 us
  transfers between devices with their start and end apart: 23, of which 9 were waited for; matrix products, arithmetic and copies ran while one was open for 5% of the time, Pallas kernels for 0%

profile of v1, /device:TPU:0, one launch (start us, length us, event | category | flops | bytes accessed | tf_op | source)
XLA Modules:
  0.0 132.0 jit_solution(8164434359684111622)
XLA Ops:
  0.7 6.7 %copy.15 = bf16[768,3072]{0,1:T(8,128)(2,1)} copy(bf16[768,3072]{1,0:T(8,128)(2,1)} %param.11) | data formatting | bytes 9437184 | tf_op jit(solution)/shard_map/reshape | solution.py:84
  7.4 3.8 %convolution_convert_fusion.1 = bf16[4,768,256]{2,1,0:T(8,128)(2,1)S(1)} fusion(bf16[768,4,768]{0,2,1:T(8,128)(2,1)} %bitcast.131, bf16[256,768]{1,0:T(8,128)(2,1)S(1)} %copy-done), kind=kOutput, calls=%fused_computation.8 | convolution fusion | flops 1208745984 | bytes 6684672 | tf_op jit(solution)/shard_map/rc,ckd->krd/dot_general | solution.py:81
  12.1 2.9 %collective-permute-start = (bf16[256,768]{0,1:T(8,128)(2,1)}, bf16[256,768]{0,1:T(8,128)(2,1)S(1)}, u32[]{:S(2)}, u32[]{:S(2)}) collective-permute-start(bf16[256,768]{0,1:T(8,128)(2,1)} %get-tuple-element.10), channel_id=1, source_target_pairs={{0,1},{1,0},{2,3},{3,2},{4,5},{5,4},{6,7},{7,6},{8,9},{9,8},{10,11... | collective-permute-start | bytes 1179656 | tf_op jit(solution)/shard_map/ppermute | solution.py:40
  15.0 1.5 %collective-permute-start.1 = (bf16[256,768]{0,1:T(8,128)(2,1)}, bf16[256,768]{0,1:T(8,128)(2,1)S(1)}, u32[]{:S(2)}, u32[]{:S(2)}) collective-permute-start(bf16[256,768]{0,1:T(8,128)(2,1)} %get-tuple-element.12), channel_id=1, source_target_pairs={{0,2},{1,3},{2,0},{3,1},{4,6},{5,7},{6,4},{7,5},{8,10},{9,11},{10,... | collective-permute-start | bytes 1179656 | tf_op jit(solution)/shard_map/ppermute | solution.py:40
  22.4 2.8 %collective-permute-done = bf16[256,768]{0,1:T(8,128)(2,1)S(1)} collective-permute-done((bf16[256,768]{0,1:T(8,128)(2,1)}, bf16[256,768]{0,1:T(8,128)(2,1)S(1)}, u32[]{:S(2)}, u32[]{:S(2)}) %collective-permute-start) | collective-permute-done | bytes 393248 | tf_op jit(solution)/shard_map/ppermute | solution.py:40
  25.2 9.1 %collective-permute-done.1 = bf16[256,768]{0,1:T(8,128)(2,1)S(1)} collective-permute-done((bf16[256,768]{0,1:T(8,128)(2,1)}, bf16[256,768]{0,1:T(8,128)(2,1)S(1)}, u32[]{:S(2)}, u32[]{:S(2)}) %collective-permute-start.1) | collective-permute-done | bytes 393248 | tf_op jit(solution)/shard_map/ppermute | solution.py:40
  36.1 1.6 %collective-permute-start.4 = (bf16[40,768]{1,0:T(8,128)(2,1)S(1)}, bf16[40,768]{1,0:T(8,128)(2,1)S(1)}, u32[]{:S(2)}, u32[]{:S(2)}) collective-permute-start(bf16[40,768]{1,0:T(8,128)(2,1)S(1)} %get-tuple-element.26), channel_id=1, source_target_pairs={{0,8},{4,12},{8,0},{12,4},{16,24},{20,28},{24,16},{28,20},{1,9},{5... | collective-permute-start | bytes 184328 | tf_op jit(solution)/shard_map/ppermute | solution.py:64
  38.0 2.6 %collective-permute-start.6 = (bf16[40,768]{1,0:T(8,128)(2,1)S(1)}, bf16[40,768]{1,0:T(8,128)(2,1)S(1)}, u32[]{:S(2)}, u32[]{:S(2)}) collective-permute-start(bf16[40,768]{1,0:T(8,128)(2,1)S(1)} %get-tuple-element.24), channel_id=1, source_target_pairs={{0,16},{4,20},{8,24},{12,28},{16,0},{20,4},{24,8},{28,12},{1,17},{... | collective-permute-start | bytes 184328 | tf_op jit(solution)/shard_map/ppermute | solution.py:64
  40.6 3.6 %collective-permute-start.8 = (bf16[40,768]{1,0:T(8,128)(2,1)S(1)}, bf16[40,768]{1,0:T(8,128)(2,1)S(1)}, u32[]{:S(2)}, u32[]{:S(2)}) collective-permute-start(bf16[40,768]{1,0:T(8,128)(2,1)S(1)} %get-tuple-element.22), channel_id=1, source_target_pairs={{0,24},{4,28},{8,16},{12,20},{16,8},{20,12},{24,0},{28,4},{1,25},{... | collective-permute-start | bytes 184328 | tf_op jit(solution)/shard_map/ppermute | solution.py:64
  44.4 6.3 %collective-permute-done.7 = bf16[40,768]{1,0:T(8,128)(2,1)S(1)} collective-permute-done((bf16[40,768]{1,0:T(8,128)(2,1)S(1)}, bf16[40,768]{1,0:T(8,128)(2,1)S(1)}, u32[]{:S(2)}, u32[]{:S(2)}) %collective-permute-start.7) | collective-permute-done | bytes 61472 | tf_op jit(solution)/shard_map/ppermute | solution.py:64
  53.5 1.4 %collective-permute-start.12 = (bf16[320,768]{1,0:T(8,128)(2,1)S(1)}, bf16[320,768]{1,0:T(8,128)(2,1)S(1)}, u32[]{:S(2)}, u32[]{:S(2)}) collective-permute-start(bf16[320,768]{1,0:T(8,128)(2,1)S(1)} %bitcast.134), channel_id=1, source_target_pairs={{0,3},{1,2},{2,1},{3,0},{4,7},{5,6},{6,5},{7,4},{8,11},{9,10},{10,... | collective-permute-start | bytes 1474568 | tf_op jit(solution)/shard_map/ppermute | solution.py:47
  55.0 10.5 %collective-permute-done.10 = bf16[320,768]{1,0:T(8,128)(2,1)S(1)} collective-permute-done((bf16[320,768]{1,0:T(8,128)(2,1)S(1)}, bf16[320,768]{1,0:T(8,128)(2,1)S(1)}, u32[]{:S(2)}, u32[]{:S(2)}) %collective-permute-start.10) | collective-permute-done | bytes 491552 | tf_op jit(solution)/shard_map/ppermute | solution.py:47
  65.5 9.0 %collective-permute-done.11 = bf16[320,768]{1,0:T(8,128)(2,1)S(1)} collective-permute-done((bf16[320,768]{1,0:T(8,128)(2,1)S(1)}, bf16[320,768]{1,0:T(8,128)(2,1)S(1)}, u32[]{:S(2)}, u32[]{:S(2)}) %collective-permute-start.11) | collective-permute-done | bytes 491552 | tf_op jit(solution)/shard_map/ppermute | solution.py:47
  74.6 1.7 %collective-permute-done.12 = bf16[320,768]{1,0:T(8,128)(2,1)S(1)} collective-permute-done((bf16[320,768]{1,0:T(8,128)(2,1)S(1)}, bf16[320,768]{1,0:T(8,128)(2,1)S(1)}, u32[]{:S(2)}, u32[]{:S(2)}) %collective-permute-start.12) | collective-permute-done | bytes 491552 | tf_op jit(solution)/shard_map/ppermute | solution.py:47
  77.1 1.6 %pad_maximum_fusion = bf16[4,320,768]{2,1,0:T(8,128)(2,1)S(1)} fusion(bf16[1,320,768]{2,1,0:T(8,128)(2,1)} %bitcast.141, bf16[1,320,768]{2,1,0:T(8,128)(2,1)} %bitcast.140, bf16[1,320,768]{2,1,0:T(8,128)(2,1)} %bitcast.139, bf16[1,320,768]{2,1,0:T(8,128)(2,1)S(1)} %bitcast.135), kind=kLoop, calls=%fused_computation.3 | loop fusion | flops 2949120 | bytes 3932160 | tf_op jit(solution)/shard_map/stack | solution.py:48
  78.7 2.0 %gather_fusion = bf16[4,320,768]{2,1,0:T(8,128)(2,1)} fusion(bf16[4,320,768]{2,1,0:T(8,128)(2,1)S(1)} %pad_maximum_fusion, s32[1024]{0:T(1024)S(1)} %pad_clamp_fusion), kind=kCustom, calls=%fused_computation.2 | custom fusion | bytes 3932176 | tf_op jit(solution)/shard_map/jit(_take)/gather | solution.py:53
  80.6 8.9 %convolution_convert_fusion = bf16[320,4,768]{2,0,1:T(8,128)(2,1)S(1)} fusion(bf16[4,768,768]{2,1,0:T(8,128)(2,1)} %bitcast.144, bf16[4,320,768]{2,1,0:T(8,128)(2,1)} %gather_fusion, pred[4]{0:T(512)(128)(4,1)S(1)} %compare_and_fusion.1, f32[768]{0:T(1024)S(1)} %reduce.1, f32[768]{0:T(1024)S(1)} %broadcast_multiply_fusion), kind=kOutput, calls=%fused_computation.7 | convolution fusion | flops 3026780160 | bytes 8656900 | tf_op jit(solution)/shard_map/so,kdo->ksd/dot_general | solution.py:115
  90.6 1.5 %collective-permute-start.14 = (bf16[320,768]{1,0:T(8,128)(2,1)S(1)}, bf16[320,768]{1,0:T(8,128)(2,1)S(1)}, u32[]{:S(2)}, u32[]{:S(2)}) collective-permute-start(bf16[320,768]{1,0:T(8,128)(2,1)S(1)} %get-tuple-element.9), channel_id=1, source_target_pairs={{0,2},{1,3},{2,0},{3,1},{4,6},{5,7},{6,4},{7,5},{8,10},{9,11},{10,... | collective-permute-start | bytes 1474568 | tf_op jit(solution)/shard_map/ppermute | solution.py:40
  93.2 10.7 %collective-permute-done.13 = bf16[320,768]{1,0:T(8,128)(2,1)S(1)} collective-permute-done((bf16[320,768]{1,0:T(8,128)(2,1)S(1)}, bf16[320,768]{1,0:T(8,128)(2,1)S(1)}, u32[]{:S(2)}, u32[]{:S(2)}) %collective-permute-start.13) | collective-permute-done | bytes 491552 | tf_op jit(solution)/shard_map/ppermute | solution.py:40
  103.9 9.0 %collective-permute-done.14 = bf16[320,768]{1,0:T(8,128)(2,1)S(1)} collective-permute-done((bf16[320,768]{1,0:T(8,128)(2,1)S(1)}, bf16[320,768]{1,0:T(8,128)(2,1)S(1)}, u32[]{:S(2)}, u32[]{:S(2)}) %collective-permute-start.14) | collective-permute-done | bytes 491552 | tf_op jit(solution)/shard_map/ppermute | solution.py:40
  114.2 3.1 %collective-permute-start.17 = (bf16[40,768]{1,0:T(8,128)(2,1)S(1)}, bf16[40,768]{1,0:T(8,128)(2,1)S(1)}, u32[]{:S(2)}, u32[]{:S(2)}) collective-permute-start(bf16[40,768]{1,0:T(8,128)(2,1)S(1)} %get-tuple-element.18), channel_id=1, source_target_pairs={{0,8},{4,12},{8,0},{12,4},{16,24},{20,28},{24,16},{28,20},{1,9},{5... | collective-permute-start | bytes 184328 | tf_op jit(solution)/shard_map/ppermute | solution.py:64
  117.5 2.7 %collective-permute-start.19 = (bf16[40,768]{1,0:T(8,128)(2,1)S(1)}, bf16[40,768]{1,0:T(8,128)(2,1)S(1)}, u32[]{:S(2)}, u32[]{:S(2)}) collective-permute-start(bf16[40,768]{1,0:T(8,128)(2,1)S(1)} %get-tuple-element.16), channel_id=1, source_target_pairs={{0,16},{4,20},{8,24},{12,28},{16,0},{20,4},{24,8},{28,12},{1,17},{... | collective-permute-start | bytes 184328 | tf_op jit(solution)/shard_map/ppermute | solution.py:64
  120.3 2.1 %collective-permute-start.21 = (bf16[40,768]{1,0:T(8,128)(2,1)S(1)}, bf16[40,768]{1,0:T(8,128)(2,1)S(1)}, u32[]{:S(2)}, u32[]{:S(2)}) collective-permute-start(bf16[40,768]{1,0:T(8,128)(2,1)S(1)} %get-tuple-element.14), channel_id=1, source_target_pairs={{0,24},{4,28},{8,16},{12,20},{16,8},{20,12},{24,0},{28,4},{1,25},{... | collective-permute-start | bytes 184328 | tf_op jit(solution)/shard_map/ppermute | solution.py:64
  123.8 6.3 %collective-permute-done.20 = bf16[40,768]{1,0:T(8,128)(2,1)S(1)} collective-permute-done((bf16[40,768]{1,0:T(8,128)(2,1)S(1)}, bf16[40,768]{1,0:T(8,128)(2,1)S(1)}, u32[]{:S(2)}, u32[]{:S(2)}) %collective-permute-start.20) | collective-permute-done | bytes 61472 | tf_op jit(solution)/shard_map/ppermute | solution.py:64
  (85 shorter events, 19.6 us)
Async XLA Ops:
  12.1 13.1 %collective-permute-start = (bf16[256,768]{0,1:T(8,128)(2,1)}, bf16[256,768]{0,1:T(8,128)(2,1)S(1)}, u32[]{:S(2)}, u32[]{:S(2)}) collective-permute-start(bf16[256,768]{0,1:T(8,128)(2,1)} %get-tuple-element.10), channel_id=1, source_target_pairs={{0,1},{1,0},{2,3},{3,2},{4,5},{5,4},{6,7},{7,6},{8,9},{9,8},{10,11... | collective-permute-start | bytes 1179656 | tf_op jit(solution)/shard_map/ppermute | solution.py:40
  15.0 19.2 %collective-permute-start.1 = (bf16[256,768]{0,1:T(8,128)(2,1)}, bf16[256,768]{0,1:T(8,128)(2,1)S(1)}, u32[]{:S(2)}, u32[]{:S(2)}) collective-permute-start(bf16[256,768]{0,1:T(8,128)(2,1)} %get-tuple-element.12), channel_id=1, source_target_pairs={{0,2},{1,3},{2,0},{3,1},{4,6},{5,7},{6,4},{7,5},{8,10},{9,11},{10,... | collective-permute-start | bytes 1179656 | tf_op jit(solution)/shard_map/ppermute | solution.py:40
  16.6 17.7 %collective-permute-start.2 = (bf16[256,768]{0,1:T(8,128)(2,1)S(1)}, bf16[256,768]{0,1:T(8,128)(2,1)}, u32[]{:S(2)}, u32[]{:S(2)}) collective-permute-start(bf16[256,768]{0,1:T(8,128)(2,1)S(1)} %get-tuple-element.11), channel_id=1, source_target_pairs={{0,3},{1,2},{2,1},{3,0},{4,7},{5,6},{6,5},{7,4},{8,11},{9,10},{10,... | collective-permute-start | bytes 1179656 | tf_op jit(solution)/shard_map/ppermute | solution.py:40
  35.9 19.0 %copy-start.4 = (f32[1,768]{1,0:T(1,128)S(1)}, f32[1,768]{1,0:T(1,128)}, u32[]{:S(2)}) copy-start(f32[1,768]{1,0:T(1,128)} %param.15) | copy-start | bytes 9220
  36.0 4.6 %collective-permute-start.3 = (bf16[40,768]{1,0:T(8,128)(2,1)S(1)}, bf16[40,768]{1,0:T(8,128)(2,1)S(1)}, u32[]{:S(2)}, u32[]{:S(2)}) collective-permute-start(bf16[40,768]{1,0:T(8,128)(2,1)S(1)} %get-tuple-element.27), channel_id=1, source_target_pairs={{0,4},{4,0},{8,12},{12,8},{16,20},{20,16},{24,28},{28,24},{1,5},{5... | collective-permute-start | bytes 184328 | tf_op jit(solution)/shard_map/ppermute | solution.py:64
  36.1 8.1 %collective-permute-start.4 = (bf16[40,768]{1,0:T(8,128)(2,1)S(1)}, bf16[40,768]{1,0:T(8,128)(2,1)S(1)}, u32[]{:S(2)}, u32[]{:S(2)}) collective-permute-start(bf16[40,768]{1,0:T(8,128)(2,1)S(1)} %get-tuple-element.26), channel_id=1, source_target_pairs={{0,8},{4,12},{8,0},{12,4},{16,24},{20,28},{24,16},{28,20},{1,9},{5... | collective-permute-start | bytes 184328 | tf_op jit(solution)/shard_map/ppermute | solution.py:64
  37.8 6.6 %collective-permute-start.5 = (bf16[40,768]{1,0:T(8,128)(2,1)S(1)}, bf16[40,768]{1,0:T(8,128)(2,1)S(1)}, u32[]{:S(2)}, u32[]{:S(2)}) collective-permute-start(bf16[40,768]{1,0:T(8,128)(2,1)S(1)} %get-tuple-element.25), channel_id=1, source_target_pairs={{0,12},{4,8},{8,4},{12,0},{16,28},{20,24},{24,20},{28,16},{1,13},{... | collective-permute-start | bytes 184328 | tf_op jit(solution)/shard_map/ppermute | solution.py:64
  38.0 6.4 %collective-permute-start.6 = (bf16[40,768]{1,0:T(8,128)(2,1)S(1)}, bf16[40,768]{1,0:T(8,128)(2,1)S(1)}, u32[]{:S(2)}, u32[]{:S(2)}) collective-permute-start(bf16[40,768]{1,0:T(8,128)(2,1)S(1)} %get-tuple-element.24), channel_id=1, source_target_pairs={{0,16},{4,20},{8,24},{12,28},{16,0},{20,4},{24,8},{28,12},{1,17},{... | collective-permute-start | bytes 184328 | tf_op jit(solution)/shard_map/ppermute | solution.py:64
  40.6 10.1 %collective-permute-start.7 = (bf16[40,768]{1,0:T(8,128)(2,1)S(1)}, bf16[40,768]{1,0:T(8,128)(2,1)S(1)}, u32[]{:S(2)}, u32[]{:S(2)}) collective-permute-start(bf16[40,768]{1,0:T(8,128)(2,1)S(1)} %get-tuple-element.23), channel_id=1, source_target_pairs={{0,20},{4,16},{8,28},{12,24},{16,4},{20,0},{24,12},{28,8},{1,21},{... | collective-permute-start | bytes 184328 | tf_op jit(solution)/shard_map/ppermute | solution.py:64
  40.6 10.1 %collective-permute-start.8 = (bf16[40,768]{1,0:T(8,128)(2,1)S(1)}, bf16[40,768]{1,0:T(8,128)(2,1)S(1)}, u32[]{:S(2)}, u32[]{:S(2)}) collective-permute-start(bf16[40,768]{1,0:T(8,128)(2,1)S(1)} %get-tuple-element.22), channel_id=1, source_target_pairs={{0,24},{4,28},{8,16},{12,20},{16,8},{20,12},{24,0},{28,4},{1,25},{... | collective-permute-start | bytes 184328 | tf_op jit(solution)/shard_map/ppermute | solution.py:64
  44.2 6.5 %collective-permute-start.9 = (bf16[40,768]{1,0:T(8,128)(2,1)S(1)}, bf16[40,768]{1,0:T(8,128)(2,1)S(1)}, u32[]{:S(2)}, u32[]{:S(2)}) collective-permute-start(bf16[40,768]{1,0:T(8,128)(2,1)S(1)} %get-tuple-element.21), channel_id=1, source_target_pairs={{0,28},{4,24},{8,20},{12,16},{16,12},{20,8},{24,4},{28,0},{1,29},{... | collective-permute-start | bytes 184328 | tf_op jit(solution)/shard_map/ppermute | solution.py:64
  51.4 14.1 %collective-permute-start.10 = (bf16[320,768]{1,0:T(8,128)(2,1)S(1)}, bf16[320,768]{1,0:T(8,128)(2,1)S(1)}, u32[]{:S(2)}, u32[]{:S(2)}) collective-permute-start(bf16[320,768]{1,0:T(8,128)(2,1)S(1)} %bitcast.132), channel_id=1, source_target_pairs={{0,1},{1,0},{2,3},{3,2},{4,5},{5,4},{6,7},{7,6},{8,9},{9,8},{10,11... | collective-permute-start | bytes 1474568 | tf_op jit(solution)/shard_map/ppermute | solution.py:47
  52.8 21.8 %collective-permute-start.11 = (bf16[320,768]{1,0:T(8,128)(2,1)S(1)}, bf16[320,768]{1,0:T(8,128)(2,1)S(1)}, u32[]{:S(2)}, u32[]{:S(2)}) collective-permute-start(bf16[320,768]{1,0:T(8,128)(2,1)S(1)} %bitcast.133), channel_id=1, source_target_pairs={{0,2},{1,3},{2,0},{3,1},{4,6},{5,7},{6,4},{7,5},{8,10},{9,11},{10,... | collective-permute-start | bytes 1474568 | tf_op jit(solution)/shard_map/ppermute | solution.py:47
  53.5 22.8 %collective-permute-start.12 = (bf16[320,768]{1,0:T(8,128)(2,1)S(1)}, bf16[320,768]{1,0:T(8,128)(2,1)S(1)}, u32[]{:S(2)}, u32[]{:S(2)}) collective-permute-start(bf16[320,768]{1,0:T(8,128)(2,1)S(1)} %bitcast.134), channel_id=1, source_target_pairs={{0,3},{1,2},{2,1},{3,0},{4,7},{5,6},{6,5},{7,4},{8,11},{9,10},{10,... | collective-permute-start | bytes 1474568 | tf_op jit(solution)/shard_map/ppermute | solution.py:47
  89.7 14.2 %collective-permute-start.13 = (bf16[320,768]{1,0:T(8,128)(2,1)S(1)}, bf16[320,768]{1,0:T(8,128)(2,1)S(1)}, u32[]{:S(2)}, u32[]{:S(2)}) collective-permute-start(bf16[320,768]{1,0:T(8,128)(2,1)S(1)} %get-tuple-element.7), channel_id=1, source_target_pairs={{0,1},{1,0},{2,3},{3,2},{4,5},{5,4},{6,7},{7,6},{8,9},{9,8},{10,11... | collective-permute-start | bytes 1474568 | tf_op jit(solution)/shard_map/ppermute | solution.py:40
  90.6 22.3 %collective-permute-start.14 = (bf16[320,768]{1,0:T(8,128)(2,1)S(1)}, bf16[320,768]{1,0:T(8,128)(2,1)S(1)}, u32[]{:S(2)}, u32[]{:S(2)}) collective-permute-start(bf16[320,768]{1,0:T(8,128)(2,1)S(1)} %get-tuple-element.9), channel_id=1, source_target_pairs={{0,2},{1,3},{2,0},{3,1},{4,6},{5,7},{6,4},{7,5},{8,10},{9,11},{10,... | collective-permute-start | bytes 1474568 | tf_op jit(solution)/shard_map/ppermute | solution.py:40
  92.1 20.8 %collective-permute-start.15 = (bf16[320,768]{1,0:T(8,128)(2,1)S(1)}, bf16[320,768]{1,0:T(8,128)(2,1)S(1)}, u32[]{:S(2)}, u32[]{:S(2)}) collective-permute-start(bf16[320,768]{1,0:T(8,128)(2,1)S(1)} %get-tuple-element.8), channel_id=1, source_target_pairs={{0,3},{1,2},{2,1},{3,0},{4,7},{5,6},{6,5},{7,4},{8,11},{9,10},{10,... | collective-permute-start | bytes 1474568 | tf_op jit(solution)/shard_map/ppermute | solution.py:40
  113.2 7.0 %collective-permute-start.16 = (bf16[40,768]{1,0:T(8,128)(2,1)S(1)}, bf16[40,768]{1,0:T(8,128)(2,1)S(1)}, u32[]{:S(2)}, u32[]{:S(2)}) collective-permute-start(bf16[40,768]{1,0:T(8,128)(2,1)S(1)} %get-tuple-element.19), channel_id=1, source_target_pairs={{0,4},{4,0},{8,12},{12,8},{16,20},{20,16},{24,28},{28,24},{1,5},{5... | collective-permute-start | bytes 184328 | tf_op jit(solution)/shard_map/ppermute | solution.py:64
  114.2 8.1 %collective-permute-start.17 = (bf16[40,768]{1,0:T(8,128)(2,1)S(1)}, bf16[40,768]{1,0:T(8,128)(2,1)S(1)}, u32[]{:S(2)}, u32[]{:S(2)}) collective-permute-start(bf16[40,768]{1,0:T(8,128)(2,1)S(1)} %get-tuple-element.18), channel_id=1, source_target_pairs={{0,8},{4,12},{8,0},{12,4},{16,24},{20,28},{24,16},{28,20},{1,9},{5... | collective-permute-start | bytes 184328 | tf_op jit(solution)/shard_map/ppermute | solution.py:64
  117.4 6.4 %collective-permute-start.18 = (bf16[40,768]{1,0:T(8,128)(2,1)S(1)}, bf16[40,768]{1,0:T(8,128)(2,1)S(1)}, u32[]{:S(2)}, u32[]{:S(2)}) collective-permute-start(bf16[40,768]{1,0:T(8,128)(2,1)S(1)} %get-tuple-element.17), channel_id=1, source_target_pairs={{0,12},{4,8},{8,4},{12,0},{16,28},{20,24},{24,20},{28,16},{1,13},{... | collective-permute-start | bytes 184328 | tf_op jit(solution)/shard_map/ppermute | solution.py:64
  117.5 6.3 %collective-permute-start.19 = (bf16[40,768]{1,0:T(8,128)(2,1)S(1)}, bf16[40,768]{1,0:T(8,128)(2,1)S(1)}, u32[]{:S(2)}, u32[]{:S(2)}) collective-permute-start(bf16[40,768]{1,0:T(8,128)(2,1)S(1)} %get-tuple-element.16), channel_id=1, source_target_pairs={{0,16},{4,20},{8,24},{12,28},{16,0},{20,4},{24,8},{28,12},{1,17},{... | collective-permute-start | bytes 184328 | tf_op jit(solution)/shard_map/ppermute | solution.py:64
  120.2 9.9 %collective-permute-start.20 = (bf16[40,768]{1,0:T(8,128)(2,1)S(1)}, bf16[40,768]{1,0:T(8,128)(2,1)S(1)}, u32[]{:S(2)}, u32[]{:S(2)}) collective-permute-start(bf16[40,768]{1,0:T(8,128)(2,1)S(1)} %get-tuple-element.15), channel_id=1, source_target_pairs={{0,20},{4,16},{8,28},{12,24},{16,4},{20,0},{24,12},{28,8},{1,21},{... | collective-permute-start | bytes 184328 | tf_op jit(solution)/shard_map/ppermute | solution.py:64
  120.3 9.9 %collective-permute-start.21 = (bf16[40,768]{1,0:T(8,128)(2,1)S(1)}, bf16[40,768]{1,0:T(8,128)(2,1)S(1)}, u32[]{:S(2)}, u32[]{:S(2)}) collective-permute-start(bf16[40,768]{1,0:T(8,128)(2,1)S(1)} %get-tuple-element.14), channel_id=1, source_target_pairs={{0,24},{4,28},{8,16},{12,20},{16,8},{20,12},{24,0},{28,4},{1,25},{... | collective-permute-start | bytes 184328 | tf_op jit(solution)/shard_map/ppermute | solution.py:64
  122.3 7.8 %collective-permute-start.22 = (bf16[40,768]{1,0:T(8,128)(2,1)S(1)}, bf16[40,768]{1,0:T(8,128)(2,1)S(1)}, u32[]{:S(2)}, u32[]{:S(2)}) collective-permute-start(bf16[40,768]{1,0:T(8,128)(2,1)S(1)} %get-tuple-element.13), channel_id=1, source_target_pairs={{0,28},{4,24},{8,20},{12,16},{16,12},{20,8},{24,4},{28,0},{1,29},{... | collective-permute-start | bytes 184328 | tf_op jit(solution)/shard_map/ppermute | solution.py:64
  (6 other events, 30.9 us)

commit v2 on v1

--- a/solution.py
+++ b/solution.py
@@ -70,22 +70,31 @@
     return jnp.take(stacked, order, axis=0)
 
 
+SLOT_CHUNKS = 1
+
+
 def shards(context, residual_in, out_proj, members, host_group, member_proj, member_head):
     tok_rows, width = context.shape
     group_count = lax.axis_size("dp")
     tensor_count = lax.axis_size("tensor")
     capacity = max(2, (5 * tok_rows + 4 * group_count - 1) // (4 * group_count))
-    slot_count = group_count * capacity
+    chunks = SLOT_CHUNKS if capacity % SLOT_CHUNKS == 0 else 1
+    chunk_cap = capacity // chunks
+    chunk_slots = group_count * chunk_cap
+    me_t = lax.axis_index("tensor")
+    partners = [partner_of(me_t, s, tensor_count) for s in range(tensor_count)]
     projection = member_proj[0]
+    proj_blocks = projection.reshape(tensor_count, width, projection.shape[1])
+    proj_parts = [lax.dynamic_index_in_dim(proj_blocks, p, 0, keepdims=False) for p in partners]
 
-    head_blocks = jnp.einsum(
-        "rc,ckd->krd",
-        context,
-        out_proj.reshape(width, tensor_count, width),
-        preferred_element_type=jnp.float32,
-    ).astype(jnp.bfloat16)
-    summed = reduce_blocks(head_blocks, "tensor")
-    generated = (summed + residual_in.astype(jnp.float32)).astype(jnp.bfloat16)
+    head_terms = jnp.dot(context, out_proj, preferred_element_type=jnp.float32).astype(jnp.bfloat16)
+    head_blocks = head_terms.reshape(tok_rows, tensor_count, width)
+    summed = lax.dynamic_index_in_dim(head_blocks, me_t, 1, keepdims=False).astype(jnp.float32)
+    summed = summed + residual_in.astype(jnp.float32)
+    for s in range(1, tensor_count):
+        chunk = lax.dynamic_index_in_dim(head_blocks, partners[s], 1, keepdims=False)
+        summed = summed + lax.ppermute(chunk, "tensor", pairs_for(s, tensor_count)).astype(jnp.float32)
+    generated = summed.astype(jnp.bfloat16)
 
     group_ids = lax.iota(jnp.int32, group_count)
     member_ids = members[:, 0]
@@ -95,34 +104,42 @@
     dest_hot = (destination[:, None] == group_ids[None, :]).astype(jnp.int32)
     earlier = jnp.cumsum(dest_hot, axis=0) - dest_hot
     rank_in = jnp.sum(earlier * dest_hot, axis=1)
-    slot_of = destination * capacity + rank_in
-    placing = (slot_of[:, None] == lax.iota(jnp.int32, slot_count)[None, :]).astype(jnp.bfloat16)
+    slot_ids = lax.iota(jnp.int32, chunk_slots)
+    head_row = member_head[0][None, :]
 
-    outgoing = lax.dot_general(
-        placing, generated, (((0,), (0,)), ((), ())), preferred_element_type=jnp.float32
-    ).astype(jnp.bfloat16)
-    arrived = swap_blocks(outgoing.reshape(group_count, capacity, width), "dp")
-    arrived = arrived.reshape(slot_count, width)
-    gathered = gather_blocks(arrived, "tensor")
-    pre_act = jnp.einsum(
-        "ksd,kdo->so",
-        gathered,
-        projection.reshape(tensor_count, width, width),
-        preferred_element_type=jnp.float32,
-    )
-    head_row = jnp.broadcast_to(member_head[0][None, :], pre_act.shape)
-    pre_grad = (-slope_times(pre_act, head_row)).astype(jnp.bfloat16)
-    back_blocks = jnp.einsum(
-        "so,kdo->ksd",
-        pre_grad,
-        projection.reshape(tensor_count, width, width),
-        preferred_element_type=jnp.float32,
-    ).astype(jnp.bfloat16)
-    critic_grad = reduce_blocks(back_blocks, "tensor").astype(jnp.bfloat16)
-    returned = swap_blocks(critic_grad.reshape(group_count, capacity, width), "dp")
-    returned = returned.reshape(slot_count, width)
-    input_grad = jnp.dot(placing, returned, preferred_element_type=jnp.float32).astype(jnp.bfloat16)
-    return (generated, input_grad)
+    input_grad = None
+    for c in range(chunks):
+        local_rank = rank_in - c * chunk_cap
+        inside = (local_rank >= 0) & (local_rank < chunk_cap)
+        slot_of = destination * chunk_cap + local_rank
+        placing = ((slot_of[:, None] == slot_ids[None, :]) & inside[:, None]).astype(jnp.bfloat16)
+        outgoing = lax.dot_general(
+            placing, generated, (((0,), (0,)), ((), ())), preferred_element_type=jnp.float32
+        ).astype(jnp.bfloat16)
+        arrived = swap_blocks(outgoing.reshape(group_count, chunk_cap, width), "dp")
+        arrived = arrived.reshape(chunk_slots, width)
+        pre_act = jnp.dot(arrived, proj_parts[0], preferred_element_type=jnp.float32)
+        for s in range(1, tensor_count):
+            got = lax.ppermute(arrived, "tensor", pairs_for(s, tensor_count))
+            pre_act = pre_act + jnp.dot(got, proj_parts[s], preferred_element_type=jnp.float32)
+        pre_grad = (-slope_times(pre_act, jnp.broadcast_to(head_row, pre_act.shape))).astype(jnp.bfloat16)
+        back = [
+            lax.dot_general(
+                pre_grad, part, (((1,), (1,)), ((), ())), preferred_element_type=jnp.float32
+            ).astype(jnp.bfloat16)
+            for part in proj_parts
+        ]
+        critic_grad = back[0].astype(jnp.float32)
+        for s in range(1, tensor_count):
+            critic_grad = critic_grad + lax.ppermute(
+                back[s], "tensor", pairs_for(s, tensor_count)
+            ).astype(jnp.float32)
+        critic_grad = critic_grad.astype(jnp.bfloat16)
+        returned = swap_blocks(critic_grad.reshape(group_count, chunk_cap, width), "dp")
+        returned = returned.reshape(chunk_slots, width)
+        part = jnp.dot(placing, returned, preferred_element_type=jnp.float32)
+        input_grad = part if input_grad is None else input_grad + part
+    return (generated, input_grad.astype(jnp.bfloat16))
 
 
 def solution(mesh):

time: 133 us -> 123 us (0.925)
  local copies, waits for them, and re-layouts: 16 us -> 7.84 us
  waiting for transfers between devices: 65.4 us -> 62.9 us
  matrix products: 14.3 us -> 15.8 us
    reshape x1, local copies, waits for them, and re-layouts: 6.69 us -> 1.23 us  [shards(): head_blocks = head_terms.reshape(tok_rows, tensor_count, width)]
    dynamic_slice x0 -> x1, local copies, waits for them, and re-layouts: none -> 3.3 us  [shards(): lax.dynamic_index_in_dim(head_blocks, me_t, 1, keepdims=False)]
    another operation x3 -> x2, other arithmetic: 3.38 us -> 0.61 us
    ppermute x9, waiting for transfers between devices: 52.8 us -> 50.2 us  [the longest x3 19.7 us: shards(): lax.ppermute(back[s], 'tensor', pairs_for(s, tensor_count))]
    gather x1 -> x0, local copies, waits for them, and re-layouts: 1.98 us -> none  [gather_blocks(): return jnp.take(stacked, order, axis=0)]
    dot_general x3 -> x10, matrix products: 13.8 us -> 15.3 us  [the longest x3 6.15 us: shards(): jnp.dot(got, proj_parts[s], preferred_element_type=jnp.float32)]
    unnamed x28 -> x37, local copies, waits for them, and re-layouts: 2.97 us -> 1.8 us
  transfers between devices with their start and end apart: 23 -> 23, of which waited for: 9 -> 8; matrix products, arithmetic and copies ran while one was open for 5% -> 8% of each run, Pallas kernels for 0% -> 0%
where the time goes in v2:
time: 123 us; the launch traced here: 122 us
  waiting for transfers between devices  62.9 us (51%)
  starting transfers between devices  29.7 us (24%)
  matrix products  15.8 us (13%)
  local copies, waits for them, and re-layouts  7.84 us (6%)
  other arithmetic  4.81 us (4%)
    ppermute x3, waiting for transfers between devices, shards(): lax.ppermute(back[s], 'tensor', pairs_for(s, tensor_count))  19.7 us
    ppermute x14, starting transfers between devices, swap_blocks(): got.append(lax.ppermute(chunk, axis, pairs_for(s, n)))  17.8 us
    ppermute x3, waiting for transfers between devices, shards(): got = lax.ppermute(arrived, 'tensor', pairs_for(s, tensor_count))  17.4 us
    ppermute x3, waiting for transfers between devices, shards(): lax.ppermute(chunk, 'tensor', pairs_for(s, tensor_count))  13.2 us
    ppermute x14, waiting for transfers between devices, swap_blocks(): got.append(lax.ppermute(chunk, axis, pairs_for(s, n)))  12.6 us
    dot_general x3, matrix products, shards(): jnp.dot(got, proj_parts[s], preferred_element_type=jnp.float32)  6.15 us
    ppermute x3, starting transfers between devices, shards(): lax.ppermute(chunk, 'tensor', pairs_for(s, tensor_count))  4.66 us
    dot_general x1, matrix products, shards(): jnp.dot(context, out_proj, preferred_element_type=jnp.float32)  3.72 us
  transfers between devices with their start and end apart: 23, of which 8 were waited for; matrix products, arithmetic and copies ran while one was open for 8% of the time, Pallas kernels for 0%

profile of v2, /device:TPU:0, one launch (start us, length us, event | category | flops | bytes accessed | tf_op | source)
XLA Modules:
  0.0 122.1 jit_solution(16576258339733600162)
XLA Ops:
  1.6 3.7 %convolution_convert_fusion = bf16[256,3072]{1,0:T(8,128)(2,1)S(1)} fusion(bf16[256,768]{1,0:T(8,128)(2,1)S(1)} %copy-done, bf16[768,3072]{1,0:T(8,128)(2,1)} %param.11), kind=kOutput, calls=%fused_computation.2 | convolution fusion | flops 1208745984 | bytes 6684672 | tf_op jit(solution)/shard_map/dot_general | solution.py:90
  6.7 3.3 %constant_dynamic-slice_fusion.3 = (bf16[256,1,768]{2,1,0:T(2,128)(2,1)S(1)}, bf16[256,1,768]{2,1,0:T(2,128)(2,1)S(1)}, bf16[256,1,768]{2,1,0:T(2,128)(2,1)S(1)}, bf16[256,1,768]{2,1,0:T(2,128)(2,1)S(1)}) fusion(bf16[256,4,768]{2,1,0:T(4,128)(2,1)S(1)} %reshape.54, s32[]{:T(128)S(6)} %select_n.62, s32[]{:T(128)S(6)} %select_n.64, s32[]{:T(128)S(6)} %select_n.63, ...), kind=kLoop, calls=%fused_computation.109 | loop fusion | bytes 3145744 | tf_op jit(solution)/shard_map/jit(dynamic_index_in_dim)/dynamic_slice | solution.py:92
  10.0 3.0 %collective-permute-start = (bf16[256,768]{1,0:T(8,128)(2,1)S(1)}, bf16[256,768]{1,0:T(8,128)(2,1)S(1)}, u32[]{:S(2)}, u32[]{:S(2)}) collective-permute-start(bf16[256,768]{1,0:T(8,128)(2,1)S(1)} %bitcast.128), channel_id=1, source_target_pairs={{0,1},{1,0},{2,3},{3,2},{4,5},{5,4},{6,7},{7,6},{8,9},{9,8},{10,11... | collective-permute-start | bytes 1179656 | tf_op jit(solution)/shard_map/ppermute | solution.py:96
  13.1 1.6 %collective-permute-start.1 = (bf16[256,768]{1,0:T(8,128)(2,1)S(1)}, bf16[256,768]{1,0:T(8,128)(2,1)S(1)}, u32[]{:S(2)}, u32[]{:S(2)}) collective-permute-start(bf16[256,768]{1,0:T(8,128)(2,1)S(1)} %bitcast.129), channel_id=1, source_target_pairs={{0,2},{1,3},{2,0},{3,1},{4,6},{5,7},{6,4},{7,5},{8,10},{9,11},{10,... | collective-permute-start | bytes 1179656 | tf_op jit(solution)/shard_map/ppermute | solution.py:96
  19.0 4.0 %collective-permute-done = bf16[256,768]{1,0:T(8,128)(2,1)S(1)} collective-permute-done((bf16[256,768]{1,0:T(8,128)(2,1)S(1)}, bf16[256,768]{1,0:T(8,128)(2,1)S(1)}, u32[]{:S(2)}, u32[]{:S(2)}) %collective-permute-start) | collective-permute-done | bytes 393248 | tf_op jit(solution)/shard_map/ppermute | solution.py:96
  23.0 9.2 %collective-permute-done.1 = bf16[256,768]{1,0:T(8,128)(2,1)S(1)} collective-permute-done((bf16[256,768]{1,0:T(8,128)(2,1)S(1)}, bf16[256,768]{1,0:T(8,128)(2,1)S(1)}, u32[]{:S(2)}, u32[]{:S(2)}) %collective-permute-start.1) | collective-permute-done | bytes 393248 | tf_op jit(solution)/shard_map/ppermute | solution.py:96
  34.0 1.6 %collective-permute-start.4 = (bf16[40,768]{1,0:T(8,128)(2,1)S(1)}, bf16[40,768]{1,0:T(8,128)(2,1)S(1)}, u32[]{:S(2)}, u32[]{:S(2)}) collective-permute-start(bf16[40,768]{1,0:T(8,128)(2,1)S(1)} %get-tuple-element.20), channel_id=1, source_target_pairs={{0,8},{4,12},{8,0},{12,4},{16,24},{20,28},{24,16},{28,20},{1,9},{5... | collective-permute-start | bytes 184328 | tf_op jit(solution)/shard_map/ppermute | solution.py:64
  35.8 2.6 %collective-permute-start.6 = (bf16[40,768]{1,0:T(8,128)(2,1)S(1)}, bf16[40,768]{1,0:T(8,128)(2,1)S(1)}, u32[]{:S(2)}, u32[]{:S(2)}) collective-permute-start(bf16[40,768]{1,0:T(8,128)(2,1)S(1)} %get-tuple-element.18), channel_id=1, source_target_pairs={{0,16},{4,20},{8,24},{12,28},{16,0},{20,4},{24,8},{28,12},{1,17},{... | collective-permute-start | bytes 184328 | tf_op jit(solution)/shard_map/ppermute | solution.py:64
  38.5 3.6 %collective-permute-start.8 = (bf16[40,768]{1,0:T(8,128)(2,1)S(1)}, bf16[40,768]{1,0:T(8,128)(2,1)S(1)}, u32[]{:S(2)}, u32[]{:S(2)}) collective-permute-start(bf16[40,768]{1,0:T(8,128)(2,1)S(1)} %get-tuple-element.16), channel_id=1, source_target_pairs={{0,24},{4,28},{8,16},{12,20},{16,8},{20,12},{24,0},{28,4},{1,25},{... | collective-permute-start | bytes 184328 | tf_op jit(solution)/shard_map/ppermute | solution.py:64
  42.2 6.3 %collective-permute-done.7 = bf16[40,768]{1,0:T(8,128)(2,1)S(1)} collective-permute-done((bf16[40,768]{1,0:T(8,128)(2,1)S(1)}, bf16[40,768]{1,0:T(8,128)(2,1)S(1)}, u32[]{:S(2)}, u32[]{:S(2)}) %collective-permute-start.7) | collective-permute-done | bytes 61472 | tf_op jit(solution)/shard_map/ppermute | solution.py:64
  50.9 1.6 %collective-permute-start.10 = (bf16[320,768]{1,0:T(8,128)(2,1)S(1)}, bf16[320,768]{1,0:T(8,128)(2,1)S(1)}, u32[]{:S(2)}, u32[]{:S(2)}) collective-permute-start(bf16[320,768]{1,0:T(8,128)(2,1)S(1)} %bitcast.123), channel_id=1, source_target_pairs={{0,1},{1,0},{2,3},{3,2},{4,5},{5,4},{6,7},{7,6},{8,9},{9,8},{10,11... | collective-permute-start | bytes 1474568 | tf_op jit(solution)/shard_map/ppermute | solution.py:123
  52.9 1.8 %fusion.10 = f32[320,768]{1,0:T(8,128)S(1)} fusion(bf16[320,768]{1,0:T(8,128)(2,1)S(1)} %bitcast.125, bf16[4,768,768]{2,1,0:T(8,128)(2,1)} %bitcast.131, s32[]{:T(128)S(6)} %select_n.62), kind=kOutput, calls=%fused_computation.23 | convolution fusion | flops 377487360 | bytes 2654212 | tf_op jit(solution)/shard_map/dot_general | solution.py:121
  54.8 9.6 %collective-permute-done.12 = bf16[320,768]{1,0:T(8,128)(2,1)S(1)} collective-permute-done((bf16[320,768]{1,0:T(8,128)(2,1)S(1)}, bf16[320,768]{1,0:T(8,128)(2,1)S(1)}, u32[]{:S(2)}, u32[]{:S(2)}) %collective-permute-start.12) | collective-permute-done | bytes 491552 | tf_op jit(solution)/shard_map/ppermute | solution.py:123
  64.4 2.0 %fusion.3 = f32[320,768]{1,0:T(8,128)S(1)} fusion(bf16[320,768]{1,0:T(8,128)(2,1)S(1)} %collective-permute-done.12, bf16[4,768,768]{2,1,0:T(8,128)(2,1)} %bitcast.132, s32[]{:T(128)S(6)} %select_n.65), kind=kOutput, calls=%fused_computation.16 | convolution fusion | flops 377487360 | bytes 2654212 | tf_op jit(solution)/shard_map/dot_general | solution.py:124
  66.4 7.8 %collective-permute-done.10 = bf16[320,768]{1,0:T(8,128)(2,1)S(1)} collective-permute-done((bf16[320,768]{1,0:T(8,128)(2,1)S(1)}, bf16[320,768]{1,0:T(8,128)(2,1)S(1)}, u32[]{:S(2)}, u32[]{:S(2)}) %collective-permute-start.10) | collective-permute-done | bytes 491552 | tf_op jit(solution)/shard_map/ppermute | solution.py:123
  74.1 1.8 %convolution_add_fusion.1 = f32[320,768]{1,0:T(8,128)S(1)} fusion(f32[320,768]{1,0:T(8,128)S(1)} %fusion.10, bf16[320,768]{1,0:T(8,128)(2,1)S(1)} %collective-permute-done.10, bf16[4,768,768]{2,1,0:T(8,128)(2,1)} %bitcast.133, s32[]{:T(128)S(6)} %select_n.63), kind=kOutput, calls=%fused_computation.7 | convolution fusion | flops 377733120 | bytes 3637252 | tf_op jit(solution)/shard_map/dot_general | solution.py:124
  76.0 2.4 %fusion.27 = bf16[320,768]{1,0:T(8,128)(2,1)S(1)} fusion(f32[320,768]{1,0:T(8,128)S(1)} %fusion.3, f32[320,768]{1,0:T(8,128)S(1)} %convolution_add_fusion.1, bf16[320,768]{1,0:T(8,128)(2,1)S(1)} %collective-permute-done.11, bf16[4,768,768]{2,1,0:T(8,128)(2,1)} %bitcast.134, s32[]{:T(128)S(6)} %select_n.64, f32[768]{0:T(1024)S(1)} %reduce.1, ...), kind=kOutput, calls=%fused_computation.40 | convolution fusion | flops 382894080 | bytes 4134916 | tf_op jit(solution)/shard_map/dot_general | solution.py:124
  82.0 1.8 %collective-permute-start.15 = (bf16[320,768]{1,0:T(8,128)(2,1)S(1)}, bf16[320,768]{1,0:T(8,128)(2,1)S(1)}, u32[]{:S(2)}, u32[]{:S(2)}) collective-permute-start(bf16[320,768]{1,0:T(8,128)(2,1)S(1)} %convolution_convert_fusion.2), channel_id=1, source_target_pairs={{0,3},{1,2},{2,1},{3,0},{4,7},{5,6},{6,5},{7,4},{8,11},{9,10},{10,... | collective-permute-start | bytes 1474568 | tf_op jit(solution)/shard_map/ppermute | solution.py:134
  83.7 10.7 %collective-permute-done.13 = bf16[320,768]{1,0:T(8,128)(2,1)S(1)} collective-permute-done((bf16[320,768]{1,0:T(8,128)(2,1)S(1)}, bf16[320,768]{1,0:T(8,128)(2,1)S(1)}, u32[]{:S(2)}, u32[]{:S(2)}) %collective-permute-start.13) | collective-permute-done | bytes 491552 | tf_op jit(solution)/shard_map/ppermute | solution.py:134
  94.4 9.0 %collective-permute-done.14 = bf16[320,768]{1,0:T(8,128)(2,1)S(1)} collective-permute-done((bf16[320,768]{1,0:T(8,128)(2,1)S(1)}, bf16[320,768]{1,0:T(8,128)(2,1)S(1)}, u32[]{:S(2)}, u32[]{:S(2)}) %collective-permute-start.14) | collective-permute-done | bytes 491552 | tf_op jit(solution)/shard_map/ppermute | solution.py:134
  104.3 3.2 %collective-permute-start.17 = (bf16[40,768]{1,0:T(8,128)(2,1)S(1)}, bf16[40,768]{1,0:T(8,128)(2,1)S(1)}, u32[]{:S(2)}, u32[]{:S(2)}) collective-permute-start(bf16[40,768]{1,0:T(8,128)(2,1)S(1)} %get-tuple-element.12), channel_id=1, source_target_pairs={{0,8},{4,12},{8,0},{12,4},{16,24},{20,28},{24,16},{28,20},{1,9},{5... | collective-permute-start | bytes 184328 | tf_op jit(solution)/shard_map/ppermute | solution.py:64
  107.6 2.8 %collective-permute-start.19 = (bf16[40,768]{1,0:T(8,128)(2,1)S(1)}, bf16[40,768]{1,0:T(8,128)(2,1)S(1)}, u32[]{:S(2)}, u32[]{:S(2)}) collective-permute-start(bf16[40,768]{1,0:T(8,128)(2,1)S(1)} %get-tuple-element.10), channel_id=1, source_target_pairs={{0,16},{4,20},{8,24},{12,28},{16,0},{20,4},{24,8},{28,12},{1,17},{... | collective-permute-start | bytes 184328 | tf_op jit(solution)/shard_map/ppermute | solution.py:64
  110.3 2.1 %collective-permute-start.21 = (bf16[40,768]{1,0:T(8,128)(2,1)S(1)}, bf16[40,768]{1,0:T(8,128)(2,1)S(1)}, u32[]{:S(2)}, u32[]{:S(2)}) collective-permute-start(bf16[40,768]{1,0:T(8,128)(2,1)S(1)} %get-tuple-element.8), channel_id=1, source_target_pairs={{0,24},{4,28},{8,16},{12,20},{16,8},{20,12},{24,0},{28,4},{1,25},{... | collective-permute-start | bytes 184328 | tf_op jit(solution)/shard_map/ppermute | solution.py:64
  113.9 6.3 %collective-permute-done.20 = bf16[40,768]{1,0:T(8,128)(2,1)S(1)} collective-permute-done((bf16[40,768]{1,0:T(8,128)(2,1)S(1)}, bf16[40,768]{1,0:T(8,128)(2,1)S(1)}, u32[]{:S(2)}, u32[]{:S(2)}) %collective-permute-start.20) | collective-permute-done | bytes 61472 | tf_op jit(solution)/shard_map/ppermute | solution.py:64
  (96 shorter events, 19.4 us)
Async XLA Ops:
  10.0 12.9 %collective-permute-start = (bf16[256,768]{1,0:T(8,128)(2,1)S(1)}, bf16[256,768]{1,0:T(8,128)(2,1)S(1)}, u32[]{:S(2)}, u32[]{:S(2)}) collective-permute-start(bf16[256,768]{1,0:T(8,128)(2,1)S(1)} %bitcast.128), channel_id=1, source_target_pairs={{0,1},{1,0},{2,3},{3,2},{4,5},{5,4},{6,7},{7,6},{8,9},{9,8},{10,11... | collective-permute-start | bytes 1179656 | tf_op jit(solution)/shard_map/ppermute | solution.py:96
  13.1 19.1 %collective-permute-start.1 = (bf16[256,768]{1,0:T(8,128)(2,1)S(1)}, bf16[256,768]{1,0:T(8,128)(2,1)S(1)}, u32[]{:S(2)}, u32[]{:S(2)}) collective-permute-start(bf16[256,768]{1,0:T(8,128)(2,1)S(1)} %bitcast.129), channel_id=1, source_target_pairs={{0,2},{1,3},{2,0},{3,1},{4,6},{5,7},{6,4},{7,5},{8,10},{9,11},{10,... | collective-permute-start | bytes 1179656 | tf_op jit(solution)/shard_map/ppermute | solution.py:96
  14.7 17.4 %collective-permute-start.2 = (bf16[256,768]{1,0:T(8,128)(2,1)S(1)}, bf16[256,768]{1,0:T(8,128)(2,1)}, u32[]{:S(2)}, u32[]{:S(2)}) collective-permute-start(bf16[256,768]{1,0:T(8,128)(2,1)S(1)} %bitcast.130), channel_id=1, source_target_pairs={{0,3},{1,2},{2,1},{3,0},{4,7},{5,6},{6,5},{7,4},{8,11},{9,10},{10,... | collective-permute-start | bytes 1179656 | tf_op jit(solution)/shard_map/ppermute | solution.py:96
  33.9 4.6 %collective-permute-start.3 = (bf16[40,768]{1,0:T(8,128)(2,1)S(1)}, bf16[40,768]{1,0:T(8,128)(2,1)S(1)}, u32[]{:S(2)}, u32[]{:S(2)}) collective-permute-start(bf16[40,768]{1,0:T(8,128)(2,1)S(1)} %get-tuple-element.21), channel_id=1, source_target_pairs={{0,4},{4,0},{8,12},{12,8},{16,20},{20,16},{24,28},{28,24},{1,5},{5... | collective-permute-start | bytes 184328 | tf_op jit(solution)/shard_map/ppermute | solution.py:64
  34.0 8.1 %collective-permute-start.4 = (bf16[40,768]{1,0:T(8,128)(2,1)S(1)}, bf16[40,768]{1,0:T(8,128)(2,1)S(1)}, u32[]{:S(2)}, u32[]{:S(2)}) collective-permute-start(bf16[40,768]{1,0:T(8,128)(2,1)S(1)} %get-tuple-element.20), channel_id=1, source_target_pairs={{0,8},{4,12},{8,0},{12,4},{16,24},{20,28},{24,16},{28,20},{1,9},{5... | collective-permute-start | bytes 184328 | tf_op jit(solution)/shard_map/ppermute | solution.py:64
  35.6 6.6 %collective-permute-start.5 = (bf16[40,768]{1,0:T(8,128)(2,1)S(1)}, bf16[40,768]{1,0:T(8,128)(2,1)S(1)}, u32[]{:S(2)}, u32[]{:S(2)}) collective-permute-start(bf16[40,768]{1,0:T(8,128)(2,1)S(1)} %get-tuple-element.19), channel_id=1, source_target_pairs={{0,12},{4,8},{8,4},{12,0},{16,28},{20,24},{24,20},{28,16},{1,13},{... | collective-permute-start | bytes 184328 | tf_op jit(solution)/shard_map/ppermute | solution.py:64
  35.8 6.4 %collective-permute-start.6 = (bf16[40,768]{1,0:T(8,128)(2,1)S(1)}, bf16[40,768]{1,0:T(8,128)(2,1)S(1)}, u32[]{:S(2)}, u32[]{:S(2)}) collective-permute-start(bf16[40,768]{1,0:T(8,128)(2,1)S(1)} %get-tuple-element.18), channel_id=1, source_target_pairs={{0,16},{4,20},{8,24},{12,28},{16,0},{20,4},{24,8},{28,12},{1,17},{... | collective-permute-start | bytes 184328 | tf_op jit(solution)/shard_map/ppermute | solution.py:64
  38.4 10.1 %collective-permute-start.7 = (bf16[40,768]{1,0:T(8,128)(2,1)S(1)}, bf16[40,768]{1,0:T(8,128)(2,1)S(1)}, u32[]{:S(2)}, u32[]{:S(2)}) collective-permute-start(bf16[40,768]{1,0:T(8,128)(2,1)S(1)} %get-tuple-element.17), channel_id=1, source_target_pairs={{0,20},{4,16},{8,28},{12,24},{16,4},{20,0},{24,12},{28,8},{1,21},{... | collective-permute-start | bytes 184328 | tf_op jit(solution)/shard_map/ppermute | solution.py:64
  38.5 10.1 %collective-permute-start.8 = (bf16[40,768]{1,0:T(8,128)(2,1)S(1)}, bf16[40,768]{1,0:T(8,128)(2,1)S(1)}, u32[]{:S(2)}, u32[]{:S(2)}) collective-permute-start(bf16[40,768]{1,0:T(8,128)(2,1)S(1)} %get-tuple-element.16), channel_id=1, source_target_pairs={{0,24},{4,28},{8,16},{12,20},{16,8},{20,12},{24,0},{28,4},{1,25},{... | collective-permute-start | bytes 184328 | tf_op jit(solution)/shard_map/ppermute | solution.py:64
  42.1 6.5 %collective-permute-start.9 = (bf16[40,768]{1,0:T(8,128)(2,1)S(1)}, bf16[40,768]{1,0:T(8,128)(2,1)S(1)}, u32[]{:S(2)}, u32[]{:S(2)}) collective-permute-start(bf16[40,768]{1,0:T(8,128)(2,1)S(1)} %get-tuple-element.15), channel_id=1, source_target_pairs={{0,28},{4,24},{8,20},{12,16},{16,12},{20,8},{24,4},{28,0},{1,29},{... | collective-permute-start | bytes 184328 | tf_op jit(solution)/shard_map/ppermute | solution.py:64
  49.3 15.1 %collective-permute-start.12 = (bf16[320,768]{1,0:T(8,128)(2,1)S(1)}, bf16[320,768]{1,0:T(8,128)(2,1)S(1)}, u32[]{:S(2)}, u32[]{:S(2)}) collective-permute-start(bf16[320,768]{1,0:T(8,128)(2,1)S(1)} %bitcast.122), channel_id=1, source_target_pairs={{0,3},{1,2},{2,1},{3,0},{4,7},{5,6},{6,5},{7,4},{8,11},{9,10},{10,... | collective-permute-start | bytes 1474568 | tf_op jit(solution)/shard_map/ppermute | solution.py:123
  50.9 23.3 %collective-permute-start.10 = (bf16[320,768]{1,0:T(8,128)(2,1)S(1)}, bf16[320,768]{1,0:T(8,128)(2,1)S(1)}, u32[]{:S(2)}, u32[]{:S(2)}) collective-permute-start(bf16[320,768]{1,0:T(8,128)(2,1)S(1)} %bitcast.123), channel_id=1, source_target_pairs={{0,1},{1,0},{2,3},{3,2},{4,5},{5,4},{6,7},{7,6},{8,9},{9,8},{10,11... | collective-permute-start | bytes 1474568 | tf_op jit(solution)/shard_map/ppermute | solution.py:123
  52.4 23.5 %collective-permute-start.11 = (bf16[320,768]{1,0:T(8,128)(2,1)S(1)}, bf16[320,768]{1,0:T(8,128)(2,1)S(1)}, u32[]{:S(2)}, u32[]{:S(2)}) collective-permute-start(bf16[320,768]{1,0:T(8,128)(2,1)S(1)} %bitcast.124), channel_id=1, source_target_pairs={{0,2},{1,3},{2,0},{3,1},{4,6},{5,7},{6,4},{7,5},{8,10},{9,11},{10,... | collective-permute-start | bytes 1474568 | tf_op jit(solution)/shard_map/ppermute | solution.py:123
  79.6 41.4 %copy-start.7 = (pred[256]{0:T(512)(128)(4,1)S(1)}, pred[256]{0:T(512)(128)(4,1)}, u32[]{:S(2)}) copy-start(pred[256]{0:T(512)(128)(4,1)} %copy-done.6) | copy-start | bytes 772
  80.2 14.2 %collective-permute-start.13 = (bf16[320,768]{1,0:T(8,128)(2,1)S(1)}, bf16[320,768]{1,0:T(8,128)(2,1)S(1)}, u32[]{:S(2)}, u32[]{:S(2)}) collective-permute-start(bf16[320,768]{1,0:T(8,128)(2,1)S(1)} %convolution_convert_fusion.4), channel_id=1, source_target_pairs={{0,1},{1,0},{2,3},{3,2},{4,5},{5,4},{6,7},{7,6},{8,9},{9,8},{10,11... | collective-permute-start | bytes 1474568 | tf_op jit(solution)/shard_map/ppermute | solution.py:134
  80.8 22.7 %collective-permute-start.14 = (bf16[320,768]{1,0:T(8,128)(2,1)S(1)}, bf16[320,768]{1,0:T(8,128)(2,1)S(1)}, u32[]{:S(2)}, u32[]{:S(2)}) collective-permute-start(bf16[320,768]{1,0:T(8,128)(2,1)S(1)} %convolution_convert_fusion.3), channel_id=1, source_target_pairs={{0,2},{1,3},{2,0},{3,1},{4,6},{5,7},{6,4},{7,5},{8,10},{9,11},{10,... | collective-permute-start | bytes 1474568 | tf_op jit(solution)/shard_map/ppermute | solution.py:134
  82.0 21.5 %collective-permute-start.15 = (bf16[320,768]{1,0:T(8,128)(2,1)S(1)}, bf16[320,768]{1,0:T(8,128)(2,1)S(1)}, u32[]{:S(2)}, u32[]{:S(2)}) collective-permute-start(bf16[320,768]{1,0:T(8,128)(2,1)S(1)} %convolution_convert_fusion.2), channel_id=1, source_target_pairs={{0,3},{1,2},{2,1},{3,0},{4,7},{5,6},{6,5},{7,4},{8,11},{9,10},{10,... | collective-permute-start | bytes 1474568 | tf_op jit(solution)/shard_map/ppermute | solution.py:134
  104.2 6.1 %collective-permute-start.16 = (bf16[40,768]{1,0:T(8,128)(2,1)S(1)}, bf16[40,768]{1,0:T(8,128)(2,1)S(1)}, u32[]{:S(2)}, u32[]{:S(2)}) collective-permute-start(bf16[40,768]{1,0:T(8,128)(2,1)S(1)} %get-tuple-element.13), channel_id=1, source_target_pairs={{0,4},{4,0},{8,12},{12,8},{16,20},{20,16},{24,28},{28,24},{1,5},{5... | collective-permute-start | bytes 184328 | tf_op jit(solution)/shard_map/ppermute | solution.py:64
  104.3 8.2 %collective-permute-start.17 = (bf16[40,768]{1,0:T(8,128)(2,1)S(1)}, bf16[40,768]{1,0:T(8,128)(2,1)S(1)}, u32[]{:S(2)}, u32[]{:S(2)}) collective-permute-start(bf16[40,768]{1,0:T(8,128)(2,1)S(1)} %get-tuple-element.12), channel_id=1, source_target_pairs={{0,8},{4,12},{8,0},{12,4},{16,24},{20,28},{24,16},{28,20},{1,9},{5... | collective-permute-start | bytes 184328 | tf_op jit(solution)/shard_map/ppermute | solution.py:64
  107.5 6.3 %collective-permute-start.18 = (bf16[40,768]{1,0:T(8,128)(2,1)S(1)}, bf16[40,768]{1,0:T(8,128)(2,1)S(1)}, u32[]{:S(2)}, u32[]{:S(2)}) collective-permute-start(bf16[40,768]{1,0:T(8,128)(2,1)S(1)} %get-tuple-element.11), channel_id=1, source_target_pairs={{0,12},{4,8},{8,4},{12,0},{16,28},{20,24},{24,20},{28,16},{1,13},{... | collective-permute-start | bytes 184328 | tf_op jit(solution)/shard_map/ppermute | solution.py:64
  107.6 6.3 %collective-permute-start.19 = (bf16[40,768]{1,0:T(8,128)(2,1)S(1)}, bf16[40,768]{1,0:T(8,128)(2,1)S(1)}, u32[]{:S(2)}, u32[]{:S(2)}) collective-permute-start(bf16[40,768]{1,0:T(8,128)(2,1)S(1)} %get-tuple-element.10), channel_id=1, source_target_pairs={{0,16},{4,20},{8,24},{12,28},{16,0},{20,4},{24,8},{28,12},{1,17},{... | collective-permute-start | bytes 184328 | tf_op jit(solution)/shard_map/ppermute | solution.py:64
  110.3 9.9 %collective-permute-start.20 = (bf16[40,768]{1,0:T(8,128)(2,1)S(1)}, bf16[40,768]{1,0:T(8,128)(2,1)S(1)}, u32[]{:S(2)}, u32[]{:S(2)}) collective-permute-start(bf16[40,768]{1,0:T(8,128)(2,1)S(1)} %get-tuple-element.9), channel_id=1, source_target_pairs={{0,20},{4,16},{8,28},{12,24},{16,4},{20,0},{24,12},{28,8},{1,21},{... | collective-permute-start | bytes 184328 | tf_op jit(solution)/shard_map/ppermute | solution.py:64
  110.3 9.9 %collective-permute-start.21 = (bf16[40,768]{1,0:T(8,128)(2,1)S(1)}, bf16[40,768]{1,0:T(8,128)(2,1)S(1)}, u32[]{:S(2)}, u32[]{:S(2)}) collective-permute-start(bf16[40,768]{1,0:T(8,128)(2,1)S(1)} %get-tuple-element.8), channel_id=1, source_target_pairs={{0,24},{4,28},{8,16},{12,20},{16,8},{20,12},{24,0},{28,4},{1,25},{... | collective-permute-start | bytes 184328 | tf_op jit(solution)/shard_map/ppermute | solution.py:64
  112.5 7.8 %collective-permute-start.22 = (bf16[40,768]{1,0:T(8,128)(2,1)S(1)}, bf16[40,768]{1,0:T(8,128)(2,1)S(1)}, u32[]{:S(2)}, u32[]{:S(2)}) collective-permute-start(bf16[40,768]{1,0:T(8,128)(2,1)S(1)} %get-tuple-element.7), channel_id=1, source_target_pairs={{0,28},{4,24},{8,20},{12,16},{16,12},{20,8},{24,4},{28,0},{1,29},{... | collective-permute-start | bytes 184328 | tf_op jit(solution)/shard_map/ppermute | solution.py:64
  (10 other events, 167.8 us)

commit v3 on v2

--- a/solution.py
+++ b/solution.py
@@ -70,7 +70,7 @@
     return jnp.take(stacked, order, axis=0)
 
 
-SLOT_CHUNKS = 1
+SLOT_CHUNKS = 2
 
 
 def shards(context, residual_in, out_proj, members, host_group, member_proj, member_head):

time: 123 us -> 170 us (1.38)
  starting transfers between devices: 29.7 us -> 48.4 us
  waiting for transfers between devices: 62.9 us -> 77.2 us
  matrix products: 15.8 us -> 24.5 us
  other arithmetic: 4.81 us -> 8.67 us
    ppermute x14 -> x28, waiting for transfers between devices: 12.6 us -> 29.7 us  [swap_blocks(): got.append(lax.ppermute(chunk, axis, pairs_for(s, n)))]
    ppermute x14 -> x28, starting transfers between devices: 17.8 us -> 28.5 us  [swap_blocks(): got.append(lax.ppermute(chunk, axis, pairs_for(s, n)))]
    ppermute x3 -> x6, starting transfers between devices: 3.62 us -> 8.12 us  [shards(): got = lax.ppermute(arrived, 'tensor', pairs_for(s, tensor_count))]
    dot_general x3 -> x6, matrix products: 6.15 us -> 10.2 us  [shards(): jnp.dot(got, proj_parts[s], preferred_element_type=jnp.float32)]
    ppermute x3 -> x6, starting transfers between devices: 3.55 us -> 7.11 us  [shards(): lax.ppermute(back[s], 'tensor', pairs_for(s, tensor_count))]
    ppermute x3, waiting for transfers between devices: 13.2 us -> 10 us  [shards(): lax.ppermute(chunk, 'tensor', pairs_for(s, tensor_count))]
    dot_general x4 -> x8, matrix products: 2.46 us -> 4.48 us  [shards(): lax.dot_general(pre_grad, part, (((1,), (1,)), ((), ())), preferred_eleme...]
    ppermute x3 -> x6, waiting for transfers between devices: 17.4 us -> 18 us  [shards(): got = lax.ppermute(arrived, 'tensor', pairs_for(s, tensor_count))]
  transfers between devices with their start and end apart: 23 -> 43, of which waited for: 8 -> 22; matrix products, arithmetic and copies ran while one was open for 8% -> 14% of each run, Pallas kernels for 0% -> 0%
where the time goes in v3:
time: 170 us
  waiting for transfers between devices  77.2 us (45%)
  starting transfers between devices  48.4 us (28%)
  matrix products  24.5 us (14%)
  local copies, waits for them, and re-layouts  9.48 us (6%)
  other arithmetic  8.67 us (5%)
    ppermute x28, waiting for transfers between devices, swap_blocks(): got.append(lax.ppermute(chunk, axis, pairs_for(s, n)))  29.7 us
    ppermute x28, starting transfers between devices, swap_blocks(): got.append(lax.ppermute(chunk, axis, pairs_for(s, n)))  28.5 us
    ppermute x6, waiting for transfers between devices, shards(): lax.ppermute(back[s], 'tensor', pairs_for(s, tensor_count))  19.4 us
    ppermute x6, waiting for transfers between devices, shards(): got = lax.ppermute(arrived, 'tensor', pairs_for(s, tensor_count))  18 us
    dot_general x6, matrix products, shards(): jnp.dot(got, proj_parts[s], preferred_element_type=jnp.float32)  10.2 us
    ppermute x3, waiting for transfers between devices, shards(): lax.ppermute(chunk, 'tensor', pairs_for(s, tensor_count))  10 us
    ppermute x6, starting transfers between devices, shards(): got = lax.ppermute(arrived, 'tensor', pairs_for(s, tensor_count))  8.12 us
    ppermute x6, starting transfers between devices, shards(): lax.ppermute(back[s], 'tensor', pairs_for(s, tensor_count))  7.11 us
  transfers between devices with their start and end apart: 43, of which 22 were waited for; matrix products, arithmetic and copies ran while one was open for 14% of the time, Pallas kernels for 0%

profile of v3, /device:TPU:0, one launch (start us, length us, event | category | flops | bytes accessed | tf_op | source)
XLA Modules:
  0.0 169.6 jit_solution(1851050956200370670)
XLA Ops:
  1.6 3.7 %convolution_convert_fusion = bf16[256,3072]{1,0:T(8,128)(2,1)S(1)} fusion(bf16[256,768]{1,0:T(8,128)(2,1)S(1)} %copy-done, bf16[768,3072]{1,0:T(8,128)(2,1)} %param.11), kind=kOutput, calls=%fused_computation.4 | convolution fusion | flops 1208745984 | bytes 6684672 | tf_op jit(solution)/shard_map/dot_general | solution.py:90
  6.7 3.3 %constant_dynamic-slice_fusion.3 = (bf16[256,1,768]{2,1,0:T(2,128)(2,1)S(1)}, bf16[256,1,768]{2,1,0:T(2,128)(2,1)S(1)}, bf16[256,1,768]{2,1,0:T(2,128)(2,1)S(1)}, bf16[256,1,768]{2,1,0:T(2,128)(2,1)S(1)}) fusion(bf16[256,4,768]{2,1,0:T(4,128)(2,1)S(1)} %reshape.77, s32[]{:T(128)S(6)} %select_n.78, s32[]{:T(128)S(6)} %select_n.80, s32[]{:T(128)S(6)} %select_n.79, ...), kind=kLoop, calls=%fused_computation.188 | loop fusion | bytes 3145744 | tf_op jit(solution)/shard_map/jit(dynamic_index_in_dim)/dynamic_slice | solution.py:92
  10.0 3.0 %collective-permute-start = (bf16[256,768]{1,0:T(8,128)(2,1)S(1)}, bf16[256,768]{1,0:T(8,128)(2,1)S(1)}, u32[]{:S(2)}, u32[]{:S(2)}) collective-permute-start(bf16[256,768]{1,0:T(8,128)(2,1)S(1)} %bitcast.223), channel_id=1, source_target_pairs={{0,1},{1,0},{2,3},{3,2},{4,5},{5,4},{6,7},{7,6},{8,9},{9,8},{10,11... | collective-permute-start | bytes 1179656 | tf_op jit(solution)/shard_map/ppermute | solution.py:96
  23.0 9.2 %collective-permute-done.1 = bf16[256,768]{1,0:T(8,128)(2,1)S(1)} collective-permute-done((bf16[256,768]{1,0:T(8,128)(2,1)S(1)}, bf16[256,768]{1,0:T(8,128)(2,1)S(1)}, u32[]{:S(2)}, u32[]{:S(2)}) %collective-permute-start.1) | collective-permute-done | bytes 393248 | tf_op jit(solution)/shard_map/ppermute | solution.py:96
  37.2 2.6 %collective-permute-start.6 = (bf16[20,768]{1,0:T(8,128)(2,1)S(1)}, bf16[20,768]{1,0:T(8,128)(2,1)S(1)}, u32[]{:S(2)}, u32[]{:S(2)}) collective-permute-start(bf16[20,768]{1,0:T(8,128)(2,1)S(1)} %get-tuple-element.34), channel_id=1, source_target_pairs={{0,16},{4,20},{8,24},{12,28},{16,0},{20,4},{24,8},{28,12},{1,17},{... | collective-permute-start | bytes 92168 | tf_op jit(solution)/shard_map/ppermute | solution.py:64
  41.3 2.5 %collective-permute-done.24 = bf16[20,768]{1,0:T(8,128)(2,1)S(1)} collective-permute-done((bf16[20,768]{1,0:T(8,128)(2,1)S(1)}, bf16[20,768]{1,0:T(8,128)(2,1)S(1)}, u32[]{:S(2)}, u32[]{:S(2)}) %collective-permute-start.24) | collective-permute-done | bytes 30752 | tf_op jit(solution)/shard_map/ppermute | solution.py:64
  44.1 3.4 %collective-permute-done.25 = bf16[20,768]{1,0:T(8,128)(2,1)S(1)} collective-permute-done((bf16[20,768]{1,0:T(8,128)(2,1)S(1)}, bf16[20,768]{1,0:T(8,128)(2,1)S(1)}, u32[]{:S(2)}, u32[]{:S(2)}) %collective-permute-start.25) | collective-permute-done | bytes 30752 | tf_op jit(solution)/shard_map/ppermute | solution.py:64
  48.6 3.8 %collective-permute-done.26 = bf16[20,768]{1,0:T(8,128)(2,1)S(1)} collective-permute-done((bf16[20,768]{1,0:T(8,128)(2,1)S(1)}, bf16[20,768]{1,0:T(8,128)(2,1)S(1)}, u32[]{:S(2)}, u32[]{:S(2)}) %collective-permute-start.26) | collective-permute-done | bytes 30752 | tf_op jit(solution)/shard_map/ppermute | solution.py:64
  52.4 4.3 %collective-permute-done.27 = bf16[20,768]{1,0:T(8,128)(2,1)S(1)} collective-permute-done((bf16[20,768]{1,0:T(8,128)(2,1)S(1)}, bf16[20,768]{1,0:T(8,128)(2,1)S(1)}, u32[]{:S(2)}, u32[]{:S(2)}) %collective-permute-start.27) | collective-permute-done | bytes 30752 | tf_op jit(solution)/shard_map/ppermute | solution.py:64
  56.7 2.3 %collective-permute-start.28 = (bf16[20,768]{1,0:T(8,128)(2,1)S(1)}, bf16[20,768]{1,0:T(8,128)(2,1)S(1)}, u32[]{:S(2)}, u32[]{:S(2)}) collective-permute-start(bf16[20,768]{1,0:T(8,128)(2,1)S(1)} %get-tuple-element.16), channel_id=1, source_target_pairs={{0,24},{4,28},{8,16},{12,20},{16,8},{20,12},{24,0},{28,4},{1,25},{... | collective-permute-start | bytes 92168 | tf_op jit(solution)/shard_map/ppermute | solution.py:64
  58.9 3.5 %collective-permute-done.28 = bf16[20,768]{1,0:T(8,128)(2,1)S(1)} collective-permute-done((bf16[20,768]{1,0:T(8,128)(2,1)S(1)}, bf16[20,768]{1,0:T(8,128)(2,1)S(1)}, u32[]{:S(2)}, u32[]{:S(2)}) %collective-permute-start.28) | collective-permute-done | bytes 30752 | tf_op jit(solution)/shard_map/ppermute | solution.py:64
  62.5 5.2 %collective-permute-done.29 = bf16[20,768]{1,0:T(8,128)(2,1)S(1)} collective-permute-done((bf16[20,768]{1,0:T(8,128)(2,1)S(1)}, bf16[20,768]{1,0:T(8,128)(2,1)S(1)}, u32[]{:S(2)}, u32[]{:S(2)}) %collective-permute-start.29) | collective-permute-done | bytes 30752 | tf_op jit(solution)/shard_map/ppermute | solution.py:64
  69.0 2.3 %collective-permute-start.8 = (bf16[20,768]{1,0:T(8,128)(2,1)S(1)}, bf16[20,768]{1,0:T(8,128)(2,1)S(1)}, u32[]{:S(2)}, u32[]{:S(2)}) collective-permute-start(bf16[20,768]{1,0:T(8,128)(2,1)S(1)} %get-tuple-element.32), channel_id=1, source_target_pairs={{0,24},{4,28},{8,16},{12,20},{16,8},{20,12},{24,0},{28,4},{1,25},{... | collective-permute-start | bytes 92168 | tf_op jit(solution)/shard_map/ppermute | solution.py:64
  76.1 3.5 %collective-permute-done.30 = bf16[160,768]{1,0:T(8,128)(2,1)S(1)} collective-permute-done((bf16[160,768]{1,0:T(8,128)(2,1)S(1)}, bf16[160,768]{1,0:T(8,128)(2,1)S(1)}, u32[]{:S(2)}, u32[]{:S(2)}) %collective-permute-start.30) | collective-permute-done | bytes 245792 | tf_op jit(solution)/shard_map/ppermute | solution.py:123
  82.8 3.2 %collective-permute-done.32 = bf16[160,768]{1,0:T(8,128)(2,1)S(1)} collective-permute-done((bf16[160,768]{1,0:T(8,128)(2,1)S(1)}, bf16[160,768]{1,0:T(8,128)(2,1)S(1)}, u32[]{:S(2)}, u32[]{:S(2)}) %collective-permute-start.32) | collective-permute-done | bytes 245792 | tf_op jit(solution)/shard_map/ppermute | solution.py:123
  87.6 4.1 %collective-permute-done.31 = bf16[160,768]{1,0:T(8,128)(2,1)S(1)} collective-permute-done((bf16[160,768]{1,0:T(8,128)(2,1)S(1)}, bf16[160,768]{1,0:T(8,128)(2,1)S(1)}, u32[]{:S(2)}, u32[]{:S(2)}) %collective-permute-start.31) | collective-permute-done | bytes 245792 | tf_op jit(solution)/shard_map/ppermute | solution.py:123
  98.9 5.3 %collective-permute-done.33 = bf16[160,768]{1,0:T(8,128)(2,1)S(1)} collective-permute-done((bf16[160,768]{1,0:T(8,128)(2,1)S(1)}, bf16[160,768]{1,0:T(8,128)(2,1)S(1)}, u32[]{:S(2)}, u32[]{:S(2)}) %collective-permute-start.33) | collective-permute-done | bytes 245792 | tf_op jit(solution)/shard_map/ppermute | solution.py:134
  104.2 4.7 %collective-permute-done.34 = bf16[160,768]{1,0:T(8,128)(2,1)S(1)} collective-permute-done((bf16[160,768]{1,0:T(8,128)(2,1)S(1)}, bf16[160,768]{1,0:T(8,128)(2,1)S(1)}, u32[]{:S(2)}, u32[]{:S(2)}) %collective-permute-start.34) | collective-permute-done | bytes 245792 | tf_op jit(solution)/shard_map/ppermute | solution.py:134
  116.2 2.1 %collective-permute-start.42 = (bf16[20,768]{1,0:T(8,128)(2,1)S(1)}, bf16[20,768]{1,0:T(8,128)(2,1)S(1)}, u32[]{:S(2)}, u32[]{:S(2)}) collective-permute-start(bf16[20,768]{1,0:T(8,128)(2,1)S(1)} %get-tuple-element.7), channel_id=1, source_target_pairs={{0,28},{4,24},{8,20},{12,16},{16,12},{20,8},{24,4},{28,0},{1,29},{... | collective-permute-start | bytes 92168 | tf_op jit(solution)/shard_map/ppermute | solution.py:64
  127.6 3.7 %collective-permute-done.10 = bf16[160,768]{1,0:T(8,128)(2,1)S(1)} collective-permute-done((bf16[160,768]{1,0:T(8,128)(2,1)S(1)}, bf16[160,768]{1,0:T(8,128)(2,1)S(1)}, u32[]{:S(2)}, u32[]{:S(2)}) %collective-permute-start.10) | collective-permute-done | bytes 245792 | tf_op jit(solution)/shard_map/ppermute | solution.py:123
  132.9 3.5 %collective-permute-done.12 = bf16[160,768]{1,0:T(8,128)(2,1)S(1)} collective-permute-done((bf16[160,768]{1,0:T(8,128)(2,1)S(1)}, bf16[160,768]{1,0:T(8,128)(2,1)S(1)}, u32[]{:S(2)}, u32[]{:S(2)}) %collective-permute-start.12) | collective-permute-done | bytes 245792 | tf_op jit(solution)/shard_map/ppermute | solution.py:123
  145.2 5.4 %collective-permute-done.13 = bf16[160,768]{1,0:T(8,128)(2,1)S(1)} collective-permute-done((bf16[160,768]{1,0:T(8,128)(2,1)S(1)}, bf16[160,768]{1,0:T(8,128)(2,1)S(1)}, u32[]{:S(2)}, u32[]{:S(2)}) %collective-permute-start.13) | collective-permute-done | bytes 245792 | tf_op jit(solution)/shard_map/ppermute | solution.py:134
  150.6 4.0 %collective-permute-done.14 = bf16[160,768]{1,0:T(8,128)(2,1)S(1)} collective-permute-done((bf16[160,768]{1,0:T(8,128)(2,1)S(1)}, bf16[160,768]{1,0:T(8,128)(2,1)S(1)}, u32[]{:S(2)}, u32[]{:S(2)}) %collective-permute-start.14) | collective-permute-done | bytes 245792 | tf_op jit(solution)/shard_map/ppermute | solution.py:134
  159.9 2.3 %collective-permute-start.21 = (bf16[20,768]{1,0:T(8,128)(2,1)S(1)}, bf16[20,768]{1,0:T(8,128)(2,1)S(1)}, u32[]{:S(2)}, u32[]{:S(2)}) collective-permute-start(bf16[20,768]{1,0:T(8,128)(2,1)S(1)} %get-tuple-element.24), channel_id=1, source_target_pairs={{0,24},{4,28},{8,16},{12,20},{16,8},{20,12},{24,0},{28,4},{1,25},{... | collective-permute-start | bytes 92168 | tf_op jit(solution)/shard_map/ppermute | solution.py:64
  (184 shorter events, 77.3 us)
Async XLA Ops:
  10.0 12.9 %collective-permute-start = (bf16[256,768]{1,0:T(8,128)(2,1)S(1)}, bf16[256,768]{1,0:T(8,128)(2,1)S(1)}, u32[]{:S(2)}, u32[]{:S(2)}) collective-permute-start(bf16[256,768]{1,0:T(8,128)(2,1)S(1)} %bitcast.223), channel_id=1, source_target_pairs={{0,1},{1,0},{2,3},{3,2},{4,5},{5,4},{6,7},{7,6},{8,9},{9,8},{10,11... | collective-permute-start | bytes 1179656 | tf_op jit(solution)/shard_map/ppermute | solution.py:96
  13.1 19.1 %collective-permute-start.1 = (bf16[256,768]{1,0:T(8,128)(2,1)S(1)}, bf16[256,768]{1,0:T(8,128)(2,1)S(1)}, u32[]{:S(2)}, u32[]{:S(2)}) collective-permute-start(bf16[256,768]{1,0:T(8,128)(2,1)S(1)} %bitcast.224), channel_id=1, source_target_pairs={{0,2},{1,3},{2,0},{3,1},{4,6},{5,7},{6,4},{7,5},{8,10},{9,11},{10,... | collective-permute-start | bytes 1179656 | tf_op jit(solution)/shard_map/ppermute | solution.py:96
  14.7 17.4 %collective-permute-start.2 = (bf16[256,768]{1,0:T(8,128)(2,1)S(1)}, bf16[256,768]{1,0:T(8,128)(2,1)}, u32[]{:S(2)}, u32[]{:S(2)}) collective-permute-start(bf16[256,768]{1,0:T(8,128)(2,1)S(1)} %bitcast.225), channel_id=1, source_target_pairs={{0,3},{1,2},{2,1},{3,0},{4,7},{5,6},{6,5},{7,4},{8,11},{9,10},{10,... | collective-permute-start | bytes 1179656 | tf_op jit(solution)/shard_map/ppermute | solution.py:96
  35.1 33.8 %collective-permute-start.3 = (bf16[20,768]{1,0:T(8,128)(2,1)S(1)}, bf16[20,768]{1,0:T(8,128)(2,1)S(1)}, u32[]{:S(2)}, u32[]{:S(2)}) collective-permute-start(bf16[20,768]{1,0:T(8,128)(2,1)S(1)} %get-tuple-element.37), channel_id=1, source_target_pairs={{0,4},{4,0},{8,12},{12,8},{16,20},{20,16},{24,28},{28,24},{1,5},{5... | collective-permute-start | bytes 92168 | tf_op jit(solution)/shard_map/ppermute | solution.py:64
  35.7 35.6 %collective-permute-start.4 = (bf16[20,768]{1,0:T(8,128)(2,1)S(1)}, bf16[20,768]{1,0:T(8,128)(2,1)S(1)}, u32[]{:S(2)}, u32[]{:S(2)}) collective-permute-start(bf16[20,768]{1,0:T(8,128)(2,1)S(1)} %get-tuple-element.36), channel_id=1, source_target_pairs={{0,8},{4,12},{8,0},{12,4},{16,24},{20,28},{24,16},{28,20},{1,9},{5... | collective-permute-start | bytes 92168 | tf_op jit(solution)/shard_map/ppermute | solution.py:64
  37.2 34.2 %collective-permute-start.5 = (bf16[20,768]{1,0:T(8,128)(2,1)S(1)}, bf16[20,768]{1,0:T(8,128)(2,1)S(1)}, u32[]{:S(2)}, u32[]{:S(2)}) collective-permute-start(bf16[20,768]{1,0:T(8,128)(2,1)S(1)} %get-tuple-element.35), channel_id=1, source_target_pairs={{0,12},{4,8},{8,4},{12,0},{16,28},{20,24},{24,20},{28,16},{1,13},{... | collective-permute-start | bytes 92168 | tf_op jit(solution)/shard_map/ppermute | solution.py:64
  37.2 35.5 %collective-permute-start.6 = (bf16[20,768]{1,0:T(8,128)(2,1)S(1)}, bf16[20,768]{1,0:T(8,128)(2,1)S(1)}, u32[]{:S(2)}, u32[]{:S(2)}) collective-permute-start(bf16[20,768]{1,0:T(8,128)(2,1)S(1)} %get-tuple-element.34), channel_id=1, source_target_pairs={{0,16},{4,20},{8,24},{12,28},{16,0},{20,4},{24,8},{28,12},{1,17},{... | collective-permute-start | bytes 92168 | tf_op jit(solution)/shard_map/ppermute | solution.py:64
  67.6 29.5 %collective-permute-start.7 = (bf16[20,768]{1,0:T(8,128)(2,1)S(1)}, bf16[20,768]{1,0:T(8,128)(2,1)S(1)}, u32[]{:S(2)}, u32[]{:S(2)}) collective-permute-start(bf16[20,768]{1,0:T(8,128)(2,1)S(1)} %get-tuple-element.33), channel_id=1, source_target_pairs={{0,20},{4,16},{8,28},{12,24},{16,4},{20,0},{24,12},{28,8},{1,21},{... | collective-permute-start | bytes 92168 | tf_op jit(solution)/shard_map/ppermute | solution.py:64
  69.0 29.9 %collective-permute-start.8 = (bf16[20,768]{1,0:T(8,128)(2,1)S(1)}, bf16[20,768]{1,0:T(8,128)(2,1)S(1)}, u32[]{:S(2)}, u32[]{:S(2)}) collective-permute-start(bf16[20,768]{1,0:T(8,128)(2,1)S(1)} %get-tuple-element.32), channel_id=1, source_target_pairs={{0,24},{4,28},{8,16},{12,20},{16,8},{20,12},{24,0},{28,4},{1,25},{... | collective-permute-start | bytes 92168 | tf_op jit(solution)/shard_map/ppermute | solution.py:64
  71.3 38.3 %collective-permute-start.9 = (bf16[20,768]{1,0:T(8,128)(2,1)S(1)}, bf16[20,768]{1,0:T(8,128)(2,1)S(1)}, u32[]{:S(2)}, u32[]{:S(2)}) collective-permute-start(bf16[20,768]{1,0:T(8,128)(2,1)S(1)} %get-tuple-element.31), channel_id=1, source_target_pairs={{0,28},{4,24},{8,20},{12,16},{16,12},{20,8},{24,4},{28,0},{1,29},{... | collective-permute-start | bytes 92168 | tf_op jit(solution)/shard_map/ppermute | solution.py:64
  71.4 8.2 %collective-permute-start.30 = (bf16[160,768]{1,0:T(8,128)(2,1)S(1)}, bf16[160,768]{1,0:T(8,128)(2,1)S(1)}, u32[]{:S(2)}, u32[]{:S(2)}) collective-permute-start(bf16[160,768]{1,0:T(8,128)(2,1)S(1)} %reshape.84), channel_id=1, source_target_pairs={{0,1},{1,0},{2,3},{3,2},{4,5},{5,4},{6,7},{7,6},{8,9},{9,8},{10,11... | collective-permute-start | bytes 737288 | tf_op jit(solution)/shard_map/ppermute | solution.py:123
  72.7 13.3 %collective-permute-start.32 = (bf16[160,768]{1,0:T(8,128)(2,1)S(1)}, bf16[160,768]{1,0:T(8,128)(2,1)S(1)}, u32[]{:S(2)}, u32[]{:S(2)}) collective-permute-start(bf16[160,768]{1,0:T(8,128)(2,1)S(1)} %reshape.84), channel_id=1, source_target_pairs={{0,3},{1,2},{2,1},{3,0},{4,7},{5,6},{6,5},{7,4},{8,11},{9,10},{10,... | collective-permute-start | bytes 737288 | tf_op jit(solution)/shard_map/ppermute | solution.py:123
  79.6 12.1 %collective-permute-start.31 = (bf16[160,768]{1,0:T(8,128)(2,1)S(1)}, bf16[160,768]{1,0:T(8,128)(2,1)S(1)}, u32[]{:S(2)}, u32[]{:S(2)}) collective-permute-start(bf16[160,768]{1,0:T(8,128)(2,1)S(1)} %reshape.84), channel_id=1, source_target_pairs={{0,2},{1,3},{2,0},{3,1},{4,6},{5,7},{6,4},{7,5},{8,10},{9,11},{10,... | collective-permute-start | bytes 737288 | tf_op jit(solution)/shard_map/ppermute | solution.py:123
  95.3 8.9 %collective-permute-start.33 = (bf16[160,768]{1,0:T(8,128)(2,1)S(1)}, bf16[160,768]{1,0:T(8,128)(2,1)S(1)}, u32[]{:S(2)}, u32[]{:S(2)}) collective-permute-start(bf16[160,768]{1,0:T(8,128)(2,1)S(1)} %convolution_convert_fusion.3), channel_id=1, source_target_pairs={{0,1},{1,0},{2,3},{3,2},{4,5},{5,4},{6,7},{7,6},{8,9},{9,8},{10,11... | collective-permute-start | bytes 737288 | tf_op jit(solution)/shard_map/ppermute | solution.py:134
  95.9 13.0 %collective-permute-start.34 = (bf16[160,768]{1,0:T(8,128)(2,1)S(1)}, bf16[160,768]{1,0:T(8,128)(2,1)S(1)}, u32[]{:S(2)}, u32[]{:S(2)}) collective-permute-start(bf16[160,768]{1,0:T(8,128)(2,1)S(1)} %convolution_convert_fusion.2), channel_id=1, source_target_pairs={{0,2},{1,3},{2,0},{3,1},{4,6},{5,7},{6,4},{7,5},{8,10},{9,11},{10,... | collective-permute-start | bytes 737288 | tf_op jit(solution)/shard_map/ppermute | solution.py:134
  97.1 11.8 %collective-permute-start.35 = (bf16[160,768]{1,0:T(8,128)(2,1)S(1)}, bf16[160,768]{1,0:T(8,128)(2,1)S(1)}, u32[]{:S(2)}, u32[]{:S(2)}) collective-permute-start(bf16[160,768]{1,0:T(8,128)(2,1)S(1)} %convolution_convert_fusion.1), channel_id=1, source_target_pairs={{0,3},{1,2},{2,1},{3,0},{4,7},{5,6},{6,5},{7,4},{8,11},{9,10},{10,... | collective-permute-start | bytes 737288 | tf_op jit(solution)/shard_map/ppermute | solution.py:134
  110.3 8.1 %collective-permute-start.38 = (bf16[20,768]{1,0:T(8,128)(2,1)S(1)}, bf16[20,768]{1,0:T(8,128)(2,1)S(1)}, u32[]{:S(2)}, u32[]{:S(2)}) collective-permute-start(bf16[20,768]{1,0:T(8,128)(2,1)S(1)} %get-tuple-element.11), channel_id=1, source_target_pairs={{0,12},{4,8},{8,4},{12,0},{16,28},{20,24},{24,20},{28,16},{1,13},{... | collective-permute-start | bytes 92168 | tf_op jit(solution)/shard_map/ppermute | solution.py:64
  122.4 8.9 %collective-permute-start.10 = (bf16[160,768]{1,0:T(8,128)(2,1)S(1)}, bf16[160,768]{1,0:T(8,128)(2,1)S(1)}, u32[]{:S(2)}, u32[]{:S(2)}) collective-permute-start(bf16[160,768]{1,0:T(8,128)(2,1)S(1)} %reshape.80), channel_id=1, source_target_pairs={{0,1},{1,0},{2,3},{3,2},{4,5},{5,4},{6,7},{7,6},{8,9},{9,8},{10,11... | collective-permute-start | bytes 737288 | tf_op jit(solution)/shard_map/ppermute | solution.py:123
  123.7 12.8 %collective-permute-start.12 = (bf16[160,768]{1,0:T(8,128)(2,1)S(1)}, bf16[160,768]{1,0:T(8,128)(2,1)S(1)}, u32[]{:S(2)}, u32[]{:S(2)}) collective-permute-start(bf16[160,768]{1,0:T(8,128)(2,1)S(1)} %reshape.80), channel_id=1, source_target_pairs={{0,3},{1,2},{2,1},{3,0},{4,7},{5,6},{6,5},{7,4},{8,11},{9,10},{10,... | collective-permute-start | bytes 737288 | tf_op jit(solution)/shard_map/ppermute | solution.py:123
  125.1 13.0 %collective-permute-start.11 = (bf16[160,768]{1,0:T(8,128)(2,1)S(1)}, bf16[160,768]{1,0:T(8,128)(2,1)S(1)}, u32[]{:S(2)}, u32[]{:S(2)}) collective-permute-start(bf16[160,768]{1,0:T(8,128)(2,1)S(1)} %reshape.80), channel_id=1, source_target_pairs={{0,2},{1,3},{2,0},{3,1},{4,6},{5,7},{6,4},{7,5},{8,10},{9,11},{10,... | collective-permute-start | bytes 737288 | tf_op jit(solution)/shard_map/ppermute | solution.py:123
  141.7 9.0 %collective-permute-start.13 = (bf16[160,768]{1,0:T(8,128)(2,1)S(1)}, bf16[160,768]{1,0:T(8,128)(2,1)S(1)}, u32[]{:S(2)}, u32[]{:S(2)}) collective-permute-start(bf16[160,768]{1,0:T(8,128)(2,1)S(1)} %convolution_convert_fusion.8), channel_id=1, source_target_pairs={{0,1},{1,0},{2,3},{3,2},{4,5},{5,4},{6,7},{7,6},{8,9},{9,8},{10,11... | collective-permute-start | bytes 737288 | tf_op jit(solution)/shard_map/ppermute | solution.py:134
  142.6 12.1 %collective-permute-start.14 = (bf16[160,768]{1,0:T(8,128)(2,1)S(1)}, bf16[160,768]{1,0:T(8,128)(2,1)S(1)}, u32[]{:S(2)}, u32[]{:S(2)}) collective-permute-start(bf16[160,768]{1,0:T(8,128)(2,1)S(1)} %convolution_convert_fusion.7), channel_id=1, source_target_pairs={{0,2},{1,3},{2,0},{3,1},{4,6},{5,7},{6,4},{7,5},{8,10},{9,11},{10,... | collective-permute-start | bytes 737288 | tf_op jit(solution)/shard_map/ppermute | solution.py:134
  143.8 10.8 %collective-permute-start.15 = (bf16[160,768]{1,0:T(8,128)(2,1)S(1)}, bf16[160,768]{1,0:T(8,128)(2,1)S(1)}, u32[]{:S(2)}, u32[]{:S(2)}) collective-permute-start(bf16[160,768]{1,0:T(8,128)(2,1)S(1)} %convolution_convert_fusion.6), channel_id=1, source_target_pairs={{0,3},{1,2},{2,1},{3,0},{4,7},{5,6},{6,5},{7,4},{8,11},{9,10},{10,... | collective-permute-start | bytes 737288 | tf_op jit(solution)/shard_map/ppermute | solution.py:134
  155.5 6.8 %collective-permute-start.17 = (bf16[20,768]{1,0:T(8,128)(2,1)S(1)}, bf16[20,768]{1,0:T(8,128)(2,1)S(1)}, u32[]{:S(2)}, u32[]{:S(2)}) collective-permute-start(bf16[20,768]{1,0:T(8,128)(2,1)S(1)} %get-tuple-element.28), channel_id=1, source_target_pairs={{0,8},{4,12},{8,0},{12,4},{16,24},{20,28},{24,16},{28,20},{1,9},{5... | collective-permute-start | bytes 92168 | tf_op jit(solution)/shard_map/ppermute | solution.py:64
  (35 other events, 466.7 us)

commit v4 on v2

--- a/solution.py
+++ b/solution.py
@@ -87,13 +87,17 @@
     proj_blocks = projection.reshape(tensor_count, width, projection.shape[1])
     proj_parts = [lax.dynamic_index_in_dim(proj_blocks, p, 0, keepdims=False) for p in partners]
 
-    head_terms = jnp.dot(context, out_proj, preferred_element_type=jnp.float32).astype(jnp.bfloat16)
-    head_blocks = head_terms.reshape(tok_rows, tensor_count, width)
-    summed = lax.dynamic_index_in_dim(head_blocks, me_t, 1, keepdims=False).astype(jnp.float32)
-    summed = summed + residual_in.astype(jnp.float32)
-    for s in range(1, tensor_count):
-        chunk = lax.dynamic_index_in_dim(head_blocks, partners[s], 1, keepdims=False)
-        summed = summed + lax.ppermute(chunk, "tensor", pairs_for(s, tensor_count)).astype(jnp.float32)
+    def head_term(p):
+        columns = lax.dynamic_slice_in_dim(out_proj, p * width, width, axis=1)
+        return jnp.dot(context, columns, preferred_element_type=jnp.float32).astype(jnp.bfloat16)
+
+    received = [
+        lax.ppermute(head_term(partners[s]), "tensor", pairs_for(s, tensor_count))
+        for s in range(1, tensor_count)
+    ]
+    summed = head_term(me_t).astype(jnp.float32) + residual_in.astype(jnp.float32)
+    for got in received:
+        summed = summed + got.astype(jnp.float32)
     generated = summed.astype(jnp.bfloat16)
 
     group_ids = lax.iota(jnp.int32, group_count)

time: 123 us -> 120 us (0.976)
  local copies, waits for them, and re-layouts: 7.84 us -> 3.66 us
  other arithmetic: 4.81 us -> 1.07 us
  matrix products: 15.8 us -> 19.2 us
    dot_general x1 -> x4, matrix products: 3.72 us -> 7.21 us  [head_term(): jnp.dot(context, columns, preferred_element_type=jnp.float32)]
    dynamic_slice x1 -> x0, local copies, waits for them, and re-layouts: 3.3 us -> none  [shards(): lax.dynamic_index_in_dim(head_blocks, me_t, 1, keepdims=False)]
  transfers between devices with their start and end apart: 23 -> 23, of which waited for: 8 -> 8; matrix products, arithmetic and copies ran while one was open for 8% -> 10% of each run, Pallas kernels for 0% -> 0%
where the time goes in v4:
time: 120 us; the launch traced here: 119 us
  waiting for transfers between devices  64 us (53%)
  starting transfers between devices  29.7 us (25%)
  matrix products  19.2 us (16%)
  local copies, waits for them, and re-layouts  3.66 us (3%)
    ppermute x3, waiting for transfers between devices, shards(): lax.ppermute(back[s], 'tensor', pairs_for(s, tensor_count))  19.7 us
    ppermute x14, starting transfers between devices, swap_blocks(): got.append(lax.ppermute(chunk, axis, pairs_for(s, n)))  17.9 us
    ppermute x3, waiting for transfers between devices, shards(): got = lax.ppermute(arrived, 'tensor', pairs_for(s, tensor_count))  17.4 us
    ppermute x3, waiting for transfers between devices, shards(): lax.ppermute(head_term(partners[s]), 'tensor', pairs_for(s, tensor_count))  14.3 us
    ppermute x14, waiting for transfers between devices, swap_blocks(): got.append(lax.ppermute(chunk, axis, pairs_for(s, n)))  12.6 us
    dot_general x4, matrix products, head_term(): jnp.dot(context, columns, preferred_element_type=jnp.float32)  7.21 us
    dot_general x3, matrix products, shards(): jnp.dot(got, proj_parts[s], preferred_element_type=jnp.float32)  6.15 us
    ppermute x3, starting transfers between devices, shards(): lax.ppermute(head_term(partners[s]), 'tensor', pairs_for(s, tensor_count))  4.66 us
  transfers between devices with their start and end apart: 23, of which 8 were waited for; matrix products, arithmetic and copies ran while one was open for 10% of the time, Pallas kernels for 0%

profile of v4, /device:TPU:0, one launch (start us, length us, event | category | flops | bytes accessed | tf_op | source)
XLA Modules:
  0.0 118.8 jit_solution(2580613851064362069)
XLA Ops:
  1.6 1.8 %fusion.5 = bf16[256,768]{0,1:T(8,128)(2,1)S(1)} fusion(bf16[256,768]{1,0:T(8,128)(2,1)S(1)} %copy-done, bf16[768,3072]{1,0:T(8,128)(2,1)} %param.11, s32[]{:T(128)S(6)} %select_n.70), kind=kOutput, calls=%fused_computation.21 | convolution fusion | flops 302186496 | bytes 1966084 | tf_op jit(solution)/shard_map/dot_general | solution.py:92
  3.4 3.0 %collective-permute-start = (bf16[256,768]{0,1:T(8,128)(2,1)S(1)}, bf16[256,768]{0,1:T(8,128)(2,1)S(1)}, u32[]{:S(2)}, u32[]{:S(2)}) collective-permute-start(bf16[256,768]{0,1:T(8,128)(2,1)S(1)} %fusion.5), channel_id=1, source_target_pairs={{0,1},{1,0},{2,3},{3,2},{4,5},{5,4},{6,7},{7,6},{8,9},{9,8},{10,11... | collective-permute-start | bytes 1179656 | tf_op jit(solution)/shard_map/ppermute | solution.py:95
  6.4 1.8 %fusion.6 = bf16[256,768]{0,1:T(8,128)(2,1)S(1)} fusion(bf16[256,768]{1,0:T(8,128)(2,1)S(1)} %copy-done, bf16[768,3072]{1,0:T(8,128)(2,1)} %param.11, s32[]{:T(128)S(6)} %select_n.71), kind=kOutput, calls=%fused_computation.22 | convolution fusion | flops 302186496 | bytes 1966084 | tf_op jit(solution)/shard_map/dot_general | solution.py:92
  9.8 1.8 %fusion.7 = bf16[256,768]{0,1:T(8,128)(2,1)S(1)} fusion(bf16[256,768]{1,0:T(8,128)(2,1)S(1)} %copy-done, bf16[768,3072]{1,0:T(8,128)(2,1)} %param.11, s32[]{:T(128)S(6)} %select_n.72), kind=kOutput, calls=%fused_computation.23 | convolution fusion | flops 302186496 | bytes 1966084 | tf_op jit(solution)/shard_map/dot_general | solution.py:92
  13.0 3.3 %collective-permute-done = bf16[256,768]{0,1:T(8,128)(2,1)S(1)} collective-permute-done((bf16[256,768]{0,1:T(8,128)(2,1)S(1)}, bf16[256,768]{0,1:T(8,128)(2,1)S(1)}, u32[]{:S(2)}, u32[]{:S(2)}) %collective-permute-start) | collective-permute-done | bytes 393248 | tf_op jit(solution)/shard_map/ppermute | solution.py:95
  16.4 10.9 %collective-permute-done.1 = bf16[256,768]{0,1:T(8,128)(2,1)S(1)} collective-permute-done((bf16[256,768]{0,1:T(8,128)(2,1)S(1)}, bf16[256,768]{0,1:T(8,128)(2,1)S(1)}, u32[]{:S(2)}, u32[]{:S(2)}) %collective-permute-start.1) | collective-permute-done | bytes 393248 | tf_op jit(solution)/shard_map/ppermute | solution.py:95
  27.3 1.9 %add_convert_fusion.1 = bf16[256,768]{0,1:T(8,128)(2,1)S(1)} fusion(bf16[256,768]{0,1:T(8,128)(2,1)S(1)} %collective-permute-done.2, bf16[256,768]{0,1:T(8,128)(2,1)S(1)} %collective-permute-done.1, bf16[256,768]{0,1:T(8,128)(2,1)S(1)} %collective-permute-done, bf16[256,768]{0,1:T(8,128)(2,1)S(1)} %copy.11, bf16[256,768]{1,0:T(8,128)(2,1)S(1)} %copy-done, ...), kind=kOutput, calls=%fused_computation.55 | convolution fusion | flops 304152576 | bytes 3538948 | tf_op jit(solution)/shard_map/dot_general | solution.py:92
  29.8 1.6 %collective-permute-start.4 = (bf16[40,768]{1,0:T(8,128)(2,1)S(1)}, bf16[40,768]{1,0:T(8,128)(2,1)S(1)}, u32[]{:S(2)}, u32[]{:S(2)}) collective-permute-start(bf16[40,768]{1,0:T(8,128)(2,1)S(1)} %get-tuple-element.20), channel_id=1, source_target_pairs={{0,8},{4,12},{8,0},{12,4},{16,24},{20,28},{24,16},{28,20},{1,9},{5... | collective-permute-start | bytes 184328 | tf_op jit(solution)/shard_map/ppermute | solution.py:64
  31.6 2.6 %collective-permute-start.6 = (bf16[40,768]{1,0:T(8,128)(2,1)S(1)}, bf16[40,768]{1,0:T(8,128)(2,1)S(1)}, u32[]{:S(2)}, u32[]{:S(2)}) collective-permute-start(bf16[40,768]{1,0:T(8,128)(2,1)S(1)} %get-tuple-element.18), channel_id=1, source_target_pairs={{0,16},{4,20},{8,24},{12,28},{16,0},{20,4},{24,8},{28,12},{1,17},{... | collective-permute-start | bytes 184328 | tf_op jit(solution)/shard_map/ppermute | solution.py:64
  34.3 3.6 %collective-permute-start.8 = (bf16[40,768]{1,0:T(8,128)(2,1)S(1)}, bf16[40,768]{1,0:T(8,128)(2,1)S(1)}, u32[]{:S(2)}, u32[]{:S(2)}) collective-permute-start(bf16[40,768]{1,0:T(8,128)(2,1)S(1)} %get-tuple-element.16), channel_id=1, source_target_pairs={{0,24},{4,28},{8,16},{12,20},{16,8},{20,12},{24,0},{28,4},{1,25},{... | collective-permute-start | bytes 184328 | tf_op jit(solution)/shard_map/ppermute | solution.py:64
  38.0 6.3 %collective-permute-done.7 = bf16[40,768]{1,0:T(8,128)(2,1)S(1)} collective-permute-done((bf16[40,768]{1,0:T(8,128)(2,1)S(1)}, bf16[40,768]{1,0:T(8,128)(2,1)S(1)}, u32[]{:S(2)}, u32[]{:S(2)}) %collective-permute-start.7) | collective-permute-done | bytes 61472 | tf_op jit(solution)/shard_map/ppermute | solution.py:64
  48.7 1.8 %fusion.16 = f32[320,768]{1,0:T(8,128)S(1)} fusion(bf16[320,768]{1,0:T(8,128)(2,1)S(1)} %bitcast.125, bf16[4,768,768]{2,1,0:T(8,128)(2,1)} %bitcast.128, s32[]{:T(128)S(6)} %select_n.82), kind=kOutput, calls=%fused_computation.32 | convolution fusion | flops 377487360 | bytes 2654212 | tf_op jit(solution)/shard_map/dot_general | solution.py:125
  50.6 9.6 %collective-permute-done.12 = bf16[320,768]{1,0:T(8,128)(2,1)S(1)} collective-permute-done((bf16[320,768]{1,0:T(8,128)(2,1)S(1)}, bf16[320,768]{1,0:T(8,128)(2,1)S(1)}, u32[]{:S(2)}, u32[]{:S(2)}) %collective-permute-start.12) | collective-permute-done | bytes 491552 | tf_op jit(solution)/shard_map/ppermute | solution.py:127
  60.2 2.0 %fusion.9 = f32[320,768]{1,0:T(8,128)S(1)} fusion(bf16[320,768]{1,0:T(8,128)(2,1)S(1)} %collective-permute-done.12, bf16[4,768,768]{2,1,0:T(8,128)(2,1)} %bitcast.129, s32[]{:T(128)S(6)} %select_n.85), kind=kOutput, calls=%fused_computation.25 | convolution fusion | flops 377487360 | bytes 2654212 | tf_op jit(solution)/shard_map/dot_general | solution.py:128
  62.1 7.8 %collective-permute-done.10 = bf16[320,768]{1,0:T(8,128)(2,1)S(1)} collective-permute-done((bf16[320,768]{1,0:T(8,128)(2,1)S(1)}, bf16[320,768]{1,0:T(8,128)(2,1)S(1)}, u32[]{:S(2)}, u32[]{:S(2)}) %collective-permute-start.10) | collective-permute-done | bytes 491552 | tf_op jit(solution)/shard_map/ppermute | solution.py:127
  69.9 1.8 %convolution_add_fusion.1 = f32[320,768]{1,0:T(8,128)S(1)} fusion(f32[320,768]{1,0:T(8,128)S(1)} %fusion.16, bf16[320,768]{1,0:T(8,128)(2,1)S(1)} %collective-permute-done.10, bf16[4,768,768]{2,1,0:T(8,128)(2,1)} %bitcast.130, s32[]{:T(128)S(6)} %select_n.83), kind=kOutput, calls=%fused_computation.6 | convolution fusion | flops 377733120 | bytes 3637252 | tf_op jit(solution)/shard_map/dot_general | solution.py:128
  71.8 2.4 %fusion.37 = bf16[320,768]{1,0:T(8,128)(2,1)S(1)} fusion(f32[320,768]{1,0:T(8,128)S(1)} %fusion.9, f32[320,768]{1,0:T(8,128)S(1)} %convolution_add_fusion.1, bf16[320,768]{1,0:T(8,128)(2,1)S(1)} %collective-permute-done.11, bf16[4,768,768]{2,1,0:T(8,128)(2,1)} %bitcast.131, s32[]{:T(128)S(6)} %select_n.84, f32[768]{0:T(1024)S(1)} %reduce.1, ...), kind=kOutput, calls=%fused_computation.53 | convolution fusion | flops 382894080 | bytes 4134916 | tf_op jit(solution)/shard_map/dot_general | solution.py:128
  77.1 2.4 %collective-permute-start.15 = (bf16[320,768]{1,0:T(8,128)(2,1)S(1)}, bf16[320,768]{1,0:T(8,128)(2,1)S(1)}, u32[]{:S(2)}, u32[]{:S(2)}) collective-permute-start(bf16[320,768]{1,0:T(8,128)(2,1)S(1)} %convolution_convert_fusion.1), channel_id=1, source_target_pairs={{0,3},{1,2},{2,1},{3,0},{4,7},{5,6},{6,5},{7,4},{8,11},{9,10},{10,... | collective-permute-start | bytes 1474568 | tf_op jit(solution)/shard_map/ppermute | solution.py:138
  79.5 10.7 %collective-permute-done.13 = bf16[320,768]{1,0:T(8,128)(2,1)S(1)} collective-permute-done((bf16[320,768]{1,0:T(8,128)(2,1)S(1)}, bf16[320,768]{1,0:T(8,128)(2,1)S(1)}, u32[]{:S(2)}, u32[]{:S(2)}) %collective-permute-start.13) | collective-permute-done | bytes 491552 | tf_op jit(solution)/shard_map/ppermute | solution.py:138
  90.2 9.0 %collective-permute-done.14 = bf16[320,768]{1,0:T(8,128)(2,1)S(1)} collective-permute-done((bf16[320,768]{1,0:T(8,128)(2,1)S(1)}, bf16[320,768]{1,0:T(8,128)(2,1)S(1)}, u32[]{:S(2)}, u32[]{:S(2)}) %collective-permute-start.14) | collective-permute-done | bytes 491552 | tf_op jit(solution)/shard_map/ppermute | solution.py:138
  100.9 3.1 %collective-permute-start.17 = (bf16[40,768]{1,0:T(8,128)(2,1)S(1)}, bf16[40,768]{1,0:T(8,128)(2,1)S(1)}, u32[]{:S(2)}, u32[]{:S(2)}) collective-permute-start(bf16[40,768]{1,0:T(8,128)(2,1)S(1)} %get-tuple-element.12), channel_id=1, source_target_pairs={{0,8},{4,12},{8,0},{12,4},{16,24},{20,28},{24,16},{28,20},{1,9},{5... | collective-permute-start | bytes 184328 | tf_op jit(solution)/shard_map/ppermute | solution.py:64
  104.2 2.8 %collective-permute-start.19 = (bf16[40,768]{1,0:T(8,128)(2,1)S(1)}, bf16[40,768]{1,0:T(8,128)(2,1)S(1)}, u32[]{:S(2)}, u32[]{:S(2)}) collective-permute-start(bf16[40,768]{1,0:T(8,128)(2,1)S(1)} %get-tuple-element.10), channel_id=1, source_target_pairs={{0,16},{4,20},{8,24},{12,28},{16,0},{20,4},{24,8},{28,12},{1,17},{... | collective-permute-start | bytes 184328 | tf_op jit(solution)/shard_map/ppermute | solution.py:64
  107.0 2.1 %collective-permute-start.21 = (bf16[40,768]{1,0:T(8,128)(2,1)S(1)}, bf16[40,768]{1,0:T(8,128)(2,1)S(1)}, u32[]{:S(2)}, u32[]{:S(2)}) collective-permute-start(bf16[40,768]{1,0:T(8,128)(2,1)S(1)} %get-tuple-element.8), channel_id=1, source_target_pairs={{0,24},{4,28},{8,16},{12,20},{16,8},{20,12},{24,0},{28,4},{1,25},{... | collective-permute-start | bytes 184328 | tf_op jit(solution)/shard_map/ppermute | solution.py:64
  110.5 6.3 %collective-permute-done.20 = bf16[40,768]{1,0:T(8,128)(2,1)S(1)} collective-permute-done((bf16[40,768]{1,0:T(8,128)(2,1)S(1)}, bf16[40,768]{1,0:T(8,128)(2,1)S(1)}, u32[]{:S(2)}, u32[]{:S(2)}) %collective-permute-start.20) | collective-permute-done | bytes 61472 | tf_op jit(solution)/shard_map/ppermute | solution.py:64
  (87 shorter events, 17.3 us)
Async XLA Ops:
  3.4 12.9 %collective-permute-start = (bf16[256,768]{0,1:T(8,128)(2,1)S(1)}, bf16[256,768]{0,1:T(8,128)(2,1)S(1)}, u32[]{:S(2)}, u32[]{:S(2)}) collective-permute-start(bf16[256,768]{0,1:T(8,128)(2,1)S(1)} %fusion.5), channel_id=1, source_target_pairs={{0,1},{1,0},{2,3},{3,2},{4,5},{5,4},{6,7},{7,6},{8,9},{9,8},{10,11... | collective-permute-start | bytes 1179656 | tf_op jit(solution)/shard_map/ppermute | solution.py:95
  8.2 19.1 %collective-permute-start.1 = (bf16[256,768]{0,1:T(8,128)(2,1)S(1)}, bf16[256,768]{0,1:T(8,128)(2,1)S(1)}, u32[]{:S(2)}, u32[]{:S(2)}) collective-permute-start(bf16[256,768]{0,1:T(8,128)(2,1)S(1)} %fusion.6), channel_id=1, source_target_pairs={{0,2},{1,3},{2,0},{3,1},{4,6},{5,7},{6,4},{7,5},{8,10},{9,11},{10,... | collective-permute-start | bytes 1179656 | tf_op jit(solution)/shard_map/ppermute | solution.py:95
  11.6 35.0 %copy-start.2 = (f32[1,768]{1,0:T(1,128)S(1)}, f32[1,768]{1,0:T(1,128)}, u32[]{:S(2)}) copy-start(f32[1,768]{1,0:T(1,128)} %param.15) | copy-start | bytes 9220
  11.6 15.7 %collective-permute-start.2 = (bf16[256,768]{0,1:T(8,128)(2,1)S(1)}, bf16[256,768]{0,1:T(8,128)(2,1)S(1)}, u32[]{:S(2)}, u32[]{:S(2)}) collective-permute-start(bf16[256,768]{0,1:T(8,128)(2,1)S(1)} %fusion.7), channel_id=1, source_target_pairs={{0,3},{1,2},{2,1},{3,0},{4,7},{5,6},{6,5},{7,4},{8,11},{9,10},{10,... | collective-permute-start | bytes 1179656 | tf_op jit(solution)/shard_map/ppermute | solution.py:95
  29.7 4.6 %collective-permute-start.3 = (bf16[40,768]{1,0:T(8,128)(2,1)S(1)}, bf16[40,768]{1,0:T(8,128)(2,1)S(1)}, u32[]{:S(2)}, u32[]{:S(2)}) collective-permute-start(bf16[40,768]{1,0:T(8,128)(2,1)S(1)} %get-tuple-element.21), channel_id=1, source_target_pairs={{0,4},{4,0},{8,12},{12,8},{16,20},{20,16},{24,28},{28,24},{1,5},{5... | collective-permute-start | bytes 184328 | tf_op jit(solution)/shard_map/ppermute | solution.py:64
  29.8 8.1 %collective-permute-start.4 = (bf16[40,768]{1,0:T(8,128)(2,1)S(1)}, bf16[40,768]{1,0:T(8,128)(2,1)S(1)}, u32[]{:S(2)}, u32[]{:S(2)}) collective-permute-start(bf16[40,768]{1,0:T(8,128)(2,1)S(1)} %get-tuple-element.20), channel_id=1, source_target_pairs={{0,8},{4,12},{8,0},{12,4},{16,24},{20,28},{24,16},{28,20},{1,9},{5... | collective-permute-start | bytes 184328 | tf_op jit(solution)/shard_map/ppermute | solution.py:64
  31.4 6.6 %collective-permute-start.5 = (bf16[40,768]{1,0:T(8,128)(2,1)S(1)}, bf16[40,768]{1,0:T(8,128)(2,1)S(1)}, u32[]{:S(2)}, u32[]{:S(2)}) collective-permute-start(bf16[40,768]{1,0:T(8,128)(2,1)S(1)} %get-tuple-element.19), channel_id=1, source_target_pairs={{0,12},{4,8},{8,4},{12,0},{16,28},{20,24},{24,20},{28,16},{1,13},{... | collective-permute-start | bytes 184328 | tf_op jit(solution)/shard_map/ppermute | solution.py:64
  31.6 6.4 %collective-permute-start.6 = (bf16[40,768]{1,0:T(8,128)(2,1)S(1)}, bf16[40,768]{1,0:T(8,128)(2,1)S(1)}, u32[]{:S(2)}, u32[]{:S(2)}) collective-permute-start(bf16[40,768]{1,0:T(8,128)(2,1)S(1)} %get-tuple-element.18), channel_id=1, source_target_pairs={{0,16},{4,20},{8,24},{12,28},{16,0},{20,4},{24,8},{28,12},{1,17},{... | collective-permute-start | bytes 184328 | tf_op jit(solution)/shard_map/ppermute | solution.py:64
  34.2 10.1 %collective-permute-start.7 = (bf16[40,768]{1,0:T(8,128)(2,1)S(1)}, bf16[40,768]{1,0:T(8,128)(2,1)S(1)}, u32[]{:S(2)}, u32[]{:S(2)}) collective-permute-start(bf16[40,768]{1,0:T(8,128)(2,1)S(1)} %get-tuple-element.17), channel_id=1, source_target_pairs={{0,20},{4,16},{8,28},{12,24},{16,4},{20,0},{24,12},{28,8},{1,21},{... | collective-permute-start | bytes 184328 | tf_op jit(solution)/shard_map/ppermute | solution.py:64
  34.3 10.1 %collective-permute-start.8 = (bf16[40,768]{1,0:T(8,128)(2,1)S(1)}, bf16[40,768]{1,0:T(8,128)(2,1)S(1)}, u32[]{:S(2)}, u32[]{:S(2)}) collective-permute-start(bf16[40,768]{1,0:T(8,128)(2,1)S(1)} %get-tuple-element.16), channel_id=1, source_target_pairs={{0,24},{4,28},{8,16},{12,20},{16,8},{20,12},{24,0},{28,4},{1,25},{... | collective-permute-start | bytes 184328 | tf_op jit(solution)/shard_map/ppermute | solution.py:64
  37.9 6.5 %collective-permute-start.9 = (bf16[40,768]{1,0:T(8,128)(2,1)S(1)}, bf16[40,768]{1,0:T(8,128)(2,1)S(1)}, u32[]{:S(2)}, u32[]{:S(2)}) collective-permute-start(bf16[40,768]{1,0:T(8,128)(2,1)S(1)} %get-tuple-element.15), channel_id=1, source_target_pairs={{0,28},{4,24},{8,20},{12,16},{16,12},{20,8},{24,4},{28,0},{1,29},{... | collective-permute-start | bytes 184328 | tf_op jit(solution)/shard_map/ppermute | solution.py:64
  45.1 15.1 %collective-permute-start.12 = (bf16[320,768]{1,0:T(8,128)(2,1)S(1)}, bf16[320,768]{1,0:T(8,128)(2,1)S(1)}, u32[]{:S(2)}, u32[]{:S(2)}) collective-permute-start(bf16[320,768]{1,0:T(8,128)(2,1)S(1)} %bitcast.122), channel_id=1, source_target_pairs={{0,3},{1,2},{2,1},{3,0},{4,7},{5,6},{6,5},{7,4},{8,11},{9,10},{10,... | collective-permute-start | bytes 1474568 | tf_op jit(solution)/shard_map/ppermute | solution.py:127
  46.7 23.3 %collective-permute-start.10 = (bf16[320,768]{1,0:T(8,128)(2,1)S(1)}, bf16[320,768]{1,0:T(8,128)(2,1)S(1)}, u32[]{:S(2)}, u32[]{:S(2)}) collective-permute-start(bf16[320,768]{1,0:T(8,128)(2,1)S(1)} %bitcast.123), channel_id=1, source_target_pairs={{0,1},{1,0},{2,3},{3,2},{4,5},{5,4},{6,7},{7,6},{8,9},{9,8},{10,11... | collective-permute-start | bytes 1474568 | tf_op jit(solution)/shard_map/ppermute | solution.py:127
  48.2 23.5 %collective-permute-start.11 = (bf16[320,768]{1,0:T(8,128)(2,1)S(1)}, bf16[320,768]{1,0:T(8,128)(2,1)S(1)}, u32[]{:S(2)}, u32[]{:S(2)}) collective-permute-start(bf16[320,768]{1,0:T(8,128)(2,1)S(1)} %bitcast.124), channel_id=1, source_target_pairs={{0,2},{1,3},{2,0},{3,1},{4,6},{5,7},{6,4},{7,5},{8,10},{9,11},{10,... | collective-permute-start | bytes 1474568 | tf_op jit(solution)/shard_map/ppermute | solution.py:127
  75.9 14.2 %collective-permute-start.13 = (bf16[320,768]{1,0:T(8,128)(2,1)S(1)}, bf16[320,768]{1,0:T(8,128)(2,1)S(1)}, u32[]{:S(2)}, u32[]{:S(2)}) collective-permute-start(bf16[320,768]{1,0:T(8,128)(2,1)S(1)} %convolution_convert_fusion.3), channel_id=1, source_target_pairs={{0,1},{1,0},{2,3},{3,2},{4,5},{5,4},{6,7},{7,6},{8,9},{9,8},{10,11... | collective-permute-start | bytes 1474568 | tf_op jit(solution)/shard_map/ppermute | solution.py:138
  76.5 22.7 %collective-permute-start.14 = (bf16[320,768]{1,0:T(8,128)(2,1)S(1)}, bf16[320,768]{1,0:T(8,128)(2,1)S(1)}, u32[]{:S(2)}, u32[]{:S(2)}) collective-permute-start(bf16[320,768]{1,0:T(8,128)(2,1)S(1)} %convolution_convert_fusion.2), channel_id=1, source_target_pairs={{0,2},{1,3},{2,0},{3,1},{4,6},{5,7},{6,4},{7,5},{8,10},{9,11},{10,... | collective-permute-start | bytes 1474568 | tf_op jit(solution)/shard_map/ppermute | solution.py:138
  77.1 22.2 %collective-permute-start.15 = (bf16[320,768]{1,0:T(8,128)(2,1)S(1)}, bf16[320,768]{1,0:T(8,128)(2,1)S(1)}, u32[]{:S(2)}, u32[]{:S(2)}) collective-permute-start(bf16[320,768]{1,0:T(8,128)(2,1)S(1)} %convolution_convert_fusion.1), channel_id=1, source_target_pairs={{0,3},{1,2},{2,1},{3,0},{4,7},{5,6},{6,5},{7,4},{8,11},{9,10},{10,... | collective-permute-start | bytes 1474568 | tf_op jit(solution)/shard_map/ppermute | solution.py:138
  99.9 7.0 %collective-permute-start.16 = (bf16[40,768]{1,0:T(8,128)(2,1)S(1)}, bf16[40,768]{1,0:T(8,128)(2,1)S(1)}, u32[]{:S(2)}, u32[]{:S(2)}) collective-permute-start(bf16[40,768]{1,0:T(8,128)(2,1)S(1)} %get-tuple-element.13), channel_id=1, source_target_pairs={{0,4},{4,0},{8,12},{12,8},{16,20},{20,16},{24,28},{28,24},{1,5},{5... | collective-permute-start | bytes 184328 | tf_op jit(solution)/shard_map/ppermute | solution.py:64
  100.9 8.1 %collective-permute-start.17 = (bf16[40,768]{1,0:T(8,128)(2,1)S(1)}, bf16[40,768]{1,0:T(8,128)(2,1)S(1)}, u32[]{:S(2)}, u32[]{:S(2)}) collective-permute-start(bf16[40,768]{1,0:T(8,128)(2,1)S(1)} %get-tuple-element.12), channel_id=1, source_target_pairs={{0,8},{4,12},{8,0},{12,4},{16,24},{20,28},{24,16},{28,20},{1,9},{5... | collective-permute-start | bytes 184328 | tf_op jit(solution)/shard_map/ppermute | solution.py:64
  104.1 6.4 %collective-permute-start.18 = (bf16[40,768]{1,0:T(8,128)(2,1)S(1)}, bf16[40,768]{1,0:T(8,128)(2,1)S(1)}, u32[]{:S(2)}, u32[]{:S(2)}) collective-permute-start(bf16[40,768]{1,0:T(8,128)(2,1)S(1)} %get-tuple-element.11), channel_id=1, source_target_pairs={{0,12},{4,8},{8,4},{12,0},{16,28},{20,24},{24,20},{28,16},{1,13},{... | collective-permute-start | bytes 184328 | tf_op jit(solution)/shard_map/ppermute | solution.py:64
  104.2 6.3 %collective-permute-start.19 = (bf16[40,768]{1,0:T(8,128)(2,1)S(1)}, bf16[40,768]{1,0:T(8,128)(2,1)S(1)}, u32[]{:S(2)}, u32[]{:S(2)}) collective-permute-start(bf16[40,768]{1,0:T(8,128)(2,1)S(1)} %get-tuple-element.10), channel_id=1, source_target_pairs={{0,16},{4,20},{8,24},{12,28},{16,0},{20,4},{24,8},{28,12},{1,17},{... | collective-permute-start | bytes 184328 | tf_op jit(solution)/shard_map/ppermute | solution.py:64
  107.0 9.9 %collective-permute-start.20 = (bf16[40,768]{1,0:T(8,128)(2,1)S(1)}, bf16[40,768]{1,0:T(8,128)(2,1)S(1)}, u32[]{:S(2)}, u32[]{:S(2)}) collective-permute-start(bf16[40,768]{1,0:T(8,128)(2,1)S(1)} %get-tuple-element.9), channel_id=1, source_target_pairs={{0,20},{4,16},{8,28},{12,24},{16,4},{20,0},{24,12},{28,8},{1,21},{... | collective-permute-start | bytes 184328 | tf_op jit(solution)/shard_map/ppermute | solution.py:64
  107.0 9.9 %collective-permute-start.21 = (bf16[40,768]{1,0:T(8,128)(2,1)S(1)}, bf16[40,768]{1,0:T(8,128)(2,1)S(1)}, u32[]{:S(2)}, u32[]{:S(2)}) collective-permute-start(bf16[40,768]{1,0:T(8,128)(2,1)S(1)} %get-tuple-element.8), channel_id=1, source_target_pairs={{0,24},{4,28},{8,16},{12,20},{16,8},{20,12},{24,0},{28,4},{1,25},{... | collective-permute-start | bytes 184328 | tf_op jit(solution)/shard_map/ppermute | solution.py:64
  109.1 7.8 %collective-permute-start.22 = (bf16[40,768]{1,0:T(8,128)(2,1)S(1)}, bf16[40,768]{1,0:T(8,128)(2,1)S(1)}, u32[]{:S(2)}, u32[]{:S(2)}) collective-permute-start(bf16[40,768]{1,0:T(8,128)(2,1)S(1)} %get-tuple-element.7), channel_id=1, source_target_pairs={{0,28},{4,24},{8,20},{12,16},{16,12},{20,8},{24,4},{28,0},{1,29},{... | collective-permute-start | bytes 184328 | tf_op jit(solution)/shard_map/ppermute | solution.py:64
  (6 other events, 60.6 us)

commit v5 on v4

--- a/solution.py
+++ b/solution.py
@@ -68,6 +68,44 @@
     else:
         order = (me - lax.iota(jnp.int32, n)) % n
     return jnp.take(stacked, order, axis=0)
+
+
+def bit_orders(n):
+    bits = [1 << i for i in range(n.bit_length() - 1)]
+    return [bits, bits[::-1]]
+
+
+def reduce_scatter_tree(block_fn, axis, n):
+    outs = []
+    for h, order in enumerate(bit_orders(n)):
+        held = {d: block_fn(d, h) for d in range(n)}
+        for bit in order:
+            send = sorted(d for d in held if d & bit)
+            keep = sorted(d for d in held if not d & bit)
+            payload = jnp.concatenate([held[d].astype(jnp.bfloat16) for d in send], axis=0)
+            got = lax.ppermute(payload, axis, [(i, i ^ bit) for i in range(n)])
+            rows = held[keep[0]].shape[0]
+            held = {
+                d: held[d].astype(jnp.float32) + got[i * rows:(i + 1) * rows].astype(jnp.float32)
+                for i, d in enumerate(keep)
+            }
+        outs.append(held[0])
+    return outs
+
+
+def all_gather_tree(halves, axis, n):
+    outs = []
+    for h, order in enumerate(bit_orders(n)):
+        held = {0: halves[h]}
+        for bit in order:
+            have = sorted(held)
+            payload = jnp.concatenate([held[d] for d in have], axis=0)
+            got = lax.ppermute(payload, axis, [(i, i ^ bit) for i in range(n)])
+            rows = halves[h].shape[0]
+            for i, d in enumerate(have):
+                held[d ^ bit] = got[i * rows:(i + 1) * rows]
+        outs.append(held)
+    return outs
 
 
 SLOT_CHUNKS = 1
@@ -87,17 +125,29 @@
     proj_blocks = projection.reshape(tensor_count, width, projection.shape[1])
     proj_parts = [lax.dynamic_index_in_dim(proj_blocks, p, 0, keepdims=False) for p in partners]
 
+    tree = is_pow2(tensor_count) and tensor_count > 1 and width % 2 == 0
+    half = width // 2
+
     def head_term(p):
         columns = lax.dynamic_slice_in_dim(out_proj, p * width, width, axis=1)
         return jnp.dot(context, columns, preferred_element_type=jnp.float32).astype(jnp.bfloat16)
 
-    received = [
-        lax.ppermute(head_term(partners[s]), "tensor", pairs_for(s, tensor_count))
-        for s in range(1, tensor_count)
-    ]
-    summed = head_term(me_t).astype(jnp.float32) + residual_in.astype(jnp.float32)
-    for got in received:
-        summed = summed + got.astype(jnp.float32)
+    if tree:
+        def head_half(d, h):
+            start = (me_t ^ d) * width + h * half
+            columns = lax.dynamic_slice_in_dim(out_proj, start, half, axis=1)
+            return jnp.dot(context, columns, preferred_element_type=jnp.float32).astype(jnp.bfloat16)
+
+        summed = jnp.concatenate(reduce_scatter_tree(head_half, "tensor", tensor_count), axis=1)
+        summed = summed + residual_in.astype(jnp.float32)
+    else:
+        received = [
+            lax.ppermute(head_term(partners[s]), "tensor", pairs_for(s, tensor_count))
+            for s in range(1, tensor_count)
+        ]
+        summed = head_term(me_t).astype(jnp.float32) + residual_in.astype(jnp.float32)
+        for got in received:
+            summed = summed + got.astype(jnp.float32)
     generated = summed.astype(jnp.bfloat16)
 
     group_ids = lax.iota(jnp.int32, group_count)
@@ -122,23 +172,43 @@
         ).astype(jnp.bfloat16)
         arrived = swap_blocks(outgoing.reshape(group_count, chunk_cap, width), "dp")
         arrived = arrived.reshape(chunk_slots, width)
-        pre_act = jnp.dot(arrived, proj_parts[0], preferred_element_type=jnp.float32)
-        for s in range(1, tensor_count):
-            got = lax.ppermute(arrived, "tensor", pairs_for(s, tensor_count))
-            pre_act = pre_act + jnp.dot(got, proj_parts[s], preferred_element_type=jnp.float32)
+        if tree:
+            pre_act = None
+            held = all_gather_tree([arrived[:, :half], arrived[:, half:]], "tensor", tensor_count)
+            for h in range(2):
+                for d in range(tensor_count):
+                    rows_w = lax.dynamic_slice_in_dim(projection, (me_t ^ d) * width + h * half, half, axis=0)
+                    term = jnp.dot(held[h][d], rows_w, preferred_element_type=jnp.float32)
+                    pre_act = term if pre_act is None else pre_act + term
+        else:
+            pre_act = jnp.dot(arrived, proj_parts[0], preferred_element_type=jnp.float32)
+            for s in range(1, tensor_count):
+                got = lax.ppermute(arrived, "tensor", pairs_for(s, tensor_count))
+                pre_act = pre_act + jnp.dot(got, proj_parts[s], preferred_element_type=jnp.float32)
         pre_grad = (-slope_times(pre_act, jnp.broadcast_to(head_row, pre_act.shape))).astype(jnp.bfloat16)
-        back = [
-            lax.dot_general(
-                pre_grad, part, (((1,), (1,)), ((), ())), preferred_element_type=jnp.float32
+        if tree:
+            def back_half(d, h):
+                rows_w = lax.dynamic_slice_in_dim(projection, (me_t ^ d) * width + h * half, half, axis=0)
+                return lax.dot_general(
+                    pre_grad, rows_w, (((1,), (1,)), ((), ())), preferred_element_type=jnp.float32
+                ).astype(jnp.bfloat16)
+
+            critic_grad = jnp.concatenate(
+                reduce_scatter_tree(back_half, "tensor", tensor_count), axis=1
             ).astype(jnp.bfloat16)
-            for part in proj_parts
-        ]
-        critic_grad = back[0].astype(jnp.float32)
-        for s in range(1, tensor_count):
-            critic_grad = critic_grad + lax.ppermute(
-                back[s], "tensor", pairs_for(s, tensor_count)
-            ).astype(jnp.float32)
-        critic_grad = critic_grad.astype(jnp.bfloat16)
+        else:
+            back = [
+                lax.dot_general(
+                    pre_grad, part, (((1,), (1,)), ((), ())), preferred_element_type=jnp.float32
+                ).astype(jnp.bfloat16)
+                for part in proj_parts
+            ]
+            critic_grad = back[0].astype(jnp.float32)
+            for s in range(1, tensor_count):
+                critic_grad = critic_grad + lax.ppermute(
+                    back[s], "tensor", pairs_for(s, tensor_count)
+                ).astype(jnp.float32)
+            critic_grad = critic_grad.astype(jnp.bfloat16)
         returned = swap_blocks(critic_grad.reshape(group_count, chunk_cap, width), "dp")
         returned = returned.reshape(chunk_slots, width)
         part = jnp.dot(placing, returned, preferred_element_type=jnp.float32)

time: 120 us -> 112 us (0.933)
  waiting for transfers between devices: 64 us -> 50 us
  matrix products: 19.2 us -> 22.7 us
  other arithmetic: 1.07 us -> 2.89 us
  starting transfers between devices: 29.7 us -> 31.1 us
    ppermute x9 -> x12, waiting for transfers between devices: 51.3 us -> 37.7 us  [the longest x8 21.3 us: reduce_scatter_tree(): got = lax.ppermute(payload, axis, [(i, i ^ bit) for i in range(n)])]
    dot_general x12 -> x24, matrix products: 17.6 us -> 21.1 us  [the longest x8 11.5 us: head_half(): jnp.dot(context, columns, preferred_element_type=jnp.float32)]
    ppermute x9 -> x12, starting transfers between devices: 11.8 us -> 13.4 us  [the longest x8 11.2 us: reduce_scatter_tree(): got = lax.ppermute(payload, axis, [(i, i ^ bit) for i in range(n)])]
  transfers between devices with their start and end apart: 23 -> 26, of which waited for: 8 -> 15; matrix products, arithmetic and copies ran while one was open for 10% -> 14% of each run, Pallas kernels for 0% -> 0%
where the time goes in v5:
time: 112 us
  waiting for transfers between devices  50 us (45%)
  starting transfers between devices  31.1 us (28%)
  matrix products  22.7 us (20%)
  local copies, waits for them, and re-layouts  3.63 us (3%)
  other arithmetic  2.89 us (3%)
  between operations  1.31 us (1%)
    ppermute x8, waiting for transfers between devices, reduce_scatter_tree(): got = lax.ppermute(payload, axis, [(i, i ^ bit) for i in range(n)])  21.3 us
    ppermute x14, starting transfers between devices, swap_blocks(): got.append(lax.ppermute(chunk, axis, pairs_for(s, n)))  17.7 us
    ppermute x4, waiting for transfers between devices, all_gather_tree(): got = lax.ppermute(payload, axis, [(i, i ^ bit) for i in range(n)])  16.3 us
    ppermute x14, waiting for transfers between devices, swap_blocks(): got.append(lax.ppermute(chunk, axis, pairs_for(s, n)))  12.3 us
    dot_general x8, matrix products, head_half(): jnp.dot(context, columns, preferred_element_type=jnp.float32)  11.5 us
    ppermute x8, starting transfers between devices, reduce_scatter_tree(): got = lax.ppermute(payload, axis, [(i, i ^ bit) for i in range(n)])  11.2 us
    dot_general x8, matrix products, shards(): term = jnp.dot(held[h][d], rows_w, preferred_element_type=jnp.float32)  6.13 us
    dot_general x8, matrix products, back_half(): lax.dot_general(pre_grad, rows_w, (((1,), (1,)), ((), ())), preferred_ele...  3.52 us
  transfers between devices with their start and end apart: 26, of which 15 were waited for; matrix products, arithmetic and copies ran while one was open for 14% of the time, Pallas kernels for 0%

profile of v5, /device:TPU:0, one launch (start us, length us, event | category | flops | bytes accessed | tf_op | source)
XLA Modules:
  0.0 111.7 jit_solution(17257214452099123766)
XLA Ops:
  3.1 1.4 %fusion.19 = bf16[256,384]{0,1:T(8,128)(2,1)S(1)} fusion(bf16[256,768]{1,0:T(8,128)(2,1)S(1)} %copy-done, bf16[768,3072]{1,0:T(8,128)(2,1)} %param.11, s32[]{:T(128)S(6)} %select_n.90), kind=kOutput, calls=%fused_computation.44 | convolution fusion | flops 151093248 | bytes 1179652 | tf_op jit(solution)/shard_map/dot_general | solution.py:139
  4.5 3.0 %collective-permute-start.2 = (bf16[512,384]{0,1:T(8,128)(2,1)S(1)}, bf16[512,384]{0,1:T(8,128)(2,1)S(1)}, u32[]{:S(2)}, u32[]{:S(2)}) collective-permute-start(bf16[512,384]{0,1:T(8,128)(2,1)S(1)} %pad_maximum_fusion.5), channel_id=1, source_target_pairs={{0,2},{1,3},{2,0},{3,1},{4,6},{5,7},{6,4},{7,5},{8,10},{9,11},{10,... | collective-permute-start | bytes 1179656 | tf_op jit(solution)/shard_map/ppermute | solution.py:86
  10.5 1.6 %collective-permute-start = (bf16[512,384]{0,1:T(8,128)(2,1)S(1)}, bf16[512,384]{0,1:T(8,128)(2,1)}, u32[]{:S(2)}, u32[]{:S(2)}) collective-permute-start(bf16[512,384]{0,1:T(8,128)(2,1)S(1)} %pad_maximum_fusion.4), channel_id=1, source_target_pairs={{0,1},{1,0},{2,3},{3,2},{4,5},{5,4},{6,7},{7,6},{8,9},{9,8},{10,11... | collective-permute-start | bytes 1179656 | tf_op jit(solution)/shard_map/ppermute | solution.py:86
  18.1 1.8 %collective-permute-start.3 = (bf16[256,384]{0,1:T(8,128)(2,1)S(1)}, bf16[256,384]{0,1:T(8,128)(2,1)S(1)}, u32[]{:S(2)}, u32[]{:S(2)}) collective-permute-start(bf16[256,384]{0,1:T(8,128)(2,1)S(1)} %add_convert_fusion.4), channel_id=1, source_target_pairs={{0,1},{1,0},{2,3},{3,2},{4,5},{5,4},{6,7},{7,6},{8,9},{9,8},{10,11... | collective-permute-start | bytes 589832 | tf_op jit(solution)/shard_map/ppermute | solution.py:86
  19.9 2.2 %collective-permute-done = bf16[512,384]{0,1:T(8,128)(2,1)} collective-permute-done((bf16[512,384]{0,1:T(8,128)(2,1)S(1)}, bf16[512,384]{0,1:T(8,128)(2,1)}, u32[]{:S(2)}, u32[]{:S(2)}) %collective-permute-start) | collective-permute-done | bytes 393248 | tf_op jit(solution)/shard_map/ppermute | solution.py:86
  22.1 1.5 %add_convert_fusion.5 = bf16[256,384]{0,1:T(8,128)(2,1)S(1)} fusion(bf16[512,384]{0,1:T(8,128)(2,1)} %collective-permute-done, bf16[256,768]{1,0:T(8,128)(2,1)S(1)} %copy-done, bf16[768,3072]{1,0:T(8,128)(2,1)} %param.11, s32[]{:T(128)S(6)} %select_n.87), kind=kOutput, calls=%fused_computation.132 | convolution fusion | flops 151486464 | bytes 1376260 | tf_op jit(solution)/shard_map/dot_general | solution.py:139
  23.7 1.7 %collective-permute-done.3 = bf16[256,384]{0,1:T(8,128)(2,1)S(1)} collective-permute-done((bf16[256,384]{0,1:T(8,128)(2,1)S(1)}, bf16[256,384]{0,1:T(8,128)(2,1)S(1)}, u32[]{:S(2)}, u32[]{:S(2)}) %collective-permute-start.3) | collective-permute-done | bytes 196640 | tf_op jit(solution)/shard_map/ppermute | solution.py:86
  25.4 3.9 %collective-permute-done.1 = bf16[256,384]{0,1:T(8,128)(2,1)S(1)} collective-permute-done((bf16[256,384]{0,1:T(8,128)(2,1)S(1)}, bf16[256,384]{0,1:T(8,128)(2,1)S(1)}, u32[]{:S(2)}, u32[]{:S(2)}) %collective-permute-start.1) | collective-permute-done | bytes 196640 | tf_op jit(solution)/shard_map/ppermute | solution.py:86
  32.0 1.7 %collective-permute-start.5 = (bf16[40,768]{1,0:T(8,128)(2,1)S(1)}, bf16[40,768]{1,0:T(8,128)(2,1)S(1)}, u32[]{:S(2)}, u32[]{:S(2)}) collective-permute-start(bf16[40,768]{1,0:T(8,128)(2,1)S(1)} %get-tuple-element.22), channel_id=1, source_target_pairs={{0,8},{4,12},{8,0},{12,4},{16,24},{20,28},{24,16},{28,20},{1,9},{5... | collective-permute-start | bytes 184328 | tf_op jit(solution)/shard_map/ppermute | solution.py:64
  33.8 2.7 %collective-permute-start.7 = (bf16[40,768]{1,0:T(8,128)(2,1)S(1)}, bf16[40,768]{1,0:T(8,128)(2,1)S(1)}, u32[]{:S(2)}, u32[]{:S(2)}) collective-permute-start(bf16[40,768]{1,0:T(8,128)(2,1)S(1)} %get-tuple-element.20), channel_id=1, source_target_pairs={{0,16},{4,20},{8,24},{12,28},{16,0},{20,4},{24,8},{28,12},{1,17},{... | collective-permute-start | bytes 184328 | tf_op jit(solution)/shard_map/ppermute | solution.py:64
  36.5 3.6 %collective-permute-start.9 = (bf16[40,768]{1,0:T(8,128)(2,1)S(1)}, bf16[40,768]{1,0:T(8,128)(2,1)S(1)}, u32[]{:S(2)}, u32[]{:S(2)}) collective-permute-start(bf16[40,768]{1,0:T(8,128)(2,1)S(1)} %get-tuple-element.18), channel_id=1, source_target_pairs={{0,24},{4,28},{8,16},{12,20},{16,8},{20,12},{24,0},{28,4},{1,25},{... | collective-permute-start | bytes 184328 | tf_op jit(solution)/shard_map/ppermute | solution.py:64
  40.3 6.2 %collective-permute-done.8 = bf16[40,768]{1,0:T(8,128)(2,1)S(1)} collective-permute-done((bf16[40,768]{1,0:T(8,128)(2,1)S(1)}, bf16[40,768]{1,0:T(8,128)(2,1)S(1)}, u32[]{:S(2)}, u32[]{:S(2)}) %collective-permute-start.8) | collective-permute-done | bytes 61472 | tf_op jit(solution)/shard_map/ppermute | solution.py:64
  47.4 1.6 %fusion.48 = f32[320,768]{1,0:T(8,128)S(1)} fusion(bf16[1,3072,768]{2,1,0:T(8,128)(2,1)} %param.14, s32[]{:T(128)S(6)} %select_n.84, bf16[320,768]{1,0:T(8,128)(2,1)S(1)} %bitcast.158), kind=kOutput, calls=%fused_computation.90 | convolution fusion | flops 188743680 | bytes 1818628 | tf_op jit(solution)/shard_map/dot_general | solution.py:181
  49.0 1.5 %collective-permute-start.11 = (bf16[320,384]{1,0:T(8,128)(2,1)S(1)}, bf16[320,384]{1,0:T(8,128)(2,1)S(1)}, u32[]{:S(2)}, u32[]{:S(2)}) collective-permute-start(bf16[320,384]{1,0:T(8,128)(2,1)S(1)} %get-tuple-element.15), channel_id=1, source_target_pairs={{0,1},{1,0},{2,3},{3,2},{4,5},{5,4},{6,7},{7,6},{8,9},{9,8},{10,11... | collective-permute-start | bytes 737288 | tf_op jit(solution)/shard_map/ppermute | solution.py:103
  50.6 1.5 %fusion.38 = f32[320,768]{1,0:T(8,128)S(1)} fusion(bf16[1,3072,768]{2,1,0:T(8,128)(2,1)} %param.14, s32[]{:T(128)S(6)} %select_n.88, bf16[320,768]{1,0:T(8,128)(2,1)S(1)} %bitcast.159), kind=kOutput, calls=%fused_computation.80 | convolution fusion | flops 188743680 | bytes 1818628 | tf_op jit(solution)/shard_map/dot_general | solution.py:181
  52.1 5.0 %collective-permute-done.11 = bf16[320,384]{1,0:T(8,128)(2,1)S(1)} collective-permute-done((bf16[320,384]{1,0:T(8,128)(2,1)S(1)}, bf16[320,384]{1,0:T(8,128)(2,1)S(1)}, u32[]{:S(2)}, u32[]{:S(2)}) %collective-permute-start.11) | collective-permute-done | bytes 245792 | tf_op jit(solution)/shard_map/ppermute | solution.py:103
  59.8 9.8 %collective-permute-done.12 = bf16[640,384]{1,0:T(8,128)(2,1)S(1)} collective-permute-done((bf16[640,384]{1,0:T(8,128)(2,1)S(1)}, bf16[640,384]{1,0:T(8,128)(2,1)S(1)}, u32[]{:S(2)}, u32[]{:S(2)}) %collective-permute-start.12) | collective-permute-done | bytes 491552 | tf_op jit(solution)/shard_map/ppermute | solution.py:103
  75.3 1.5 %collective-permute-start.17 = (bf16[640,384]{1,0:T(8,128)(2,1)S(1)}, bf16[640,384]{1,0:T(8,128)(2,1)S(1)}, u32[]{:S(2)}, u32[]{:S(2)}) collective-permute-start(bf16[640,384]{1,0:T(8,128)(2,1)S(1)} %pad_maximum_fusion.3), channel_id=1, source_target_pairs={{0,2},{1,3},{2,0},{3,1},{4,6},{5,7},{6,4},{7,5},{8,10},{9,11},{10,... | collective-permute-start | bytes 1474568 | tf_op jit(solution)/shard_map/ppermute | solution.py:86
  77.7 7.7 %collective-permute-done.15 = bf16[640,384]{1,0:T(8,128)(2,1)S(1)} collective-permute-done((bf16[640,384]{1,0:T(8,128)(2,1)S(1)}, bf16[640,384]{1,0:T(8,128)(2,1)S(1)}, u32[]{:S(2)}, u32[]{:S(2)}) %collective-permute-start.15) | collective-permute-done | bytes 491552 | tf_op jit(solution)/shard_map/ppermute | solution.py:86
  88.9 3.2 %collective-permute-done.16 = bf16[320,384]{1,0:T(8,128)(2,1)S(1)} collective-permute-done((bf16[320,384]{1,0:T(8,128)(2,1)S(1)}, bf16[320,384]{1,0:T(8,128)(2,1)S(1)}, u32[]{:S(2)}, u32[]{:S(2)}) %collective-permute-start.16) | collective-permute-done | bytes 245792 | tf_op jit(solution)/shard_map/ppermute | solution.py:86
  92.2 2.0 %collective-permute-done.18 = bf16[320,384]{1,0:T(8,128)(2,1)S(1)} collective-permute-done((bf16[320,384]{1,0:T(8,128)(2,1)S(1)}, bf16[320,384]{1,0:T(8,128)(2,1)S(1)}, u32[]{:S(2)}, u32[]{:S(2)}) %collective-permute-start.18) | collective-permute-done | bytes 245792 | tf_op jit(solution)/shard_map/ppermute | solution.py:86
  94.4 4.4 %collective-permute-start.23 = (bf16[40,768]{1,0:T(8,128)(2,1)S(1)}, bf16[40,768]{1,0:T(8,128)(2,1)S(1)}, u32[]{:S(2)}, u32[]{:S(2)}) collective-permute-start(bf16[40,768]{1,0:T(8,128)(2,1)S(1)} %get-tuple-element.14), channel_id=1, source_target_pairs={{0,20},{4,16},{8,28},{12,24},{16,4},{20,0},{24,12},{28,8},{1,21},{... | collective-permute-start | bytes 184328 | tf_op jit(solution)/shard_map/ppermute | solution.py:64
  100.7 2.5 %collective-permute-start.24 = (bf16[40,768]{1,0:T(8,128)(2,1)S(1)}, bf16[40,768]{1,0:T(8,128)(2,1)S(1)}, u32[]{:S(2)}, u32[]{:S(2)}) collective-permute-start(bf16[40,768]{1,0:T(8,128)(2,1)S(1)} %get-tuple-element.13), channel_id=1, source_target_pairs={{0,24},{4,28},{8,16},{12,20},{16,8},{20,12},{24,0},{28,4},{1,25},{... | collective-permute-start | bytes 184328 | tf_op jit(solution)/shard_map/ppermute | solution.py:64
  104.1 5.6 %collective-permute-done.22 = bf16[40,768]{1,0:T(8,128)(2,1)S(1)} collective-permute-done((bf16[40,768]{1,0:T(8,128)(2,1)S(1)}, bf16[40,768]{1,0:T(8,128)(2,1)S(1)}, u32[]{:S(2)}, u32[]{:S(2)}) %collective-permute-start.22) | collective-permute-done | bytes 61472 | tf_op jit(solution)/shard_map/ppermute | solution.py:64
  (118 shorter events, 32.9 us)
Async XLA Ops:
  4.5 12.1 %collective-permute-start.2 = (bf16[512,384]{0,1:T(8,128)(2,1)S(1)}, bf16[512,384]{0,1:T(8,128)(2,1)S(1)}, u32[]{:S(2)}, u32[]{:S(2)}) collective-permute-start(bf16[512,384]{0,1:T(8,128)(2,1)S(1)} %pad_maximum_fusion.5), channel_id=1, source_target_pairs={{0,2},{1,3},{2,0},{3,1},{4,6},{5,7},{6,4},{7,5},{8,10},{9,11},{10,... | collective-permute-start | bytes 1179656 | tf_op jit(solution)/shard_map/ppermute | solution.py:86
  10.5 11.6 %collective-permute-start = (bf16[512,384]{0,1:T(8,128)(2,1)S(1)}, bf16[512,384]{0,1:T(8,128)(2,1)}, u32[]{:S(2)}, u32[]{:S(2)}) collective-permute-start(bf16[512,384]{0,1:T(8,128)(2,1)S(1)} %pad_maximum_fusion.4), channel_id=1, source_target_pairs={{0,1},{1,0},{2,3},{3,2},{4,5},{5,4},{6,7},{7,6},{8,9},{9,8},{10,11... | collective-permute-start | bytes 1179656 | tf_op jit(solution)/shard_map/ppermute | solution.py:86
  18.1 7.2 %collective-permute-start.3 = (bf16[256,384]{0,1:T(8,128)(2,1)S(1)}, bf16[256,384]{0,1:T(8,128)(2,1)S(1)}, u32[]{:S(2)}, u32[]{:S(2)}) collective-permute-start(bf16[256,384]{0,1:T(8,128)(2,1)S(1)} %add_convert_fusion.4), channel_id=1, source_target_pairs={{0,1},{1,0},{2,3},{3,2},{4,5},{5,4},{6,7},{7,6},{8,9},{9,8},{10,11... | collective-permute-start | bytes 589832 | tf_op jit(solution)/shard_map/ppermute | solution.py:86
  23.6 5.7 %collective-permute-start.1 = (bf16[256,384]{0,1:T(8,128)(2,1)S(1)}, bf16[256,384]{0,1:T(8,128)(2,1)S(1)}, u32[]{:S(2)}, u32[]{:S(2)}) collective-permute-start(bf16[256,384]{0,1:T(8,128)(2,1)S(1)} %add_convert_fusion.5), channel_id=1, source_target_pairs={{0,2},{1,3},{2,0},{3,1},{4,6},{5,7},{6,4},{7,5},{8,10},{9,11},{10,... | collective-permute-start | bytes 589832 | tf_op jit(solution)/shard_map/ppermute | solution.py:86
  31.0 5.6 %collective-permute-start.4 = (bf16[40,768]{1,0:T(8,128)(2,1)S(1)}, bf16[40,768]{1,0:T(8,128)(2,1)S(1)}, u32[]{:S(2)}, u32[]{:S(2)}) collective-permute-start(bf16[40,768]{1,0:T(8,128)(2,1)S(1)} %get-tuple-element.23), channel_id=1, source_target_pairs={{0,4},{4,0},{8,12},{12,8},{16,20},{20,16},{24,28},{28,24},{1,5},{5... | collective-permute-start | bytes 184328 | tf_op jit(solution)/shard_map/ppermute | solution.py:64
  32.0 8.1 %collective-permute-start.5 = (bf16[40,768]{1,0:T(8,128)(2,1)S(1)}, bf16[40,768]{1,0:T(8,128)(2,1)S(1)}, u32[]{:S(2)}, u32[]{:S(2)}) collective-permute-start(bf16[40,768]{1,0:T(8,128)(2,1)S(1)} %get-tuple-element.22), channel_id=1, source_target_pairs={{0,8},{4,12},{8,0},{12,4},{16,24},{20,28},{24,16},{28,20},{1,9},{5... | collective-permute-start | bytes 184328 | tf_op jit(solution)/shard_map/ppermute | solution.py:64
  33.7 6.6 %collective-permute-start.6 = (bf16[40,768]{1,0:T(8,128)(2,1)S(1)}, bf16[40,768]{1,0:T(8,128)(2,1)S(1)}, u32[]{:S(2)}, u32[]{:S(2)}) collective-permute-start(bf16[40,768]{1,0:T(8,128)(2,1)S(1)} %get-tuple-element.21), channel_id=1, source_target_pairs={{0,12},{4,8},{8,4},{12,0},{16,28},{20,24},{24,20},{28,16},{1,13},{... | collective-permute-start | bytes 184328 | tf_op jit(solution)/shard_map/ppermute | solution.py:64
  33.8 6.5 %collective-permute-start.7 = (bf16[40,768]{1,0:T(8,128)(2,1)S(1)}, bf16[40,768]{1,0:T(8,128)(2,1)S(1)}, u32[]{:S(2)}, u32[]{:S(2)}) collective-permute-start(bf16[40,768]{1,0:T(8,128)(2,1)S(1)} %get-tuple-element.20), channel_id=1, source_target_pairs={{0,16},{4,20},{8,24},{12,28},{16,0},{20,4},{24,8},{28,12},{1,17},{... | collective-permute-start | bytes 184328 | tf_op jit(solution)/shard_map/ppermute | solution.py:64
  36.5 10.1 %collective-permute-start.8 = (bf16[40,768]{1,0:T(8,128)(2,1)S(1)}, bf16[40,768]{1,0:T(8,128)(2,1)S(1)}, u32[]{:S(2)}, u32[]{:S(2)}) collective-permute-start(bf16[40,768]{1,0:T(8,128)(2,1)S(1)} %get-tuple-element.19), channel_id=1, source_target_pairs={{0,20},{4,16},{8,28},{12,24},{16,4},{20,0},{24,12},{28,8},{1,21},{... | collective-permute-start | bytes 184328 | tf_op jit(solution)/shard_map/ppermute | solution.py:64
  36.5 10.1 %collective-permute-start.9 = (bf16[40,768]{1,0:T(8,128)(2,1)S(1)}, bf16[40,768]{1,0:T(8,128)(2,1)S(1)}, u32[]{:S(2)}, u32[]{:S(2)}) collective-permute-start(bf16[40,768]{1,0:T(8,128)(2,1)S(1)} %get-tuple-element.18), channel_id=1, source_target_pairs={{0,24},{4,28},{8,16},{12,20},{16,8},{20,12},{24,0},{28,4},{1,25},{... | collective-permute-start | bytes 184328 | tf_op jit(solution)/shard_map/ppermute | solution.py:64
  40.1 6.5 %collective-permute-start.10 = (bf16[40,768]{1,0:T(8,128)(2,1)S(1)}, bf16[40,768]{1,0:T(8,128)(2,1)S(1)}, u32[]{:S(2)}, u32[]{:S(2)}) collective-permute-start(bf16[40,768]{1,0:T(8,128)(2,1)S(1)} %get-tuple-element.17), channel_id=1, source_target_pairs={{0,28},{4,24},{8,20},{12,16},{16,12},{20,8},{24,4},{28,0},{1,29},{... | collective-permute-start | bytes 184328 | tf_op jit(solution)/shard_map/ppermute | solution.py:64
  49.0 8.0 %collective-permute-start.11 = (bf16[320,384]{1,0:T(8,128)(2,1)S(1)}, bf16[320,384]{1,0:T(8,128)(2,1)S(1)}, u32[]{:S(2)}, u32[]{:S(2)}) collective-permute-start(bf16[320,384]{1,0:T(8,128)(2,1)S(1)} %get-tuple-element.15), channel_id=1, source_target_pairs={{0,1},{1,0},{2,3},{3,2},{4,5},{5,4},{6,7},{7,6},{8,9},{9,8},{10,11... | collective-permute-start | bytes 737288 | tf_op jit(solution)/shard_map/ppermute | solution.py:103
  50.6 7.7 %collective-permute-start.13 = (bf16[320,384]{1,0:T(8,128)(2,1)S(1)}, bf16[320,384]{1,0:T(8,128)(2,1)S(1)}, u32[]{:S(2)}, u32[]{:S(2)}) collective-permute-start(bf16[320,384]{1,0:T(8,128)(2,1)S(1)} %get-tuple-element.16), channel_id=1, source_target_pairs={{0,2},{1,3},{2,0},{3,1},{4,6},{5,7},{6,4},{7,5},{8,10},{9,11},{10,... | collective-permute-start | bytes 737288 | tf_op jit(solution)/shard_map/ppermute | solution.py:103
  57.1 12.5 %collective-permute-start.12 = (bf16[640,384]{1,0:T(8,128)(2,1)S(1)}, bf16[640,384]{1,0:T(8,128)(2,1)S(1)}, u32[]{:S(2)}, u32[]{:S(2)}) collective-permute-start(bf16[640,384]{1,0:T(8,128)(2,1)S(1)} %pad_maximum_fusion), channel_id=1, source_target_pairs={{0,2},{1,3},{2,0},{3,1},{4,6},{5,7},{6,4},{7,5},{8,10},{9,11},{10,... | collective-permute-start | bytes 1474568 | tf_op jit(solution)/shard_map/ppermute | solution.py:103
  58.3 12.2 %collective-permute-start.14 = (bf16[640,384]{1,0:T(8,128)(2,1)S(1)}, bf16[640,384]{1,0:T(8,128)(2,1)S(1)}, u32[]{:S(2)}, u32[]{:S(2)}) collective-permute-start(bf16[640,384]{1,0:T(8,128)(2,1)S(1)} %pad_maximum_fusion.1), channel_id=1, source_target_pairs={{0,1},{1,0},{2,3},{3,2},{4,5},{5,4},{6,7},{7,6},{8,9},{9,8},{10,11... | collective-permute-start | bytes 1474568 | tf_op jit(solution)/shard_map/ppermute | solution.py:103
  74.1 11.2 %collective-permute-start.15 = (bf16[640,384]{1,0:T(8,128)(2,1)S(1)}, bf16[640,384]{1,0:T(8,128)(2,1)S(1)}, u32[]{:S(2)}, u32[]{:S(2)}) collective-permute-start(bf16[640,384]{1,0:T(8,128)(2,1)S(1)} %pad_maximum_fusion.2), channel_id=1, source_target_pairs={{0,1},{1,0},{2,3},{3,2},{4,5},{5,4},{6,7},{7,6},{8,9},{9,8},{10,11... | collective-permute-start | bytes 1474568 | tf_op jit(solution)/shard_map/ppermute | solution.py:86
  75.3 12.1 %collective-permute-start.17 = (bf16[640,384]{1,0:T(8,128)(2,1)S(1)}, bf16[640,384]{1,0:T(8,128)(2,1)S(1)}, u32[]{:S(2)}, u32[]{:S(2)}) collective-permute-start(bf16[640,384]{1,0:T(8,128)(2,1)S(1)} %pad_maximum_fusion.3), channel_id=1, source_target_pairs={{0,2},{1,3},{2,0},{3,1},{4,6},{5,7},{6,4},{7,5},{8,10},{9,11},{10,... | collective-permute-start | bytes 1474568 | tf_op jit(solution)/shard_map/ppermute | solution.py:86
  85.8 6.3 %collective-permute-start.16 = (bf16[320,384]{1,0:T(8,128)(2,1)S(1)}, bf16[320,384]{1,0:T(8,128)(2,1)S(1)}, u32[]{:S(2)}, u32[]{:S(2)}) collective-permute-start(bf16[320,384]{1,0:T(8,128)(2,1)S(1)} %add_convert_fusion.3), channel_id=1, source_target_pairs={{0,2},{1,3},{2,0},{3,1},{4,6},{5,7},{6,4},{7,5},{8,10},{9,11},{10,... | collective-permute-start | bytes 737288 | tf_op jit(solution)/shard_map/ppermute | solution.py:86
  87.9 6.3 %collective-permute-start.18 = (bf16[320,384]{1,0:T(8,128)(2,1)S(1)}, bf16[320,384]{1,0:T(8,128)(2,1)S(1)}, u32[]{:S(2)}, u32[]{:S(2)}) collective-permute-start(bf16[320,384]{1,0:T(8,128)(2,1)S(1)} %add_convert_fusion.1), channel_id=1, source_target_pairs={{0,1},{1,0},{2,3},{3,2},{4,5},{5,4},{6,7},{7,6},{8,9},{9,8},{10,11... | collective-permute-start | bytes 737288 | tf_op jit(solution)/shard_map/ppermute | solution.py:86
  94.3 6.4 %collective-permute-start.19 = (bf16[40,768]{1,0:T(8,128)(2,1)S(1)}, bf16[40,768]{1,0:T(8,128)(2,1)S(1)}, u32[]{:S(2)}, u32[]{:S(2)}) collective-permute-start(bf16[40,768]{1,0:T(8,128)(2,1)S(1)} %get-tuple-element.9), channel_id=1, source_target_pairs={{0,4},{4,0},{8,12},{12,8},{16,20},{20,16},{24,28},{28,24},{1,5},{5... | collective-permute-start | bytes 184328 | tf_op jit(solution)/shard_map/ppermute | solution.py:64
  94.4 15.4 %collective-permute-start.23 = (bf16[40,768]{1,0:T(8,128)(2,1)S(1)}, bf16[40,768]{1,0:T(8,128)(2,1)S(1)}, u32[]{:S(2)}, u32[]{:S(2)}) collective-permute-start(bf16[40,768]{1,0:T(8,128)(2,1)S(1)} %get-tuple-element.14), channel_id=1, source_target_pairs={{0,20},{4,16},{8,28},{12,24},{16,4},{20,0},{24,12},{28,8},{1,21},{... | collective-permute-start | bytes 184328 | tf_op jit(solution)/shard_map/ppermute | solution.py:64
  100.1 9.7 %collective-permute-start.22 = (bf16[40,768]{1,0:T(8,128)(2,1)S(1)}, bf16[40,768]{1,0:T(8,128)(2,1)S(1)}, u32[]{:S(2)}, u32[]{:S(2)}) collective-permute-start(bf16[40,768]{1,0:T(8,128)(2,1)S(1)} %get-tuple-element.12), channel_id=1, source_target_pairs={{0,16},{4,20},{8,24},{12,28},{16,0},{20,4},{24,8},{28,12},{1,17},{... | collective-permute-start | bytes 184328 | tf_op jit(solution)/shard_map/ppermute | solution.py:64
  100.7 9.2 %collective-permute-start.24 = (bf16[40,768]{1,0:T(8,128)(2,1)S(1)}, bf16[40,768]{1,0:T(8,128)(2,1)S(1)}, u32[]{:S(2)}, u32[]{:S(2)}) collective-permute-start(bf16[40,768]{1,0:T(8,128)(2,1)S(1)} %get-tuple-element.13), channel_id=1, source_target_pairs={{0,24},{4,28},{8,16},{12,20},{16,8},{20,12},{24,0},{28,4},{1,25},{... | collective-permute-start | bytes 184328 | tf_op jit(solution)/shard_map/ppermute | solution.py:64
  103.6 6.3 %collective-permute-start.25 = (bf16[40,768]{1,0:T(8,128)(2,1)S(1)}, bf16[40,768]{1,0:T(8,128)(2,1)S(1)}, u32[]{:S(2)}, u32[]{:S(2)}) collective-permute-start(bf16[40,768]{1,0:T(8,128)(2,1)S(1)} %get-tuple-element.7), channel_id=1, source_target_pairs={{0,28},{4,24},{8,20},{12,16},{16,12},{20,8},{24,4},{28,0},{1,29},{... | collective-permute-start | bytes 184328 | tf_op jit(solution)/shard_map/ppermute | solution.py:64
  (9 other events, 111.2 us)

commit v6 on v5

--- a/solution.py
+++ b/solution.py
@@ -76,6 +76,44 @@
 
 
 def reduce_scatter_tree(block_fn, axis, n):
+    orders = bit_orders(n)
+    helds = [{d: block_fn(d, h) for d in range(n)} for h in range(len(orders))]
+    for stage in range(len(orders[0])):
+        payloads, keeps = [], []
+        for h, order in enumerate(orders):
+            bit = order[stage]
+            send = sorted(d for d in helds[h] if d & bit)
+            keeps.append(sorted(d for d in helds[h] if not d & bit))
+            payloads.append(jnp.concatenate([helds[h][d].astype(jnp.bfloat16) for d in send], axis=0))
+        payloads = lax.optimization_barrier(payloads)
+        for h, order in enumerate(orders):
+            bit = order[stage]
+            got = lax.ppermute(payloads[h], axis, [(i, i ^ bit) for i in range(n)])
+            rows = helds[h][keeps[h][0]].shape[0]
+            helds[h] = {
+                d: helds[h][d].astype(jnp.float32) + got[i * rows:(i + 1) * rows].astype(jnp.float32)
+                for i, d in enumerate(keeps[h])
+            }
+    return [held[0] for held in helds]
+
+
+def all_gather_tree(halves, axis, n):
+    orders = bit_orders(n)
+    helds = [{0: halves[h]} for h in range(len(orders))]
+    for stage in range(len(orders[0])):
+        haves = [sorted(held) for held in helds]
+        payloads = [jnp.concatenate([helds[h][d] for d in haves[h]], axis=0) for h in range(len(orders))]
+        payloads = lax.optimization_barrier(payloads)
+        for h, order in enumerate(orders):
+            bit = order[stage]
+            got = lax.ppermute(payloads[h], axis, [(i, i ^ bit) for i in range(n)])
+            rows = halves[h].shape[0]
+            for i, d in enumerate(haves[h]):
+                helds[h][d ^ bit] = got[i * rows:(i + 1) * rows]
+    return helds
+
+
+def reduce_scatter_free(block_fn, axis, n):
     outs = []
     for h, order in enumerate(bit_orders(n)):
         held = {d: block_fn(d, h) for d in range(n)}
@@ -93,7 +131,7 @@
     return outs
 
 
-def all_gather_tree(halves, axis, n):
+def all_gather_free(halves, axis, n):
     outs = []
     for h, order in enumerate(bit_orders(n)):
         held = {0: halves[h]}
@@ -133,12 +171,14 @@
         return jnp.dot(context, columns, preferred_element_type=jnp.float32).astype(jnp.bfloat16)
 
     if tree:
+        head_cols = lax.dot_general(
+            out_proj, context, (((0,), (1,)), ((), ())), preferred_element_type=jnp.float32
+        ).astype(jnp.bfloat16)
+
         def head_half(d, h):
-            start = (me_t ^ d) * width + h * half
-            columns = lax.dynamic_slice_in_dim(out_proj, start, half, axis=1)
-            return jnp.dot(context, columns, preferred_element_type=jnp.float32).astype(jnp.bfloat16)
-
-        summed = jnp.concatenate(reduce_scatter_tree(head_half, "tensor", tensor_count), axis=1)
+            return lax.dynamic_slice_in_dim(head_cols, (me_t ^ d) * width + h * half, half, axis=0)
+
+        summed = jnp.concatenate(reduce_scatter_tree(head_half, "tensor", tensor_count), axis=0).T
         summed = summed + residual_in.astype(jnp.float32)
     else:
         received = [
@@ -174,7 +214,7 @@
         arrived = arrived.reshape(chunk_slots, width)
         if tree:
             pre_act = None
-            held = all_gather_tree([arrived[:, :half], arrived[:, half:]], "tensor", tensor_count)
+            held = all_gather_free([arrived[:, :half], arrived[:, half:]], "tensor", tensor_count)
             for h in range(2):
                 for d in range(tensor_count):
                     rows_w = lax.dynamic_slice_in_dim(projection, (me_t ^ d) * width + h * half, half, axis=0)
@@ -194,7 +234,7 @@
                 ).astype(jnp.bfloat16)
 
             critic_grad = jnp.concatenate(
-                reduce_scatter_tree(back_half, "tensor", tensor_count), axis=1
+                reduce_scatter_free(back_half, "tensor", tensor_count), axis=1
             ).astype(jnp.bfloat16)
         else:
             back = [

time: 112 us -> 109 us (0.973)
  matrix products: 22.7 us -> 15.1 us
  waiting for transfers between devices: 50 us -> 53.1 us
    dot_general x8 -> x1, matrix products: 11.5 us -> 3.83 us  [shards(): lax.dot_general(out_proj, context, (((0,), (1,)), ((), ())), preferred_el...]
    ppermute x12, waiting for transfers between devices: 37.7 us -> 40.7 us  [the longest x4 15.3 us: all_gather_free(): got = lax.ppermute(payload, axis, [(i, i ^ bit) for i in range(n)])]
  transfers between devices with their start and end apart: 26 -> 26, of which waited for: 15 -> 12; matrix products, arithmetic and copies ran while one was open for 14% -> 7% of each run, Pallas kernels for 0% -> 0%
where the time goes in v6:
time: 109 us
  waiting for transfers between devices  53.1 us (49%)
  starting transfers between devices  31.5 us (29%)
  matrix products  15.1 us (14%)
  other arithmetic  3.92 us (4%)
  local copies, waits for them, and re-layouts  3.74 us (3%)
  between operations  1.17 us (1%)
    ppermute x14, starting transfers between devices, swap_blocks(): got.append(lax.ppermute(chunk, axis, pairs_for(s, n)))  17.5 us
    ppermute x4, waiting for transfers between devices, all_gather_free(): got = lax.ppermute(payload, axis, [(i, i ^ bit) for i in range(n)])  15.3 us
    ppermute x4, waiting for transfers between devices, reduce_scatter_free(): got = lax.ppermute(payload, axis, [(i, i ^ bit) for i in range(n)])  13.5 us
    ppermute x14, waiting for transfers between devices, swap_blocks(): got.append(lax.ppermute(chunk, axis, pairs_for(s, n)))  12.3 us
    ppermute x4, waiting for transfers between devices, reduce_scatter_tree(): got = lax.ppermute(payloads[h], axis, [(i, i ^ bit) for i in range(n)])  11.9 us
    ppermute x4, starting transfers between devices, reduce_scatter_tree(): got = lax.ppermute(payloads[h], axis, [(i, i ^ bit) for i in range(n)])  6.59 us
    dot_general x8, matrix products, shards(): term = jnp.dot(held[h][d], rows_w, preferred_element_type=jnp.float32)  6.14 us
    ppermute x4, starting transfers between devices, reduce_scatter_free(): got = lax.ppermute(payload, axis, [(i, i ^ bit) for i in range(n)])  4.46 us
  transfers between devices with their start and end apart: 26, of which 12 were waited for; matrix products, arithmetic and copies ran while one was open for 7% of the time, Pallas kernels for 0%

profile of v6, /device:TPU:0, one launch (start us, length us, event | category | flops | bytes accessed | tf_op | source)
XLA Modules:
  0.0 108.5 jit_solution(12614419014814111543)
XLA Ops:
  1.6 3.8 %convolution_convert_fusion = bf16[3072,256]{1,0:T(8,128)(2,1)S(1)} fusion(bf16[768,3072]{1,0:T(8,128)(2,1)} %param.11, bf16[256,768]{1,0:T(8,128)(2,1)S(1)} %copy-done), kind=kOutput, calls=%fused_computation.2 | convolution fusion | flops 1208745984 | bytes 6684672 | tf_op jit(solution)/shard_map/dot_general | solution.py:174
  6.5 2.9 %collective-permute-start = (bf16[768,256]{1,0:T(8,128)(2,1)}, bf16[768,256]{1,0:T(8,128)(2,1)S(1)}, u32[]{:S(2)}, u32[]{:S(2)}) collective-permute-start(bf16[768,256]{1,0:T(8,128)(2,1)} %get-tuple-element.7), channel_id=1, source_target_pairs={{0,1},{1,0},{2,3},{3,2},{4,5},{5,4},{6,7},{7,6},{8,9},{9,8},{10,11... | collective-permute-start | bytes 1179656 | tf_op jit(solution)/shard_map/ppermute | solution.py:91
  9.4 1.5 %collective-permute-start.1 = (bf16[768,256]{1,0:T(8,128)(2,1)}, bf16[768,256]{1,0:T(8,128)(2,1)S(1)}, u32[]{:S(2)}, u32[]{:S(2)}) collective-permute-start(bf16[768,256]{1,0:T(8,128)(2,1)} %get-tuple-element.8), channel_id=1, source_target_pairs={{0,2},{1,3},{2,0},{3,1},{4,6},{5,7},{6,4},{7,5},{8,10},{9,11},{10,... | collective-permute-start | bytes 1179656 | tf_op jit(solution)/shard_map/ppermute | solution.py:91
  13.4 5.4 %collective-permute-done = bf16[768,256]{1,0:T(8,128)(2,1)S(1)} collective-permute-done((bf16[768,256]{1,0:T(8,128)(2,1)}, bf16[768,256]{1,0:T(8,128)(2,1)S(1)}, u32[]{:S(2)}, u32[]{:S(2)}) %collective-permute-start) | collective-permute-done | bytes 393248 | tf_op jit(solution)/shard_map/ppermute | solution.py:91
  18.7 1.5 %collective-permute-done.1 = bf16[768,256]{1,0:T(8,128)(2,1)S(1)} collective-permute-done((bf16[768,256]{1,0:T(8,128)(2,1)}, bf16[768,256]{1,0:T(8,128)(2,1)S(1)}, u32[]{:S(2)}, u32[]{:S(2)}) %collective-permute-start.1) | collective-permute-done | bytes 393248 | tf_op jit(solution)/shard_map/ppermute | solution.py:91
  20.3 1.6 %collective-permute-start.2 = (bf16[384,256]{1,0:T(8,128)(2,1)S(1)}, bf16[384,256]{1,0:T(8,128)(2,1)S(1)}, u32[]{:S(2)}, u32[]{:S(2)}) collective-permute-start(bf16[384,256]{1,0:T(8,128)(2,1)S(1)} %get-tuple-element.9), channel_id=1, source_target_pairs={{0,2},{1,3},{2,0},{3,1},{4,6},{5,7},{6,4},{7,5},{8,10},{9,11},{10,... | collective-permute-start | bytes 589832 | tf_op jit(solution)/shard_map/ppermute | solution.py:91
  22.4 3.6 %collective-permute-done.2 = bf16[384,256]{1,0:T(8,128)(2,1)S(1)} collective-permute-done((bf16[384,256]{1,0:T(8,128)(2,1)S(1)}, bf16[384,256]{1,0:T(8,128)(2,1)S(1)}, u32[]{:S(2)}, u32[]{:S(2)}) %collective-permute-start.2) | collective-permute-done | bytes 196640 | tf_op jit(solution)/shard_map/ppermute | solution.py:91
  26.0 1.5 %collective-permute-done.3 = bf16[384,256]{1,0:T(8,128)(2,1)S(1)} collective-permute-done((bf16[384,256]{1,0:T(8,128)(2,1)S(1)}, bf16[384,256]{1,0:T(8,128)(2,1)S(1)}, u32[]{:S(2)}, u32[]{:S(2)}) %collective-permute-start.3) | collective-permute-done | bytes 196640 | tf_op jit(solution)/shard_map/ppermute | solution.py:91
  29.4 1.6 %collective-permute-start.5 = (bf16[40,768]{1,0:T(8,128)(2,1)S(1)}, bf16[40,768]{1,0:T(8,128)(2,1)S(1)}, u32[]{:S(2)}, u32[]{:S(2)}) collective-permute-start(bf16[40,768]{1,0:T(8,128)(2,1)S(1)} %get-tuple-element.38), channel_id=1, source_target_pairs={{0,8},{4,12},{8,0},{12,4},{16,24},{20,28},{24,16},{28,20},{1,9},{5... | collective-permute-start | bytes 184328 | tf_op jit(solution)/shard_map/ppermute | solution.py:64
  31.2 2.6 %collective-permute-start.7 = (bf16[40,768]{1,0:T(8,128)(2,1)S(1)}, bf16[40,768]{1,0:T(8,128)(2,1)S(1)}, u32[]{:S(2)}, u32[]{:S(2)}) collective-permute-start(bf16[40,768]{1,0:T(8,128)(2,1)S(1)} %get-tuple-element.36), channel_id=1, source_target_pairs={{0,16},{4,20},{8,24},{12,28},{16,0},{20,4},{24,8},{28,12},{1,17},{... | collective-permute-start | bytes 184328 | tf_op jit(solution)/shard_map/ppermute | solution.py:64
  33.8 3.6 %collective-permute-start.9 = (bf16[40,768]{1,0:T(8,128)(2,1)S(1)}, bf16[40,768]{1,0:T(8,128)(2,1)S(1)}, u32[]{:S(2)}, u32[]{:S(2)}) collective-permute-start(bf16[40,768]{1,0:T(8,128)(2,1)S(1)} %get-tuple-element.34), channel_id=1, source_target_pairs={{0,24},{4,28},{8,16},{12,20},{16,8},{20,12},{24,0},{28,4},{1,25},{... | collective-permute-start | bytes 184328 | tf_op jit(solution)/shard_map/ppermute | solution.py:64
  37.6 6.2 %collective-permute-done.8 = bf16[40,768]{1,0:T(8,128)(2,1)S(1)} collective-permute-done((bf16[40,768]{1,0:T(8,128)(2,1)S(1)}, bf16[40,768]{1,0:T(8,128)(2,1)S(1)}, u32[]{:S(2)}, u32[]{:S(2)}) %collective-permute-start.8) | collective-permute-done | bytes 61472 | tf_op jit(solution)/shard_map/ppermute | solution.py:64
  44.7 1.6 %fusion.37 = f32[320,768]{1,0:T(8,128)S(1)} fusion(bf16[1,3072,768]{2,1,0:T(8,128)(2,1)} %param.14, s32[]{:T(128)S(6)} %select_n.84, bf16[320,768]{1,0:T(8,128)(2,1)S(1)} %bitcast.138), kind=kOutput, calls=%fused_computation.72 | convolution fusion | flops 188743680 | bytes 1818628 | tf_op jit(solution)/shard_map/dot_general | solution.py:221
  47.5 1.5 %fusion.27 = f32[320,768]{1,0:T(8,128)S(1)} fusion(bf16[1,3072,768]{2,1,0:T(8,128)(2,1)} %param.14, s32[]{:T(128)S(6)} %select_n.91, bf16[320,768]{1,0:T(8,128)(2,1)S(1)} %bitcast.139), kind=kOutput, calls=%fused_computation.62 | convolution fusion | flops 188743680 | bytes 1818628 | tf_op jit(solution)/shard_map/dot_general | solution.py:221
  48.9 5.4 %collective-permute-done.11 = bf16[320,384]{1,0:T(8,128)(2,1)S(1)} collective-permute-done((bf16[320,384]{1,0:T(8,128)(2,1)S(1)}, bf16[320,384]{1,0:T(8,128)(2,1)S(1)}, u32[]{:S(2)}, u32[]{:S(2)}) %collective-permute-start.11) | collective-permute-done | bytes 245792 | tf_op jit(solution)/shard_map/ppermute | solution.py:141
  57.1 9.8 %collective-permute-done.12 = bf16[640,384]{1,0:T(8,128)(2,1)S(1)} collective-permute-done((bf16[640,384]{1,0:T(8,128)(2,1)S(1)}, bf16[640,384]{1,0:T(8,128)(2,1)S(1)}, u32[]{:S(2)}, u32[]{:S(2)}) %collective-permute-start.12) | collective-permute-done | bytes 491552 | tf_op jit(solution)/shard_map/ppermute | solution.py:141
  74.0 8.5 %collective-permute-done.15 = bf16[640,384]{1,0:T(8,128)(2,1)S(1)} collective-permute-done((bf16[640,384]{1,0:T(8,128)(2,1)S(1)}, bf16[640,384]{1,0:T(8,128)(2,1)S(1)}, u32[]{:S(2)}, u32[]{:S(2)}) %collective-permute-start.15) | collective-permute-done | bytes 491552 | tf_op jit(solution)/shard_map/ppermute | solution.py:124
  83.0 1.2 %collective-permute-start.16 = (bf16[320,384]{1,0:T(8,128)(2,1)S(1)}, bf16[320,384]{1,0:T(8,128)(2,1)S(1)}, u32[]{:S(2)}, u32[]{:S(2)}) collective-permute-start(bf16[320,384]{1,0:T(8,128)(2,1)S(1)} %add_convert_fusion.3), channel_id=1, source_target_pairs={{0,2},{1,3},{2,0},{3,1},{4,6},{5,7},{6,4},{7,5},{8,10},{9,11},{10,... | collective-permute-start | bytes 737288 | tf_op jit(solution)/shard_map/ppermute | solution.py:124
  85.8 3.4 %collective-permute-done.16 = bf16[320,384]{1,0:T(8,128)(2,1)S(1)} collective-permute-done((bf16[320,384]{1,0:T(8,128)(2,1)S(1)}, bf16[320,384]{1,0:T(8,128)(2,1)S(1)}, u32[]{:S(2)}, u32[]{:S(2)}) %collective-permute-start.16) | collective-permute-done | bytes 245792 | tf_op jit(solution)/shard_map/ppermute | solution.py:124
  89.3 1.6 %collective-permute-done.18 = bf16[320,384]{1,0:T(8,128)(2,1)S(1)} collective-permute-done((bf16[320,384]{1,0:T(8,128)(2,1)S(1)}, bf16[320,384]{1,0:T(8,128)(2,1)S(1)}, u32[]{:S(2)}, u32[]{:S(2)}) %collective-permute-start.18) | collective-permute-done | bytes 245792 | tf_op jit(solution)/shard_map/ppermute | solution.py:124
  91.2 4.3 %collective-permute-start.23 = (bf16[40,768]{1,0:T(8,128)(2,1)S(1)}, bf16[40,768]{1,0:T(8,128)(2,1)S(1)}, u32[]{:S(2)}, u32[]{:S(2)}) collective-permute-start(bf16[40,768]{1,0:T(8,128)(2,1)S(1)} %get-tuple-element.30), channel_id=1, source_target_pairs={{0,20},{4,16},{8,28},{12,24},{16,4},{20,0},{24,12},{28,8},{1,21},{... | collective-permute-start | bytes 184328 | tf_op jit(solution)/shard_map/ppermute | solution.py:64
  95.5 1.4 %collective-permute-start.21 = (bf16[40,768]{1,0:T(8,128)(2,1)S(1)}, bf16[40,768]{1,0:T(8,128)(2,1)S(1)}, u32[]{:S(2)}, u32[]{:S(2)}) collective-permute-start(bf16[40,768]{1,0:T(8,128)(2,1)S(1)} %get-tuple-element.27), channel_id=1, source_target_pairs={{0,12},{4,8},{8,4},{12,0},{16,28},{20,24},{24,20},{28,16},{1,13},{... | collective-permute-start | bytes 184328 | tf_op jit(solution)/shard_map/ppermute | solution.py:64
  97.4 2.5 %collective-permute-start.24 = (bf16[40,768]{1,0:T(8,128)(2,1)S(1)}, bf16[40,768]{1,0:T(8,128)(2,1)S(1)}, u32[]{:S(2)}, u32[]{:S(2)}) collective-permute-start(bf16[40,768]{1,0:T(8,128)(2,1)S(1)} %get-tuple-element.29), channel_id=1, source_target_pairs={{0,24},{4,28},{8,16},{12,20},{16,8},{20,12},{24,0},{28,4},{1,25},{... | collective-permute-start | bytes 184328 | tf_op jit(solution)/shard_map/ppermute | solution.py:64
  100.9 5.6 %collective-permute-done.22 = bf16[40,768]{1,0:T(8,128)(2,1)S(1)} collective-permute-done((bf16[40,768]{1,0:T(8,128)(2,1)S(1)}, bf16[40,768]{1,0:T(8,128)(2,1)S(1)}, u32[]{:S(2)}, u32[]{:S(2)}) %collective-permute-start.22) | collective-permute-done | bytes 61472 | tf_op jit(solution)/shard_map/ppermute | solution.py:64
  (119 shorter events, 24.6 us)
Async XLA Ops:
  6.5 12.3 %collective-permute-start = (bf16[768,256]{1,0:T(8,128)(2,1)}, bf16[768,256]{1,0:T(8,128)(2,1)S(1)}, u32[]{:S(2)}, u32[]{:S(2)}) collective-permute-start(bf16[768,256]{1,0:T(8,128)(2,1)} %get-tuple-element.7), channel_id=1, source_target_pairs={{0,1},{1,0},{2,3},{3,2},{4,5},{5,4},{6,7},{7,6},{8,9},{9,8},{10,11... | collective-permute-start | bytes 1179656 | tf_op jit(solution)/shard_map/ppermute | solution.py:91
  9.4 10.8 %collective-permute-start.1 = (bf16[768,256]{1,0:T(8,128)(2,1)}, bf16[768,256]{1,0:T(8,128)(2,1)S(1)}, u32[]{:S(2)}, u32[]{:S(2)}) collective-permute-start(bf16[768,256]{1,0:T(8,128)(2,1)} %get-tuple-element.8), channel_id=1, source_target_pairs={{0,2},{1,3},{2,0},{3,1},{4,6},{5,7},{6,4},{7,5},{8,10},{9,11},{10,... | collective-permute-start | bytes 1179656 | tf_op jit(solution)/shard_map/ppermute | solution.py:91
  20.3 5.7 %collective-permute-start.2 = (bf16[384,256]{1,0:T(8,128)(2,1)S(1)}, bf16[384,256]{1,0:T(8,128)(2,1)S(1)}, u32[]{:S(2)}, u32[]{:S(2)}) collective-permute-start(bf16[384,256]{1,0:T(8,128)(2,1)S(1)} %get-tuple-element.9), channel_id=1, source_target_pairs={{0,2},{1,3},{2,0},{3,1},{4,6},{5,7},{6,4},{7,5},{8,10},{9,11},{10,... | collective-permute-start | bytes 589832 | tf_op jit(solution)/shard_map/ppermute | solution.py:91
  21.9 5.7 %collective-permute-start.3 = (bf16[384,256]{1,0:T(8,128)(2,1)S(1)}, bf16[384,256]{1,0:T(8,128)(2,1)S(1)}, u32[]{:S(2)}, u32[]{:S(2)}) collective-permute-start(bf16[384,256]{1,0:T(8,128)(2,1)S(1)} %get-tuple-element.10), channel_id=1, source_target_pairs={{0,1},{1,0},{2,3},{3,2},{4,5},{5,4},{6,7},{7,6},{8,9},{9,8},{10,11... | collective-permute-start | bytes 589832 | tf_op jit(solution)/shard_map/ppermute | solution.py:91
  28.4 5.5 %collective-permute-start.4 = (bf16[40,768]{1,0:T(8,128)(2,1)S(1)}, bf16[40,768]{1,0:T(8,128)(2,1)S(1)}, u32[]{:S(2)}, u32[]{:S(2)}) collective-permute-start(bf16[40,768]{1,0:T(8,128)(2,1)S(1)} %get-tuple-element.39), channel_id=1, source_target_pairs={{0,4},{4,0},{8,12},{12,8},{16,20},{20,16},{24,28},{28,24},{1,5},{5... | collective-permute-start | bytes 184328 | tf_op jit(solution)/shard_map/ppermute | solution.py:64
  29.4 8.0 %collective-permute-start.5 = (bf16[40,768]{1,0:T(8,128)(2,1)S(1)}, bf16[40,768]{1,0:T(8,128)(2,1)S(1)}, u32[]{:S(2)}, u32[]{:S(2)}) collective-permute-start(bf16[40,768]{1,0:T(8,128)(2,1)S(1)} %get-tuple-element.38), channel_id=1, source_target_pairs={{0,8},{4,12},{8,0},{12,4},{16,24},{20,28},{24,16},{28,20},{1,9},{5... | collective-permute-start | bytes 184328 | tf_op jit(solution)/shard_map/ppermute | solution.py:64
  31.0 6.6 %collective-permute-start.6 = (bf16[40,768]{1,0:T(8,128)(2,1)S(1)}, bf16[40,768]{1,0:T(8,128)(2,1)S(1)}, u32[]{:S(2)}, u32[]{:S(2)}) collective-permute-start(bf16[40,768]{1,0:T(8,128)(2,1)S(1)} %get-tuple-element.37), channel_id=1, source_target_pairs={{0,12},{4,8},{8,4},{12,0},{16,28},{20,24},{24,20},{28,16},{1,13},{... | collective-permute-start | bytes 184328 | tf_op jit(solution)/shard_map/ppermute | solution.py:64
  31.2 6.4 %collective-permute-start.7 = (bf16[40,768]{1,0:T(8,128)(2,1)S(1)}, bf16[40,768]{1,0:T(8,128)(2,1)S(1)}, u32[]{:S(2)}, u32[]{:S(2)}) collective-permute-start(bf16[40,768]{1,0:T(8,128)(2,1)S(1)} %get-tuple-element.36), channel_id=1, source_target_pairs={{0,16},{4,20},{8,24},{12,28},{16,0},{20,4},{24,8},{28,12},{1,17},{... | collective-permute-start | bytes 184328 | tf_op jit(solution)/shard_map/ppermute | solution.py:64
  33.8 10.0 %collective-permute-start.8 = (bf16[40,768]{1,0:T(8,128)(2,1)S(1)}, bf16[40,768]{1,0:T(8,128)(2,1)S(1)}, u32[]{:S(2)}, u32[]{:S(2)}) collective-permute-start(bf16[40,768]{1,0:T(8,128)(2,1)S(1)} %get-tuple-element.35), channel_id=1, source_target_pairs={{0,20},{4,16},{8,28},{12,24},{16,4},{20,0},{24,12},{28,8},{1,21},{... | collective-permute-start | bytes 184328 | tf_op jit(solution)/shard_map/ppermute | solution.py:64
  33.8 10.0 %collective-permute-start.9 = (bf16[40,768]{1,0:T(8,128)(2,1)S(1)}, bf16[40,768]{1,0:T(8,128)(2,1)S(1)}, u32[]{:S(2)}, u32[]{:S(2)}) collective-permute-start(bf16[40,768]{1,0:T(8,128)(2,1)S(1)} %get-tuple-element.34), channel_id=1, source_target_pairs={{0,24},{4,28},{8,16},{12,20},{16,8},{20,12},{24,0},{28,4},{1,25},{... | collective-permute-start | bytes 184328 | tf_op jit(solution)/shard_map/ppermute | solution.py:64
  37.4 6.5 %collective-permute-start.10 = (bf16[40,768]{1,0:T(8,128)(2,1)S(1)}, bf16[40,768]{1,0:T(8,128)(2,1)S(1)}, u32[]{:S(2)}, u32[]{:S(2)}) collective-permute-start(bf16[40,768]{1,0:T(8,128)(2,1)S(1)} %get-tuple-element.33), channel_id=1, source_target_pairs={{0,28},{4,24},{8,20},{12,16},{16,12},{20,8},{24,4},{28,0},{1,29},{... | collective-permute-start | bytes 184328 | tf_op jit(solution)/shard_map/ppermute | solution.py:64
  46.3 8.0 %collective-permute-start.11 = (bf16[320,384]{1,0:T(8,128)(2,1)S(1)}, bf16[320,384]{1,0:T(8,128)(2,1)S(1)}, u32[]{:S(2)}, u32[]{:S(2)}) collective-permute-start(bf16[320,384]{1,0:T(8,128)(2,1)S(1)} %get-tuple-element.31), channel_id=1, source_target_pairs={{0,1},{1,0},{2,3},{3,2},{4,5},{5,4},{6,7},{7,6},{8,9},{9,8},{10,11... | collective-permute-start | bytes 737288 | tf_op jit(solution)/shard_map/ppermute | solution.py:141
  46.9 8.1 %collective-permute-start.13 = (bf16[320,384]{1,0:T(8,128)(2,1)S(1)}, bf16[320,384]{1,0:T(8,128)(2,1)S(1)}, u32[]{:S(2)}, u32[]{:S(2)}) collective-permute-start(bf16[320,384]{1,0:T(8,128)(2,1)S(1)} %get-tuple-element.32), channel_id=1, source_target_pairs={{0,2},{1,3},{2,0},{3,1},{4,6},{5,7},{6,4},{7,5},{8,10},{9,11},{10,... | collective-permute-start | bytes 737288 | tf_op jit(solution)/shard_map/ppermute | solution.py:141
  54.4 12.5 %collective-permute-start.12 = (bf16[640,384]{1,0:T(8,128)(2,1)S(1)}, bf16[640,384]{1,0:T(8,128)(2,1)S(1)}, u32[]{:S(2)}, u32[]{:S(2)}) collective-permute-start(bf16[640,384]{1,0:T(8,128)(2,1)S(1)} %pad_maximum_fusion), channel_id=1, source_target_pairs={{0,2},{1,3},{2,0},{3,1},{4,6},{5,7},{6,4},{7,5},{8,10},{9,11},{10,... | collective-permute-start | bytes 1474568 | tf_op jit(solution)/shard_map/ppermute | solution.py:141
  55.1 12.3 %collective-permute-start.14 = (bf16[640,384]{1,0:T(8,128)(2,1)S(1)}, bf16[640,384]{1,0:T(8,128)(2,1)S(1)}, u32[]{:S(2)}, u32[]{:S(2)}) collective-permute-start(bf16[640,384]{1,0:T(8,128)(2,1)S(1)} %pad_maximum_fusion.1), channel_id=1, source_target_pairs={{0,1},{1,0},{2,3},{3,2},{4,5},{5,4},{6,7},{7,6},{8,9},{9,8},{10,11... | collective-permute-start | bytes 1474568 | tf_op jit(solution)/shard_map/ppermute | solution.py:141
  71.0 11.6 %collective-permute-start.15 = (bf16[640,384]{1,0:T(8,128)(2,1)S(1)}, bf16[640,384]{1,0:T(8,128)(2,1)S(1)}, u32[]{:S(2)}, u32[]{:S(2)}) collective-permute-start(bf16[640,384]{1,0:T(8,128)(2,1)S(1)} %pad_maximum_fusion.2), channel_id=1, source_target_pairs={{0,1},{1,0},{2,3},{3,2},{4,5},{5,4},{6,7},{7,6},{8,9},{9,8},{10,11... | collective-permute-start | bytes 1474568 | tf_op jit(solution)/shard_map/ppermute | solution.py:124
  72.1 12.1 %collective-permute-start.17 = (bf16[640,384]{1,0:T(8,128)(2,1)S(1)}, bf16[640,384]{1,0:T(8,128)(2,1)S(1)}, u32[]{:S(2)}, u32[]{:S(2)}) collective-permute-start(bf16[640,384]{1,0:T(8,128)(2,1)S(1)} %pad_maximum_fusion.3), channel_id=1, source_target_pairs={{0,2},{1,3},{2,0},{3,1},{4,6},{5,7},{6,4},{7,5},{8,10},{9,11},{10,... | collective-permute-start | bytes 1474568 | tf_op jit(solution)/shard_map/ppermute | solution.py:124
  83.0 6.3 %collective-permute-start.16 = (bf16[320,384]{1,0:T(8,128)(2,1)S(1)}, bf16[320,384]{1,0:T(8,128)(2,1)S(1)}, u32[]{:S(2)}, u32[]{:S(2)}) collective-permute-start(bf16[320,384]{1,0:T(8,128)(2,1)S(1)} %add_convert_fusion.3), channel_id=1, source_target_pairs={{0,2},{1,3},{2,0},{3,1},{4,6},{5,7},{6,4},{7,5},{8,10},{9,11},{10,... | collective-permute-start | bytes 737288 | tf_op jit(solution)/shard_map/ppermute | solution.py:124
  84.7 6.3 %collective-permute-start.18 = (bf16[320,384]{1,0:T(8,128)(2,1)S(1)}, bf16[320,384]{1,0:T(8,128)(2,1)S(1)}, u32[]{:S(2)}, u32[]{:S(2)}) collective-permute-start(bf16[320,384]{1,0:T(8,128)(2,1)S(1)} %add_convert_fusion.1), channel_id=1, source_target_pairs={{0,1},{1,0},{2,3},{3,2},{4,5},{5,4},{6,7},{7,6},{8,9},{9,8},{10,11... | collective-permute-start | bytes 737288 | tf_op jit(solution)/shard_map/ppermute | solution.py:124
  91.1 6.3 %collective-permute-start.19 = (bf16[40,768]{1,0:T(8,128)(2,1)S(1)}, bf16[40,768]{1,0:T(8,128)(2,1)S(1)}, u32[]{:S(2)}, u32[]{:S(2)}) collective-permute-start(bf16[40,768]{1,0:T(8,128)(2,1)S(1)} %get-tuple-element.25), channel_id=1, source_target_pairs={{0,4},{4,0},{8,12},{12,8},{16,20},{20,16},{24,28},{28,24},{1,5},{5... | collective-permute-start | bytes 184328 | tf_op jit(solution)/shard_map/ppermute | solution.py:64
  91.2 15.4 %collective-permute-start.23 = (bf16[40,768]{1,0:T(8,128)(2,1)S(1)}, bf16[40,768]{1,0:T(8,128)(2,1)S(1)}, u32[]{:S(2)}, u32[]{:S(2)}) collective-permute-start(bf16[40,768]{1,0:T(8,128)(2,1)S(1)} %get-tuple-element.30), channel_id=1, source_target_pairs={{0,20},{4,16},{8,28},{12,24},{16,4},{20,0},{24,12},{28,8},{1,21},{... | collective-permute-start | bytes 184328 | tf_op jit(solution)/shard_map/ppermute | solution.py:64
  96.9 9.7 %collective-permute-start.22 = (bf16[40,768]{1,0:T(8,128)(2,1)S(1)}, bf16[40,768]{1,0:T(8,128)(2,1)S(1)}, u32[]{:S(2)}, u32[]{:S(2)}) collective-permute-start(bf16[40,768]{1,0:T(8,128)(2,1)S(1)} %get-tuple-element.28), channel_id=1, source_target_pairs={{0,16},{4,20},{8,24},{12,28},{16,0},{20,4},{24,8},{28,12},{1,17},{... | collective-permute-start | bytes 184328 | tf_op jit(solution)/shard_map/ppermute | solution.py:64
  97.4 9.2 %collective-permute-start.24 = (bf16[40,768]{1,0:T(8,128)(2,1)S(1)}, bf16[40,768]{1,0:T(8,128)(2,1)S(1)}, u32[]{:S(2)}, u32[]{:S(2)}) collective-permute-start(bf16[40,768]{1,0:T(8,128)(2,1)S(1)} %get-tuple-element.29), channel_id=1, source_target_pairs={{0,24},{4,28},{8,16},{12,20},{16,8},{20,12},{24,0},{28,4},{1,25},{... | collective-permute-start | bytes 184328 | tf_op jit(solution)/shard_map/ppermute | solution.py:64
  100.3 6.3 %collective-permute-start.25 = (bf16[40,768]{1,0:T(8,128)(2,1)S(1)}, bf16[40,768]{1,0:T(8,128)(2,1)S(1)}, u32[]{:S(2)}, u32[]{:S(2)}) collective-permute-start(bf16[40,768]{1,0:T(8,128)(2,1)S(1)} %get-tuple-element.23), channel_id=1, source_target_pairs={{0,28},{4,24},{8,20},{12,16},{16,12},{20,8},{24,4},{28,0},{1,29},{... | collective-permute-start | bytes 184328 | tf_op jit(solution)/shard_map/ppermute | solution.py:64
  (13 other events, 180.8 us)

commit v7 on v6

--- a/solution.py
+++ b/solution.py
@@ -146,6 +146,30 @@
     return outs
 
 
+def dispatch_rows(blocks, axis):
+    n = blocks.shape[0]
+    if n > 16 or not is_pow2(n):
+        arrived = lax.all_to_all(blocks, axis, 0, 0, tiled=True)
+        return [arrived[p] for p in range(n)]
+    me = lax.axis_index(axis)
+    got = [lax.dynamic_index_in_dim(blocks, me, 0, keepdims=False)]
+    for s in range(1, n):
+        chunk = lax.dynamic_index_in_dim(blocks, me ^ s, 0, keepdims=False)
+        got.append(lax.ppermute(chunk, axis, [(i, i ^ s) for i in range(n)]))
+    return got
+
+
+def collect_rows(parts, axis):
+    n = len(parts)
+    if n > 16 or not is_pow2(n):
+        return lax.all_to_all(jnp.stack(parts), axis, 0, 0, tiled=True)
+    me = lax.axis_index(axis)
+    got = [parts[0]] + [
+        lax.ppermute(parts[s], axis, [(i, i ^ s) for i in range(n)]) for s in range(1, n)
+    ]
+    return jnp.take(jnp.stack(got), lax.iota(jnp.int32, n) ^ me, axis=0)
+
+
 SLOT_CHUNKS = 1
 
 
@@ -200,6 +224,43 @@
     rank_in = jnp.sum(earlier * dest_hot, axis=1)
     slot_ids = lax.iota(jnp.int32, chunk_slots)
     head_row = member_head[0][None, :]
+
+    if tree:
+        rank_ok = rank_in < capacity
+        slot_of = destination * capacity + rank_in
+        placing = ((slot_of[:, None] == lax.iota(jnp.int32, group_count * capacity)[None, :])
+                   & rank_ok[:, None]).astype(jnp.bfloat16)
+        outgoing = lax.dot_general(
+            placing, generated, (((0,), (0,)), ((), ())), preferred_element_type=jnp.float32
+        ).astype(jnp.bfloat16)
+        arrived = dispatch_rows(outgoing.reshape(group_count, capacity, width), "dp")
+        wave = max(1, group_count // 2)
+        waves = [arrived[:wave], arrived[wave:]] if group_count > 1 else [arrived]
+        grads = []
+        for blocks in waves:
+            rows_in = jnp.concatenate(blocks, axis=0)
+            held = all_gather_free([rows_in[:, :half], rows_in[:, half:]], "tensor", tensor_count)
+            pre_act = None
+            for h in range(2):
+                for d in range(tensor_count):
+                    rows_w = lax.dynamic_slice_in_dim(projection, (me_t ^ d) * width + h * half, half, axis=0)
+                    term = jnp.dot(held[h][d], rows_w, preferred_element_type=jnp.float32)
+                    pre_act = term if pre_act is None else pre_act + term
+            pre_grad = (-slope_times(pre_act, jnp.broadcast_to(head_row, pre_act.shape))).astype(jnp.bfloat16)
+
+            def back_half(d, h, pre_grad=pre_grad):
+                rows_w = lax.dynamic_slice_in_dim(projection, (me_t ^ d) * width + h * half, half, axis=0)
+                return lax.dot_general(
+                    pre_grad, rows_w, (((1,), (1,)), ((), ())), preferred_element_type=jnp.float32
+                ).astype(jnp.bfloat16)
+
+            grad = jnp.concatenate(
+                reduce_scatter_free(back_half, "tensor", tensor_count), axis=1
+            ).astype(jnp.bfloat16)
+            grads.extend(jnp.split(grad, len(blocks), axis=0))
+        returned = collect_rows(grads, "dp").reshape(group_count * capacity, width)
+        input_grad = jnp.dot(placing, returned, preferred_element_type=jnp.float32)
+        return (generated, input_grad.astype(jnp.bfloat16))
 
     input_grad = None
     for c in range(chunks):

time: 109 us -> 104 us (0.954)
  waiting for transfers between devices: 53.1 us -> 31.5 us
  starting transfers between devices: 31.5 us -> 42.5 us
  matrix products: 15.1 us -> 19.8 us
    ppermute x4 -> x8, waiting for transfers between devices: 15.3 us -> 4.66 us  [all_gather_free(): got = lax.ppermute(payload, axis, [(i, i ^ bit) for i in range(n)])]
    ppermute x14, waiting for transfers between devices: 12.3 us -> 5.73 us  [the longest x7 3.61 us: collect_rows(): lax.ppermute(parts[s], axis, [(i, i ^ s) for i in range(n)])]
    ppermute x4 -> x8, starting transfers between devices: 2.87 us -> 8.37 us  [all_gather_free(): got = lax.ppermute(payload, axis, [(i, i ^ bit) for i in range(n)])]
    ppermute x4 -> x8, waiting for transfers between devices: 13.5 us -> 8.13 us  [reduce_scatter_free(): got = lax.ppermute(payload, axis, [(i, i ^ bit) for i in range(n)])]
    ppermute x4 -> x8, starting transfers between devices: 4.46 us -> 9.62 us  [reduce_scatter_free(): got = lax.ppermute(payload, axis, [(i, i ^ bit) for i in range(n)])]
    dot_general x8 -> x16, matrix products: 6.14 us -> 8.56 us  [shards(): term = jnp.dot(held[h][d], rows_w, preferred_element_type=jnp.float32)]
    dot_general x8 -> x16, matrix products: 3.54 us -> 5.76 us  [back_half(): lax.dot_general(pre_grad, rows_w, (((1,), (1,)), ((), ())), preferred_ele...]
  transfers between devices with their start and end apart: 26 -> 34, of which waited for: 12 -> 15; matrix products, arithmetic and copies ran while one was open for 7% -> 14% of each run, Pallas kernels for 0% -> 0%
where the time goes in v7:
time: 104 us; the launch traced here: 103 us
  starting transfers between devices  42.5 us (41%)
  waiting for transfers between devices  31.5 us (30%)
  matrix products  19.8 us (19%)
  other arithmetic  4.57 us (4%)
  local copies, waits for them, and re-layouts  3.27 us (3%)
  between operations  1.17 us (1%)
    ppermute x4, waiting for transfers between devices, reduce_scatter_tree(): got = lax.ppermute(payloads[h], axis, [(i, i ^ bit) for i in range(n)])  13 us
    ppermute x7, starting transfers between devices, collect_rows(): lax.ppermute(parts[s], axis, [(i, i ^ s) for i in range(n)])  9.68 us
    ppermute x8, starting transfers between devices, reduce_scatter_free(): got = lax.ppermute(payload, axis, [(i, i ^ bit) for i in range(n)])  9.62 us
    dot_general x16, matrix products, shards(): term = jnp.dot(held[h][d], rows_w, preferred_element_type=jnp.float32)  8.56 us
    ppermute x8, starting transfers between devices, all_gather_free(): got = lax.ppermute(payload, axis, [(i, i ^ bit) for i in range(n)])  8.37 us
    ppermute x7, starting transfers between devices, dispatch_rows(): got.append(lax.ppermute(chunk, axis, [(i, i ^ s) for i in range(n)]))  8.27 us
    ppermute x8, waiting for transfers between devices, reduce_scatter_free(): got = lax.ppermute(payload, axis, [(i, i ^ bit) for i in range(n)])  8.13 us
    ppermute x4, starting transfers between devices, reduce_scatter_tree(): got = lax.ppermute(payloads[h], axis, [(i, i ^ bit) for i in range(n)])  6.59 us
  transfers between devices with their start and end apart: 34, of which 15 were waited for; matrix products, arithmetic and copies ran while one was open for 14% of the time, Pallas kernels for 0%

profile of v7, /device:TPU:0, one launch (start us, length us, event | category | flops | bytes accessed | tf_op | source)
XLA Modules:
  0.0 102.9 jit_solution(6920686424440486688)
XLA Ops:
  1.6 3.8 %convolution_convert_fusion = bf16[3072,256]{1,0:T(8,128)(2,1)S(1)} fusion(bf16[768,3072]{1,0:T(8,128)(2,1)} %param.9, bf16[256,768]{1,0:T(8,128)(2,1)S(1)} %copy-done), kind=kOutput, calls=%fused_computation.1 | convolution fusion | flops 1208745984 | bytes 6684672 | tf_op jit(solution)/shard_map/dot_general | solution.py:198
  6.5 2.9 %collective-permute-start = (bf16[768,256]{1,0:T(8,128)(2,1)}, bf16[768,256]{1,0:T(8,128)(2,1)S(1)}, u32[]{:S(2)}, u32[]{:S(2)}) collective-permute-start(bf16[768,256]{1,0:T(8,128)(2,1)} %get-tuple-element.6), channel_id=1, source_target_pairs={{0,1},{1,0},{2,3},{3,2},{4,5},{5,4},{6,7},{7,6},{8,9},{9,8},{10,11... | collective-permute-start | bytes 1179656 | tf_op jit(solution)/shard_map/ppermute | solution.py:91
  12.4 6.3 %collective-permute-done = bf16[768,256]{1,0:T(8,128)(2,1)S(1)} collective-permute-done((bf16[768,256]{1,0:T(8,128)(2,1)}, bf16[768,256]{1,0:T(8,128)(2,1)S(1)}, u32[]{:S(2)}, u32[]{:S(2)}) %collective-permute-start) | collective-permute-done | bytes 393248 | tf_op jit(solution)/shard_map/ppermute | solution.py:91
  18.7 1.6 %collective-permute-done.1 = bf16[768,256]{1,0:T(8,128)(2,1)} collective-permute-done((bf16[768,256]{1,0:T(8,128)(2,1)}, bf16[768,256]{1,0:T(8,128)(2,1)}, u32[]{:S(2)}, u32[]{:S(2)}) %collective-permute-start.1) | collective-permute-done | bytes 393248 | tf_op jit(solution)/shard_map/ppermute | solution.py:91
  21.4 1.6 %collective-permute-start.2 = (bf16[384,256]{1,0:T(8,128)(2,1)S(1)}, bf16[384,256]{1,0:T(8,128)(2,1)S(1)}, u32[]{:S(2)}, u32[]{:S(2)}) collective-permute-start(bf16[384,256]{1,0:T(8,128)(2,1)S(1)} %get-tuple-element.8), channel_id=1, source_target_pairs={{0,2},{1,3},{2,0},{3,1},{4,6},{5,7},{6,4},{7,5},{8,10},{9,11},{10,... | collective-permute-start | bytes 589832 | tf_op jit(solution)/shard_map/ppermute | solution.py:91
  23.5 3.6 %collective-permute-done.2 = bf16[384,256]{1,0:T(8,128)(2,1)S(1)} collective-permute-done((bf16[384,256]{1,0:T(8,128)(2,1)S(1)}, bf16[384,256]{1,0:T(8,128)(2,1)S(1)}, u32[]{:S(2)}, u32[]{:S(2)}) %collective-permute-start.2) | collective-permute-done | bytes 196640 | tf_op jit(solution)/shard_map/ppermute | solution.py:91
  27.1 1.5 %collective-permute-done.3 = bf16[384,256]{1,0:T(8,128)(2,1)S(1)} collective-permute-done((bf16[384,256]{1,0:T(8,128)(2,1)S(1)}, bf16[384,256]{1,0:T(8,128)(2,1)S(1)}, u32[]{:S(2)}, u32[]{:S(2)}) %collective-permute-start.3) | collective-permute-done | bytes 196640 | tf_op jit(solution)/shard_map/ppermute | solution.py:91
  30.4 2.6 %collective-permute-start.18 = (bf16[40,768]{1,0:T(8,128)(2,1)S(1)}, bf16[40,768]{1,0:T(8,128)(2,1)S(1)}, u32[]{:S(2)}, u32[]{:S(2)}) collective-permute-start(bf16[40,768]{1,0:T(8,128)(2,1)S(1)} %get-tuple-element.25), channel_id=1, source_target_pairs={{0,16},{4,20},{8,24},{12,28},{16,0},{20,4},{24,8},{28,12},{1,17},{... | collective-permute-start | bytes 184328 | tf_op jit(solution)/shard_map/ppermute | solution.py:158
  35.3 2.3 %collective-permute-start.21 = (bf16[40,768]{1,0:T(8,128)(2,1)S(1)}, bf16[40,768]{1,0:T(8,128)(2,1)S(1)}, u32[]{:S(2)}, u32[]{:S(2)}) collective-permute-start(bf16[40,768]{1,0:T(8,128)(2,1)S(1)} %get-tuple-element.22), channel_id=1, source_target_pairs={{0,28},{4,24},{8,20},{12,16},{16,12},{20,8},{24,4},{28,0},{1,29},{... | collective-permute-start | bytes 184328 | tf_op jit(solution)/shard_map/ppermute | solution.py:158
  37.9 1.6 %collective-permute-start.5 = (bf16[40,768]{1,0:T(8,128)(2,1)S(1)}, bf16[40,768]{1,0:T(8,128)(2,1)S(1)}, u32[]{:S(2)}, u32[]{:S(2)}) collective-permute-start(bf16[40,768]{1,0:T(8,128)(2,1)S(1)} %get-tuple-element.27), channel_id=1, source_target_pairs={{0,8},{4,12},{8,0},{12,4},{16,24},{20,28},{24,16},{28,20},{1,9},{5... | collective-permute-start | bytes 184328 | tf_op jit(solution)/shard_map/ppermute | solution.py:158
  45.6 1.5 %collective-permute-start.7 = (bf16[160,384]{1,0:T(8,128)(2,1)S(1)}, bf16[160,384]{1,0:T(8,128)(2,1)S(1)}, u32[]{:S(2)}, u32[]{:S(2)}) collective-permute-start(bf16[160,384]{1,0:T(8,128)(2,1)S(1)} %get-tuple-element.39), channel_id=1, source_target_pairs={{0,1},{1,0},{2,3},{3,2},{4,5},{5,4},{6,7},{7,6},{8,9},{9,8},{10,11... | collective-permute-start | bytes 368648 | tf_op jit(solution)/shard_map/ppermute | solution.py:141
  51.4 1.6 %collective-permute-start.8 = (bf16[320,384]{1,0:T(8,128)(2,1)S(1)}, bf16[320,384]{1,0:T(8,128)(2,1)S(1)}, u32[]{:S(2)}, u32[]{:S(2)}) collective-permute-start(bf16[320,384]{1,0:T(8,128)(2,1)S(1)} %pad_maximum_fusion.3), channel_id=1, source_target_pairs={{0,2},{1,3},{2,0},{3,1},{4,6},{5,7},{6,4},{7,5},{8,10},{9,11},{10,... | collective-permute-start | bytes 737288 | tf_op jit(solution)/shard_map/ppermute | solution.py:141
  62.0 1.6 %collective-permute-done.8 = bf16[320,384]{1,0:T(8,128)(2,1)S(1)} collective-permute-done((bf16[320,384]{1,0:T(8,128)(2,1)S(1)}, bf16[320,384]{1,0:T(8,128)(2,1)S(1)}, u32[]{:S(2)}, u32[]{:S(2)}) %collective-permute-start.8) | collective-permute-done | bytes 245792 | tf_op jit(solution)/shard_map/ppermute | solution.py:141
  68.3 1.6 %collective-permute-start.28 = (bf16[320,384]{1,0:T(8,128)(2,1)S(1)}, bf16[320,384]{1,0:T(8,128)(2,1)S(1)}, u32[]{:S(2)}, u32[]{:S(2)}) collective-permute-start(bf16[320,384]{1,0:T(8,128)(2,1)S(1)} %pad_maximum_fusion.10), channel_id=1, source_target_pairs={{0,2},{1,3},{2,0},{3,1},{4,6},{5,7},{6,4},{7,5},{8,10},{9,11},{10,... | collective-permute-start | bytes 737288 | tf_op jit(solution)/shard_map/ppermute | solution.py:124
  70.9 1.5 %collective-permute-start.11 = (bf16[320,384]{1,0:T(8,128)(2,1)S(1)}, bf16[320,384]{1,0:T(8,128)(2,1)S(1)}, u32[]{:S(2)}, u32[]{:S(2)}) collective-permute-start(bf16[320,384]{1,0:T(8,128)(2,1)S(1)} %pad_maximum_fusion.5), channel_id=1, source_target_pairs={{0,1},{1,0},{2,3},{3,2},{4,5},{5,4},{6,7},{7,6},{8,9},{9,8},{10,11... | collective-permute-start | bytes 737288 | tf_op jit(solution)/shard_map/ppermute | solution.py:124
  72.4 4.1 %collective-permute-done.26 = bf16[320,384]{1,0:T(8,128)(2,1)S(1)} collective-permute-done((bf16[320,384]{1,0:T(8,128)(2,1)S(1)}, bf16[320,384]{1,0:T(8,128)(2,1)S(1)}, u32[]{:S(2)}, u32[]{:S(2)}) %collective-permute-start.26) | collective-permute-done | bytes 245792 | tf_op jit(solution)/shard_map/ppermute | solution.py:124
  76.9 1.6 %collective-permute-start.27 = (bf16[160,384]{1,0:T(8,128)(2,1)S(1)}, bf16[160,384]{1,0:T(8,128)(2,1)S(1)}, u32[]{:S(2)}, u32[]{:S(2)}) collective-permute-start(bf16[160,384]{1,0:T(8,128)(2,1)S(1)} %add_convert_fusion.5), channel_id=1, source_target_pairs={{0,2},{1,3},{2,0},{3,1},{4,6},{5,7},{6,4},{7,5},{8,10},{9,11},{10,... | collective-permute-start | bytes 368648 | tf_op jit(solution)/shard_map/ppermute | solution.py:124
  79.5 3.0 %collective-permute-done.13 = bf16[320,384]{1,0:T(8,128)(2,1)S(1)} collective-permute-done((bf16[320,384]{1,0:T(8,128)(2,1)S(1)}, bf16[320,384]{1,0:T(8,128)(2,1)S(1)}, u32[]{:S(2)}, u32[]{:S(2)}) %collective-permute-start.13) | collective-permute-done | bytes 245792 | tf_op jit(solution)/shard_map/ppermute | solution.py:124
  82.9 1.5 %collective-permute-start.14 = (bf16[160,384]{1,0:T(8,128)(2,1)S(1)}, bf16[160,384]{1,0:T(8,128)(2,1)S(1)}, u32[]{:S(2)}, u32[]{:S(2)}) collective-permute-start(bf16[160,384]{1,0:T(8,128)(2,1)S(1)} %add_convert_fusion.7), channel_id=1, source_target_pairs={{0,1},{1,0},{2,3},{3,2},{4,5},{5,4},{6,7},{7,6},{8,9},{9,8},{10,11... | collective-permute-start | bytes 368648 | tf_op jit(solution)/shard_map/ppermute | solution.py:124
  84.8 1.6 %collective-permute-start.12 = (bf16[160,384]{1,0:T(8,128)(2,1)S(1)}, bf16[160,384]{1,0:T(8,128)(2,1)S(1)}, u32[]{:S(2)}, u32[]{:S(2)}) collective-permute-start(bf16[160,384]{1,0:T(8,128)(2,1)S(1)} %add_convert_fusion.9), channel_id=1, source_target_pairs={{0,2},{1,3},{2,0},{3,1},{4,6},{5,7},{6,4},{7,5},{8,10},{9,11},{10,... | collective-permute-start | bytes 368648 | tf_op jit(solution)/shard_map/ppermute | solution.py:124
  86.5 2.2 %collective-permute-start.30 = (bf16[40,768]{1,0:T(8,128)(2,1)S(1)}, bf16[40,768]{1,0:T(8,128)(2,1)S(1)}, u32[]{:S(2)}, u32[]{:S(2)}) collective-permute-start(bf16[40,768]{1,0:T(8,128)(2,1)S(1)} %get-tuple-element.31), channel_id=1, source_target_pairs={{0,16},{4,20},{8,24},{12,28},{16,0},{20,4},{24,8},{28,12},{1,17},{... | collective-permute-start | bytes 184328 | tf_op jit(solution)/shard_map/ppermute | solution.py:168
  91.7 2.1 %collective-permute-start.31 = (bf16[40,768]{1,0:T(8,128)(2,1)S(1)}, bf16[40,768]{1,0:T(8,128)(2,1)S(1)}, u32[]{:S(2)}, u32[]{:S(2)}) collective-permute-start(bf16[40,768]{1,0:T(8,128)(2,1)S(1)} %get-tuple-element.32), channel_id=1, source_target_pairs={{0,20},{4,16},{8,28},{12,24},{16,4},{20,0},{24,12},{28,8},{1,21},{... | collective-permute-start | bytes 184328 | tf_op jit(solution)/shard_map/ppermute | solution.py:168
  94.9 2.5 %collective-permute-start.33 = (bf16[40,768]{1,0:T(8,128)(2,1)S(1)}, bf16[40,768]{1,0:T(8,128)(2,1)S(1)}, u32[]{:S(2)}, u32[]{:S(2)}) collective-permute-start(bf16[40,768]{1,0:T(8,128)(2,1)S(1)} %get-tuple-element.30), channel_id=1, source_target_pairs={{0,28},{4,24},{8,20},{12,16},{16,12},{20,8},{24,4},{28,0},{1,29},{... | collective-permute-start | bytes 184328 | tf_op jit(solution)/shard_map/ppermute | solution.py:168
  97.4 2.9 %collective-permute-done.32 = bf16[40,768]{1,0:T(8,128)(2,1)S(1)} collective-permute-done((bf16[40,768]{1,0:T(8,128)(2,1)S(1)}, bf16[40,768]{1,0:T(8,128)(2,1)S(1)}, u32[]{:S(2)}, u32[]{:S(2)}) %collective-permute-start.32) | collective-permute-done | bytes 61472 | tf_op jit(solution)/shard_map/ppermute | solution.py:168
  (149 shorter events, 44.4 us)
Async XLA Ops:
  6.5 12.3 %collective-permute-start = (bf16[768,256]{1,0:T(8,128)(2,1)}, bf16[768,256]{1,0:T(8,128)(2,1)S(1)}, u32[]{:S(2)}, u32[]{:S(2)}) collective-permute-start(bf16[768,256]{1,0:T(8,128)(2,1)} %get-tuple-element.6), channel_id=1, source_target_pairs={{0,1},{1,0},{2,3},{3,2},{4,5},{5,4},{6,7},{7,6},{8,9},{9,8},{10,11... | collective-permute-start | bytes 1179656 | tf_op jit(solution)/shard_map/ppermute | solution.py:91
  9.4 10.9 %collective-permute-start.1 = (bf16[768,256]{1,0:T(8,128)(2,1)}, bf16[768,256]{1,0:T(8,128)(2,1)}, u32[]{:S(2)}, u32[]{:S(2)}) collective-permute-start(bf16[768,256]{1,0:T(8,128)(2,1)} %get-tuple-element.7), channel_id=1, source_target_pairs={{0,2},{1,3},{2,0},{3,1},{4,6},{5,7},{6,4},{7,5},{8,10},{9,11},{10,... | collective-permute-start | bytes 1179656 | tf_op jit(solution)/shard_map/ppermute | solution.py:91
  30.4 7.5 %collective-permute-start.18 = (bf16[40,768]{1,0:T(8,128)(2,1)S(1)}, bf16[40,768]{1,0:T(8,128)(2,1)S(1)}, u32[]{:S(2)}, u32[]{:S(2)}) collective-permute-start(bf16[40,768]{1,0:T(8,128)(2,1)S(1)} %get-tuple-element.25), channel_id=1, source_target_pairs={{0,16},{4,20},{8,24},{12,28},{16,0},{20,4},{24,8},{28,12},{1,17},{... | collective-permute-start | bytes 184328 | tf_op jit(solution)/shard_map/ppermute | solution.py:158
  33.9 6.7 %collective-permute-start.20 = (bf16[40,768]{1,0:T(8,128)(2,1)S(1)}, bf16[40,768]{1,0:T(8,128)(2,1)S(1)}, u32[]{:S(2)}, u32[]{:S(2)}) collective-permute-start(bf16[40,768]{1,0:T(8,128)(2,1)S(1)} %get-tuple-element.23), channel_id=1, source_target_pairs={{0,24},{4,28},{8,16},{12,20},{16,8},{20,12},{24,0},{28,4},{1,25},{... | collective-permute-start | bytes 184328 | tf_op jit(solution)/shard_map/ppermute | solution.py:158
  35.3 6.4 %collective-permute-start.21 = (bf16[40,768]{1,0:T(8,128)(2,1)S(1)}, bf16[40,768]{1,0:T(8,128)(2,1)S(1)}, u32[]{:S(2)}, u32[]{:S(2)}) collective-permute-start(bf16[40,768]{1,0:T(8,128)(2,1)S(1)} %get-tuple-element.22), channel_id=1, source_target_pairs={{0,28},{4,24},{8,20},{12,16},{16,12},{20,8},{24,4},{28,0},{1,29},{... | collective-permute-start | bytes 184328 | tf_op jit(solution)/shard_map/ppermute | solution.py:158
  37.6 6.5 %collective-permute-start.4 = (bf16[40,768]{1,0:T(8,128)(2,1)S(1)}, bf16[40,768]{1,0:T(8,128)(2,1)S(1)}, u32[]{:S(2)}, u32[]{:S(2)}) collective-permute-start(bf16[40,768]{1,0:T(8,128)(2,1)S(1)} %get-tuple-element.28), channel_id=1, source_target_pairs={{0,4},{4,0},{8,12},{12,8},{16,20},{20,16},{24,28},{28,24},{1,5},{5... | collective-permute-start | bytes 184328 | tf_op jit(solution)/shard_map/ppermute | solution.py:158
  37.9 6.3 %collective-permute-start.5 = (bf16[40,768]{1,0:T(8,128)(2,1)S(1)}, bf16[40,768]{1,0:T(8,128)(2,1)S(1)}, u32[]{:S(2)}, u32[]{:S(2)}) collective-permute-start(bf16[40,768]{1,0:T(8,128)(2,1)S(1)} %get-tuple-element.27), channel_id=1, source_target_pairs={{0,8},{4,12},{8,0},{12,4},{16,24},{20,28},{24,16},{28,20},{1,9},{5... | collective-permute-start | bytes 184328 | tf_op jit(solution)/shard_map/ppermute | solution.py:158
  41.7 7.0 %collective-permute-start.22 = (bf16[160,384]{1,0:T(8,128)(2,1)S(1)}, bf16[160,384]{1,0:T(8,128)(2,1)S(1)}, u32[]{:S(2)}, u32[]{:S(2)}) collective-permute-start(bf16[160,384]{1,0:T(8,128)(2,1)S(1)} %get-tuple-element.34), channel_id=1, source_target_pairs={{0,1},{1,0},{2,3},{3,2},{4,5},{5,4},{6,7},{7,6},{8,9},{9,8},{10,11... | collective-permute-start | bytes 368648 | tf_op jit(solution)/shard_map/ppermute | solution.py:141
  42.3 7.0 %collective-permute-start.24 = (bf16[160,384]{1,0:T(8,128)(2,1)S(1)}, bf16[160,384]{1,0:T(8,128)(2,1)S(1)}, u32[]{:S(2)}, u32[]{:S(2)}) collective-permute-start(bf16[160,384]{1,0:T(8,128)(2,1)S(1)} %get-tuple-element.35), channel_id=1, source_target_pairs={{0,2},{1,3},{2,0},{3,1},{4,6},{5,7},{6,4},{7,5},{8,10},{9,11},{10,... | collective-permute-start | bytes 368648 | tf_op jit(solution)/shard_map/ppermute | solution.py:141
  47.2 5.9 %collective-permute-start.9 = (bf16[160,384]{1,0:T(8,128)(2,1)S(1)}, bf16[160,384]{1,0:T(8,128)(2,1)S(1)}, u32[]{:S(2)}, u32[]{:S(2)}) collective-permute-start(bf16[160,384]{1,0:T(8,128)(2,1)S(1)} %get-tuple-element.40), channel_id=1, source_target_pairs={{0,2},{1,3},{2,0},{3,1},{4,6},{5,7},{6,4},{7,5},{8,10},{9,11},{10,... | collective-permute-start | bytes 368648 | tf_op jit(solution)/shard_map/ppermute | solution.py:141
  48.7 9.6 %collective-permute-start.23 = (bf16[320,384]{1,0:T(8,128)(2,1)S(1)}, bf16[320,384]{1,0:T(8,128)(2,1)S(1)}, u32[]{:S(2)}, u32[]{:S(2)}) collective-permute-start(bf16[320,384]{1,0:T(8,128)(2,1)S(1)} %pad_maximum_fusion.7), channel_id=1, source_target_pairs={{0,2},{1,3},{2,0},{3,1},{4,6},{5,7},{6,4},{7,5},{8,10},{9,11},{10,... | collective-permute-start | bytes 737288 | tf_op jit(solution)/shard_map/ppermute | solution.py:141
  49.3 9.6 %collective-permute-start.25 = (bf16[320,384]{1,0:T(8,128)(2,1)S(1)}, bf16[320,384]{1,0:T(8,128)(2,1)S(1)}, u32[]{:S(2)}, u32[]{:S(2)}) collective-permute-start(bf16[320,384]{1,0:T(8,128)(2,1)S(1)} %pad_maximum_fusion.8), channel_id=1, source_target_pairs={{0,1},{1,0},{2,3},{3,2},{4,5},{5,4},{6,7},{7,6},{8,9},{9,8},{10,11... | collective-permute-start | bytes 737288 | tf_op jit(solution)/shard_map/ppermute | solution.py:141
  51.4 12.2 %collective-permute-start.8 = (bf16[320,384]{1,0:T(8,128)(2,1)S(1)}, bf16[320,384]{1,0:T(8,128)(2,1)S(1)}, u32[]{:S(2)}, u32[]{:S(2)}) collective-permute-start(bf16[320,384]{1,0:T(8,128)(2,1)S(1)} %pad_maximum_fusion.3), channel_id=1, source_target_pairs={{0,2},{1,3},{2,0},{3,1},{4,6},{5,7},{6,4},{7,5},{8,10},{9,11},{10,... | collective-permute-start | bytes 737288 | tf_op jit(solution)/shard_map/ppermute | solution.py:141
  53.1 11.5 %collective-permute-start.10 = (bf16[320,384]{1,0:T(8,128)(2,1)S(1)}, bf16[320,384]{1,0:T(8,128)(2,1)S(1)}, u32[]{:S(2)}, u32[]{:S(2)}) collective-permute-start(bf16[320,384]{1,0:T(8,128)(2,1)S(1)} %pad_maximum_fusion.4), channel_id=1, source_target_pairs={{0,1},{1,0},{2,3},{3,2},{4,5},{5,4},{6,7},{7,6},{8,9},{9,8},{10,11... | collective-permute-start | bytes 737288 | tf_op jit(solution)/shard_map/ppermute | solution.py:141
  67.7 8.9 %collective-permute-start.26 = (bf16[320,384]{1,0:T(8,128)(2,1)S(1)}, bf16[320,384]{1,0:T(8,128)(2,1)S(1)}, u32[]{:S(2)}, u32[]{:S(2)}) collective-permute-start(bf16[320,384]{1,0:T(8,128)(2,1)S(1)} %pad_maximum_fusion.9), channel_id=1, source_target_pairs={{0,1},{1,0},{2,3},{3,2},{4,5},{5,4},{6,7},{7,6},{8,9},{9,8},{10,11... | collective-permute-start | bytes 737288 | tf_op jit(solution)/shard_map/ppermute | solution.py:124
  68.3 10.2 %collective-permute-start.28 = (bf16[320,384]{1,0:T(8,128)(2,1)S(1)}, bf16[320,384]{1,0:T(8,128)(2,1)S(1)}, u32[]{:S(2)}, u32[]{:S(2)}) collective-permute-start(bf16[320,384]{1,0:T(8,128)(2,1)S(1)} %pad_maximum_fusion.10), channel_id=1, source_target_pairs={{0,2},{1,3},{2,0},{3,1},{4,6},{5,7},{6,4},{7,5},{8,10},{9,11},{10,... | collective-permute-start | bytes 737288 | tf_op jit(solution)/shard_map/ppermute | solution.py:124
  69.9 12.6 %collective-permute-start.13 = (bf16[320,384]{1,0:T(8,128)(2,1)S(1)}, bf16[320,384]{1,0:T(8,128)(2,1)S(1)}, u32[]{:S(2)}, u32[]{:S(2)}) collective-permute-start(bf16[320,384]{1,0:T(8,128)(2,1)S(1)} %pad_maximum_fusion.6), channel_id=1, source_target_pairs={{0,2},{1,3},{2,0},{3,1},{4,6},{5,7},{6,4},{7,5},{8,10},{9,11},{10,... | collective-permute-start | bytes 737288 | tf_op jit(solution)/shard_map/ppermute | solution.py:124
  70.9 13.5 %collective-permute-start.11 = (bf16[320,384]{1,0:T(8,128)(2,1)S(1)}, bf16[320,384]{1,0:T(8,128)(2,1)S(1)}, u32[]{:S(2)}, u32[]{:S(2)}) collective-permute-start(bf16[320,384]{1,0:T(8,128)(2,1)S(1)} %pad_maximum_fusion.5), channel_id=1, source_target_pairs={{0,1},{1,0},{2,3},{3,2},{4,5},{5,4},{6,7},{7,6},{8,9},{9,8},{10,11... | collective-permute-start | bytes 737288 | tf_op jit(solution)/shard_map/ppermute | solution.py:124
  76.9 9.5 %collective-permute-start.27 = (bf16[160,384]{1,0:T(8,128)(2,1)S(1)}, bf16[160,384]{1,0:T(8,128)(2,1)S(1)}, u32[]{:S(2)}, u32[]{:S(2)}) collective-permute-start(bf16[160,384]{1,0:T(8,128)(2,1)S(1)} %add_convert_fusion.5), channel_id=1, source_target_pairs={{0,2},{1,3},{2,0},{3,1},{4,6},{5,7},{6,4},{7,5},{8,10},{9,11},{10,... | collective-permute-start | bytes 368648 | tf_op jit(solution)/shard_map/ppermute | solution.py:124
  78.9 7.6 %collective-permute-start.29 = (bf16[160,384]{1,0:T(8,128)(2,1)S(1)}, bf16[160,384]{1,0:T(8,128)(2,1)S(1)}, u32[]{:S(2)}, u32[]{:S(2)}) collective-permute-start(bf16[160,384]{1,0:T(8,128)(2,1)S(1)} %add_convert_fusion.3), channel_id=1, source_target_pairs={{0,1},{1,0},{2,3},{3,2},{4,5},{5,4},{6,7},{7,6},{8,9},{9,8},{10,11... | collective-permute-start | bytes 368648 | tf_op jit(solution)/shard_map/ppermute | solution.py:124
  86.5 10.8 %collective-permute-start.30 = (bf16[40,768]{1,0:T(8,128)(2,1)S(1)}, bf16[40,768]{1,0:T(8,128)(2,1)S(1)}, u32[]{:S(2)}, u32[]{:S(2)}) collective-permute-start(bf16[40,768]{1,0:T(8,128)(2,1)S(1)} %get-tuple-element.31), channel_id=1, source_target_pairs={{0,16},{4,20},{8,24},{12,28},{16,0},{20,4},{24,8},{28,12},{1,17},{... | collective-permute-start | bytes 184328 | tf_op jit(solution)/shard_map/ppermute | solution.py:168
  90.7 6.7 %collective-permute-start.17 = (bf16[40,768]{1,0:T(8,128)(2,1)S(1)}, bf16[40,768]{1,0:T(8,128)(2,1)S(1)}, u32[]{:S(2)}, u32[]{:S(2)}) collective-permute-start(bf16[40,768]{1,0:T(8,128)(2,1)S(1)} %get-tuple-element.36), channel_id=1, source_target_pairs={{0,12},{4,8},{8,4},{12,0},{16,28},{20,24},{24,20},{28,16},{1,13},{... | collective-permute-start | bytes 184328 | tf_op jit(solution)/shard_map/ppermute | solution.py:168
  93.9 6.4 %collective-permute-start.32 = (bf16[40,768]{1,0:T(8,128)(2,1)S(1)}, bf16[40,768]{1,0:T(8,128)(2,1)S(1)}, u32[]{:S(2)}, u32[]{:S(2)}) collective-permute-start(bf16[40,768]{1,0:T(8,128)(2,1)S(1)} %get-tuple-element.33), channel_id=1, source_target_pairs={{0,24},{4,28},{8,16},{12,20},{16,8},{20,12},{24,0},{28,4},{1,25},{... | collective-permute-start | bytes 184328 | tf_op jit(solution)/shard_map/ppermute | solution.py:168
  94.9 6.1 %collective-permute-start.33 = (bf16[40,768]{1,0:T(8,128)(2,1)S(1)}, bf16[40,768]{1,0:T(8,128)(2,1)S(1)}, u32[]{:S(2)}, u32[]{:S(2)}) collective-permute-start(bf16[40,768]{1,0:T(8,128)(2,1)S(1)} %get-tuple-element.30), channel_id=1, source_target_pairs={{0,28},{4,24},{8,20},{12,16},{16,12},{20,8},{24,4},{28,0},{1,29},{... | collective-permute-start | bytes 184328 | tf_op jit(solution)/shard_map/ppermute | solution.py:168
  (17 other events, 146.7 us)

commit v8 on v7

--- a/solution.py
+++ b/solution.py
@@ -195,14 +195,14 @@
         return jnp.dot(context, columns, preferred_element_type=jnp.float32).astype(jnp.bfloat16)
 
     if tree:
-        head_cols = lax.dot_general(
-            out_proj, context, (((0,), (1,)), ((), ())), preferred_element_type=jnp.float32
-        ).astype(jnp.bfloat16)
+        head_rows = jnp.dot(context, out_proj, preferred_element_type=jnp.float32).astype(jnp.bfloat16)
+        row_half = tok_rows // 2
 
         def head_half(d, h):
-            return lax.dynamic_slice_in_dim(head_cols, (me_t ^ d) * width + h * half, half, axis=0)
-
-        summed = jnp.concatenate(reduce_scatter_tree(head_half, "tensor", tensor_count), axis=0).T
+            rows = head_rows[h * row_half:(h + 1) * row_half]
+            return lax.dynamic_slice_in_dim(rows, (me_t ^ d) * width, width, axis=1)
+
+        summed = jnp.concatenate(reduce_scatter_tree(head_half, "tensor", tensor_count), axis=0)
         summed = summed + residual_in.astype(jnp.float32)
     else:
         received = [

time: 104 us -> 102 us (0.981)
  starting transfers between devices: 42.5 us -> 48.9 us
  waiting for transfers between devices: 31.5 us -> 28 us
  matrix products: 19.8 us -> 16.5 us
    dot_general x16, matrix products: 8.56 us -> 5.37 us  [shards(): term = jnp.dot(held[h][d], rows_w, preferred_element_type=jnp.float32)]
    ppermute x7, starting transfers between devices: 9.68 us -> 12.6 us  [collect_rows(): lax.ppermute(parts[s], axis, [(i, i ^ s) for i in range(n)])]
    ppermute x7, starting transfers between devices: 8.27 us -> 11 us  [dispatch_rows(): got.append(lax.ppermute(chunk, axis, [(i, i ^ s) for i in range(n)]))]
    ppermute x7, waiting for transfers between devices: 2.12 us -> 0.42 us  [dispatch_rows(): got.append(lax.ppermute(chunk, axis, [(i, i ^ s) for i in range(n)]))]
    ppermute x8, waiting for transfers between devices: 8.13 us -> 6.52 us  [reduce_scatter_free(): got = lax.ppermute(payload, axis, [(i, i ^ bit) for i in range(n)])]
    ppermute x8, starting transfers between devices: 8.37 us -> 9.75 us  [all_gather_free(): got = lax.ppermute(payload, axis, [(i, i ^ bit) for i in range(n)])]
    ppermute x4, waiting for transfers between devices: 13 us -> 11.8 us  [reduce_scatter_tree(): got = lax.ppermute(payloads[h], axis, [(i, i ^ bit) for i in range(n)])]
    unnamed x25 -> x23, local copies, waits for them, and re-layouts: 2.12 us -> 1.07 us
  transfers between devices with their start and end apart: 34 -> 34, of which waited for: 15 -> 13; matrix products, arithmetic and copies ran while one was open for 14% -> 10% of each run, Pallas kernels for 0% -> 0%
where the time goes in v8:
time: 102 us; the launch traced here: 101 us
  starting transfers between devices  48.9 us (48%)
  waiting for transfers between devices  28 us (27%)
  matrix products  16.5 us (16%)
  other arithmetic  4.28 us (4%)
  local copies, waits for them, and re-layouts  2.34 us (2%)
  between operations  1.31 us (1%)
    ppermute x7, starting transfers between devices, collect_rows(): lax.ppermute(parts[s], axis, [(i, i ^ s) for i in range(n)])  12.6 us
    ppermute x4, waiting for transfers between devices, reduce_scatter_tree(): got = lax.ppermute(payloads[h], axis, [(i, i ^ bit) for i in range(n)])  11.8 us
    ppermute x7, starting transfers between devices, dispatch_rows(): got.append(lax.ppermute(chunk, axis, [(i, i ^ s) for i in range(n)]))  11 us
    ppermute x8, starting transfers between devices, all_gather_free(): got = lax.ppermute(payload, axis, [(i, i ^ bit) for i in range(n)])  9.75 us
    ppermute x8, starting transfers between devices, reduce_scatter_free(): got = lax.ppermute(payload, axis, [(i, i ^ bit) for i in range(n)])  8.98 us
    ppermute x4, starting transfers between devices, reduce_scatter_tree(): got = lax.ppermute(payloads[h], axis, [(i, i ^ bit) for i in range(n)])  6.54 us
    ppermute x8, waiting for transfers between devices, reduce_scatter_free(): got = lax.ppermute(payload, axis, [(i, i ^ bit) for i in range(n)])  6.52 us
    dot_general x16, matrix products, back_half(): lax.dot_general(pre_grad, rows_w, (((1,), (1,)), ((), ())), preferred_ele...  5.76 us
  transfers between devices with their start and end apart: 34, of which 13 were waited for; matrix products, arithmetic and copies ran while one was open for 10% of the time, Pallas kernels for 0%

profile of v8, /device:TPU:0, one launch (start us, length us, event | category | flops | bytes accessed | tf_op | source)
XLA Modules:
  0.0 101.3 jit_solution(236317659422221346)
XLA Ops:
  1.6 3.7 %convolution_convert_fusion = bf16[256,3072]{1,0:T(8,128)(2,1)S(1)} fusion(bf16[256,768]{1,0:T(8,128)(2,1)S(1)} %copy-done, bf16[768,3072]{1,0:T(8,128)(2,1)} %param.9), kind=kOutput, calls=%fused_computation.1 | convolution fusion | flops 1208745984 | bytes 6684672 | tf_op jit(solution)/shard_map/dot_general | solution.py:198
  7.2 3.0 %collective-permute-start.1 = (bf16[256,768]{1,0:T(8,128)(2,1)}, bf16[256,768]{1,0:T(8,128)(2,1)S(1)}, u32[]{:S(2)}, u32[]{:S(2)}) collective-permute-start(bf16[256,768]{1,0:T(8,128)(2,1)} %pad_maximum_fusion.1), channel_id=1, source_target_pairs={{0,2},{1,3},{2,0},{3,1},{4,6},{5,7},{6,4},{7,5},{8,10},{9,11},{10,... | collective-permute-start | bytes 1179656 | tf_op jit(solution)/shard_map/ppermute | solution.py:91
  10.1 1.5 %collective-permute-start = (bf16[256,768]{1,0:T(8,128)(2,1)}, bf16[256,768]{1,0:T(8,128)(2,1)S(1)}, u32[]{:S(2)}, u32[]{:S(2)}) collective-permute-start(bf16[256,768]{1,0:T(8,128)(2,1)} %pad_maximum_fusion), channel_id=1, source_target_pairs={{0,1},{1,0},{2,3},{3,2},{4,5},{5,4},{6,7},{7,6},{8,9},{9,8},{10,11... | collective-permute-start | bytes 1179656 | tf_op jit(solution)/shard_map/ppermute | solution.py:91
  13.0 6.5 %collective-permute-done.1 = bf16[256,768]{1,0:T(8,128)(2,1)S(1)} collective-permute-done((bf16[256,768]{1,0:T(8,128)(2,1)}, bf16[256,768]{1,0:T(8,128)(2,1)S(1)}, u32[]{:S(2)}, u32[]{:S(2)}) %collective-permute-start.1) | collective-permute-done | bytes 393248 | tf_op jit(solution)/shard_map/ppermute | solution.py:91
  21.4 1.7 %collective-permute-start.3 = (bf16[128,768]{1,0:T(8,128)(2,1)S(1)}, bf16[128,768]{1,0:T(8,128)(2,1)S(1)}, u32[]{:S(2)}, u32[]{:S(2)}) collective-permute-start(bf16[128,768]{1,0:T(8,128)(2,1)S(1)} %add_convert_fusion), channel_id=1, source_target_pairs={{0,1},{1,0},{2,3},{3,2},{4,5},{5,4},{6,7},{7,6},{8,9},{9,8},{10,11... | collective-permute-start | bytes 589832 | tf_op jit(solution)/shard_map/ppermute | solution.py:91
  23.1 3.7 %collective-permute-done.2 = bf16[128,768]{1,0:T(8,128)(2,1)S(1)} collective-permute-done((bf16[128,768]{1,0:T(8,128)(2,1)S(1)}, bf16[128,768]{1,0:T(8,128)(2,1)S(1)}, u32[]{:S(2)}, u32[]{:S(2)}) %collective-permute-start.2) | collective-permute-done | bytes 196640 | tf_op jit(solution)/shard_map/ppermute | solution.py:91
  28.8 2.8 %collective-permute-start.18 = (bf16[40,768]{1,0:T(8,128)(2,1)S(1)}, bf16[40,768]{1,0:T(8,128)(2,1)S(1)}, u32[]{:S(2)}, u32[]{:S(2)}) collective-permute-start(bf16[40,768]{1,0:T(8,128)(2,1)S(1)} %get-tuple-element.19), channel_id=1, source_target_pairs={{0,16},{4,20},{8,24},{12,28},{16,0},{20,4},{24,8},{28,12},{1,17},{... | collective-permute-start | bytes 184328 | tf_op jit(solution)/shard_map/ppermute | solution.py:158
  31.6 1.4 %collective-permute-start.20 = (bf16[40,768]{1,0:T(8,128)(2,1)S(1)}, bf16[40,768]{1,0:T(8,128)(2,1)S(1)}, u32[]{:S(2)}, u32[]{:S(2)}) collective-permute-start(bf16[40,768]{1,0:T(8,128)(2,1)S(1)} %get-tuple-element.17), channel_id=1, source_target_pairs={{0,24},{4,28},{8,16},{12,20},{16,8},{20,12},{24,0},{28,4},{1,25},{... | collective-permute-start | bytes 184328 | tf_op jit(solution)/shard_map/ppermute | solution.py:158
  33.0 2.3 %collective-permute-start.21 = (bf16[40,768]{1,0:T(8,128)(2,1)S(1)}, bf16[40,768]{1,0:T(8,128)(2,1)S(1)}, u32[]{:S(2)}, u32[]{:S(2)}) collective-permute-start(bf16[40,768]{1,0:T(8,128)(2,1)S(1)} %get-tuple-element.16), channel_id=1, source_target_pairs={{0,28},{4,24},{8,20},{12,16},{16,12},{20,8},{24,4},{28,0},{1,29},{... | collective-permute-start | bytes 184328 | tf_op jit(solution)/shard_map/ppermute | solution.py:158
  35.6 4.1 %collective-permute-start.5 = (bf16[40,768]{1,0:T(8,128)(2,1)S(1)}, bf16[40,768]{1,0:T(8,128)(2,1)S(1)}, u32[]{:S(2)}, u32[]{:S(2)}) collective-permute-start(bf16[40,768]{1,0:T(8,128)(2,1)S(1)} %get-tuple-element.21), channel_id=1, source_target_pairs={{0,8},{4,12},{8,0},{12,4},{16,24},{20,28},{24,16},{28,20},{1,9},{5... | collective-permute-start | bytes 184328 | tf_op jit(solution)/shard_map/ppermute | solution.py:158
  39.9 1.7 %collective-permute-start.22 = (bf16[160,384]{1,0:T(8,128)(2,1)S(1)}, bf16[160,384]{1,0:T(8,128)(2,1)S(1)}, u32[]{:S(2)}, u32[]{:S(2)}) collective-permute-start(bf16[160,384]{1,0:T(8,128)(2,1)S(1)} %get-tuple-element.28), channel_id=1, source_target_pairs={{0,1},{1,0},{2,3},{3,2},{4,5},{5,4},{6,7},{7,6},{8,9},{9,8},{10,11... | collective-permute-start | bytes 368648 | tf_op jit(solution)/shard_map/ppermute | solution.py:141
  41.6 1.5 %collective-permute-start.24 = (bf16[160,384]{1,0:T(8,128)(2,1)S(1)}, bf16[160,384]{1,0:T(8,128)(2,1)S(1)}, u32[]{:S(2)}, u32[]{:S(2)}) collective-permute-start(bf16[160,384]{1,0:T(8,128)(2,1)S(1)} %get-tuple-element.29), channel_id=1, source_target_pairs={{0,2},{1,3},{2,0},{3,1},{4,6},{5,7},{6,4},{7,5},{8,10},{9,11},{10,... | collective-permute-start | bytes 368648 | tf_op jit(solution)/shard_map/ppermute | solution.py:141
  44.2 1.7 %collective-permute-start.7 = (bf16[160,384]{1,0:T(8,128)(2,1)S(1)}, bf16[160,384]{1,0:T(8,128)(2,1)S(1)}, u32[]{:S(2)}, u32[]{:S(2)}) collective-permute-start(bf16[160,384]{1,0:T(8,128)(2,1)S(1)} %get-tuple-element.33), channel_id=1, source_target_pairs={{0,1},{1,0},{2,3},{3,2},{4,5},{5,4},{6,7},{7,6},{8,9},{9,8},{10,11... | collective-permute-start | bytes 368648 | tf_op jit(solution)/shard_map/ppermute | solution.py:141
  45.9 1.5 %collective-permute-start.9 = (bf16[160,384]{1,0:T(8,128)(2,1)S(1)}, bf16[160,384]{1,0:T(8,128)(2,1)S(1)}, u32[]{:S(2)}, u32[]{:S(2)}) collective-permute-start(bf16[160,384]{1,0:T(8,128)(2,1)S(1)} %get-tuple-element.34), channel_id=1, source_target_pairs={{0,2},{1,3},{2,0},{3,1},{4,6},{5,7},{6,4},{7,5},{8,10},{9,11},{10,... | collective-permute-start | bytes 368648 | tf_op jit(solution)/shard_map/ppermute | solution.py:141
  54.0 3.4 %collective-permute-done.23 = bf16[320,384]{1,0:T(8,128)(2,1)S(1)} collective-permute-done((bf16[320,384]{1,0:T(8,128)(2,1)S(1)}, bf16[320,384]{1,0:T(8,128)(2,1)S(1)}, u32[]{:S(2)}, u32[]{:S(2)}) %collective-permute-start.23) | collective-permute-done | bytes 245792 | tf_op jit(solution)/shard_map/ppermute | solution.py:141
  70.1 3.6 %collective-permute-done.26 = bf16[320,384]{1,0:T(8,128)(2,1)S(1)} collective-permute-done((bf16[320,384]{1,0:T(8,128)(2,1)S(1)}, bf16[320,384]{1,0:T(8,128)(2,1)S(1)}, u32[]{:S(2)}, u32[]{:S(2)}) %collective-permute-start.26) | collective-permute-done | bytes 245792 | tf_op jit(solution)/shard_map/ppermute | solution.py:124
  74.1 2.1 %collective-permute-start.27 = (bf16[160,384]{1,0:T(8,128)(2,1)S(1)}, bf16[160,384]{1,0:T(8,128)(2,1)S(1)}, u32[]{:S(2)}, u32[]{:S(2)}) collective-permute-start(bf16[160,384]{1,0:T(8,128)(2,1)S(1)} %add_convert_fusion.5), channel_id=1, source_target_pairs={{0,2},{1,3},{2,0},{3,1},{4,6},{5,7},{6,4},{7,5},{8,10},{9,11},{10,... | collective-permute-start | bytes 368648 | tf_op jit(solution)/shard_map/ppermute | solution.py:124
  77.3 2.9 %collective-permute-done.13 = bf16[320,384]{1,0:T(8,128)(2,1)S(1)} collective-permute-done((bf16[320,384]{1,0:T(8,128)(2,1)S(1)}, bf16[320,384]{1,0:T(8,128)(2,1)S(1)}, u32[]{:S(2)}, u32[]{:S(2)}) %collective-permute-start.13) | collective-permute-done | bytes 245792 | tf_op jit(solution)/shard_map/ppermute | solution.py:124
  81.3 1.5 %collective-permute-start.12 = (bf16[160,384]{1,0:T(8,128)(2,1)S(1)}, bf16[160,384]{1,0:T(8,128)(2,1)S(1)}, u32[]{:S(2)}, u32[]{:S(2)}) collective-permute-start(bf16[160,384]{1,0:T(8,128)(2,1)S(1)} %add_convert_fusion.9), channel_id=1, source_target_pairs={{0,2},{1,3},{2,0},{3,1},{4,6},{5,7},{6,4},{7,5},{8,10},{9,11},{10,... | collective-permute-start | bytes 368648 | tf_op jit(solution)/shard_map/ppermute | solution.py:124
  82.9 4.2 %collective-permute-start.30 = (bf16[40,768]{1,0:T(8,128)(2,1)S(1)}, bf16[40,768]{1,0:T(8,128)(2,1)S(1)}, u32[]{:S(2)}, u32[]{:S(2)}) collective-permute-start(bf16[40,768]{1,0:T(8,128)(2,1)S(1)} %get-tuple-element.25), channel_id=1, source_target_pairs={{0,16},{4,20},{8,24},{12,28},{16,0},{20,4},{24,8},{28,12},{1,17},{... | collective-permute-start | bytes 184328 | tf_op jit(solution)/shard_map/ppermute | solution.py:168
  87.3 1.5 %collective-permute-start.16 = (bf16[40,768]{1,0:T(8,128)(2,1)S(1)}, bf16[40,768]{1,0:T(8,128)(2,1)S(1)}, u32[]{:S(2)}, u32[]{:S(2)}) collective-permute-start(bf16[40,768]{1,0:T(8,128)(2,1)S(1)} %get-tuple-element.32), channel_id=1, source_target_pairs={{0,8},{4,12},{8,0},{12,4},{16,24},{20,28},{24,16},{28,20},{1,9},{5... | collective-permute-start | bytes 184328 | tf_op jit(solution)/shard_map/ppermute | solution.py:168
  89.2 3.1 %collective-permute-start.31 = (bf16[40,768]{1,0:T(8,128)(2,1)S(1)}, bf16[40,768]{1,0:T(8,128)(2,1)S(1)}, u32[]{:S(2)}, u32[]{:S(2)}) collective-permute-start(bf16[40,768]{1,0:T(8,128)(2,1)S(1)} %get-tuple-element.26), channel_id=1, source_target_pairs={{0,20},{4,16},{8,28},{12,24},{16,4},{20,0},{24,12},{28,8},{1,21},{... | collective-permute-start | bytes 184328 | tf_op jit(solution)/shard_map/ppermute | solution.py:168
  93.2 2.5 %collective-permute-start.33 = (bf16[40,768]{1,0:T(8,128)(2,1)S(1)}, bf16[40,768]{1,0:T(8,128)(2,1)S(1)}, u32[]{:S(2)}, u32[]{:S(2)}) collective-permute-start(bf16[40,768]{1,0:T(8,128)(2,1)S(1)} %get-tuple-element.24), channel_id=1, source_target_pairs={{0,28},{4,24},{8,20},{12,16},{16,12},{20,8},{24,4},{28,0},{1,29},{... | collective-permute-start | bytes 184328 | tf_op jit(solution)/shard_map/ppermute | solution.py:168
  95.8 3.0 %collective-permute-done.32 = bf16[40,768]{1,0:T(8,128)(2,1)S(1)} collective-permute-done((bf16[40,768]{1,0:T(8,128)(2,1)S(1)}, bf16[40,768]{1,0:T(8,128)(2,1)S(1)}, u32[]{:S(2)}, u32[]{:S(2)}) %collective-permute-start.32) | collective-permute-done | bytes 61472 | tf_op jit(solution)/shard_map/ppermute | solution.py:168
  (151 shorter events, 35.2 us)
Async XLA Ops:
  7.2 12.3 %collective-permute-start.1 = (bf16[256,768]{1,0:T(8,128)(2,1)}, bf16[256,768]{1,0:T(8,128)(2,1)S(1)}, u32[]{:S(2)}, u32[]{:S(2)}) collective-permute-start(bf16[256,768]{1,0:T(8,128)(2,1)} %pad_maximum_fusion.1), channel_id=1, source_target_pairs={{0,2},{1,3},{2,0},{3,1},{4,6},{5,7},{6,4},{7,5},{8,10},{9,11},{10,... | collective-permute-start | bytes 1179656 | tf_op jit(solution)/shard_map/ppermute | solution.py:91
  10.1 10.8 %collective-permute-start = (bf16[256,768]{1,0:T(8,128)(2,1)}, bf16[256,768]{1,0:T(8,128)(2,1)S(1)}, u32[]{:S(2)}, u32[]{:S(2)}) collective-permute-start(bf16[256,768]{1,0:T(8,128)(2,1)} %pad_maximum_fusion), channel_id=1, source_target_pairs={{0,1},{1,0},{2,3},{3,2},{4,5},{5,4},{6,7},{7,6},{8,9},{9,8},{10,11... | collective-permute-start | bytes 1179656 | tf_op jit(solution)/shard_map/ppermute | solution.py:91
  28.8 6.8 %collective-permute-start.18 = (bf16[40,768]{1,0:T(8,128)(2,1)S(1)}, bf16[40,768]{1,0:T(8,128)(2,1)S(1)}, u32[]{:S(2)}, u32[]{:S(2)}) collective-permute-start(bf16[40,768]{1,0:T(8,128)(2,1)S(1)} %get-tuple-element.19), channel_id=1, source_target_pairs={{0,16},{4,20},{8,24},{12,28},{16,0},{20,4},{24,8},{28,12},{1,17},{... | collective-permute-start | bytes 184328 | tf_op jit(solution)/shard_map/ppermute | solution.py:158
  31.6 8.1 %collective-permute-start.19 = (bf16[40,768]{1,0:T(8,128)(2,1)S(1)}, bf16[40,768]{1,0:T(8,128)(2,1)S(1)}, u32[]{:S(2)}, u32[]{:S(2)}) collective-permute-start(bf16[40,768]{1,0:T(8,128)(2,1)S(1)} %get-tuple-element.18), channel_id=1, source_target_pairs={{0,20},{4,16},{8,28},{12,24},{16,4},{20,0},{24,12},{28,8},{1,21},{... | collective-permute-start | bytes 184328 | tf_op jit(solution)/shard_map/ppermute | solution.py:158
  31.6 8.2 %collective-permute-start.20 = (bf16[40,768]{1,0:T(8,128)(2,1)S(1)}, bf16[40,768]{1,0:T(8,128)(2,1)S(1)}, u32[]{:S(2)}, u32[]{:S(2)}) collective-permute-start(bf16[40,768]{1,0:T(8,128)(2,1)S(1)} %get-tuple-element.17), channel_id=1, source_target_pairs={{0,24},{4,28},{8,16},{12,20},{16,8},{20,12},{24,0},{28,4},{1,25},{... | collective-permute-start | bytes 184328 | tf_op jit(solution)/shard_map/ppermute | solution.py:158
  33.0 6.8 %collective-permute-start.21 = (bf16[40,768]{1,0:T(8,128)(2,1)S(1)}, bf16[40,768]{1,0:T(8,128)(2,1)S(1)}, u32[]{:S(2)}, u32[]{:S(2)}) collective-permute-start(bf16[40,768]{1,0:T(8,128)(2,1)S(1)} %get-tuple-element.16), channel_id=1, source_target_pairs={{0,28},{4,24},{8,20},{12,16},{16,12},{20,8},{24,4},{28,0},{1,29},{... | collective-permute-start | bytes 184328 | tf_op jit(solution)/shard_map/ppermute | solution.py:158
  35.3 8.2 %collective-permute-start.4 = (bf16[40,768]{1,0:T(8,128)(2,1)S(1)}, bf16[40,768]{1,0:T(8,128)(2,1)S(1)}, u32[]{:S(2)}, u32[]{:S(2)}) collective-permute-start(bf16[40,768]{1,0:T(8,128)(2,1)S(1)} %get-tuple-element.22), channel_id=1, source_target_pairs={{0,4},{4,0},{8,12},{12,8},{16,20},{20,16},{24,28},{28,24},{1,5},{5... | collective-permute-start | bytes 184328 | tf_op jit(solution)/shard_map/ppermute | solution.py:158
  35.6 7.8 %collective-permute-start.5 = (bf16[40,768]{1,0:T(8,128)(2,1)S(1)}, bf16[40,768]{1,0:T(8,128)(2,1)S(1)}, u32[]{:S(2)}, u32[]{:S(2)}) collective-permute-start(bf16[40,768]{1,0:T(8,128)(2,1)S(1)} %get-tuple-element.21), channel_id=1, source_target_pairs={{0,8},{4,12},{8,0},{12,4},{16,24},{20,28},{24,16},{28,20},{1,9},{5... | collective-permute-start | bytes 184328 | tf_op jit(solution)/shard_map/ppermute | solution.py:158
  39.9 7.6 %collective-permute-start.22 = (bf16[160,384]{1,0:T(8,128)(2,1)S(1)}, bf16[160,384]{1,0:T(8,128)(2,1)S(1)}, u32[]{:S(2)}, u32[]{:S(2)}) collective-permute-start(bf16[160,384]{1,0:T(8,128)(2,1)S(1)} %get-tuple-element.28), channel_id=1, source_target_pairs={{0,1},{1,0},{2,3},{3,2},{4,5},{5,4},{6,7},{7,6},{8,9},{9,8},{10,11... | collective-permute-start | bytes 368648 | tf_op jit(solution)/shard_map/ppermute | solution.py:141
  41.6 6.4 %collective-permute-start.24 = (bf16[160,384]{1,0:T(8,128)(2,1)S(1)}, bf16[160,384]{1,0:T(8,128)(2,1)S(1)}, u32[]{:S(2)}, u32[]{:S(2)}) collective-permute-start(bf16[160,384]{1,0:T(8,128)(2,1)S(1)} %get-tuple-element.29), channel_id=1, source_target_pairs={{0,2},{1,3},{2,0},{3,1},{4,6},{5,7},{6,4},{7,5},{8,10},{9,11},{10,... | collective-permute-start | bytes 368648 | tf_op jit(solution)/shard_map/ppermute | solution.py:141
  47.5 9.9 %collective-permute-start.23 = (bf16[320,384]{1,0:T(8,128)(2,1)S(1)}, bf16[320,384]{1,0:T(8,128)(2,1)S(1)}, u32[]{:S(2)}, u32[]{:S(2)}) collective-permute-start(bf16[320,384]{1,0:T(8,128)(2,1)S(1)} %pad_maximum_fusion.7), channel_id=1, source_target_pairs={{0,2},{1,3},{2,0},{3,1},{4,6},{5,7},{6,4},{7,5},{8,10},{9,11},{10,... | collective-permute-start | bytes 737288 | tf_op jit(solution)/shard_map/ppermute | solution.py:141
  48.1 9.9 %collective-permute-start.25 = (bf16[320,384]{1,0:T(8,128)(2,1)S(1)}, bf16[320,384]{1,0:T(8,128)(2,1)S(1)}, u32[]{:S(2)}, u32[]{:S(2)}) collective-permute-start(bf16[320,384]{1,0:T(8,128)(2,1)S(1)} %pad_maximum_fusion.8), channel_id=1, source_target_pairs={{0,1},{1,0},{2,3},{3,2},{4,5},{5,4},{6,7},{7,6},{8,9},{9,8},{10,11... | collective-permute-start | bytes 737288 | tf_op jit(solution)/shard_map/ppermute | solution.py:141
  50.1 11.2 %collective-permute-start.8 = (bf16[320,384]{1,0:T(8,128)(2,1)S(1)}, bf16[320,384]{1,0:T(8,128)(2,1)S(1)}, u32[]{:S(2)}, u32[]{:S(2)}) collective-permute-start(bf16[320,384]{1,0:T(8,128)(2,1)S(1)} %pad_maximum_fusion.3), channel_id=1, source_target_pairs={{0,2},{1,3},{2,0},{3,1},{4,6},{5,7},{6,4},{7,5},{8,10},{9,11},{10,... | collective-permute-start | bytes 737288 | tf_op jit(solution)/shard_map/ppermute | solution.py:141
  52.1 10.1 %collective-permute-start.10 = (bf16[320,384]{1,0:T(8,128)(2,1)S(1)}, bf16[320,384]{1,0:T(8,128)(2,1)S(1)}, u32[]{:S(2)}, u32[]{:S(2)}) collective-permute-start(bf16[320,384]{1,0:T(8,128)(2,1)S(1)} %pad_maximum_fusion.4), channel_id=1, source_target_pairs={{0,1},{1,0},{2,3},{3,2},{4,5},{5,4},{6,7},{7,6},{8,9},{9,8},{10,11... | collective-permute-start | bytes 737288 | tf_op jit(solution)/shard_map/ppermute | solution.py:141
  65.4 8.4 %collective-permute-start.26 = (bf16[320,384]{1,0:T(8,128)(2,1)S(1)}, bf16[320,384]{1,0:T(8,128)(2,1)S(1)}, u32[]{:S(2)}, u32[]{:S(2)}) collective-permute-start(bf16[320,384]{1,0:T(8,128)(2,1)S(1)} %pad_maximum_fusion.9), channel_id=1, source_target_pairs={{0,1},{1,0},{2,3},{3,2},{4,5},{5,4},{6,7},{7,6},{8,9},{9,8},{10,11... | collective-permute-start | bytes 737288 | tf_op jit(solution)/shard_map/ppermute | solution.py:124
  66.5 9.7 %collective-permute-start.28 = (bf16[320,384]{1,0:T(8,128)(2,1)S(1)}, bf16[320,384]{1,0:T(8,128)(2,1)S(1)}, u32[]{:S(2)}, u32[]{:S(2)}) collective-permute-start(bf16[320,384]{1,0:T(8,128)(2,1)S(1)} %pad_maximum_fusion.10), channel_id=1, source_target_pairs={{0,2},{1,3},{2,0},{3,1},{4,6},{5,7},{6,4},{7,5},{8,10},{9,11},{10,... | collective-permute-start | bytes 737288 | tf_op jit(solution)/shard_map/ppermute | solution.py:124
  67.6 12.5 %collective-permute-start.13 = (bf16[320,384]{1,0:T(8,128)(2,1)S(1)}, bf16[320,384]{1,0:T(8,128)(2,1)S(1)}, u32[]{:S(2)}, u32[]{:S(2)}) collective-permute-start(bf16[320,384]{1,0:T(8,128)(2,1)S(1)} %pad_maximum_fusion.6), channel_id=1, source_target_pairs={{0,2},{1,3},{2,0},{3,1},{4,6},{5,7},{6,4},{7,5},{8,10},{9,11},{10,... | collective-permute-start | bytes 737288 | tf_op jit(solution)/shard_map/ppermute | solution.py:124
  69.1 11.9 %collective-permute-start.11 = (bf16[320,384]{1,0:T(8,128)(2,1)S(1)}, bf16[320,384]{1,0:T(8,128)(2,1)S(1)}, u32[]{:S(2)}, u32[]{:S(2)}) collective-permute-start(bf16[320,384]{1,0:T(8,128)(2,1)S(1)} %pad_maximum_fusion.5), channel_id=1, source_target_pairs={{0,1},{1,0},{2,3},{3,2},{4,5},{5,4},{6,7},{7,6},{8,9},{9,8},{10,11... | collective-permute-start | bytes 737288 | tf_op jit(solution)/shard_map/ppermute | solution.py:124
  74.1 8.7 %collective-permute-start.27 = (bf16[160,384]{1,0:T(8,128)(2,1)S(1)}, bf16[160,384]{1,0:T(8,128)(2,1)S(1)}, u32[]{:S(2)}, u32[]{:S(2)}) collective-permute-start(bf16[160,384]{1,0:T(8,128)(2,1)S(1)} %add_convert_fusion.5), channel_id=1, source_target_pairs={{0,2},{1,3},{2,0},{3,1},{4,6},{5,7},{6,4},{7,5},{8,10},{9,11},{10,... | collective-permute-start | bytes 368648 | tf_op jit(solution)/shard_map/ppermute | solution.py:124
  80.5 6.6 %collective-permute-start.14 = (bf16[160,384]{1,0:T(8,128)(2,1)S(1)}, bf16[160,384]{1,0:T(8,128)(2,1)S(1)}, u32[]{:S(2)}, u32[]{:S(2)}) collective-permute-start(bf16[160,384]{1,0:T(8,128)(2,1)S(1)} %add_convert_fusion.7), channel_id=1, source_target_pairs={{0,1},{1,0},{2,3},{3,2},{4,5},{5,4},{6,7},{7,6},{8,9},{9,8},{10,11... | collective-permute-start | bytes 368648 | tf_op jit(solution)/shard_map/ppermute | solution.py:124
  82.9 12.8 %collective-permute-start.30 = (bf16[40,768]{1,0:T(8,128)(2,1)S(1)}, bf16[40,768]{1,0:T(8,128)(2,1)S(1)}, u32[]{:S(2)}, u32[]{:S(2)}) collective-permute-start(bf16[40,768]{1,0:T(8,128)(2,1)S(1)} %get-tuple-element.25), channel_id=1, source_target_pairs={{0,16},{4,20},{8,24},{12,28},{16,0},{20,4},{24,8},{28,12},{1,17},{... | collective-permute-start | bytes 184328 | tf_op jit(solution)/shard_map/ppermute | solution.py:168
  88.8 6.9 %collective-permute-start.17 = (bf16[40,768]{1,0:T(8,128)(2,1)S(1)}, bf16[40,768]{1,0:T(8,128)(2,1)S(1)}, u32[]{:S(2)}, u32[]{:S(2)}) collective-permute-start(bf16[40,768]{1,0:T(8,128)(2,1)S(1)} %get-tuple-element.30), channel_id=1, source_target_pairs={{0,12},{4,8},{8,4},{12,0},{16,28},{20,24},{24,20},{28,16},{1,13},{... | collective-permute-start | bytes 184328 | tf_op jit(solution)/shard_map/ppermute | solution.py:168
  89.2 6.6 %collective-permute-start.31 = (bf16[40,768]{1,0:T(8,128)(2,1)S(1)}, bf16[40,768]{1,0:T(8,128)(2,1)S(1)}, u32[]{:S(2)}, u32[]{:S(2)}) collective-permute-start(bf16[40,768]{1,0:T(8,128)(2,1)S(1)} %get-tuple-element.26), channel_id=1, source_target_pairs={{0,20},{4,16},{8,28},{12,24},{16,4},{20,0},{24,12},{28,8},{1,21},{... | collective-permute-start | bytes 184328 | tf_op jit(solution)/shard_map/ppermute | solution.py:168
  92.3 6.5 %collective-permute-start.32 = (bf16[40,768]{1,0:T(8,128)(2,1)S(1)}, bf16[40,768]{1,0:T(8,128)(2,1)S(1)}, u32[]{:S(2)}, u32[]{:S(2)}) collective-permute-start(bf16[40,768]{1,0:T(8,128)(2,1)S(1)} %get-tuple-element.27), channel_id=1, source_target_pairs={{0,24},{4,28},{8,16},{12,20},{16,8},{20,12},{24,0},{28,4},{1,25},{... | collective-permute-start | bytes 184328 | tf_op jit(solution)/shard_map/ppermute | solution.py:168
  (17 other events, 170.4 us)

commit v9 on v8

--- a/solution.py
+++ b/solution.py
@@ -202,7 +202,7 @@
             rows = head_rows[h * row_half:(h + 1) * row_half]
             return lax.dynamic_slice_in_dim(rows, (me_t ^ d) * width, width, axis=1)
 
-        summed = jnp.concatenate(reduce_scatter_tree(head_half, "tensor", tensor_count), axis=0)
+        summed = jnp.concatenate(reduce_scatter_free(head_half, "tensor", tensor_count), axis=0)
         summed = summed + residual_in.astype(jnp.float32)
     else:
         received = [

time: 102 us -> 101 us (level)
  waiting for transfers between devices: 28 us -> 26.8 us
    ppermute x4 -> x0, waiting for transfers between devices: 11.8 us -> none  [reduce_scatter_tree(): got = lax.ppermute(payloads[h], axis, [(i, i ^ bit) for i in range(n)])]
    ppermute x8 -> x12, waiting for transfers between devices: 6.52 us -> 17 us  [reduce_scatter_free(): got = lax.ppermute(payload, axis, [(i, i ^ bit) for i in range(n)])]
    ppermute x8 -> x12, starting transfers between devices: 8.98 us -> 16.9 us  [reduce_scatter_free(): got = lax.ppermute(payload, axis, [(i, i ^ bit) for i in range(n)])]
    ppermute x4 -> x0, starting transfers between devices: 6.54 us -> none  [reduce_scatter_tree(): got = lax.ppermute(payloads[h], axis, [(i, i ^ bit) for i in range(n)])]
    concatenate x4 -> x6, other arithmetic: 0.11 us -> 1.65 us  [reduce_scatter_free(): jnp.concatenate([held[d].astype(jnp.bfloat16) for d in send], axis=0)]
    concatenate x2 -> x0, other arithmetic: 1.54 us -> none  [reduce_scatter_tree(): jnp.concatenate([helds[h][d].astype(jnp.bfloat16) for d in send], axis=0)]
    ppermute x7, waiting for transfers between devices: 0.42 us -> 1.75 us  [dispatch_rows(): got.append(lax.ppermute(chunk, axis, [(i, i ^ s) for i in range(n)]))]
    ppermute x8, waiting for transfers between devices: 5.62 us -> 4.45 us  [all_gather_free(): got = lax.ppermute(payload, axis, [(i, i ^ bit) for i in range(n)])]
  transfers between devices with their start and end apart: 34 -> 34, of which waited for: 13 -> 13; matrix products, arithmetic and copies ran while one was open for 10% -> 11% of each run, Pallas kernels for 0% -> 0%
where the time goes in v9:
time: 101 us; the launch traced here: 100 us
  starting transfers between devices  49.2 us (49%)
  waiting for transfers between devices  26.8 us (27%)
  matrix products  16.5 us (16%)
  other arithmetic  4.28 us (4%)
  local copies, waits for them, and re-layouts  2.34 us (2%)
  between operations  1.31 us (1%)
    ppermute x12, waiting for transfers between devices, reduce_scatter_free(): got = lax.ppermute(payload, axis, [(i, i ^ bit) for i in range(n)])  17 us
    ppermute x12, starting transfers between devices, reduce_scatter_free(): got = lax.ppermute(payload, axis, [(i, i ^ bit) for i in range(n)])  16.9 us
    ppermute x7, starting transfers between devices, collect_rows(): lax.ppermute(parts[s], axis, [(i, i ^ s) for i in range(n)])  12.3 us
    ppermute x7, starting transfers between devices, dispatch_rows(): got.append(lax.ppermute(chunk, axis, [(i, i ^ s) for i in range(n)]))  11 us
    ppermute x8, starting transfers between devices, all_gather_free(): got = lax.ppermute(payload, axis, [(i, i ^ bit) for i in range(n)])  9.03 us
    dot_general x16, matrix products, back_half(): lax.dot_general(pre_grad, rows_w, (((1,), (1,)), ((), ())), preferred_ele...  5.76 us
    dot_general x16, matrix products, shards(): term = jnp.dot(held[h][d], rows_w, preferred_element_type=jnp.float32)  5.37 us
    ppermute x8, waiting for transfers between devices, all_gather_free(): got = lax.ppermute(payload, axis, [(i, i ^ bit) for i in range(n)])  4.45 us
  transfers between devices with their start and end apart: 34, of which 13 were waited for; matrix products, arithmetic and copies ran while one was open for 11% of the time, Pallas kernels for 0%

profile of v9, /device:TPU:0, one launch (start us, length us, event | category | flops | bytes accessed | tf_op | source)
XLA Modules:
  0.0 100.4 jit_solution(14504481603627973423)
XLA Ops:
  1.6 3.7 %convolution_convert_fusion = bf16[256,3072]{1,0:T(8,128)(2,1)S(1)} fusion(bf16[256,768]{1,0:T(8,128)(2,1)S(1)} %copy-done, bf16[768,3072]{1,0:T(8,128)(2,1)} %param.9), kind=kOutput, calls=%fused_computation.1 | convolution fusion | flops 1208745984 | bytes 6684672 | tf_op jit(solution)/shard_map/dot_general | solution.py:198
  6.4 2.9 %collective-permute-start = (bf16[256,768]{1,0:T(8,128)(2,1)}, bf16[256,768]{1,0:T(8,128)(2,1)S(1)}, u32[]{:S(2)}, u32[]{:S(2)}) collective-permute-start(bf16[256,768]{1,0:T(8,128)(2,1)} %pad_maximum_fusion), channel_id=1, source_target_pairs={{0,1},{1,0},{2,3},{3,2},{4,5},{5,4},{6,7},{7,6},{8,9},{9,8},{10,11... | collective-permute-start | bytes 1179656 | tf_op jit(solution)/shard_map/ppermute | solution.py:124
  10.1 1.5 %collective-permute-start.2 = (bf16[256,768]{1,0:T(8,128)(2,1)}, bf16[256,768]{1,0:T(8,128)(2,1)S(1)}, u32[]{:S(2)}, u32[]{:S(2)}) collective-permute-start(bf16[256,768]{1,0:T(8,128)(2,1)} %pad_maximum_fusion.1), channel_id=1, source_target_pairs={{0,2},{1,3},{2,0},{3,1},{4,6},{5,7},{6,4},{7,5},{8,10},{9,11},{10,... | collective-permute-start | bytes 1179656 | tf_op jit(solution)/shard_map/ppermute | solution.py:124
  13.0 5.6 %collective-permute-done = bf16[256,768]{1,0:T(8,128)(2,1)S(1)} collective-permute-done((bf16[256,768]{1,0:T(8,128)(2,1)}, bf16[256,768]{1,0:T(8,128)(2,1)S(1)}, u32[]{:S(2)}, u32[]{:S(2)}) %collective-permute-start) | collective-permute-done | bytes 393248 | tf_op jit(solution)/shard_map/ppermute | solution.py:124
  18.7 1.8 %collective-permute-start.1 = (bf16[128,768]{1,0:T(8,128)(2,1)S(1)}, bf16[128,768]{1,0:T(8,128)(2,1)S(1)}, u32[]{:S(2)}, u32[]{:S(2)}) collective-permute-start(bf16[128,768]{1,0:T(8,128)(2,1)S(1)} %add_convert_fusion.1), channel_id=1, source_target_pairs={{0,2},{1,3},{2,0},{3,1},{4,6},{5,7},{6,4},{7,5},{8,10},{9,11},{10,... | collective-permute-start | bytes 589832 | tf_op jit(solution)/shard_map/ppermute | solution.py:124
  22.1 3.0 %collective-permute-done.1 = bf16[128,768]{1,0:T(8,128)(2,1)S(1)} collective-permute-done((bf16[128,768]{1,0:T(8,128)(2,1)S(1)}, bf16[128,768]{1,0:T(8,128)(2,1)S(1)}, u32[]{:S(2)}, u32[]{:S(2)}) %collective-permute-start.1) | collective-permute-done | bytes 196640 | tf_op jit(solution)/shard_map/ppermute | solution.py:124
  25.2 1.7 %collective-permute-done.3 = bf16[128,768]{1,0:T(8,128)(2,1)S(1)} collective-permute-done((bf16[128,768]{1,0:T(8,128)(2,1)S(1)}, bf16[128,768]{1,0:T(8,128)(2,1)S(1)}, u32[]{:S(2)}, u32[]{:S(2)}) %collective-permute-start.3) | collective-permute-done | bytes 196640 | tf_op jit(solution)/shard_map/ppermute | solution.py:124
  28.6 2.7 %collective-permute-start.18 = (bf16[40,768]{1,0:T(8,128)(2,1)S(1)}, bf16[40,768]{1,0:T(8,128)(2,1)S(1)}, u32[]{:S(2)}, u32[]{:S(2)}) collective-permute-start(bf16[40,768]{1,0:T(8,128)(2,1)S(1)} %get-tuple-element.11), channel_id=1, source_target_pairs={{0,16},{4,20},{8,24},{12,28},{16,0},{20,4},{24,8},{28,12},{1,17},{... | collective-permute-start | bytes 184328 | tf_op jit(solution)/shard_map/ppermute | solution.py:158
  31.3 1.4 %collective-permute-start.20 = (bf16[40,768]{1,0:T(8,128)(2,1)S(1)}, bf16[40,768]{1,0:T(8,128)(2,1)S(1)}, u32[]{:S(2)}, u32[]{:S(2)}) collective-permute-start(bf16[40,768]{1,0:T(8,128)(2,1)S(1)} %get-tuple-element.9), channel_id=1, source_target_pairs={{0,24},{4,28},{8,16},{12,20},{16,8},{20,12},{24,0},{28,4},{1,25},{... | collective-permute-start | bytes 184328 | tf_op jit(solution)/shard_map/ppermute | solution.py:158
  32.7 2.3 %collective-permute-start.21 = (bf16[40,768]{1,0:T(8,128)(2,1)S(1)}, bf16[40,768]{1,0:T(8,128)(2,1)S(1)}, u32[]{:S(2)}, u32[]{:S(2)}) collective-permute-start(bf16[40,768]{1,0:T(8,128)(2,1)S(1)} %get-tuple-element.8), channel_id=1, source_target_pairs={{0,28},{4,24},{8,20},{12,16},{16,12},{20,8},{24,4},{28,0},{1,29},{... | collective-permute-start | bytes 184328 | tf_op jit(solution)/shard_map/ppermute | solution.py:158
  35.3 4.2 %collective-permute-start.5 = (bf16[40,768]{1,0:T(8,128)(2,1)S(1)}, bf16[40,768]{1,0:T(8,128)(2,1)S(1)}, u32[]{:S(2)}, u32[]{:S(2)}) collective-permute-start(bf16[40,768]{1,0:T(8,128)(2,1)S(1)} %get-tuple-element.13), channel_id=1, source_target_pairs={{0,8},{4,12},{8,0},{12,4},{16,24},{20,28},{24,16},{28,20},{1,9},{5... | collective-permute-start | bytes 184328 | tf_op jit(solution)/shard_map/ppermute | solution.py:158
  41.9 1.7 %collective-permute-done.6 = bf16[40,768]{1,0:T(8,128)(2,1)S(1)} collective-permute-done((bf16[40,768]{1,0:T(8,128)(2,1)S(1)}, bf16[40,768]{1,0:T(8,128)(2,1)S(1)}, u32[]{:S(2)}, u32[]{:S(2)}) %collective-permute-start.6) | collective-permute-done | bytes 61472 | tf_op jit(solution)/shard_map/ppermute | solution.py:158
  49.2 1.7 %collective-permute-start.8 = (bf16[320,384]{1,0:T(8,128)(2,1)S(1)}, bf16[320,384]{1,0:T(8,128)(2,1)S(1)}, u32[]{:S(2)}, u32[]{:S(2)}) collective-permute-start(bf16[320,384]{1,0:T(8,128)(2,1)S(1)} %pad_maximum_fusion.3), channel_id=1, source_target_pairs={{0,2},{1,3},{2,0},{3,1},{4,6},{5,7},{6,4},{7,5},{8,10},{9,11},{10,... | collective-permute-start | bytes 737288 | tf_op jit(solution)/shard_map/ppermute | solution.py:141
  53.6 2.9 %collective-permute-done.23 = bf16[320,384]{1,0:T(8,128)(2,1)S(1)} collective-permute-done((bf16[320,384]{1,0:T(8,128)(2,1)S(1)}, bf16[320,384]{1,0:T(8,128)(2,1)S(1)}, u32[]{:S(2)}, u32[]{:S(2)}) %collective-permute-start.23) | collective-permute-done | bytes 245792 | tf_op jit(solution)/shard_map/ppermute | solution.py:141
  65.7 1.6 %collective-permute-start.28 = (bf16[320,384]{1,0:T(8,128)(2,1)S(1)}, bf16[320,384]{1,0:T(8,128)(2,1)S(1)}, u32[]{:S(2)}, u32[]{:S(2)}) collective-permute-start(bf16[320,384]{1,0:T(8,128)(2,1)S(1)} %pad_maximum_fusion.10), channel_id=1, source_target_pairs={{0,2},{1,3},{2,0},{3,1},{4,6},{5,7},{6,4},{7,5},{8,10},{9,11},{10,... | collective-permute-start | bytes 737288 | tf_op jit(solution)/shard_map/ppermute | solution.py:124
  69.4 4.2 %collective-permute-done.26 = bf16[320,384]{1,0:T(8,128)(2,1)S(1)} collective-permute-done((bf16[320,384]{1,0:T(8,128)(2,1)S(1)}, bf16[320,384]{1,0:T(8,128)(2,1)S(1)}, u32[]{:S(2)}, u32[]{:S(2)}) %collective-permute-start.26) | collective-permute-done | bytes 245792 | tf_op jit(solution)/shard_map/ppermute | solution.py:124
  75.2 1.6 %collective-permute-start.29 = (bf16[160,384]{1,0:T(8,128)(2,1)S(1)}, bf16[160,384]{1,0:T(8,128)(2,1)S(1)}, u32[]{:S(2)}, u32[]{:S(2)}) collective-permute-start(bf16[160,384]{1,0:T(8,128)(2,1)S(1)} %add_convert_fusion.3), channel_id=1, source_target_pairs={{0,1},{1,0},{2,3},{3,2},{4,5},{5,4},{6,7},{7,6},{8,9},{9,8},{10,11... | collective-permute-start | bytes 368648 | tf_op jit(solution)/shard_map/ppermute | solution.py:124
  76.8 1.9 %collective-permute-done.13 = bf16[320,384]{1,0:T(8,128)(2,1)S(1)} collective-permute-done((bf16[320,384]{1,0:T(8,128)(2,1)S(1)}, bf16[320,384]{1,0:T(8,128)(2,1)S(1)}, u32[]{:S(2)}, u32[]{:S(2)}) %collective-permute-start.13) | collective-permute-done | bytes 245792 | tf_op jit(solution)/shard_map/ppermute | solution.py:124
  80.7 1.5 %collective-permute-start.12 = (bf16[160,384]{1,0:T(8,128)(2,1)S(1)}, bf16[160,384]{1,0:T(8,128)(2,1)S(1)}, u32[]{:S(2)}, u32[]{:S(2)}) collective-permute-start(bf16[160,384]{1,0:T(8,128)(2,1)S(1)} %add_convert_fusion.9), channel_id=1, source_target_pairs={{0,2},{1,3},{2,0},{3,1},{4,6},{5,7},{6,4},{7,5},{8,10},{9,11},{10,... | collective-permute-start | bytes 368648 | tf_op jit(solution)/shard_map/ppermute | solution.py:124
  82.4 3.3 %collective-permute-start.30 = (bf16[40,768]{1,0:T(8,128)(2,1)S(1)}, bf16[40,768]{1,0:T(8,128)(2,1)S(1)}, u32[]{:S(2)}, u32[]{:S(2)}) collective-permute-start(bf16[40,768]{1,0:T(8,128)(2,1)S(1)} %get-tuple-element.17), channel_id=1, source_target_pairs={{0,16},{4,20},{8,24},{12,28},{16,0},{20,4},{24,8},{28,12},{1,17},{... | collective-permute-start | bytes 184328 | tf_op jit(solution)/shard_map/ppermute | solution.py:168
  85.9 1.7 %collective-permute-start.16 = (bf16[40,768]{1,0:T(8,128)(2,1)S(1)}, bf16[40,768]{1,0:T(8,128)(2,1)S(1)}, u32[]{:S(2)}, u32[]{:S(2)}) collective-permute-start(bf16[40,768]{1,0:T(8,128)(2,1)S(1)} %get-tuple-element.24), channel_id=1, source_target_pairs={{0,8},{4,12},{8,0},{12,4},{16,24},{20,28},{24,16},{28,20},{1,9},{5... | collective-permute-start | bytes 184328 | tf_op jit(solution)/shard_map/ppermute | solution.py:168
  87.7 3.7 %collective-permute-start.31 = (bf16[40,768]{1,0:T(8,128)(2,1)S(1)}, bf16[40,768]{1,0:T(8,128)(2,1)S(1)}, u32[]{:S(2)}, u32[]{:S(2)}) collective-permute-start(bf16[40,768]{1,0:T(8,128)(2,1)S(1)} %get-tuple-element.18), channel_id=1, source_target_pairs={{0,20},{4,16},{8,28},{12,24},{16,4},{20,0},{24,12},{28,8},{1,21},{... | collective-permute-start | bytes 184328 | tf_op jit(solution)/shard_map/ppermute | solution.py:168
  92.3 2.6 %collective-permute-start.33 = (bf16[40,768]{1,0:T(8,128)(2,1)S(1)}, bf16[40,768]{1,0:T(8,128)(2,1)S(1)}, u32[]{:S(2)}, u32[]{:S(2)}) collective-permute-start(bf16[40,768]{1,0:T(8,128)(2,1)S(1)} %get-tuple-element.16), channel_id=1, source_target_pairs={{0,28},{4,24},{8,20},{12,16},{16,12},{20,8},{24,4},{28,0},{1,29},{... | collective-permute-start | bytes 184328 | tf_op jit(solution)/shard_map/ppermute | solution.py:168
  95.0 2.9 %collective-permute-done.32 = bf16[40,768]{1,0:T(8,128)(2,1)S(1)} collective-permute-done((bf16[40,768]{1,0:T(8,128)(2,1)S(1)}, bf16[40,768]{1,0:T(8,128)(2,1)S(1)}, u32[]{:S(2)}, u32[]{:S(2)}) %collective-permute-start.32) | collective-permute-done | bytes 61472 | tf_op jit(solution)/shard_map/ppermute | solution.py:168
  (152 shorter events, 36.8 us)
Async XLA Ops:
  6.4 12.3 %collective-permute-start = (bf16[256,768]{1,0:T(8,128)(2,1)}, bf16[256,768]{1,0:T(8,128)(2,1)S(1)}, u32[]{:S(2)}, u32[]{:S(2)}) collective-permute-start(bf16[256,768]{1,0:T(8,128)(2,1)} %pad_maximum_fusion), channel_id=1, source_target_pairs={{0,1},{1,0},{2,3},{3,2},{4,5},{5,4},{6,7},{7,6},{8,9},{9,8},{10,11... | collective-permute-start | bytes 1179656 | tf_op jit(solution)/shard_map/ppermute | solution.py:124
  10.1 11.0 %collective-permute-start.2 = (bf16[256,768]{1,0:T(8,128)(2,1)}, bf16[256,768]{1,0:T(8,128)(2,1)S(1)}, u32[]{:S(2)}, u32[]{:S(2)}) collective-permute-start(bf16[256,768]{1,0:T(8,128)(2,1)} %pad_maximum_fusion.1), channel_id=1, source_target_pairs={{0,2},{1,3},{2,0},{3,1},{4,6},{5,7},{6,4},{7,5},{8,10},{9,11},{10,... | collective-permute-start | bytes 1179656 | tf_op jit(solution)/shard_map/ppermute | solution.py:124
  28.6 6.7 %collective-permute-start.18 = (bf16[40,768]{1,0:T(8,128)(2,1)S(1)}, bf16[40,768]{1,0:T(8,128)(2,1)S(1)}, u32[]{:S(2)}, u32[]{:S(2)}) collective-permute-start(bf16[40,768]{1,0:T(8,128)(2,1)S(1)} %get-tuple-element.11), channel_id=1, source_target_pairs={{0,16},{4,20},{8,24},{12,28},{16,0},{20,4},{24,8},{28,12},{1,17},{... | collective-permute-start | bytes 184328 | tf_op jit(solution)/shard_map/ppermute | solution.py:158
  31.3 8.2 %collective-permute-start.19 = (bf16[40,768]{1,0:T(8,128)(2,1)S(1)}, bf16[40,768]{1,0:T(8,128)(2,1)S(1)}, u32[]{:S(2)}, u32[]{:S(2)}) collective-permute-start(bf16[40,768]{1,0:T(8,128)(2,1)S(1)} %get-tuple-element.10), channel_id=1, source_target_pairs={{0,20},{4,16},{8,28},{12,24},{16,4},{20,0},{24,12},{28,8},{1,21},{... | collective-permute-start | bytes 184328 | tf_op jit(solution)/shard_map/ppermute | solution.py:158
  31.3 8.3 %collective-permute-start.20 = (bf16[40,768]{1,0:T(8,128)(2,1)S(1)}, bf16[40,768]{1,0:T(8,128)(2,1)S(1)}, u32[]{:S(2)}, u32[]{:S(2)}) collective-permute-start(bf16[40,768]{1,0:T(8,128)(2,1)S(1)} %get-tuple-element.9), channel_id=1, source_target_pairs={{0,24},{4,28},{8,16},{12,20},{16,8},{20,12},{24,0},{28,4},{1,25},{... | collective-permute-start | bytes 184328 | tf_op jit(solution)/shard_map/ppermute | solution.py:158
  32.7 6.9 %collective-permute-start.21 = (bf16[40,768]{1,0:T(8,128)(2,1)S(1)}, bf16[40,768]{1,0:T(8,128)(2,1)S(1)}, u32[]{:S(2)}, u32[]{:S(2)}) collective-permute-start(bf16[40,768]{1,0:T(8,128)(2,1)S(1)} %get-tuple-element.8), channel_id=1, source_target_pairs={{0,28},{4,24},{8,20},{12,16},{16,12},{20,8},{24,4},{28,0},{1,29},{... | collective-permute-start | bytes 184328 | tf_op jit(solution)/shard_map/ppermute | solution.py:158
  35.0 6.9 %collective-permute-start.4 = (bf16[40,768]{1,0:T(8,128)(2,1)S(1)}, bf16[40,768]{1,0:T(8,128)(2,1)S(1)}, u32[]{:S(2)}, u32[]{:S(2)}) collective-permute-start(bf16[40,768]{1,0:T(8,128)(2,1)S(1)} %get-tuple-element.14), channel_id=1, source_target_pairs={{0,4},{4,0},{8,12},{12,8},{16,20},{20,16},{24,28},{28,24},{1,5},{5... | collective-permute-start | bytes 184328 | tf_op jit(solution)/shard_map/ppermute | solution.py:158
  35.3 6.6 %collective-permute-start.5 = (bf16[40,768]{1,0:T(8,128)(2,1)S(1)}, bf16[40,768]{1,0:T(8,128)(2,1)S(1)}, u32[]{:S(2)}, u32[]{:S(2)}) collective-permute-start(bf16[40,768]{1,0:T(8,128)(2,1)S(1)} %get-tuple-element.13), channel_id=1, source_target_pairs={{0,8},{4,12},{8,0},{12,4},{16,24},{20,28},{24,16},{28,20},{1,9},{5... | collective-permute-start | bytes 184328 | tf_op jit(solution)/shard_map/ppermute | solution.py:158
  40.7 6.5 %collective-permute-start.24 = (bf16[160,384]{1,0:T(8,128)(2,1)S(1)}, bf16[160,384]{1,0:T(8,128)(2,1)S(1)}, u32[]{:S(2)}, u32[]{:S(2)}) collective-permute-start(bf16[160,384]{1,0:T(8,128)(2,1)S(1)} %get-tuple-element.21), channel_id=1, source_target_pairs={{0,2},{1,3},{2,0},{3,1},{4,6},{5,7},{6,4},{7,5},{8,10},{9,11},{10,... | collective-permute-start | bytes 368648 | tf_op jit(solution)/shard_map/ppermute | solution.py:141
  46.0 10.5 %collective-permute-start.23 = (bf16[320,384]{1,0:T(8,128)(2,1)S(1)}, bf16[320,384]{1,0:T(8,128)(2,1)S(1)}, u32[]{:S(2)}, u32[]{:S(2)}) collective-permute-start(bf16[320,384]{1,0:T(8,128)(2,1)S(1)} %pad_maximum_fusion.7), channel_id=1, source_target_pairs={{0,2},{1,3},{2,0},{3,1},{4,6},{5,7},{6,4},{7,5},{8,10},{9,11},{10,... | collective-permute-start | bytes 737288 | tf_op jit(solution)/shard_map/ppermute | solution.py:141
  47.2 9.9 %collective-permute-start.25 = (bf16[320,384]{1,0:T(8,128)(2,1)S(1)}, bf16[320,384]{1,0:T(8,128)(2,1)S(1)}, u32[]{:S(2)}, u32[]{:S(2)}) collective-permute-start(bf16[320,384]{1,0:T(8,128)(2,1)S(1)} %pad_maximum_fusion.8), channel_id=1, source_target_pairs={{0,1},{1,0},{2,3},{3,2},{4,5},{5,4},{6,7},{7,6},{8,9},{9,8},{10,11... | collective-permute-start | bytes 737288 | tf_op jit(solution)/shard_map/ppermute | solution.py:141
  49.2 11.3 %collective-permute-start.8 = (bf16[320,384]{1,0:T(8,128)(2,1)S(1)}, bf16[320,384]{1,0:T(8,128)(2,1)S(1)}, u32[]{:S(2)}, u32[]{:S(2)}) collective-permute-start(bf16[320,384]{1,0:T(8,128)(2,1)S(1)} %pad_maximum_fusion.3), channel_id=1, source_target_pairs={{0,2},{1,3},{2,0},{3,1},{4,6},{5,7},{6,4},{7,5},{8,10},{9,11},{10,... | collective-permute-start | bytes 737288 | tf_op jit(solution)/shard_map/ppermute | solution.py:141
  51.2 10.3 %collective-permute-start.10 = (bf16[320,384]{1,0:T(8,128)(2,1)S(1)}, bf16[320,384]{1,0:T(8,128)(2,1)S(1)}, u32[]{:S(2)}, u32[]{:S(2)}) collective-permute-start(bf16[320,384]{1,0:T(8,128)(2,1)S(1)} %pad_maximum_fusion.4), channel_id=1, source_target_pairs={{0,1},{1,0},{2,3},{3,2},{4,5},{5,4},{6,7},{7,6},{8,9},{9,8},{10,11... | collective-permute-start | bytes 737288 | tf_op jit(solution)/shard_map/ppermute | solution.py:141
  64.6 9.0 %collective-permute-start.26 = (bf16[320,384]{1,0:T(8,128)(2,1)S(1)}, bf16[320,384]{1,0:T(8,128)(2,1)S(1)}, u32[]{:S(2)}, u32[]{:S(2)}) collective-permute-start(bf16[320,384]{1,0:T(8,128)(2,1)S(1)} %pad_maximum_fusion.9), channel_id=1, source_target_pairs={{0,1},{1,0},{2,3},{3,2},{4,5},{5,4},{6,7},{7,6},{8,9},{9,8},{10,11... | collective-permute-start | bytes 737288 | tf_op jit(solution)/shard_map/ppermute | solution.py:124
  65.7 9.1 %collective-permute-start.28 = (bf16[320,384]{1,0:T(8,128)(2,1)S(1)}, bf16[320,384]{1,0:T(8,128)(2,1)S(1)}, u32[]{:S(2)}, u32[]{:S(2)}) collective-permute-start(bf16[320,384]{1,0:T(8,128)(2,1)S(1)} %pad_maximum_fusion.10), channel_id=1, source_target_pairs={{0,2},{1,3},{2,0},{3,1},{4,6},{5,7},{6,4},{7,5},{8,10},{9,11},{10,... | collective-permute-start | bytes 737288 | tf_op jit(solution)/shard_map/ppermute | solution.py:124
  67.3 11.4 %collective-permute-start.13 = (bf16[320,384]{1,0:T(8,128)(2,1)S(1)}, bf16[320,384]{1,0:T(8,128)(2,1)S(1)}, u32[]{:S(2)}, u32[]{:S(2)}) collective-permute-start(bf16[320,384]{1,0:T(8,128)(2,1)S(1)} %pad_maximum_fusion.6), channel_id=1, source_target_pairs={{0,2},{1,3},{2,0},{3,1},{4,6},{5,7},{6,4},{7,5},{8,10},{9,11},{10,... | collective-permute-start | bytes 737288 | tf_op jit(solution)/shard_map/ppermute | solution.py:124
  68.3 12.1 %collective-permute-start.11 = (bf16[320,384]{1,0:T(8,128)(2,1)S(1)}, bf16[320,384]{1,0:T(8,128)(2,1)S(1)}, u32[]{:S(2)}, u32[]{:S(2)}) collective-permute-start(bf16[320,384]{1,0:T(8,128)(2,1)S(1)} %pad_maximum_fusion.5), channel_id=1, source_target_pairs={{0,1},{1,0},{2,3},{3,2},{4,5},{5,4},{6,7},{7,6},{8,9},{9,8},{10,11... | collective-permute-start | bytes 737288 | tf_op jit(solution)/shard_map/ppermute | solution.py:124
  74.0 8.3 %collective-permute-start.27 = (bf16[160,384]{1,0:T(8,128)(2,1)S(1)}, bf16[160,384]{1,0:T(8,128)(2,1)S(1)}, u32[]{:S(2)}, u32[]{:S(2)}) collective-permute-start(bf16[160,384]{1,0:T(8,128)(2,1)S(1)} %add_convert_fusion.5), channel_id=1, source_target_pairs={{0,2},{1,3},{2,0},{3,1},{4,6},{5,7},{6,4},{7,5},{8,10},{9,11},{10,... | collective-permute-start | bytes 368648 | tf_op jit(solution)/shard_map/ppermute | solution.py:124
  75.2 7.1 %collective-permute-start.29 = (bf16[160,384]{1,0:T(8,128)(2,1)S(1)}, bf16[160,384]{1,0:T(8,128)(2,1)S(1)}, u32[]{:S(2)}, u32[]{:S(2)}) collective-permute-start(bf16[160,384]{1,0:T(8,128)(2,1)S(1)} %add_convert_fusion.3), channel_id=1, source_target_pairs={{0,1},{1,0},{2,3},{3,2},{4,5},{5,4},{6,7},{7,6},{8,9},{9,8},{10,11... | collective-permute-start | bytes 368648 | tf_op jit(solution)/shard_map/ppermute | solution.py:124
  79.1 6.5 %collective-permute-start.14 = (bf16[160,384]{1,0:T(8,128)(2,1)S(1)}, bf16[160,384]{1,0:T(8,128)(2,1)S(1)}, u32[]{:S(2)}, u32[]{:S(2)}) collective-permute-start(bf16[160,384]{1,0:T(8,128)(2,1)S(1)} %add_convert_fusion.7), channel_id=1, source_target_pairs={{0,1},{1,0},{2,3},{3,2},{4,5},{5,4},{6,7},{7,6},{8,9},{9,8},{10,11... | collective-permute-start | bytes 368648 | tf_op jit(solution)/shard_map/ppermute | solution.py:124
  82.4 12.5 %collective-permute-start.30 = (bf16[40,768]{1,0:T(8,128)(2,1)S(1)}, bf16[40,768]{1,0:T(8,128)(2,1)S(1)}, u32[]{:S(2)}, u32[]{:S(2)}) collective-permute-start(bf16[40,768]{1,0:T(8,128)(2,1)S(1)} %get-tuple-element.17), channel_id=1, source_target_pairs={{0,16},{4,20},{8,24},{12,28},{16,0},{20,4},{24,8},{28,12},{1,17},{... | collective-permute-start | bytes 184328 | tf_op jit(solution)/shard_map/ppermute | solution.py:168
  87.5 7.3 %collective-permute-start.17 = (bf16[40,768]{1,0:T(8,128)(2,1)S(1)}, bf16[40,768]{1,0:T(8,128)(2,1)S(1)}, u32[]{:S(2)}, u32[]{:S(2)}) collective-permute-start(bf16[40,768]{1,0:T(8,128)(2,1)S(1)} %get-tuple-element.22), channel_id=1, source_target_pairs={{0,12},{4,8},{8,4},{12,0},{16,28},{20,24},{24,20},{28,16},{1,13},{... | collective-permute-start | bytes 184328 | tf_op jit(solution)/shard_map/ppermute | solution.py:168
  87.7 7.2 %collective-permute-start.31 = (bf16[40,768]{1,0:T(8,128)(2,1)S(1)}, bf16[40,768]{1,0:T(8,128)(2,1)S(1)}, u32[]{:S(2)}, u32[]{:S(2)}) collective-permute-start(bf16[40,768]{1,0:T(8,128)(2,1)S(1)} %get-tuple-element.18), channel_id=1, source_target_pairs={{0,20},{4,16},{8,28},{12,24},{16,4},{20,0},{24,12},{28,8},{1,21},{... | collective-permute-start | bytes 184328 | tf_op jit(solution)/shard_map/ppermute | solution.py:168
  91.4 6.5 %collective-permute-start.32 = (bf16[40,768]{1,0:T(8,128)(2,1)S(1)}, bf16[40,768]{1,0:T(8,128)(2,1)S(1)}, u32[]{:S(2)}, u32[]{:S(2)}) collective-permute-start(bf16[40,768]{1,0:T(8,128)(2,1)S(1)} %get-tuple-element.19), channel_id=1, source_target_pairs={{0,24},{4,28},{8,16},{12,20},{16,8},{20,12},{24,0},{28,4},{1,25},{... | collective-permute-start | bytes 184328 | tf_op jit(solution)/shard_map/ppermute | solution.py:168
  (17 other events, 167.5 us)

commit v10 on v9

--- a/solution.py
+++ b/solution.py
@@ -241,18 +241,25 @@
             rows_in = jnp.concatenate(blocks, axis=0)
             held = all_gather_free([rows_in[:, :half], rows_in[:, half:]], "tensor", tensor_count)
             pre_act = None
-            for h in range(2):
-                for d in range(tensor_count):
-                    rows_w = lax.dynamic_slice_in_dim(projection, (me_t ^ d) * width + h * half, half, axis=0)
-                    term = jnp.dot(held[h][d], rows_w, preferred_element_type=jnp.float32)
-                    pre_act = term if pre_act is None else pre_act + term
+            for d in range(tensor_count):
+                rows_w = lax.dynamic_slice_in_dim(projection, (me_t ^ d) * width, width, axis=0)
+                both = jnp.concatenate([held[0][d], held[1][d]], axis=1)
+                term = jnp.dot(both, rows_w, preferred_element_type=jnp.float32)
+                pre_act = term if pre_act is None else pre_act + term
             pre_grad = (-slope_times(pre_act, jnp.broadcast_to(head_row, pre_act.shape))).astype(jnp.bfloat16)
 
-            def back_half(d, h, pre_grad=pre_grad):
-                rows_w = lax.dynamic_slice_in_dim(projection, (me_t ^ d) * width + h * half, half, axis=0)
-                return lax.dot_general(
-                    pre_grad, rows_w, (((1,), (1,)), ((), ())), preferred_element_type=jnp.float32
+            back_full = [
+                lax.dot_general(
+                    pre_grad,
+                    lax.dynamic_slice_in_dim(projection, (me_t ^ d) * width, width, axis=0),
+                    (((1,), (1,)), ((), ())),
+                    preferred_element_type=jnp.float32,
                 ).astype(jnp.bfloat16)
+                for d in range(tensor_count)
+            ]
+
+            def back_half(d, h, back_full=back_full):
+                return back_full[d][:, h * half:(h + 1) * half]
 
             grad = jnp.concatenate(
                 reduce_scatter_free(back_half, "tensor", tensor_count), axis=1

time: 101 us -> 99.9 us (0.989)
  waiting for transfers between devices: 26.8 us -> 33.3 us
  starting transfers between devices: 49.2 us -> 44.3 us
  matrix products: 16.5 us -> 13.3 us
    dot_general x32 -> x16, matrix products: 11.1 us -> 7.95 us  [the longest x8 4.45 us: shards(): lax.dot_general(pre_grad, lax.dynamic_slice_in_dim(projection, (me_t ^ d)...]
    ppermute x7, starting transfers between devices: 11 us -> 8.37 us  [dispatch_rows(): got.append(lax.ppermute(chunk, axis, [(i, i ^ s) for i in range(n)]))]
    ppermute x7, waiting for transfers between devices: 1.75 us -> 4.17 us  [dispatch_rows(): got.append(lax.ppermute(chunk, axis, [(i, i ^ s) for i in range(n)]))]
    ppermute x8, waiting for transfers between devices: 4.45 us -> 6.01 us  [all_gather_free(): got = lax.ppermute(payload, axis, [(i, i ^ bit) for i in range(n)])]
    ppermute x7, waiting for transfers between devices: 3.58 us -> 5.04 us  [collect_rows(): lax.ppermute(parts[s], axis, [(i, i ^ s) for i in range(n)])]
    ppermute x7, starting transfers between devices: 12.3 us -> 10.9 us  [collect_rows(): lax.ppermute(parts[s], axis, [(i, i ^ s) for i in range(n)])]
    ppermute x12, waiting for transfers between devices: 17 us -> 18.1 us  [reduce_scatter_free(): got = lax.ppermute(payload, axis, [(i, i ^ bit) for i in range(n)])]
  transfers between devices with their start and end apart: 34 -> 34, of which waited for: 13 -> 15; matrix products, arithmetic and copies ran while one was open for 11% -> 8% of each run, Pallas kernels for 0% -> 0%
where the time goes in v10:
time: 99.9 us; the launch traced here: 99.3 us
  starting transfers between devices  44.3 us (44%)
  waiting for transfers between devices  33.3 us (33%)
  matrix products  13.3 us (13%)
  other arithmetic  4.6 us (5%)
  local copies, waits for them, and re-layouts  2.55 us (3%)
  between operations  1.27 us (1%)
    ppermute x12, waiting for transfers between devices, reduce_scatter_free(): got = lax.ppermute(payload, axis, [(i, i ^ bit) for i in range(n)])  18.1 us
    ppermute x12, starting transfers between devices, reduce_scatter_free(): got = lax.ppermute(payload, axis, [(i, i ^ bit) for i in range(n)])  16.5 us
    ppermute x7, starting transfers between devices, collect_rows(): lax.ppermute(parts[s], axis, [(i, i ^ s) for i in range(n)])  10.9 us
    ppermute x8, starting transfers between devices, all_gather_free(): got = lax.ppermute(payload, axis, [(i, i ^ bit) for i in range(n)])  8.5 us
    ppermute x7, starting transfers between devices, dispatch_rows(): got.append(lax.ppermute(chunk, axis, [(i, i ^ s) for i in range(n)]))  8.37 us
    ppermute x8, waiting for transfers between devices, all_gather_free(): got = lax.ppermute(payload, axis, [(i, i ^ bit) for i in range(n)])  6.01 us
    ppermute x7, waiting for transfers between devices, collect_rows(): lax.ppermute(parts[s], axis, [(i, i ^ s) for i in range(n)])  5.04 us
    dot_general x8, matrix products, shards(): lax.dot_general(pre_grad, lax.dynamic_slice_in_dim(projection, (me_t ^ d)...  4.45 us
  transfers between devices with their start and end apart: 34, of which 15 were waited for; matrix products, arithmetic and copies ran while one was open for 8% of the time, Pallas kernels for 0%

profile of v10, /device:TPU:0, one launch (start us, length us, event | category | flops | bytes accessed | tf_op | source)
XLA Modules:
  0.0 99.3 jit_solution(471417207618347254)
XLA Ops:
  1.6 3.7 %convolution_convert_fusion = bf16[256,3072]{1,0:T(8,128)(2,1)S(1)} fusion(bf16[256,768]{1,0:T(8,128)(2,1)S(1)} %copy-done, bf16[768,3072]{1,0:T(8,128)(2,1)} %param.9), kind=kOutput, calls=%fused_computation.1 | convolution fusion | flops 1208745984 | bytes 6684672 | tf_op jit(solution)/shard_map/dot_general | solution.py:198
  6.4 3.0 %collective-permute-start.2 = (bf16[256,768]{1,0:T(8,128)(2,1)}, bf16[256,768]{1,0:T(8,128)(2,1)S(1)}, u32[]{:S(2)}, u32[]{:S(2)}) collective-permute-start(bf16[256,768]{1,0:T(8,128)(2,1)} %pad_maximum_fusion.1), channel_id=1, source_target_pairs={{0,2},{1,3},{2,0},{3,1},{4,6},{5,7},{6,4},{7,5},{8,10},{9,11},{10,... | collective-permute-start | bytes 1179656 | tf_op jit(solution)/shard_map/ppermute | solution.py:124
  10.1 1.5 %collective-permute-start = (bf16[256,768]{1,0:T(8,128)(2,1)}, bf16[256,768]{1,0:T(8,128)(2,1)S(1)}, u32[]{:S(2)}, u32[]{:S(2)}) collective-permute-start(bf16[256,768]{1,0:T(8,128)(2,1)} %pad_maximum_fusion), channel_id=1, source_target_pairs={{0,1},{1,0},{2,3},{3,2},{4,5},{5,4},{6,7},{7,6},{8,9},{9,8},{10,11... | collective-permute-start | bytes 1179656 | tf_op jit(solution)/shard_map/ppermute | solution.py:124
  12.9 5.7 %collective-permute-done.2 = bf16[256,768]{1,0:T(8,128)(2,1)S(1)} collective-permute-done((bf16[256,768]{1,0:T(8,128)(2,1)}, bf16[256,768]{1,0:T(8,128)(2,1)S(1)}, u32[]{:S(2)}, u32[]{:S(2)}) %collective-permute-start.2) | collective-permute-done | bytes 393248 | tf_op jit(solution)/shard_map/ppermute | solution.py:124
  18.7 1.8 %collective-permute-start.3 = (bf16[128,768]{1,0:T(8,128)(2,1)S(1)}, bf16[128,768]{1,0:T(8,128)(2,1)S(1)}, u32[]{:S(2)}, u32[]{:S(2)}) collective-permute-start(bf16[128,768]{1,0:T(8,128)(2,1)S(1)} %add_convert_fusion), channel_id=1, source_target_pairs={{0,1},{1,0},{2,3},{3,2},{4,5},{5,4},{6,7},{7,6},{8,9},{9,8},{10,11... | collective-permute-start | bytes 589832 | tf_op jit(solution)/shard_map/ppermute | solution.py:124
  22.1 3.0 %collective-permute-done.3 = bf16[128,768]{1,0:T(8,128)(2,1)S(1)} collective-permute-done((bf16[128,768]{1,0:T(8,128)(2,1)S(1)}, bf16[128,768]{1,0:T(8,128)(2,1)S(1)}, u32[]{:S(2)}, u32[]{:S(2)}) %collective-permute-start.3) | collective-permute-done | bytes 196640 | tf_op jit(solution)/shard_map/ppermute | solution.py:124
  25.2 1.7 %collective-permute-done.1 = bf16[128,768]{1,0:T(8,128)(2,1)S(1)} collective-permute-done((bf16[128,768]{1,0:T(8,128)(2,1)S(1)}, bf16[128,768]{1,0:T(8,128)(2,1)S(1)}, u32[]{:S(2)}, u32[]{:S(2)}) %collective-permute-start.1) | collective-permute-done | bytes 196640 | tf_op jit(solution)/shard_map/ppermute | solution.py:124
  28.9 1.8 %collective-permute-start.5 = (bf16[40,768]{1,0:T(8,128)(2,1)S(1)}, bf16[40,768]{1,0:T(8,128)(2,1)S(1)}, u32[]{:S(2)}, u32[]{:S(2)}) collective-permute-start(bf16[40,768]{1,0:T(8,128)(2,1)S(1)} %get-tuple-element.13), channel_id=1, source_target_pairs={{0,8},{4,12},{8,0},{12,4},{16,24},{20,28},{24,16},{28,20},{1,9},{5... | collective-permute-start | bytes 184328 | tf_op jit(solution)/shard_map/ppermute | solution.py:158
  30.7 2.7 %collective-permute-start.18 = (bf16[40,768]{1,0:T(8,128)(2,1)S(1)}, bf16[40,768]{1,0:T(8,128)(2,1)S(1)}, u32[]{:S(2)}, u32[]{:S(2)}) collective-permute-start(bf16[40,768]{1,0:T(8,128)(2,1)S(1)} %get-tuple-element.11), channel_id=1, source_target_pairs={{0,16},{4,20},{8,24},{12,28},{16,0},{20,4},{24,8},{28,12},{1,17},{... | collective-permute-start | bytes 184328 | tf_op jit(solution)/shard_map/ppermute | solution.py:158
  33.4 3.3 %collective-permute-start.20 = (bf16[40,768]{1,0:T(8,128)(2,1)S(1)}, bf16[40,768]{1,0:T(8,128)(2,1)S(1)}, u32[]{:S(2)}, u32[]{:S(2)}) collective-permute-start(bf16[40,768]{1,0:T(8,128)(2,1)S(1)} %get-tuple-element.9), channel_id=1, source_target_pairs={{0,24},{4,28},{8,16},{12,20},{16,8},{20,12},{24,0},{28,4},{1,25},{... | collective-permute-start | bytes 184328 | tf_op jit(solution)/shard_map/ppermute | solution.py:158
  39.0 4.2 %collective-permute-done.19 = bf16[40,768]{1,0:T(8,128)(2,1)S(1)} collective-permute-done((bf16[40,768]{1,0:T(8,128)(2,1)S(1)}, bf16[40,768]{1,0:T(8,128)(2,1)S(1)}, u32[]{:S(2)}, u32[]{:S(2)}) %collective-permute-start.19) | collective-permute-done | bytes 61472 | tf_op jit(solution)/shard_map/ppermute | solution.py:158
  47.6 1.5 %collective-permute-done.23 = bf16[160,384]{1,0:T(8,128)(2,1)S(1)} collective-permute-done((bf16[160,384]{1,0:T(8,128)(2,1)S(1)}, bf16[160,384]{1,0:T(8,128)(2,1)S(1)}, u32[]{:S(2)}, u32[]{:S(2)}) %collective-permute-start.23) | collective-permute-done | bytes 122912 | tf_op jit(solution)/shard_map/ppermute | solution.py:141
  49.1 2.0 %collective-permute-start.24 = (bf16[320,384]{1,0:T(8,128)(2,1)S(1)}, bf16[320,384]{1,0:T(8,128)(2,1)S(1)}, u32[]{:S(2)}, u32[]{:S(2)}) collective-permute-start(bf16[320,384]{1,0:T(8,128)(2,1)S(1)} %pad_maximum_fusion.7), channel_id=1, source_target_pairs={{0,1},{1,0},{2,3},{3,2},{4,5},{5,4},{6,7},{7,6},{8,9},{9,8},{10,11... | collective-permute-start | bytes 737288 | tf_op jit(solution)/shard_map/ppermute | solution.py:141
  51.6 3.9 %collective-permute-done.9 = bf16[320,384]{1,0:T(8,128)(2,1)S(1)} collective-permute-done((bf16[320,384]{1,0:T(8,128)(2,1)S(1)}, bf16[320,384]{1,0:T(8,128)(2,1)S(1)}, u32[]{:S(2)}, u32[]{:S(2)}) %collective-permute-start.9) | collective-permute-done | bytes 245792 | tf_op jit(solution)/shard_map/ppermute | solution.py:141
  65.2 1.6 %collective-permute-start.11 = (bf16[320,384]{1,0:T(8,128)(2,1)S(1)}, bf16[320,384]{1,0:T(8,128)(2,1)S(1)}, u32[]{:S(2)}, u32[]{:S(2)}) collective-permute-start(bf16[320,384]{1,0:T(8,128)(2,1)S(1)} %pad_maximum_fusion.5), channel_id=1, source_target_pairs={{0,1},{1,0},{2,3},{3,2},{4,5},{5,4},{6,7},{7,6},{8,9},{9,8},{10,11... | collective-permute-start | bytes 737288 | tf_op jit(solution)/shard_map/ppermute | solution.py:124
  68.9 3.9 %collective-permute-done.13 = bf16[320,384]{1,0:T(8,128)(2,1)S(1)} collective-permute-done((bf16[320,384]{1,0:T(8,128)(2,1)S(1)}, bf16[320,384]{1,0:T(8,128)(2,1)S(1)}, u32[]{:S(2)}, u32[]{:S(2)}) %collective-permute-start.13) | collective-permute-done | bytes 245792 | tf_op jit(solution)/shard_map/ppermute | solution.py:124
  74.2 1.6 %collective-permute-start.12 = (bf16[160,384]{1,0:T(8,128)(2,1)S(1)}, bf16[160,384]{1,0:T(8,128)(2,1)S(1)}, u32[]{:S(2)}, u32[]{:S(2)}) collective-permute-start(bf16[160,384]{1,0:T(8,128)(2,1)S(1)} %add_convert_fusion.9), channel_id=1, source_target_pairs={{0,2},{1,3},{2,0},{3,1},{4,6},{5,7},{6,4},{7,5},{8,10},{9,11},{10,... | collective-permute-start | bytes 368648 | tf_op jit(solution)/shard_map/ppermute | solution.py:124
  75.8 1.6 %collective-permute-done.28 = bf16[320,384]{1,0:T(8,128)(2,1)S(1)} collective-permute-done((bf16[320,384]{1,0:T(8,128)(2,1)S(1)}, bf16[320,384]{1,0:T(8,128)(2,1)S(1)}, u32[]{:S(2)}, u32[]{:S(2)}) %collective-permute-start.28) | collective-permute-done | bytes 245792 | tf_op jit(solution)/shard_map/ppermute | solution.py:124
  81.2 3.2 %collective-permute-start.16 = (bf16[40,768]{1,0:T(8,128)(2,1)S(1)}, bf16[40,768]{1,0:T(8,128)(2,1)S(1)}, u32[]{:S(2)}, u32[]{:S(2)}) collective-permute-start(bf16[40,768]{1,0:T(8,128)(2,1)S(1)} %get-tuple-element.32), channel_id=1, source_target_pairs={{0,8},{4,12},{8,0},{12,4},{16,24},{20,28},{24,16},{28,20},{1,9},{5... | collective-permute-start | bytes 184328 | tf_op jit(solution)/shard_map/ppermute | solution.py:168
  84.7 4.1 %collective-permute-start.30 = (bf16[40,768]{1,0:T(8,128)(2,1)S(1)}, bf16[40,768]{1,0:T(8,128)(2,1)S(1)}, u32[]{:S(2)}, u32[]{:S(2)}) collective-permute-start(bf16[40,768]{1,0:T(8,128)(2,1)S(1)} %get-tuple-element.17), channel_id=1, source_target_pairs={{0,16},{4,20},{8,24},{12,28},{16,0},{20,4},{24,8},{28,12},{1,17},{... | collective-permute-start | bytes 184328 | tf_op jit(solution)/shard_map/ppermute | solution.py:168
  88.8 1.4 %collective-permute-start.32 = (bf16[40,768]{1,0:T(8,128)(2,1)S(1)}, bf16[40,768]{1,0:T(8,128)(2,1)S(1)}, u32[]{:S(2)}, u32[]{:S(2)}) collective-permute-start(bf16[40,768]{1,0:T(8,128)(2,1)S(1)} %get-tuple-element.19), channel_id=1, source_target_pairs={{0,24},{4,28},{8,16},{12,20},{16,8},{20,12},{24,0},{28,4},{1,25},{... | collective-permute-start | bytes 184328 | tf_op jit(solution)/shard_map/ppermute | solution.py:168
  90.2 2.1 %collective-permute-start.33 = (bf16[40,768]{1,0:T(8,128)(2,1)S(1)}, bf16[40,768]{1,0:T(8,128)(2,1)S(1)}, u32[]{:S(2)}, u32[]{:S(2)}) collective-permute-start(bf16[40,768]{1,0:T(8,128)(2,1)S(1)} %get-tuple-element.16), channel_id=1, source_target_pairs={{0,28},{4,24},{8,20},{12,16},{16,12},{20,8},{24,4},{28,0},{1,29},{... | collective-permute-start | bytes 184328 | tf_op jit(solution)/shard_map/ppermute | solution.py:168
  92.3 2.7 %collective-permute-done.30 = bf16[40,768]{1,0:T(8,128)(2,1)S(1)} collective-permute-done((bf16[40,768]{1,0:T(8,128)(2,1)S(1)}, bf16[40,768]{1,0:T(8,128)(2,1)S(1)}, u32[]{:S(2)}, u32[]{:S(2)}) %collective-permute-start.30) | collective-permute-done | bytes 61472 | tf_op jit(solution)/shard_map/ppermute | solution.py:168
  95.0 2.4 %collective-permute-done.31 = bf16[40,768]{1,0:T(8,128)(2,1)S(1)} collective-permute-done((bf16[40,768]{1,0:T(8,128)(2,1)S(1)}, bf16[40,768]{1,0:T(8,128)(2,1)S(1)}, u32[]{:S(2)}, u32[]{:S(2)}) %collective-permute-start.31) | collective-permute-done | bytes 61472 | tf_op jit(solution)/shard_map/ppermute | solution.py:168
  (148 shorter events, 33.9 us)
Async XLA Ops:
  6.4 12.3 %collective-permute-start.2 = (bf16[256,768]{1,0:T(8,128)(2,1)}, bf16[256,768]{1,0:T(8,128)(2,1)S(1)}, u32[]{:S(2)}, u32[]{:S(2)}) collective-permute-start(bf16[256,768]{1,0:T(8,128)(2,1)} %pad_maximum_fusion.1), channel_id=1, source_target_pairs={{0,2},{1,3},{2,0},{3,1},{4,6},{5,7},{6,4},{7,5},{8,10},{9,11},{10,... | collective-permute-start | bytes 1179656 | tf_op jit(solution)/shard_map/ppermute | solution.py:124
  10.1 11.0 %collective-permute-start = (bf16[256,768]{1,0:T(8,128)(2,1)}, bf16[256,768]{1,0:T(8,128)(2,1)S(1)}, u32[]{:S(2)}, u32[]{:S(2)}) collective-permute-start(bf16[256,768]{1,0:T(8,128)(2,1)} %pad_maximum_fusion), channel_id=1, source_target_pairs={{0,1},{1,0},{2,3},{3,2},{4,5},{5,4},{6,7},{7,6},{8,9},{9,8},{10,11... | collective-permute-start | bytes 1179656 | tf_op jit(solution)/shard_map/ppermute | solution.py:124
  28.9 7.9 %collective-permute-start.5 = (bf16[40,768]{1,0:T(8,128)(2,1)S(1)}, bf16[40,768]{1,0:T(8,128)(2,1)S(1)}, u32[]{:S(2)}, u32[]{:S(2)}) collective-permute-start(bf16[40,768]{1,0:T(8,128)(2,1)S(1)} %get-tuple-element.13), channel_id=1, source_target_pairs={{0,8},{4,12},{8,0},{12,4},{16,24},{20,28},{24,16},{28,20},{1,9},{5... | collective-permute-start | bytes 184328 | tf_op jit(solution)/shard_map/ppermute | solution.py:158
  30.7 7.4 %collective-permute-start.18 = (bf16[40,768]{1,0:T(8,128)(2,1)S(1)}, bf16[40,768]{1,0:T(8,128)(2,1)S(1)}, u32[]{:S(2)}, u32[]{:S(2)}) collective-permute-start(bf16[40,768]{1,0:T(8,128)(2,1)S(1)} %get-tuple-element.11), channel_id=1, source_target_pairs={{0,16},{4,20},{8,24},{12,28},{16,0},{20,4},{24,8},{28,12},{1,17},{... | collective-permute-start | bytes 184328 | tf_op jit(solution)/shard_map/ppermute | solution.py:158
  33.4 9.8 %collective-permute-start.19 = (bf16[40,768]{1,0:T(8,128)(2,1)S(1)}, bf16[40,768]{1,0:T(8,128)(2,1)S(1)}, u32[]{:S(2)}, u32[]{:S(2)}) collective-permute-start(bf16[40,768]{1,0:T(8,128)(2,1)S(1)} %get-tuple-element.10), channel_id=1, source_target_pairs={{0,20},{4,16},{8,28},{12,24},{16,4},{20,0},{24,12},{28,8},{1,21},{... | collective-permute-start | bytes 184328 | tf_op jit(solution)/shard_map/ppermute | solution.py:158
  33.4 9.7 %collective-permute-start.20 = (bf16[40,768]{1,0:T(8,128)(2,1)S(1)}, bf16[40,768]{1,0:T(8,128)(2,1)S(1)}, u32[]{:S(2)}, u32[]{:S(2)}) collective-permute-start(bf16[40,768]{1,0:T(8,128)(2,1)S(1)} %get-tuple-element.9), channel_id=1, source_target_pairs={{0,24},{4,28},{8,16},{12,20},{16,8},{20,12},{24,0},{28,4},{1,25},{... | collective-permute-start | bytes 184328 | tf_op jit(solution)/shard_map/ppermute | solution.py:158
  37.2 7.8 %collective-permute-start.8 = (bf16[160,384]{1,0:T(8,128)(2,1)S(1)}, bf16[160,384]{1,0:T(8,128)(2,1)S(1)}, u32[]{:S(2)}, u32[]{:S(2)}) collective-permute-start(bf16[160,384]{1,0:T(8,128)(2,1)S(1)} %get-tuple-element.42), channel_id=1, source_target_pairs={{0,2},{1,3},{2,0},{3,1},{4,6},{5,7},{6,4},{7,5},{8,10},{9,11},{10,... | collective-permute-start | bytes 368648 | tf_op jit(solution)/shard_map/ppermute | solution.py:141
  38.1 8.1 %collective-permute-start.7 = (bf16[160,384]{1,0:T(8,128)(2,1)S(1)}, bf16[160,384]{1,0:T(8,128)(2,1)S(1)}, u32[]{:S(2)}, u32[]{:S(2)}) collective-permute-start(bf16[160,384]{1,0:T(8,128)(2,1)S(1)} %get-tuple-element.41), channel_id=1, source_target_pairs={{0,1},{1,0},{2,3},{3,2},{4,5},{5,4},{6,7},{7,6},{8,9},{9,8},{10,11... | collective-permute-start | bytes 368648 | tf_op jit(solution)/shard_map/ppermute | solution.py:141
  45.0 10.5 %collective-permute-start.9 = (bf16[320,384]{1,0:T(8,128)(2,1)S(1)}, bf16[320,384]{1,0:T(8,128)(2,1)S(1)}, u32[]{:S(2)}, u32[]{:S(2)}) collective-permute-start(bf16[320,384]{1,0:T(8,128)(2,1)S(1)} %pad_maximum_fusion.3), channel_id=1, source_target_pairs={{0,1},{1,0},{2,3},{3,2},{4,5},{5,4},{6,7},{7,6},{8,9},{9,8},{10,11... | collective-permute-start | bytes 737288 | tf_op jit(solution)/shard_map/ppermute | solution.py:141
  46.2 9.3 %collective-permute-start.10 = (bf16[320,384]{1,0:T(8,128)(2,1)S(1)}, bf16[320,384]{1,0:T(8,128)(2,1)S(1)}, u32[]{:S(2)}, u32[]{:S(2)}) collective-permute-start(bf16[320,384]{1,0:T(8,128)(2,1)S(1)} %pad_maximum_fusion.4), channel_id=1, source_target_pairs={{0,2},{1,3},{2,0},{3,1},{4,6},{5,7},{6,4},{7,5},{8,10},{9,11},{10,... | collective-permute-start | bytes 737288 | tf_op jit(solution)/shard_map/ppermute | solution.py:141
  49.1 10.6 %collective-permute-start.24 = (bf16[320,384]{1,0:T(8,128)(2,1)S(1)}, bf16[320,384]{1,0:T(8,128)(2,1)S(1)}, u32[]{:S(2)}, u32[]{:S(2)}) collective-permute-start(bf16[320,384]{1,0:T(8,128)(2,1)S(1)} %pad_maximum_fusion.7), channel_id=1, source_target_pairs={{0,1},{1,0},{2,3},{3,2},{4,5},{5,4},{6,7},{7,6},{8,9},{9,8},{10,11... | collective-permute-start | bytes 737288 | tf_op jit(solution)/shard_map/ppermute | solution.py:141
  51.1 9.2 %collective-permute-start.25 = (bf16[320,384]{1,0:T(8,128)(2,1)S(1)}, bf16[320,384]{1,0:T(8,128)(2,1)S(1)}, u32[]{:S(2)}, u32[]{:S(2)}) collective-permute-start(bf16[320,384]{1,0:T(8,128)(2,1)S(1)} %pad_maximum_fusion.8), channel_id=1, source_target_pairs={{0,2},{1,3},{2,0},{3,1},{4,6},{5,7},{6,4},{7,5},{8,10},{9,11},{10,... | collective-permute-start | bytes 737288 | tf_op jit(solution)/shard_map/ppermute | solution.py:141
  63.8 9.0 %collective-permute-start.13 = (bf16[320,384]{1,0:T(8,128)(2,1)S(1)}, bf16[320,384]{1,0:T(8,128)(2,1)S(1)}, u32[]{:S(2)}, u32[]{:S(2)}) collective-permute-start(bf16[320,384]{1,0:T(8,128)(2,1)S(1)} %pad_maximum_fusion.6), channel_id=1, source_target_pairs={{0,2},{1,3},{2,0},{3,1},{4,6},{5,7},{6,4},{7,5},{8,10},{9,11},{10,... | collective-permute-start | bytes 737288 | tf_op jit(solution)/shard_map/ppermute | solution.py:124
  65.2 9.0 %collective-permute-start.11 = (bf16[320,384]{1,0:T(8,128)(2,1)S(1)}, bf16[320,384]{1,0:T(8,128)(2,1)S(1)}, u32[]{:S(2)}, u32[]{:S(2)}) collective-permute-start(bf16[320,384]{1,0:T(8,128)(2,1)S(1)} %pad_maximum_fusion.5), channel_id=1, source_target_pairs={{0,1},{1,0},{2,3},{3,2},{4,5},{5,4},{6,7},{7,6},{8,9},{9,8},{10,11... | collective-permute-start | bytes 737288 | tf_op jit(solution)/shard_map/ppermute | solution.py:124
  66.9 10.5 %collective-permute-start.28 = (bf16[320,384]{1,0:T(8,128)(2,1)S(1)}, bf16[320,384]{1,0:T(8,128)(2,1)S(1)}, u32[]{:S(2)}, u32[]{:S(2)}) collective-permute-start(bf16[320,384]{1,0:T(8,128)(2,1)S(1)} %pad_maximum_fusion.10), channel_id=1, source_target_pairs={{0,2},{1,3},{2,0},{3,1},{4,6},{5,7},{6,4},{7,5},{8,10},{9,11},{10,... | collective-permute-start | bytes 737288 | tf_op jit(solution)/shard_map/ppermute | solution.py:124
  67.9 11.5 %collective-permute-start.26 = (bf16[320,384]{1,0:T(8,128)(2,1)S(1)}, bf16[320,384]{1,0:T(8,128)(2,1)S(1)}, u32[]{:S(2)}, u32[]{:S(2)}) collective-permute-start(bf16[320,384]{1,0:T(8,128)(2,1)S(1)} %pad_maximum_fusion.9), channel_id=1, source_target_pairs={{0,1},{1,0},{2,3},{3,2},{4,5},{5,4},{6,7},{7,6},{8,9},{9,8},{10,11... | collective-permute-start | bytes 737288 | tf_op jit(solution)/shard_map/ppermute | solution.py:124
  72.8 8.2 %collective-permute-start.14 = (bf16[160,384]{1,0:T(8,128)(2,1)S(1)}, bf16[160,384]{1,0:T(8,128)(2,1)S(1)}, u32[]{:S(2)}, u32[]{:S(2)}) collective-permute-start(bf16[160,384]{1,0:T(8,128)(2,1)S(1)} %add_convert_fusion.7), channel_id=1, source_target_pairs={{0,1},{1,0},{2,3},{3,2},{4,5},{5,4},{6,7},{7,6},{8,9},{9,8},{10,11... | collective-permute-start | bytes 368648 | tf_op jit(solution)/shard_map/ppermute | solution.py:124
  77.4 7.2 %collective-permute-start.29 = (bf16[160,384]{1,0:T(8,128)(2,1)S(1)}, bf16[160,384]{1,0:T(8,128)(2,1)S(1)}, u32[]{:S(2)}, u32[]{:S(2)}) collective-permute-start(bf16[160,384]{1,0:T(8,128)(2,1)S(1)} %add_convert_fusion.3), channel_id=1, source_target_pairs={{0,1},{1,0},{2,3},{3,2},{4,5},{5,4},{6,7},{7,6},{8,9},{9,8},{10,11... | collective-permute-start | bytes 368648 | tf_op jit(solution)/shard_map/ppermute | solution.py:124
  81.2 7.6 %collective-permute-start.15 = (bf16[40,768]{1,0:T(8,128)(2,1)S(1)}, bf16[40,768]{1,0:T(8,128)(2,1)S(1)}, u32[]{:S(2)}, u32[]{:S(2)}) collective-permute-start(bf16[40,768]{1,0:T(8,128)(2,1)S(1)} %get-tuple-element.31), channel_id=1, source_target_pairs={{0,4},{4,0},{8,12},{12,8},{16,20},{20,16},{24,28},{28,24},{1,5},{5... | collective-permute-start | bytes 184328 | tf_op jit(solution)/shard_map/ppermute | solution.py:168
  81.2 9.0 %collective-permute-start.16 = (bf16[40,768]{1,0:T(8,128)(2,1)S(1)}, bf16[40,768]{1,0:T(8,128)(2,1)S(1)}, u32[]{:S(2)}, u32[]{:S(2)}) collective-permute-start(bf16[40,768]{1,0:T(8,128)(2,1)S(1)} %get-tuple-element.32), channel_id=1, source_target_pairs={{0,8},{4,12},{8,0},{12,4},{16,24},{20,28},{24,16},{28,20},{1,9},{5... | collective-permute-start | bytes 184328 | tf_op jit(solution)/shard_map/ppermute | solution.py:168
  84.5 7.8 %collective-permute-start.17 = (bf16[40,768]{1,0:T(8,128)(2,1)S(1)}, bf16[40,768]{1,0:T(8,128)(2,1)S(1)}, u32[]{:S(2)}, u32[]{:S(2)}) collective-permute-start(bf16[40,768]{1,0:T(8,128)(2,1)S(1)} %get-tuple-element.30), channel_id=1, source_target_pairs={{0,12},{4,8},{8,4},{12,0},{16,28},{20,24},{24,20},{28,16},{1,13},{... | collective-permute-start | bytes 184328 | tf_op jit(solution)/shard_map/ppermute | solution.py:168
  84.7 10.3 %collective-permute-start.30 = (bf16[40,768]{1,0:T(8,128)(2,1)S(1)}, bf16[40,768]{1,0:T(8,128)(2,1)S(1)}, u32[]{:S(2)}, u32[]{:S(2)}) collective-permute-start(bf16[40,768]{1,0:T(8,128)(2,1)S(1)} %get-tuple-element.17), channel_id=1, source_target_pairs={{0,16},{4,20},{8,24},{12,28},{16,0},{20,4},{24,8},{28,12},{1,17},{... | collective-permute-start | bytes 184328 | tf_op jit(solution)/shard_map/ppermute | solution.py:168
  88.8 8.6 %collective-permute-start.31 = (bf16[40,768]{1,0:T(8,128)(2,1)S(1)}, bf16[40,768]{1,0:T(8,128)(2,1)S(1)}, u32[]{:S(2)}, u32[]{:S(2)}) collective-permute-start(bf16[40,768]{1,0:T(8,128)(2,1)S(1)} %get-tuple-element.18), channel_id=1, source_target_pairs={{0,20},{4,16},{8,28},{12,24},{16,4},{20,0},{24,12},{28,8},{1,21},{... | collective-permute-start | bytes 184328 | tf_op jit(solution)/shard_map/ppermute | solution.py:168
  88.8 8.5 %collective-permute-start.32 = (bf16[40,768]{1,0:T(8,128)(2,1)S(1)}, bf16[40,768]{1,0:T(8,128)(2,1)S(1)}, u32[]{:S(2)}, u32[]{:S(2)}) collective-permute-start(bf16[40,768]{1,0:T(8,128)(2,1)S(1)} %get-tuple-element.19), channel_id=1, source_target_pairs={{0,24},{4,28},{8,16},{12,20},{16,8},{20,12},{24,0},{28,4},{1,25},{... | collective-permute-start | bytes 184328 | tf_op jit(solution)/shard_map/ppermute | solution.py:168
  (17 other events, 189.4 us)

commit v11 on v10

--- a/solution.py
+++ b/solution.py
@@ -226,6 +226,9 @@
     head_row = member_head[0][None, :]
 
     if tree:
+        def proj_parts_of(d):
+            return lax.dynamic_slice_in_dim(projection, (me_t ^ d) * width, width, axis=0)
+
         rank_ok = rank_in < capacity
         slot_of = destination * capacity + rank_in
         placing = ((slot_of[:, None] == lax.iota(jnp.int32, group_count * capacity)[None, :])
@@ -239,31 +242,21 @@
         grads = []
         for blocks in waves:
             rows_in = jnp.concatenate(blocks, axis=0)
-            held = all_gather_free([rows_in[:, :half], rows_in[:, half:]], "tensor", tensor_count)
-            pre_act = None
-            for d in range(tensor_count):
-                rows_w = lax.dynamic_slice_in_dim(projection, (me_t ^ d) * width, width, axis=0)
-                both = jnp.concatenate([held[0][d], held[1][d]], axis=1)
-                term = jnp.dot(both, rows_w, preferred_element_type=jnp.float32)
-                pre_act = term if pre_act is None else pre_act + term
+            pre_act = jnp.dot(rows_in, proj_parts_of(0), preferred_element_type=jnp.float32)
+            for s in range(1, tensor_count):
+                got = lax.ppermute(rows_in, "tensor", pairs_for(s, tensor_count))
+                pre_act = pre_act + jnp.dot(got, proj_parts_of(s), preferred_element_type=jnp.float32)
             pre_grad = (-slope_times(pre_act, jnp.broadcast_to(head_row, pre_act.shape))).astype(jnp.bfloat16)
-
             back_full = [
                 lax.dot_general(
-                    pre_grad,
-                    lax.dynamic_slice_in_dim(projection, (me_t ^ d) * width, width, axis=0),
-                    (((1,), (1,)), ((), ())),
-                    preferred_element_type=jnp.float32,
+                    pre_grad, proj_parts_of(d), (((1,), (1,)), ((), ())), preferred_element_type=jnp.float32
                 ).astype(jnp.bfloat16)
                 for d in range(tensor_count)
             ]
-
-            def back_half(d, h, back_full=back_full):
-                return back_full[d][:, h * half:(h + 1) * half]
-
-            grad = jnp.concatenate(
-                reduce_scatter_free(back_half, "tensor", tensor_count), axis=1
-            ).astype(jnp.bfloat16)
+            grad = back_full[0].astype(jnp.float32)
+            for s in range(1, tensor_count):
+                grad = grad + lax.ppermute(back_full[s], "tensor", pairs_for(s, tensor_count)).astype(jnp.float32)
+            grad = grad.astype(jnp.bfloat16)
             grads.extend(jnp.split(grad, len(blocks), axis=0))
         returned = collect_rows(grads, "dp").reshape(group_count * capacity, width)
         input_grad = jnp.dot(placing, returned, preferred_element_type=jnp.float32)

time: 99.9 us -> 97.5 us (0.976)
  starting transfers between devices: 44.3 us -> 38.3 us
  waiting for transfers between devices: 33.3 us -> 37.9 us
    ppermute x8 -> x12, waiting for transfers between devices: 6.01 us -> 19.3 us  [the longest x6 12.6 us: shards(): lax.ppermute(back_full[s], 'tensor', pairs_for(s, tensor_count))]
    ppermute x12 -> x4, starting transfers between devices: 16.5 us -> 7.18 us  [reduce_scatter_free(): got = lax.ppermute(payload, axis, [(i, i ^ bit) for i in range(n)])]
    ppermute x8 -> x12, starting transfers between devices: 8.5 us -> 15.9 us  [the longest x6 8.25 us: shards(): got = lax.ppermute(rows_in, 'tensor', pairs_for(s, tensor_count))]
    ppermute x12 -> x4, waiting for transfers between devices: 18.1 us -> 11.1 us  [reduce_scatter_free(): got = lax.ppermute(payload, axis, [(i, i ^ bit) for i in range(n)])]
    ppermute x7, starting transfers between devices: 10.9 us -> 6.83 us  [collect_rows(): lax.ppermute(parts[s], axis, [(i, i ^ s) for i in range(n)])]
    ppermute x7, waiting for transfers between devices: 4.17 us -> 2.94 us  [dispatch_rows(): got.append(lax.ppermute(chunk, axis, [(i, i ^ s) for i in range(n)]))]
  transfers between devices with their start and end apart: 34 -> 30, of which waited for: 15 -> 13; matrix products, arithmetic and copies ran while one was open for 8% -> 11% of each run, Pallas kernels for 0% -> 0%
where the time goes in v11:
time: 97.5 us; the launch traced here: 96.7 us
  starting transfers between devices  38.3 us (39%)
  waiting for transfers between devices  37.9 us (39%)
  matrix products  13.2 us (14%)
  other arithmetic  3.84 us (4%)
  local copies, waits for them, and re-layouts  2.32 us (2%)
  between operations  1.09 us (1%)
    ppermute x6, waiting for transfers between devices, shards(): lax.ppermute(back_full[s], 'tensor', pairs_for(s, tensor_count))  12.6 us
    ppermute x4, waiting for transfers between devices, reduce_scatter_free(): got = lax.ppermute(payload, axis, [(i, i ^ bit) for i in range(n)])  11.1 us
    ppermute x7, starting transfers between devices, dispatch_rows(): got.append(lax.ppermute(chunk, axis, [(i, i ^ s) for i in range(n)]))  8.37 us
    ppermute x6, starting transfers between devices, shards(): got = lax.ppermute(rows_in, 'tensor', pairs_for(s, tensor_count))  8.25 us
    ppermute x6, starting transfers between devices, shards(): lax.ppermute(back_full[s], 'tensor', pairs_for(s, tensor_count))  7.63 us
    ppermute x4, starting transfers between devices, reduce_scatter_free(): got = lax.ppermute(payload, axis, [(i, i ^ bit) for i in range(n)])  7.18 us
    ppermute x7, starting transfers between devices, collect_rows(): lax.ppermute(parts[s], axis, [(i, i ^ s) for i in range(n)])  6.83 us
    ppermute x6, waiting for transfers between devices, shards(): got = lax.ppermute(rows_in, 'tensor', pairs_for(s, tensor_count))  6.7 us
  transfers between devices with their start and end apart: 30, of which 13 were waited for; matrix products, arithmetic and copies ran while one was open for 11% of the time, Pallas kernels for 0%

profile of v11, /device:TPU:0, one launch (start us, length us, event | category | flops | bytes accessed | tf_op | source)
XLA Modules:
  0.0 96.7 jit_solution(14440724533642429046)
XLA Ops:
  1.6 3.7 %convolution_convert_fusion = bf16[256,3072]{1,0:T(8,128)(2,1)S(1)} fusion(bf16[256,768]{1,0:T(8,128)(2,1)S(1)} %copy-done, bf16[768,3072]{1,0:T(8,128)(2,1)} %param.9), kind=kOutput, calls=%fused_computation.1 | convolution fusion | flops 1208745984 | bytes 6684672 | tf_op jit(solution)/shard_map/dot_general | solution.py:198
  6.4 3.0 %collective-permute-start.2 = (bf16[256,768]{1,0:T(8,128)(2,1)}, bf16[256,768]{1,0:T(8,128)(2,1)S(1)}, u32[]{:S(2)}, u32[]{:S(2)}) collective-permute-start(bf16[256,768]{1,0:T(8,128)(2,1)} %pad_maximum_fusion.1), channel_id=1, source_target_pairs={{0,2},{1,3},{2,0},{3,1},{4,6},{5,7},{6,4},{7,5},{8,10},{9,11},{10,... | collective-permute-start | bytes 1179656 | tf_op jit(solution)/shard_map/ppermute | solution.py:124
  10.1 1.5 %collective-permute-start = (bf16[256,768]{1,0:T(8,128)(2,1)}, bf16[256,768]{1,0:T(8,128)(2,1)S(1)}, u32[]{:S(2)}, u32[]{:S(2)}) collective-permute-start(bf16[256,768]{1,0:T(8,128)(2,1)} %pad_maximum_fusion), channel_id=1, source_target_pairs={{0,1},{1,0},{2,3},{3,2},{4,5},{5,4},{6,7},{7,6},{8,9},{9,8},{10,11... | collective-permute-start | bytes 1179656 | tf_op jit(solution)/shard_map/ppermute | solution.py:124
  13.0 5.7 %collective-permute-done.2 = bf16[256,768]{1,0:T(8,128)(2,1)S(1)} collective-permute-done((bf16[256,768]{1,0:T(8,128)(2,1)}, bf16[256,768]{1,0:T(8,128)(2,1)S(1)}, u32[]{:S(2)}, u32[]{:S(2)}) %collective-permute-start.2) | collective-permute-done | bytes 393248 | tf_op jit(solution)/shard_map/ppermute | solution.py:124
  18.7 1.8 %collective-permute-start.3 = (bf16[128,768]{1,0:T(8,128)(2,1)S(1)}, bf16[128,768]{1,0:T(8,128)(2,1)S(1)}, u32[]{:S(2)}, u32[]{:S(2)}) collective-permute-start(bf16[128,768]{1,0:T(8,128)(2,1)S(1)} %add_convert_fusion.2), channel_id=1, source_target_pairs={{0,1},{1,0},{2,3},{3,2},{4,5},{5,4},{6,7},{7,6},{8,9},{9,8},{10,11... | collective-permute-start | bytes 589832 | tf_op jit(solution)/shard_map/ppermute | solution.py:124
  22.1 3.0 %collective-permute-done.3 = bf16[128,768]{1,0:T(8,128)(2,1)S(1)} collective-permute-done((bf16[128,768]{1,0:T(8,128)(2,1)S(1)}, bf16[128,768]{1,0:T(8,128)(2,1)S(1)}, u32[]{:S(2)}, u32[]{:S(2)}) %collective-permute-start.3) | collective-permute-done | bytes 196640 | tf_op jit(solution)/shard_map/ppermute | solution.py:124
  25.2 1.7 %collective-permute-done.1 = bf16[128,768]{1,0:T(8,128)(2,1)S(1)} collective-permute-done((bf16[128,768]{1,0:T(8,128)(2,1)S(1)}, bf16[128,768]{1,0:T(8,128)(2,1)S(1)}, u32[]{:S(2)}, u32[]{:S(2)}) %collective-permute-start.1) | collective-permute-done | bytes 196640 | tf_op jit(solution)/shard_map/ppermute | solution.py:124
  28.7 1.8 %collective-permute-start.5 = (bf16[40,768]{1,0:T(8,128)(2,1)S(1)}, bf16[40,768]{1,0:T(8,128)(2,1)S(1)}, u32[]{:S(2)}, u32[]{:S(2)}) collective-permute-start(bf16[40,768]{1,0:T(8,128)(2,1)S(1)} %get-tuple-element.13), channel_id=1, source_target_pairs={{0,8},{4,12},{8,0},{12,4},{16,24},{20,28},{24,16},{28,20},{1,9},{5... | collective-permute-start | bytes 184328 | tf_op jit(solution)/shard_map/ppermute | solution.py:158
  30.5 2.7 %collective-permute-start.16 = (bf16[40,768]{1,0:T(8,128)(2,1)S(1)}, bf16[40,768]{1,0:T(8,128)(2,1)S(1)}, u32[]{:S(2)}, u32[]{:S(2)}) collective-permute-start(bf16[40,768]{1,0:T(8,128)(2,1)S(1)} %get-tuple-element.11), channel_id=1, source_target_pairs={{0,16},{4,20},{8,24},{12,28},{16,0},{20,4},{24,8},{28,12},{1,17},{... | collective-permute-start | bytes 184328 | tf_op jit(solution)/shard_map/ppermute | solution.py:158
  33.3 3.3 %collective-permute-start.18 = (bf16[40,768]{1,0:T(8,128)(2,1)S(1)}, bf16[40,768]{1,0:T(8,128)(2,1)S(1)}, u32[]{:S(2)}, u32[]{:S(2)}) collective-permute-start(bf16[40,768]{1,0:T(8,128)(2,1)S(1)} %get-tuple-element.9), channel_id=1, source_target_pairs={{0,24},{4,28},{8,16},{12,20},{16,8},{20,12},{24,0},{28,4},{1,25},{... | collective-permute-start | bytes 184328 | tf_op jit(solution)/shard_map/ppermute | solution.py:158
  38.2 1.8 %collective-permute-start.8 = (bf16[160,768]{1,0:T(8,128)(2,1)S(1)}, bf16[160,768]{1,0:T(8,128)(2,1)S(1)}, u32[]{:S(2)}, u32[]{:S(2)}) collective-permute-start(bf16[160,768]{1,0:T(8,128)(2,1)S(1)} %pad_maximum_fusion.2), channel_id=1, source_target_pairs={{0,2},{1,3},{2,0},{3,1},{4,6},{5,7},{6,4},{7,5},{8,10},{9,11},{10,... | collective-permute-start | bytes 737288 | tf_op jit(solution)/shard_map/ppermute | solution.py:247
  40.1 2.9 %collective-permute-done.17 = bf16[40,768]{1,0:T(8,128)(2,1)S(1)} collective-permute-done((bf16[40,768]{1,0:T(8,128)(2,1)S(1)}, bf16[40,768]{1,0:T(8,128)(2,1)S(1)}, u32[]{:S(2)}, u32[]{:S(2)}) %collective-permute-start.17) | collective-permute-done | bytes 61472 | tf_op jit(solution)/shard_map/ppermute | solution.py:158
  43.0 1.5 %collective-permute-start.7 = (bf16[160,768]{1,0:T(8,128)(2,1)S(1)}, bf16[160,768]{1,0:T(8,128)(2,1)S(1)}, u32[]{:S(2)}, u32[]{:S(2)}) collective-permute-start(bf16[160,768]{1,0:T(8,128)(2,1)S(1)} %pad_maximum_fusion.2), channel_id=1, source_target_pairs={{0,1},{1,0},{2,3},{3,2},{4,5},{5,4},{6,7},{7,6},{8,9},{9,8},{10,11... | collective-permute-start | bytes 737288 | tf_op jit(solution)/shard_map/ppermute | solution.py:247
  46.6 1.7 %collective-permute-start.20 = (bf16[160,768]{1,0:T(8,128)(2,1)S(1)}, bf16[160,768]{1,0:T(8,128)(2,1)S(1)}, u32[]{:S(2)}, u32[]{:S(2)}) collective-permute-start(bf16[160,768]{1,0:T(8,128)(2,1)S(1)} %constant_dynamic-update-slice_fusion), channel_id=1, source_target_pairs={{0,1},{1,0},{2,3},{3,2},{4,5},{5,4},{6,7},{7,6},{8,9},{9,8},{10,11... | collective-permute-start | bytes 737288 | tf_op jit(solution)/shard_map/ppermute | solution.py:247
  48.7 3.4 %collective-permute-done.8 = bf16[160,768]{1,0:T(8,128)(2,1)S(1)} collective-permute-done((bf16[160,768]{1,0:T(8,128)(2,1)S(1)}, bf16[160,768]{1,0:T(8,128)(2,1)S(1)}, u32[]{:S(2)}, u32[]{:S(2)}) %collective-permute-start.8) | collective-permute-done | bytes 245792 | tf_op jit(solution)/shard_map/ppermute | solution.py:247
  56.3 1.9 %collective-permute-start.11 = (bf16[160,768]{1,0:T(8,128)(2,1)S(1)}, bf16[160,768]{1,0:T(8,128)(2,1)S(1)}, u32[]{:S(2)}, u32[]{:S(2)}) collective-permute-start(bf16[160,768]{1,0:T(8,128)(2,1)S(1)} %convolution_convert_fusion.8), channel_id=1, source_target_pairs={{0,2},{1,3},{2,0},{3,1},{4,6},{5,7},{6,4},{7,5},{8,10},{9,11},{10,... | collective-permute-start | bytes 737288 | tf_op jit(solution)/shard_map/ppermute | solution.py:258
  59.2 3.3 %collective-permute-done.21 = bf16[160,768]{1,0:T(8,128)(2,1)S(1)} collective-permute-done((bf16[160,768]{1,0:T(8,128)(2,1)S(1)}, bf16[160,768]{1,0:T(8,128)(2,1)S(1)}, u32[]{:S(2)}, u32[]{:S(2)}) %collective-permute-start.21) | collective-permute-done | bytes 245792 | tf_op jit(solution)/shard_map/ppermute | solution.py:247
  66.3 1.8 %collective-permute-start.24 = (bf16[160,768]{1,0:T(8,128)(2,1)S(1)}, bf16[160,768]{1,0:T(8,128)(2,1)S(1)}, u32[]{:S(2)}, u32[]{:S(2)}) collective-permute-start(bf16[160,768]{1,0:T(8,128)(2,1)S(1)} %convolution_convert_fusion.4), channel_id=1, source_target_pairs={{0,2},{1,3},{2,0},{3,1},{4,6},{5,7},{6,4},{7,5},{8,10},{9,11},{10,... | collective-permute-start | bytes 737288 | tf_op jit(solution)/shard_map/ppermute | solution.py:258
  69.5 3.6 %collective-permute-done.11 = bf16[160,768]{1,0:T(8,128)(2,1)S(1)} collective-permute-done((bf16[160,768]{1,0:T(8,128)(2,1)S(1)}, bf16[160,768]{1,0:T(8,128)(2,1)S(1)}, u32[]{:S(2)}, u32[]{:S(2)}) %collective-permute-start.11) | collective-permute-done | bytes 245792 | tf_op jit(solution)/shard_map/ppermute | solution.py:258
  74.1 4.3 %collective-permute-done.25 = bf16[160,768]{1,0:T(8,128)(2,1)S(1)} collective-permute-done((bf16[160,768]{1,0:T(8,128)(2,1)S(1)}, bf16[160,768]{1,0:T(8,128)(2,1)S(1)}, u32[]{:S(2)}, u32[]{:S(2)}) %collective-permute-start.25) | collective-permute-done | bytes 245792 | tf_op jit(solution)/shard_map/ppermute | solution.py:258
  78.5 4.7 %collective-permute-done.24 = bf16[160,768]{1,0:T(8,128)(2,1)S(1)} collective-permute-done((bf16[160,768]{1,0:T(8,128)(2,1)S(1)}, bf16[160,768]{1,0:T(8,128)(2,1)S(1)}, u32[]{:S(2)}, u32[]{:S(2)}) %collective-permute-start.24) | collective-permute-done | bytes 245792 | tf_op jit(solution)/shard_map/ppermute | solution.py:258
  84.3 1.8 %collective-permute-start.27 = (bf16[40,768]{1,0:T(8,128)(2,1)S(1)}, bf16[40,768]{1,0:T(8,128)(2,1)S(1)}, u32[]{:S(2)}, u32[]{:S(2)}) collective-permute-start(bf16[40,768]{1,0:T(8,128)(2,1)S(1)} %get-tuple-element.18), channel_id=1, source_target_pairs={{0,20},{4,16},{8,28},{12,24},{16,4},{20,0},{24,12},{28,8},{1,21},{... | collective-permute-start | bytes 184328 | tf_op jit(solution)/shard_map/ppermute | solution.py:168
  86.1 3.0 %collective-permute-start.28 = (bf16[40,768]{1,0:T(8,128)(2,1)S(1)}, bf16[40,768]{1,0:T(8,128)(2,1)S(1)}, u32[]{:S(2)}, u32[]{:S(2)}) collective-permute-start(bf16[40,768]{1,0:T(8,128)(2,1)S(1)} %get-tuple-element.17), channel_id=1, source_target_pairs={{0,24},{4,28},{8,16},{12,20},{16,8},{20,12},{24,0},{28,4},{1,25},{... | collective-permute-start | bytes 184328 | tf_op jit(solution)/shard_map/ppermute | solution.py:168
  90.5 3.0 %collective-permute-done.27 = bf16[40,768]{1,0:T(8,128)(2,1)S(1)} collective-permute-done((bf16[40,768]{1,0:T(8,128)(2,1)S(1)}, bf16[40,768]{1,0:T(8,128)(2,1)S(1)}, u32[]{:S(2)}, u32[]{:S(2)}) %collective-permute-start.27) | collective-permute-done | bytes 61472 | tf_op jit(solution)/shard_map/ppermute | solution.py:168
  (114 shorter events, 28.8 us)
Async XLA Ops:
  6.4 12.3 %collective-permute-start.2 = (bf16[256,768]{1,0:T(8,128)(2,1)}, bf16[256,768]{1,0:T(8,128)(2,1)S(1)}, u32[]{:S(2)}, u32[]{:S(2)}) collective-permute-start(bf16[256,768]{1,0:T(8,128)(2,1)} %pad_maximum_fusion.1), channel_id=1, source_target_pairs={{0,2},{1,3},{2,0},{3,1},{4,6},{5,7},{6,4},{7,5},{8,10},{9,11},{10,... | collective-permute-start | bytes 1179656 | tf_op jit(solution)/shard_map/ppermute | solution.py:124
  10.1 11.0 %collective-permute-start = (bf16[256,768]{1,0:T(8,128)(2,1)}, bf16[256,768]{1,0:T(8,128)(2,1)S(1)}, u32[]{:S(2)}, u32[]{:S(2)}) collective-permute-start(bf16[256,768]{1,0:T(8,128)(2,1)} %pad_maximum_fusion), channel_id=1, source_target_pairs={{0,1},{1,0},{2,3},{3,2},{4,5},{5,4},{6,7},{7,6},{8,9},{9,8},{10,11... | collective-permute-start | bytes 1179656 | tf_op jit(solution)/shard_map/ppermute | solution.py:124
  28.7 7.9 %collective-permute-start.5 = (bf16[40,768]{1,0:T(8,128)(2,1)S(1)}, bf16[40,768]{1,0:T(8,128)(2,1)S(1)}, u32[]{:S(2)}, u32[]{:S(2)}) collective-permute-start(bf16[40,768]{1,0:T(8,128)(2,1)S(1)} %get-tuple-element.13), channel_id=1, source_target_pairs={{0,8},{4,12},{8,0},{12,4},{16,24},{20,28},{24,16},{28,20},{1,9},{5... | collective-permute-start | bytes 184328 | tf_op jit(solution)/shard_map/ppermute | solution.py:158
  30.5 7.7 %collective-permute-start.16 = (bf16[40,768]{1,0:T(8,128)(2,1)S(1)}, bf16[40,768]{1,0:T(8,128)(2,1)S(1)}, u32[]{:S(2)}, u32[]{:S(2)}) collective-permute-start(bf16[40,768]{1,0:T(8,128)(2,1)S(1)} %get-tuple-element.11), channel_id=1, source_target_pairs={{0,16},{4,20},{8,24},{12,28},{16,0},{20,4},{24,8},{28,12},{1,17},{... | collective-permute-start | bytes 184328 | tf_op jit(solution)/shard_map/ppermute | solution.py:158
  33.2 9.8 %collective-permute-start.17 = (bf16[40,768]{1,0:T(8,128)(2,1)S(1)}, bf16[40,768]{1,0:T(8,128)(2,1)S(1)}, u32[]{:S(2)}, u32[]{:S(2)}) collective-permute-start(bf16[40,768]{1,0:T(8,128)(2,1)S(1)} %get-tuple-element.10), channel_id=1, source_target_pairs={{0,20},{4,16},{8,28},{12,24},{16,4},{20,0},{24,12},{28,8},{1,21},{... | collective-permute-start | bytes 184328 | tf_op jit(solution)/shard_map/ppermute | solution.py:158
  33.3 11.2 %collective-permute-start.18 = (bf16[40,768]{1,0:T(8,128)(2,1)S(1)}, bf16[40,768]{1,0:T(8,128)(2,1)S(1)}, u32[]{:S(2)}, u32[]{:S(2)}) collective-permute-start(bf16[40,768]{1,0:T(8,128)(2,1)S(1)} %get-tuple-element.9), channel_id=1, source_target_pairs={{0,24},{4,28},{8,16},{12,20},{16,8},{20,12},{24,0},{28,4},{1,25},{... | collective-permute-start | bytes 184328 | tf_op jit(solution)/shard_map/ppermute | solution.py:158
  36.6 7.9 %collective-permute-start.19 = (bf16[40,768]{1,0:T(8,128)(2,1)S(1)}, bf16[40,768]{1,0:T(8,128)(2,1)S(1)}, u32[]{:S(2)}, u32[]{:S(2)}) collective-permute-start(bf16[40,768]{1,0:T(8,128)(2,1)S(1)} %get-tuple-element.8), channel_id=1, source_target_pairs={{0,28},{4,24},{8,20},{12,16},{16,12},{20,8},{24,4},{28,0},{1,29},{... | collective-permute-start | bytes 184328 | tf_op jit(solution)/shard_map/ppermute | solution.py:158
  37.0 9.6 %collective-permute-start.9 = (bf16[160,768]{1,0:T(8,128)(2,1)S(1)}, bf16[160,768]{1,0:T(8,128)(2,1)S(1)}, u32[]{:S(2)}, u32[]{:S(2)}) collective-permute-start(bf16[160,768]{1,0:T(8,128)(2,1)S(1)} %pad_maximum_fusion.2), channel_id=1, source_target_pairs={{0,3},{1,2},{2,1},{3,0},{4,7},{5,6},{6,5},{7,4},{8,11},{9,10},{10,... | collective-permute-start | bytes 737288 | tf_op jit(solution)/shard_map/ppermute | solution.py:247
  38.2 13.8 %collective-permute-start.8 = (bf16[160,768]{1,0:T(8,128)(2,1)S(1)}, bf16[160,768]{1,0:T(8,128)(2,1)S(1)}, u32[]{:S(2)}, u32[]{:S(2)}) collective-permute-start(bf16[160,768]{1,0:T(8,128)(2,1)S(1)} %pad_maximum_fusion.2), channel_id=1, source_target_pairs={{0,2},{1,3},{2,0},{3,1},{4,6},{5,7},{6,4},{7,5},{8,10},{9,11},{10,... | collective-permute-start | bytes 737288 | tf_op jit(solution)/shard_map/ppermute | solution.py:247
  43.0 9.4 %collective-permute-start.7 = (bf16[160,768]{1,0:T(8,128)(2,1)S(1)}, bf16[160,768]{1,0:T(8,128)(2,1)S(1)}, u32[]{:S(2)}, u32[]{:S(2)}) collective-permute-start(bf16[160,768]{1,0:T(8,128)(2,1)S(1)} %pad_maximum_fusion.2), channel_id=1, source_target_pairs={{0,1},{1,0},{2,3},{3,2},{4,5},{5,4},{6,7},{7,6},{8,9},{9,8},{10,11... | collective-permute-start | bytes 737288 | tf_op jit(solution)/shard_map/ppermute | solution.py:247
  44.5 13.7 %collective-permute-start.22 = (bf16[160,768]{1,0:T(8,128)(2,1)S(1)}, bf16[160,768]{1,0:T(8,128)(2,1)S(1)}, u32[]{:S(2)}, u32[]{:S(2)}) collective-permute-start(bf16[160,768]{1,0:T(8,128)(2,1)S(1)} %constant_dynamic-update-slice_fusion), channel_id=1, source_target_pairs={{0,3},{1,2},{2,1},{3,0},{4,7},{5,6},{6,5},{7,4},{8,11},{9,10},{10,... | collective-permute-start | bytes 737288 | tf_op jit(solution)/shard_map/ppermute | solution.py:247
  45.3 17.2 %collective-permute-start.21 = (bf16[160,768]{1,0:T(8,128)(2,1)S(1)}, bf16[160,768]{1,0:T(8,128)(2,1)S(1)}, u32[]{:S(2)}, u32[]{:S(2)}) collective-permute-start(bf16[160,768]{1,0:T(8,128)(2,1)S(1)} %constant_dynamic-update-slice_fusion), channel_id=1, source_target_pairs={{0,2},{1,3},{2,0},{3,1},{4,6},{5,7},{6,4},{7,5},{8,10},{9,11},{10,... | collective-permute-start | bytes 737288 | tf_op jit(solution)/shard_map/ppermute | solution.py:247
  46.6 16.3 %collective-permute-start.20 = (bf16[160,768]{1,0:T(8,128)(2,1)S(1)}, bf16[160,768]{1,0:T(8,128)(2,1)S(1)}, u32[]{:S(2)}, u32[]{:S(2)}) collective-permute-start(bf16[160,768]{1,0:T(8,128)(2,1)S(1)} %constant_dynamic-update-slice_fusion), channel_id=1, source_target_pairs={{0,1},{1,0},{2,3},{3,2},{4,5},{5,4},{6,7},{7,6},{8,9},{9,8},{10,11... | collective-permute-start | bytes 737288 | tf_op jit(solution)/shard_map/ppermute | solution.py:247
  55.1 13.6 %collective-permute-start.12 = (bf16[160,768]{1,0:T(8,128)(2,1)S(1)}, bf16[160,768]{1,0:T(8,128)(2,1)S(1)}, u32[]{:S(2)}, u32[]{:S(2)}) collective-permute-start(bf16[160,768]{1,0:T(8,128)(2,1)S(1)} %convolution_convert_fusion.7), channel_id=1, source_target_pairs={{0,3},{1,2},{2,1},{3,0},{4,7},{5,6},{6,5},{7,4},{8,11},{9,10},{10,... | collective-permute-start | bytes 737288 | tf_op jit(solution)/shard_map/ppermute | solution.py:258
  56.3 16.7 %collective-permute-start.11 = (bf16[160,768]{1,0:T(8,128)(2,1)S(1)}, bf16[160,768]{1,0:T(8,128)(2,1)S(1)}, u32[]{:S(2)}, u32[]{:S(2)}) collective-permute-start(bf16[160,768]{1,0:T(8,128)(2,1)S(1)} %convolution_convert_fusion.8), channel_id=1, source_target_pairs={{0,2},{1,3},{2,0},{3,1},{4,6},{5,7},{6,4},{7,5},{8,10},{9,11},{10,... | collective-permute-start | bytes 737288 | tf_op jit(solution)/shard_map/ppermute | solution.py:258
  58.2 14.8 %collective-permute-start.10 = (bf16[160,768]{1,0:T(8,128)(2,1)S(1)}, bf16[160,768]{1,0:T(8,128)(2,1)S(1)}, u32[]{:S(2)}, u32[]{:S(2)}) collective-permute-start(bf16[160,768]{1,0:T(8,128)(2,1)S(1)} %convolution_convert_fusion.9), channel_id=1, source_target_pairs={{0,1},{1,0},{2,3},{3,2},{4,5},{5,4},{6,7},{7,6},{8,9},{9,8},{10,11... | collective-permute-start | bytes 737288 | tf_op jit(solution)/shard_map/ppermute | solution.py:258
  65.0 13.4 %collective-permute-start.25 = (bf16[160,768]{1,0:T(8,128)(2,1)S(1)}, bf16[160,768]{1,0:T(8,128)(2,1)S(1)}, u32[]{:S(2)}, u32[]{:S(2)}) collective-permute-start(bf16[160,768]{1,0:T(8,128)(2,1)S(1)} %convolution_convert_fusion.3), channel_id=1, source_target_pairs={{0,3},{1,2},{2,1},{3,0},{4,7},{5,6},{6,5},{7,4},{8,11},{9,10},{10,... | collective-permute-start | bytes 737288 | tf_op jit(solution)/shard_map/ppermute | solution.py:258
  66.3 16.8 %collective-permute-start.24 = (bf16[160,768]{1,0:T(8,128)(2,1)S(1)}, bf16[160,768]{1,0:T(8,128)(2,1)S(1)}, u32[]{:S(2)}, u32[]{:S(2)}) collective-permute-start(bf16[160,768]{1,0:T(8,128)(2,1)S(1)} %convolution_convert_fusion.4), channel_id=1, source_target_pairs={{0,2},{1,3},{2,0},{3,1},{4,6},{5,7},{6,4},{7,5},{8,10},{9,11},{10,... | collective-permute-start | bytes 737288 | tf_op jit(solution)/shard_map/ppermute | solution.py:258
  68.7 14.5 %collective-permute-start.23 = (bf16[160,768]{1,0:T(8,128)(2,1)S(1)}, bf16[160,768]{1,0:T(8,128)(2,1)S(1)}, u32[]{:S(2)}, u32[]{:S(2)}) collective-permute-start(bf16[160,768]{1,0:T(8,128)(2,1)S(1)} %convolution_convert_fusion.5), channel_id=1, source_target_pairs={{0,1},{1,0},{2,3},{3,2},{4,5},{5,4},{6,7},{7,6},{8,9},{9,8},{10,11... | collective-permute-start | bytes 737288 | tf_op jit(solution)/shard_map/ppermute | solution.py:258
  73.6 12.5 %collective-permute-start.13 = (bf16[40,768]{1,0:T(8,128)(2,1)S(1)}, bf16[40,768]{1,0:T(8,128)(2,1)S(1)}, u32[]{:S(2)}, u32[]{:S(2)}) collective-permute-start(bf16[40,768]{1,0:T(8,128)(2,1)S(1)} %get-tuple-element.22), channel_id=1, source_target_pairs={{0,4},{4,0},{8,12},{12,8},{16,20},{20,16},{24,28},{28,24},{1,5},{5... | collective-permute-start | bytes 184328 | tf_op jit(solution)/shard_map/ppermute | solution.py:168
  73.7 15.5 %collective-permute-start.14 = (bf16[40,768]{1,0:T(8,128)(2,1)S(1)}, bf16[40,768]{1,0:T(8,128)(2,1)S(1)}, u32[]{:S(2)}, u32[]{:S(2)}) collective-permute-start(bf16[40,768]{1,0:T(8,128)(2,1)S(1)} %get-tuple-element.21), channel_id=1, source_target_pairs={{0,8},{4,12},{8,0},{12,4},{16,24},{20,28},{24,16},{28,20},{1,9},{5... | collective-permute-start | bytes 184328 | tf_op jit(solution)/shard_map/ppermute | solution.py:168
  78.5 11.6 %collective-permute-start.15 = (bf16[40,768]{1,0:T(8,128)(2,1)S(1)}, bf16[40,768]{1,0:T(8,128)(2,1)S(1)}, u32[]{:S(2)}, u32[]{:S(2)}) collective-permute-start(bf16[40,768]{1,0:T(8,128)(2,1)S(1)} %get-tuple-element.20), channel_id=1, source_target_pairs={{0,12},{4,8},{8,4},{12,0},{16,28},{20,24},{24,20},{28,16},{1,13},{... | collective-permute-start | bytes 184328 | tf_op jit(solution)/shard_map/ppermute | solution.py:168
  84.3 9.1 %collective-permute-start.27 = (bf16[40,768]{1,0:T(8,128)(2,1)S(1)}, bf16[40,768]{1,0:T(8,128)(2,1)S(1)}, u32[]{:S(2)}, u32[]{:S(2)}) collective-permute-start(bf16[40,768]{1,0:T(8,128)(2,1)S(1)} %get-tuple-element.18), channel_id=1, source_target_pairs={{0,20},{4,16},{8,28},{12,24},{16,4},{20,0},{24,12},{28,8},{1,21},{... | collective-permute-start | bytes 184328 | tf_op jit(solution)/shard_map/ppermute | solution.py:168
  86.1 7.3 %collective-permute-start.28 = (bf16[40,768]{1,0:T(8,128)(2,1)S(1)}, bf16[40,768]{1,0:T(8,128)(2,1)S(1)}, u32[]{:S(2)}, u32[]{:S(2)}) collective-permute-start(bf16[40,768]{1,0:T(8,128)(2,1)S(1)} %get-tuple-element.17), channel_id=1, source_target_pairs={{0,24},{4,28},{8,16},{12,20},{16,8},{20,12},{24,0},{28,4},{1,25},{... | collective-permute-start | bytes 184328 | tf_op jit(solution)/shard_map/ppermute | solution.py:168
  (13 other events, 160.1 us)
